TPU v7x, 32 devices: a whole 2x2x4 slice. The times are simulated.
32 devices in a mesh: grp: 8 (over y, x, core), mem: 4 (over z).
Axes of the slice: x: 2, y: 2, z: 4, core: 2. Of those that a mesh axis runs over, the one named last changes fastest.
Arguments:
- points: float32 [16, 32768], P(None, ('grp', 'mem')), may hold values from -6 to 6
- residual: float32 [16, 32768], P(None, ('grp', 'mem')), may hold values from -6 to 6
- coef: float32 [16, 32768], P(None, ('grp', 'mem')), may hold values from -3 to 3
- block_of: int32 [32768], P(('grp', 'mem')), may hold values from 0 to 7, as said below
- order: int32 [2], replicated, may hold values from 0 to 7
- inverse: float32 [8, 4096, 4096], P('grp', 'mem'), may hold values from -1 to 2
Outputs:
- residual_out: float32 [16, 32768], P(None, ('grp', 'mem'))
- coef_out: float32 [16, 32768], P(None, ('grp', 'mem'))
Inputs may be any that keep to these rules, and one draw needn't show every extreme that they name: `block_of`: each run of 1024 consecutive points (the points of one device) holds exactly 128 points of every block.
All inputs are finite; a program needn't handle non-finite values.
Results may differ from a plain program's by a relative error of at most 0.00013.
Values sent between devices are 32-bit elements; how exact they have to be, the bound alone decides.
No kernel may reach another device: no remote copies, remote signals or barrier semaphores. Data moves between devices by JAX's collectives and lax.ppermute only.
A program may use at most 128 MiB of HBM per device.

v0:
```python
import jax
import jax.numpy as jnp
from jax import lax
from jax.sharding import PartitionSpec as P

B = 4096
STEPS = 2


ridge_weight = 0.5
kernel_scale = 0.125


def from_root(value, axis, source):
    kept = jnp.where(lax.axis_index(axis) == source, value, 0).astype(value.dtype)
    return lax.psum(kept, axis)


def body(points, residual, coef, block_of, order, inverse):
    highest = lax.Precision.HIGHEST
    n_mem = lax.axis_size("mem")
    per = B // (lax.axis_size("grp") * n_mem)
    slots = inverse.shape[0]
    mine = lax.axis_index("grp") * n_mem + lax.axis_index("mem")
    norms_local = jnp.sum(points * points, axis=0)
    for step_index in range(STEPS):
        block_id = order[step_index]
        inside = block_of == block_id
        position = jnp.cumsum(inside.astype(jnp.int32)) - 1
        select = (
            (position[:, None] == jnp.arange(per, dtype=jnp.int32)[None, :]) & inside[:, None]
        ).astype(jnp.float32)
        chosen_res = jnp.dot(residual, select, precision=highest)
        chosen_pts = jnp.dot(points, select, precision=highest)
        block_res, block_pts = (
            lax.all_gather(chosen_res, ("grp", "mem"), axis=1, tiled=True),
            lax.all_gather(chosen_pts, ("grp", "mem"), axis=1, tiled=True),
        )
        matrix_rows = lax.dynamic_index_in_dim(inverse, block_id % slots, 0, keepdims=False)
        solved = lax.dot_general(
            block_res, matrix_rows, (((1,), (1,)), ((), ())), precision=highest
        )
        owner = block_id // slots
        norms_block = jnp.sum(block_pts * block_pts, axis=0)
        assembled = lax.all_gather(solved, "mem", axis=1, tiled=True)
        assembled = from_root(assembled, "grp", owner)
        width = assembled.shape[1]
        cross = lax.dot_general(points, block_pts, (((0,), (0,)), ((), ())), precision=highest)
        kernel = jnp.exp(
            -kernel_scale * (norms_local[:, None] + norms_block[None, :] - 2.0 * cross)
        )
        total_update = lax.dot_general(
            assembled, kernel, (((1,), (1,)), ((), ())), precision=highest
        )
        ranks = jnp.arange(width, dtype=jnp.int32)
        wanted = mine * per + jnp.arange(per, dtype=jnp.int32)
        picker = (ranks[:, None] == wanted[None, :]).astype(jnp.float32)
        owned = jnp.dot(assembled, picker, precision=highest)
        update, owned = (total_update, owned)
        spread_back = lax.dot_general(owned, select, (((1,), (1,)), ((), ())), precision=highest)
        residual = residual - update - ridge_weight * spread_back
        coef = coef + spread_back
    return (residual, coef)


def solution(mesh):
    in_specs = (
        P(None, ("grp", "mem")),
        P(None, ("grp", "mem")),
        P(None, ("grp", "mem")),
        P(("grp", "mem")),
        P(),
        P("grp", "mem", None),
    )
    out_specs = (P(None, ("grp", "mem")), P(None, ("grp", "mem")))
    return jax.shard_map(body, mesh=mesh, in_specs=in_specs, out_specs=out_specs, check_vma=False)
```

profile of v0, /device:TPU:0, one launch (start us, length us, event | category | flops | bytes accessed | tf_op | source)
XLA Modules:
  0.0 461.2 jit_solution(17110810315561444372)
XLA Ops:
  7.2 0.0 copy-start
  7.2 0.0 all-reduce.3.cloned.1.call-start
  7.2 1.3 fusion.67
  8.5 2.0 convert_bitcast_fusion
  10.5 0.3 reduce-window.16
  10.8 0.1 slice.21
  10.9 0.1 slice_reduce_fusion.1
  11.0 0.1 add_bitcast_fusion.1
  11.1 1.4 convolution_bitcast_fusion.2
  12.5 71.8 %all_gather.18 = f32[16,4096]{1,0:T(8,128)S(1)} all-gather(f32[16,128]{1,0:T(8,128)S(1)} %convolution_bitcast_fusion.2), channel_id=1, replica_groups=mesh['grp'=8,'mem'=4] {'grp','mem'}, dimensions={1}, use_global_device_ids=true | all-gather | bytes 270336 | tf_op jit(solution)/shard_map/all_gather | solution.py:36
  84.3 17.1 %fusion.10 = f32[16,1024]{1,0:T(8,128)S(1)} fusion(f32[16,4096]{1,0:T(8,128)S(1)} %all_gather.18, f32[1,1024,4096]{2,1,0:T(8,128)} %param.11), kind=kOutput, calls=%fused_computation.10 | convolution fusion | flops 805306368 | bytes 17104896 | tf_op jit(solution)/shard_map/dot_general | solution.py:40
  101.4 0.0 copy-start.1
  101.4 14.3 %all_gather.19 = f32[16,4096]{1,0:T(8,128)S(1)} all-gather(f32[16,1024]{1,0:T(8,128)S(1)} %fusion.10), channel_id=1, replica_groups=mesh['grp'=8,'mem'=4] {'mem'}, dimensions={1}, use_global_device_ids=true | all-gather | bytes 327680 | tf_op jit(solution)/shard_map/all_gather | solution.py:45
  116.4 0.7 broadcast_select_fusion.1
  117.1 0.0 all-reduce.3.cloned.1.call-update
  117.1 0.0 all-reduce.5.cloned.1.call-start
  117.2 0.0 copy-done
  117.2 0.5 convolution_bitcast_fusion.1
  117.7 65.6 %all_gather.20 = f32[16,4096]{1,0:T(8,128)S(1)} all-gather(f32[16,128]{1,0:T(8,128)S(1)} %convolution_bitcast_fusion.1), channel_id=1, replica_groups=mesh['grp'=8,'mem'=4] {'grp','mem'}, dimensions={1}, use_global_device_ids=true | all-gather | bytes 270336 | tf_op jit(solution)/shard_map/all_gather | solution.py:37
  183.3 15.9 %fusion.68 = f32[4096,1024]{1,0:T(8,128)} fusion(f32[16,4096]{1,0:T(8,128)S(1)} %all_gather.20, f32[16,1024]{1,0:T(8,128)S(1)} %copy-done), kind=kOutput, calls=%fused_computation.75 | convolution fusion | flops 805306368 | bytes 17104896 | tf_op jit(solution)/shard_map/dot_general | solution.py:48
  199.3 0.3 reduce-window.24
  199.5 0.1 slice.24
  199.6 0.1 slice_reduce_fusion
  199.8 0.1 add_bitcast_fusion
  199.8 0.5 convolution_bitcast_fusion
  201.0 67.7 %all_gather.23 = f32[16,4096]{1,0:T(8,128)S(1)} all-gather(f32[16,128]{1,0:T(8,128)S(1)} %convolution_bitcast_fusion), channel_id=1, replica_groups=mesh['grp'=8,'mem'=4] {'grp','mem'}, dimensions={1}, use_global_device_ids=true | all-gather | bytes 270336 | tf_op jit(solution)/shard_map/all_gather | solution.py:37
  268.7 0.0 all-reduce.3.cloned.1.call-done
  268.7 1.7 fusion.25
  270.5 1.2 fusion.41
  271.6 0.0 copy-done.1
  271.6 14.8 %fusion.29 = f32[16,1024]{1,0:T(8,128)S(1)} fusion(f32[16,1024]{1,0:T(8,128)S(1)} %copy-done.1, f32[16,4096]{1,0:T(8,128)} %all-reduce.3.cloned.1.call-done, f32[4096,1024]{1,0:T(8,128)} %fusion.68, f32[4096]{0:T(1024)S(1)} %multiply_reduce_fusion.1, f32[1024]{0:T(1024)S(1)} %multiply_reduce_fusion.2, f32[16,1024]{1,0:T(8,128)S(1)} %fusion.41), kind=kOutput, calls=%fused_computation.28 | convolution fusion | flops 822132736 | bytes 17256448 | tf_op jit(solution)/shard_map/dot_general | solution.py:52
  286.4 0.5 fusion.49
  286.9 65.5 %all_gather.21 = f32[16,4096]{1,0:T(8,128)S(1)} all-gather(f32[16,128]{1,0:T(8,128)S(1)} %fusion.49), channel_id=1, replica_groups=mesh['grp'=8,'mem'=4] {'grp','mem'}, dimensions={1}, use_global_device_ids=true | all-gather | bytes 270336 | tf_op jit(solution)/shard_map/all_gather | solution.py:36
  352.4 0.0 copy-start.2
  352.4 17.2 %fusion.8 = f32[16,1024]{1,0:T(8,128)S(1)} fusion(f32[16,4096]{1,0:T(8,128)S(1)} %all_gather.21, f32[1,1024,4096]{2,1,0:T(8,128)} %param.11), kind=kOutput, calls=%fused_computation.8 | convolution fusion | flops 805306368 | bytes 17104896 | tf_op jit(solution)/shard_map/dot_general | solution.py:40
  369.6 14.3 %all_gather.22 = f32[16,4096]{1,0:T(8,128)S(1)} all-gather(f32[16,1024]{1,0:T(8,128)S(1)} %fusion.8), channel_id=1, replica_groups=mesh['grp'=8,'mem'=4] {'mem'}, dimensions={1}, use_global_device_ids=true | all-gather | bytes 327680 | tf_op jit(solution)/shard_map/all_gather | solution.py:45
  383.9 0.7 broadcast_select_fusion
  384.6 0.0 all-reduce.5.cloned.1.call-update
  384.6 15.9 %fusion.69 = f32[4096,1024]{1,0:T(8,128)} fusion(f32[16,4096]{1,0:T(8,128)S(1)} %all_gather.23, f32[16,1024]{1,0:T(8,128)S(1)} %copy-done), kind=kOutput, calls=%fused_computation.76 | convolution fusion | flops 805306368 | bytes 17104896 | tf_op jit(solution)/shard_map/dot_general | solution.py:48
  400.6 35.4 %all-reduce.5.cloned.1.call-done = f32[16,4096]{1,0:T(8,128)} async-done(((f32[16,4096]{1,0:T(8,128)}), f32[16,4096]{1,0:T(8,128)}) %all-reduce.5.cloned.1.call-update) | async-done | bytes 262160 | tf_op jit(solution)/shard_map/psum | solution.py:16
  436.0 1.7 fusion.24
  437.8 0.0 copy-done.2
  437.8 1.2 add_add_fusion
  439.0 15.4 %fusion.35 = f32[16,1024]{1,0:T(8,128)} fusion(f32[16,1024]{1,0:T(8,128)S(1)} %fusion.29, f32[16,4096]{1,0:T(8,128)} %all-reduce.5.cloned.1.call-done, f32[4096,1024]{1,0:T(8,128)} %fusion.69, f32[4096]{0:T(1024)S(1)} %multiply_reduce_fusion, f32[1024]{0:T(1024)S(1)} %multiply_reduce_fusion.2, f32[16,1024]{1,0:T(8,128)S(1)} %get-tuple-element.11), kind=kOutput, calls=%fused_computation.30 | convolution fusion | flops 822132736 | bytes 17256448 | tf_op jit(solution)/shard_map/dot_general | solution.py:52
  (6 shorter events, 0.2 us)
Async XLA Ops:
  7.2 110.0 %copy-start = (f32[16,1024]{1,0:T(8,128)S(1)}, f32[16,1024]{1,0:T(8,128)}, u32[]{:S(2)}) copy-start(f32[16,1024]{1,0:T(8,128)} %param.6) | copy-start | bytes 196612
  7.2 261.5 %all-reduce.3.cloned.1.call-start = ((), (), s32[]{:S(2)}) async-start(), calls=%async_computation | async-start | bytes 524288 | tf_op jit(solution)/shard_map/psum | solution.py:16
  101.4 170.2 %copy-start.1 = (f32[16,1024]{1,0:T(8,128)S(1)}, f32[16,1024]{1,0:T(8,128)}, u32[]{:S(2)}) copy-start(f32[16,1024]{1,0:T(8,128)} %param.7) | copy-start | bytes 196612
  117.1 318.9 %all-reduce.5.cloned.1.call-start = ((), (), s32[]{:S(2)}) async-start(), calls=%async_computation.1 | async-start | bytes 524288 | tf_op jit(solution)/shard_map/psum | solution.py:16
  352.4 85.3 %copy-start.2 = (f32[16,1024]{1,0:T(8,128)S(1)}, f32[16,1024]{1,0:T(8,128)}, u32[]{:S(2)}) copy-start(f32[16,1024]{1,0:T(8,128)} %param.8) | copy-start | bytes 196612
Sparse Core Ops, SparseCore 0:
  117.3 49.9 all-reduce.2
  384.7 51.2 all-reduce.4
where the time goes:
time: 462 us; the launch traced here: 461 us
  blocking collectives  299 us (65%)
  matrix products  105 us (23%)
  waiting for transfers between devices  35.5 us (8%)
  between operations  15.5 us (3%)
    all_gather x2, blocking collectives, body(): lax.all_gather(chosen_res, ('grp', 'mem'), axis=1, tiled=True)  137 us
    all_gather x2, blocking collectives, body(): lax.all_gather(chosen_pts, ('grp', 'mem'), axis=1, tiled=True)  133 us
    psum x2, waiting for transfers between devices, from_root(): return lax.psum(kept, axis)  35.4 us
    dot_general x2, matrix products, body(): lax.dot_general(block_res, matrix_rows, (((1,), (1,)), ((), ())), precisi...  34.3 us
    dot_general x2, matrix products, body(): lax.dot_general(points, block_pts, (((0,), (0,)), ((), ())), precision=hi...  31.8 us
    dot_general x2, matrix products, body(): lax.dot_general(assembled, kernel, (((1,), (1,)), ((), ())), precision=hi...  30.2 us
    all_gather x2, blocking collectives, body(): assembled = lax.all_gather(solved, 'mem', axis=1, tiled=True)  28.6 us
  transfers between devices with their start and end apart: 2, of which 1 were waited for; matrix products, arithmetic and copies ran while one was open for 7% of the time, Pallas kernels for 0%

commit v1 on v0

v1 whole, which is shorter than its diff:
```python
import jax
import jax.numpy as jnp
from jax import lax
from jax.sharding import PartitionSpec as P

B = 4096
STEPS = 2

ridge_weight = 0.5
kernel_scale = 0.125
ALL = ("grp", "mem")


def gather_all(piece, n_dev):
    sent = jnp.broadcast_to(piece[None], (n_dev,) + piece.shape)
    return lax.all_to_all(sent, ALL, 0, 0, tiled=True)


def body(points, residual, coef, block_of, order, inverse):
    highest = lax.Precision.HIGHEST
    high = lax.Precision.HIGH
    n_grp = lax.axis_size("grp")
    n_mem = lax.axis_size("mem")
    n_dev = n_grp * n_mem
    per = B // n_dev
    chunk = B // n_mem
    slots = inverse.shape[0]
    feat = points.shape[0]
    rhs = residual.shape[0]
    mine = lax.axis_index("grp") * n_mem + lax.axis_index("mem")
    norms_local = jnp.sum(points * points, axis=0)
    for step_index in range(STEPS):
        block_id = order[step_index]
        inside = block_of == block_id
        position = jnp.cumsum(inside.astype(jnp.int32)) - 1
        select = (
            (position[:, None] == jnp.arange(per, dtype=jnp.int32)[None, :]) & inside[:, None]
        ).astype(jnp.float32)
        chosen = jnp.dot(jnp.concatenate([residual, points], axis=0), select, precision=highest)
        gathered = gather_all(chosen, n_dev)
        gathered = jnp.transpose(gathered, (1, 0, 2)).reshape(rhs + feat, B)
        block_res = gathered[:rhs]
        block_pts = gathered[rhs:]
        matrix_rows = lax.dynamic_index_in_dim(inverse, block_id % slots, 0, keepdims=False)
        solved = lax.dot_general(
            block_res, matrix_rows, (((1,), (1,)), ((), ())), precision=high
        )
        owner = block_id // slots
        pieces = jnp.transpose(solved.reshape(rhs, n_grp, per), (1, 0, 2))
        scattered = lax.all_to_all(pieces, "grp", 0, 0, tiled=True)
        piece = lax.dynamic_index_in_dim(scattered, owner, 0, keepdims=False)
        pieces_all = gather_all(piece, n_dev)
        pieces_all = jnp.transpose(pieces_all.reshape(n_grp, n_mem, rhs, per), (2, 1, 0, 3))
        delta = pieces_all.reshape(rhs, B)
        norms_block = jnp.sum(block_pts * block_pts, axis=0)
        cross = lax.dot_general(points, block_pts, (((0,), (0,)), ((), ())), precision=highest)
        kernel = jnp.exp(
            -kernel_scale * (norms_local[:, None] + norms_block[None, :] - 2.0 * cross)
        )
        update = lax.dot_general(delta, kernel, (((1,), (1,)), ((), ())), precision=high)
        owned = lax.dynamic_slice_in_dim(delta, mine * per, per, axis=1)
        spread_back = lax.dot_general(owned, select, (((1,), (1,)), ((), ())), precision=highest)
        residual = residual - update - ridge_weight * spread_back
        coef = coef + spread_back
    return (residual, coef)


def solution(mesh):
    in_specs = (
        P(None, ("grp", "mem")),
        P(None, ("grp", "mem")),
        P(None, ("grp", "mem")),
        P(("grp", "mem")),
        P(),
        P("grp", "mem", None),
    )
    out_specs = (P(None, ("grp", "mem")), P(None, ("grp", "mem")))
    return jax.shard_map(body, mesh=mesh, in_specs=in_specs, out_specs=out_specs, check_vma=False)
```

time: 462 us -> 153 us (0.33)
  blocking collectives: 299 us -> 20 us
  matrix products: 105 us -> 79.4 us
  starting transfers between devices: 0.08 us -> 20.2 us
  waiting for transfers between devices: 35.5 us -> 19.9 us
  between operations: 15.5 us -> 4.69 us
    all_gather x6 -> x0, blocking collectives: 299 us -> none  [the longest x2 137 us: body(): lax.all_gather(chosen_res, ('grp', 'mem'), axis=1, tiled=True)]
    psum x2 -> x0, waiting for transfers between devices: 35.4 us -> none  [from_root(): return lax.psum(kept, axis)]
    all_to_all x0 -> x5, starting transfers between devices: none -> 20.2 us  [the longest x3 13.1 us: gather_all(): return lax.all_to_all(sent, ALL, 0, 0, tiled=True)]
    all_to_all x0 -> x1, blocking collectives: none -> 20 us  [gather_all(): return lax.all_to_all(sent, ALL, 0, 0, tiled=True)]
    all_to_all x0 -> x5, waiting for transfers between devices: none -> 19.9 us  [the longest x3 11.9 us: gather_all(): return lax.all_to_all(sent, ALL, 0, 0, tiled=True)]
    dot_general x8 -> x4, matrix products: 36.5 us -> 23.7 us  [the longest x2 21.8 us: body(): lax.dot_general(delta, kernel, (((1,), (1,)), ((), ())), precision=high)]
    dot_general x2, matrix products: 34.3 us -> 21.6 us  [body(): lax.dot_general(block_res, matrix_rows, (((1,), (1,)), ((), ())), precisi...]
  transfers between devices with their start and end apart: 2 -> 5, of which waited for: 1 -> 3; matrix products, arithmetic and copies ran while one was open for 7% -> 21% of each run, Pallas kernels for 0% -> 0%
where the time goes in v1:
time: 153 us; the launch traced here: 152 us
  matrix products  79.4 us (52%)
  starting transfers between devices  20.2 us (13%)
  blocking collectives  20 us (13%)
  waiting for transfers between devices  19.9 us (13%)
  local copies, waits for them, and re-layouts  4.97 us (3%)
  between operations  4.69 us (3%)
  other arithmetic  2.89 us (2%)
    dot_general x2, matrix products, body(): lax.dot_general(points, block_pts, (((0,), (0,)), ((), ())), precision=hi...  31.8 us
    dot_general x2, matrix products, body(): lax.dot_general(delta, kernel, (((1,), (1,)), ((), ())), precision=high)  21.8 us
    dot_general x2, matrix products, body(): lax.dot_general(block_res, matrix_rows, (((1,), (1,)), ((), ())), precisi...  21.6 us
    all_to_all x1, blocking collectives, gather_all(): return lax.all_to_all(sent, ALL, 0, 0, tiled=True)  20 us
    all_to_all x3, starting transfers between devices, gather_all(): return lax.all_to_all(sent, ALL, 0, 0, tiled=True)  13.1 us
    all_to_all x3, waiting for transfers between devices, gather_all(): return lax.all_to_all(sent, ALL, 0, 0, tiled=True)  11.9 us
    all_to_all x2, waiting for transfers between devices, body(): scattered = lax.all_to_all(pieces, 'grp', 0, 0, tiled=True)  8.07 us
    all_to_all x2, starting transfers between devices, body(): scattered = lax.all_to_all(pieces, 'grp', 0, 0, tiled=True)  7.1 us
  transfers between devices with their start and end apart: 5, of which 3 were waited for; matrix products, arithmetic and copies ran while one was open for 21% of the time, Pallas kernels for 0%

profile of v1, /device:TPU:0, one launch (start us, length us, event | category | flops | bytes accessed | tf_op | source)
XLA Modules:
  0.0 152.2 jit_solution(10185112442205629938)
XLA Ops:
  0.6 0.0 copy-start
  0.6 1.3 fusion.70
  2.0 2.0 %convert_bitcast_fusion = (s32[8,128]{1,0:T(8,128)S(1)}, pred[1024]{0:T(1024)(128)(4,1)S(1)}, s32[8,128]{1,0:T(8,128)S(1)}, pred[1024]{0:T(1024)(128)(4,1)S(1)}) fusion(s32[1024]{0:T(1024)} %param.9, s32[]{:T(128)} %bitcast.11, s32[]{:T(128)} %bitcast), kind=kLoop, calls=%fused_computation.66 | loop fusion | flops 4096 | bytes 14344 | tf_op jit(solution)/shard_map/convert.1
  3.9 0.3 reduce-window.16
  4.2 0.1 slice.45
  4.3 0.1 slice_reduce_fusion.1
  4.4 0.1 add_bitcast_fusion.1
  4.5 1.4 fusion.35
  5.9 0.9 broadcast_in_dim.12
  6.8 7.3 %all-to-all-start = ((f32[32,32,128]{2,1,0:T(8,128)}), f32[32,32,128]{2,1,0:T(8,128)S(1)}, u32[]{:S(2)}, u32[]{:S(2)}) async-start(f32[32,32,128]{2,1,0:T(8,128)} %broadcast_in_dim.12), calls=%async_computation | async-start | bytes 1048576 | tf_op jit(solution)/shard_map/all_to_all | solution.py:16
  15.4 0.3 reduce-window.24
  15.7 0.1 slice.52
  16.4 0.1 slice_reduce_fusion
  16.5 0.1 add_bitcast_fusion
  16.6 11.8 %all-to-all-done = f32[32,32,128]{2,1,0:T(8,128)S(1)} async-done(((f32[32,32,128]{2,1,0:T(8,128)}), f32[32,32,128]{2,1,0:T(8,128)S(1)}, u32[]{:S(2)}, u32[]{:S(2)}) %all-to-all-start) | async-done | bytes 524320 | tf_op jit(solution)/shard_map/all_to_all | solution.py:16
  28.4 0.1 fusion.69
  28.5 0.1 copy.14
  28.6 0.1 reshape.103
  28.7 0.0 copy-start.1
  28.7 10.8 %convolution_bitcast_fusion.1 = f32[8,16,128]{2,1,0:T(8,128)} fusion(f32[16,4096,1]{1,0,2:T(8,128)S(1)} %reshape.103, f32[8,128,4096]{2,1,0:T(8,128)} %bitcast.79), kind=kOutput, calls=%fused_computation.21 | convolution fusion | flops 402653184 | bytes 17104896 | tf_op jit(solution)/shard_map/dot_general | solution.py:45
  39.5 3.5 %all-to-all-start.1 = ((f32[8,16,128]{2,1,0:T(8,128)}), f32[8,16,128]{2,1,0:T(8,128)S(1)}, u32[]{:S(2)}, u32[]{:S(2)}) async-start(f32[8,16,128]{2,1,0:T(8,128)} %convolution_bitcast_fusion.1), calls=%async_computation.1 | async-start | bytes 131072 | tf_op jit(solution)/shard_map/all_to_all | solution.py:50
  43.0 5.0 %all-to-all-done.1 = f32[8,16,128]{2,1,0:T(8,128)S(1)} async-done(((f32[8,16,128]{2,1,0:T(8,128)}), f32[8,16,128]{2,1,0:T(8,128)S(1)}, u32[]{:S(2)}, u32[]{:S(2)}) %all-to-all-start.1) | async-done | bytes 65568 | tf_op jit(solution)/shard_map/all_to_all | solution.py:50
  48.0 0.7 broadcast_in_dim.14
  48.7 2.9 %all-to-all-start.2 = ((f32[32,16,128]{2,1,0:T(8,128)}), f32[32,16,128]{2,1,0:T(8,128)S(1)}, u32[]{:S(2)}, u32[]{:S(2)}) async-start(f32[32,16,128]{2,1,0:T(8,128)} %broadcast_in_dim.14), calls=%async_computation.2 | async-start | bytes 524288 | tf_op jit(solution)/shard_map/all_to_all | solution.py:16
  51.7 15.9 %fusion.45 = f32[4096,1024]{1,0:T(8,128)} fusion(f32[16,1024]{1,0:T(8,128)S(1)} %copy-done, f32[32,2,8,128]{3,2,1,0:T(8,128)S(1)} %get-tuple-element.10), kind=kOutput, calls=%fused_computation.39 | convolution fusion | flops 805306368 | bytes 17104896 | tf_op jit(solution)/shard_map/dot_general | solution.py:56
  67.6 0.0 all-to-all-done.2
  67.6 0.2 copy.15
  67.7 0.2 copy.37
  67.9 1.2 fusion.33
  69.1 10.6 %fusion.23 = f32[16,1024]{1,0:T(8,128)S(1)} fusion(f32[16,1024]{1,0:T(8,128)S(1)} %copy-done.1, f32[4096,1024]{1,0:T(8,128)} %fusion.45, f32[4096]{0:T(1024)S(1)} %bitcast.92, f32[1024]{0:T(1024)S(1)} %multiply_reduce_fusion.2, f32[16,1024]{1,0:T(8,128)S(1)} %fusion.33, f32[2,8,32,128]{3,2,1,0:T(8,128)S(1)} %bitcast.88), kind=kOutput, calls=%fused_computation.23 | convolution fusion | flops 419479552 | bytes 17256448 | tf_op jit(solution)/shard_map/dot_general | solution.py:60
  79.7 0.5 fusion.40
  80.2 0.1 broadcast_in_dim.15
  80.3 20.0 %all_to_all.30 = f32[32,32,128]{2,1,0:T(8,128)S(1)} all-to-all(f32[32,32,128]{2,1,0:T(8,128)S(1)} %broadcast_in_dim.15), channel_id=1, replica_groups=mesh['grp'=8,'mem'=4] {'grp','mem'}, dimensions={0} | all-to-all | bytes 1048576 | tf_op jit(solution)/shard_map/all_to_all | solution.py:16
  100.3 0.1 fusion.68
  100.3 0.1 copy.17
  100.4 0.1 reshape.104
  100.5 0.0 copy-start.2
  100.5 10.8 %convolution_bitcast_fusion = f32[8,16,128]{2,1,0:T(8,128)} fusion(f32[16,4096,1]{1,0,2:T(8,128)S(1)} %reshape.104, f32[8,128,4096]{2,1,0:T(8,128)} %bitcast.80), kind=kOutput, calls=%fused_computation.20 | convolution fusion | flops 402653184 | bytes 17104896 | tf_op jit(solution)/shard_map/dot_general | solution.py:45
  111.3 3.5 %all-to-all-start.4 = ((f32[8,16,128]{2,1,0:T(8,128)}), f32[8,16,128]{2,1,0:T(8,128)S(1)}, u32[]{:S(2)}, u32[]{:S(2)}) async-start(f32[8,16,128]{2,1,0:T(8,128)} %convolution_bitcast_fusion), calls=%async_computation.4 | async-start | bytes 131072 | tf_op jit(solution)/shard_map/all_to_all | solution.py:50
  116.8 3.1 %all-to-all-done.4 = f32[8,16,128]{2,1,0:T(8,128)S(1)} async-done(((f32[8,16,128]{2,1,0:T(8,128)}), f32[8,16,128]{2,1,0:T(8,128)S(1)}, u32[]{:S(2)}, u32[]{:S(2)}) %all-to-all-start.4) | async-done | bytes 65568 | tf_op jit(solution)/shard_map/all_to_all | solution.py:50
  119.9 0.7 broadcast_in_dim.17
  120.6 2.9 %all-to-all-start.5 = ((f32[32,16,128]{2,1,0:T(8,128)}), f32[32,16,128]{2,1,0:T(8,128)S(1)}, u32[]{:S(2)}, u32[]{:S(2)}) async-start(f32[32,16,128]{2,1,0:T(8,128)} %broadcast_in_dim.17), calls=%async_computation.5 | async-start | bytes 524288 | tf_op jit(solution)/shard_map/all_to_all | solution.py:16
  123.5 15.9 %fusion.42 = f32[4096,1024]{1,0:T(8,128)} fusion(f32[16,1024]{1,0:T(8,128)S(1)} %copy-done, f32[32,2,8,128]{3,2,1,0:T(8,128)S(1)} %get-tuple-element.7), kind=kOutput, calls=%fused_computation.36 | convolution fusion | flops 805306368 | bytes 17104896 | tf_op jit(solution)/shard_map/dot_general | solution.py:56
  139.4 0.0 all-to-all-done.5
  139.4 0.2 copy.18
  139.5 0.2 copy.36
  139.7 1.2 add_add_fusion
  141.0 11.2 %fusion.29 = f32[16,1024]{1,0:T(8,128)} fusion(f32[16,1024]{1,0:T(8,128)S(1)} %fusion.23, f32[4096,1024]{1,0:T(8,128)} %fusion.42, f32[4096]{0:T(1024)S(1)} %bitcast.91, f32[1024]{0:T(1024)S(1)} %multiply_reduce_fusion.2, f32[16,1024]{1,0:T(8,128)S(1)} %get-tuple-element.17, f32[2,8,32,128]{3,2,1,0:T(8,128)S(1)} %bitcast.84), kind=kOutput, calls=%fused_computation.25 | convolution fusion | flops 419479552 | bytes 17256448 | tf_op jit(solution)/shard_map/dot_general | solution.py:60
  (8 shorter events, 0.1 us)
Async XLA Ops:
  0.6 42.4 %copy-start = (f32[16,1024]{1,0:T(8,128)S(1)}, f32[16,1024]{1,0:T(8,128)}, u32[]{:S(2)}) copy-start(f32[16,1024]{1,0:T(8,128)} %param.6) | copy-start | bytes 196612
  6.8 21.7 %all-to-all-start = ((f32[32,32,128]{2,1,0:T(8,128)}), f32[32,32,128]{2,1,0:T(8,128)S(1)}, u32[]{:S(2)}, u32[]{:S(2)}) async-start(f32[32,32,128]{2,1,0:T(8,128)} %broadcast_in_dim.12), calls=%async_computation | async-start | bytes 1048576 | tf_op jit(solution)/shard_map/all_to_all | solution.py:16
  28.7 40.4 %copy-start.1 = (f32[16,1024]{1,0:T(8,128)S(1)}, f32[16,1024]{1,0:T(8,128)}, u32[]{:S(2)}) copy-start(f32[16,1024]{1,0:T(8,128)} %param.7) | copy-start | bytes 196612
  39.5 8.6 %all-to-all-start.1 = ((f32[8,16,128]{2,1,0:T(8,128)}), f32[8,16,128]{2,1,0:T(8,128)S(1)}, u32[]{:S(2)}, u32[]{:S(2)}) async-start(f32[8,16,128]{2,1,0:T(8,128)} %convolution_bitcast_fusion.1), calls=%async_computation.1 | async-start | bytes 131072 | tf_op jit(solution)/shard_map/all_to_all | solution.py:50
  48.7 18.8 %all-to-all-start.2 = ((f32[32,16,128]{2,1,0:T(8,128)}), f32[32,16,128]{2,1,0:T(8,128)S(1)}, u32[]{:S(2)}, u32[]{:S(2)}) async-start(f32[32,16,128]{2,1,0:T(8,128)} %broadcast_in_dim.14), calls=%async_computation.2 | async-start | bytes 524288 | tf_op jit(solution)/shard_map/all_to_all | solution.py:16
  100.5 39.2 %copy-start.2 = (f32[16,1024]{1,0:T(8,128)S(1)}, f32[16,1024]{1,0:T(8,128)}, u32[]{:S(2)}) copy-start(f32[16,1024]{1,0:T(8,128)} %param.8) | copy-start | bytes 196612
  111.3 8.6 %all-to-all-start.4 = ((f32[8,16,128]{2,1,0:T(8,128)}), f32[8,16,128]{2,1,0:T(8,128)S(1)}, u32[]{:S(2)}, u32[]{:S(2)}) async-start(f32[8,16,128]{2,1,0:T(8,128)} %convolution_bitcast_fusion), calls=%async_computation.4 | async-start | bytes 131072 | tf_op jit(solution)/shard_map/all_to_all | solution.py:50
  120.6 18.8 %all-to-all-start.5 = ((f32[32,16,128]{2,1,0:T(8,128)}), f32[32,16,128]{2,1,0:T(8,128)S(1)}, u32[]{:S(2)}, u32[]{:S(2)}) async-start(f32[32,16,128]{2,1,0:T(8,128)} %broadcast_in_dim.17), calls=%async_computation.5 | async-start | bytes 524288 | tf_op jit(solution)/shard_map/all_to_all | solution.py:16

commit v2 on v1

v2 whole, which is shorter than its diff:
```python
import jax
import jax.numpy as jnp
from jax import lax
from jax.sharding import PartitionSpec as P

B = 4096
STEPS = 2

ridge_weight = 0.5
kernel_scale = 0.125
ALL = ("grp", "mem")
HIGHEST = lax.Precision.HIGHEST
HIGH = lax.Precision.HIGH


def gather_all(piece, n_dev):
    sent = jnp.broadcast_to(piece[None], (n_dev,) + piece.shape)
    return lax.all_to_all(sent, ALL, 0, 0, tiled=True)


def split3(x):
    x1 = lax.reduce_precision(x, exponent_bits=8, mantissa_bits=7)
    r1 = x - x1
    x2 = lax.reduce_precision(r1, exponent_bits=8, mantissa_bits=7)
    r2 = r1 - x2
    return x1.astype(jnp.bfloat16), x2.astype(jnp.bfloat16), r2.astype(jnp.bfloat16)


def kern(u, v):
    nu = jnp.sum(u * u, axis=0, keepdims=True)
    nv = jnp.sum(v * v, axis=0, keepdims=True)
    u1, u2, u3 = split3(u)
    v1, v2, v3 = split3(-2.0 * v)
    a1, a2, a3 = split3(nu)
    b1, b2, b3 = split3(nv)
    one_u = jnp.ones_like(a1)
    one_v = jnp.ones_like(b1)
    left = jnp.concatenate([u1, u1, u2, u1, u3, u2, a1, a2, a3, one_u, one_u, one_u], axis=0)
    right = jnp.concatenate([v1, v2, v1, v3, v1, v2, one_v, one_v, one_v, b1, b2, b3], axis=0)
    dist = lax.dot_general(left, right, (((0,), (0,)), ((), ())), preferred_element_type=jnp.float32)
    return jnp.exp(-kernel_scale * dist)


def apply_kernel(delta, kernel):
    return lax.dot_general(delta, kernel, (((1,), (1,)), ((), ())), precision=HIGH)


def body(points, residual, coef, block_of, order, inverse):
    n_grp = lax.axis_size("grp")
    n_mem = lax.axis_size("mem")
    n_dev = n_grp * n_mem
    per = B // n_dev
    slots = inverse.shape[0]
    feat = points.shape[0]
    rhs = residual.shape[0]
    mine = lax.axis_index("grp") * n_mem + lax.axis_index("mem")

    def selector(block_id):
        inside = block_of == block_id
        position = jnp.cumsum(inside.astype(jnp.int32)) - 1
        return (
            (position[:, None] == jnp.arange(per, dtype=jnp.int32)[None, :]) & inside[:, None]
        ).astype(jnp.float32)

    def solve(block_res, block_id):
        matrix_rows = lax.dynamic_index_in_dim(inverse, block_id % slots, 0, keepdims=False)
        solved = lax.dot_general(
            block_res, matrix_rows, (((1,), (1,)), ((), ())), precision=HIGH
        )
        owner = block_id // slots
        pieces = jnp.transpose(solved.reshape(rhs, n_grp, per), (1, 0, 2))
        scattered = lax.all_to_all(pieces, "grp", 0, 0, tiled=True)
        piece = lax.dynamic_index_in_dim(scattered, owner, 0, keepdims=False)
        pieces_all = gather_all(piece, n_dev)
        pieces_all = jnp.transpose(pieces_all.reshape(n_grp, n_mem, rhs, per), (2, 1, 0, 3))
        return pieces_all.reshape(rhs, B)

    def to_block(gathered, rows):
        return jnp.transpose(gathered, (1, 0, 2)).reshape(rows, B)

    block0, block1 = order[0], order[1]
    sel0 = selector(block0)
    sel1 = selector(block1)
    chosen0 = jnp.dot(jnp.concatenate([residual, points], axis=0), sel0, precision=HIGHEST)
    chosen1 = jnp.dot(jnp.concatenate([residual, points], axis=0), sel1, precision=HIGHEST)
    res1_start = chosen1[:rhs]
    pts1_local = chosen1[rhs:]
    gathered = to_block(gather_all(jnp.concatenate([chosen0, pts1_local], axis=0), n_dev), rhs + 2 * feat)
    block_res0 = gathered[:rhs]
    block_pts0 = gathered[rhs:rhs + feat]
    block_pts1 = gathered[rhs + feat:]

    delta0 = solve(block_res0, block0)
    owned0 = lax.dynamic_slice_in_dim(delta0, mine * per, per, axis=1)
    early = apply_kernel(delta0, kern(pts1_local, block_pts0))
    overlap = jnp.dot(sel0.T, sel1, precision=HIGHEST)
    res1_local = res1_start - early - ridge_weight * jnp.dot(owned0, overlap, precision=HIGHEST)
    block_res1 = to_block(gather_all(res1_local, n_dev), rhs)

    spread0 = lax.dot_general(owned0, sel0, (((1,), (1,)), ((), ())), precision=HIGHEST)
    update0 = apply_kernel(delta0, kern(points, block_pts0))
    residual = residual - update0 - ridge_weight * spread0
    coef = coef + spread0
    kernel1 = kern(points, block_pts1)

    delta1 = solve(block_res1, block1)
    owned1 = lax.dynamic_slice_in_dim(delta1, mine * per, per, axis=1)
    spread1 = lax.dot_general(owned1, sel1, (((1,), (1,)), ((), ())), precision=HIGHEST)
    update1 = apply_kernel(delta1, kernel1)
    residual = residual - update1 - ridge_weight * spread1
    coef = coef + spread1
    return (residual, coef)


def solution(mesh):
    in_specs = (
        P(None, ("grp", "mem")),
        P(None, ("grp", "mem")),
        P(None, ("grp", "mem")),
        P(("grp", "mem")),
        P(),
        P("grp", "mem", None),
    )
    out_specs = (P(None, ("grp", "mem")), P(None, ("grp", "mem")))
    return jax.shard_map(body, mesh=mesh, in_specs=in_specs, out_specs=out_specs, check_vma=False)
```

time: 153 us -> 151 us (0.987)
  blocking collectives: 20 us -> 0 us
  waiting for transfers between devices: 19.9 us -> 31.8 us
  matrix products: 79.4 us -> 69.3 us
  local copies, waits for them, and re-layouts: 4.97 us -> 13 us
  starting transfers between devices: 20.2 us -> 24.9 us
  other arithmetic: 2.89 us -> 6.01 us
    all_to_all x1 -> x0, blocking collectives: 20 us -> none  [gather_all(): return lax.all_to_all(sent, ALL, 0, 0, tiled=True)]
    all_to_all x3 -> x4, waiting for transfers between devices: 11.9 us -> 27.6 us  [gather_all(): return lax.all_to_all(sent, ALL, 0, 0, tiled=True)]
    dot_general x10 -> x14, matrix products: 79.4 us -> 69.3 us  [the longest x3 23.6 us: apply_kernel(): lax.dot_general(delta, kernel, (((1,), (1,)), ((), ())), precision=HIGH)]
    concatenate x0 -> x5, local copies, waits for them, and re-layouts: none -> 4.53 us  [the longest x3 4.24 us: kern(): jnp.concatenate([u1, u1, u2, u1, u3, u2, a1, a2, a3, one_u, one_u, one_u]...]
    all_to_all x3 -> x4, starting transfers between devices: 13.1 us -> 17.5 us  [gather_all(): return lax.all_to_all(sent, ALL, 0, 0, tiled=True)]
    all_to_all x2, waiting for transfers between devices: 8.07 us -> 4.21 us  [solve(): scattered = lax.all_to_all(pieces, 'grp', 0, 0, tiled=True)]
    unnamed x8 -> x35, local copies, waits for them, and re-layouts: 0.33 us -> 2.15 us
    convert_element_type x0 -> x5, other arithmetic: none -> 1.63 us  [split3(): r2.astype(jnp.bfloat16)]
  transfers between devices with their start and end apart: 5 -> 6, of which waited for: 3 -> 5; matrix products, arithmetic and copies ran while one was open for 21% -> 18% of each run, Pallas kernels for 0% -> 0%
where the time goes in v2:
time: 151 us; the launch traced here: 150 us
  matrix products  69.3 us (46%)
  waiting for transfers between devices  31.8 us (21%)
  starting transfers between devices  24.9 us (16%)
  local copies, waits for them, and re-layouts  13 us (9%)
  other arithmetic  6.01 us (4%)
  between operations  4.85 us (3%)
    all_to_all x4, waiting for transfers between devices, gather_all(): return lax.all_to_all(sent, ALL, 0, 0, tiled=True)  27.6 us
    dot_general x3, matrix products, apply_kernel(): lax.dot_general(delta, kernel, (((1,), (1,)), ((), ())), precision=HIGH)  23.6 us
    dot_general x2, matrix products, solve(): lax.dot_general(block_res, matrix_rows, (((1,), (1,)), ((), ())), precisi...  21.5 us
    all_to_all x4, starting transfers between devices, gather_all(): return lax.all_to_all(sent, ALL, 0, 0, tiled=True)  17.5 us
    dot_general x3, matrix products, kern(): lax.dot_general(left, right, (((0,), (0,)), ((), ())), preferred_element_...  17.4 us
    all_to_all x2, starting transfers between devices, solve(): scattered = lax.all_to_all(pieces, 'grp', 0, 0, tiled=True)  7.37 us
    concatenate x3, local copies, waits for them, and re-layouts, kern(): jnp.concatenate([u1, u1, u2, u1, u3, u2, a1, a2, a3, one_u, one_u, one_u]...  4.24 us
    all_to_all x2, waiting for transfers between devices, solve(): scattered = lax.all_to_all(pieces, 'grp', 0, 0, tiled=True)  4.21 us
  transfers between devices with their start and end apart: 6, of which 5 were waited for; matrix products, arithmetic and copies ran while one was open for 18% of the time, Pallas kernels for 0%

profile of v2, /device:TPU:0, one launch (start us, length us, event | category | flops | bytes accessed | tf_op | source)
XLA Modules:
  0.0 149.9 jit_solution(13154883131571543989)
XLA Ops:
  0.6 0.8 constant_dynamic-update-slice_fusion.1
  1.5 1.3 fusion.63
  2.8 2.0 %convert_bitcast_fusion.1 = (s32[8,128]{1,0:T(8,128)S(1)}, pred[1024]{0:T(1024)(128)(4,1)S(1)}, s32[8,128]{1,0:T(8,128)S(1)}, pred[1024]{0:T(1024)(128)(4,1)S(1)}) fusion(s32[1024]{0:T(1024)} %param.9, s32[]{:T(128)} %bitcast, s32[]{:T(128)} %bitcast.3), kind=kLoop, calls=%fused_computation.95 | loop fusion | flops 4096 | bytes 14344 | tf_op jit(solution)/shard_map/convert
  4.8 0.3 reduce-window.24
  5.4 0.9 constant_dynamic-update-slice_fusion
  6.2 0.5 fusion.33
  6.8 0.3 reduce-window.16
  7.1 0.3 copy-done.6
  7.5 0.1 slice_reduce_fusion.1
  7.7 0.5 fusion.27
  8.2 0.9 broadcast_in_dim.12
  9.1 7.3 %all-to-all-start = ((f32[32,48,128]{2,1,0:T(8,128)}), f32[32,48,128]{2,1,0:T(8,128)S(1)}, u32[]{:S(2)}, u32[]{:S(2)}) async-start(f32[32,48,128]{2,1,0:T(8,128)} %broadcast_in_dim.12), calls=%async_computation | async-start | bytes 1572864 | tf_op jit(solution)/shard_map/all_to_all | solution.py:18
  20.4 4.2 %concatenate.29 = bf16[102,128]{1,0:T(8,128)(2,1)} concatenate(bf16[16,128]{1,0:T(8,128)(2,1)S(1)} %get-tuple-element.26, bf16[16,128]{1,0:T(8,128)(2,1)S(1)} %get-tuple-element.26, bf16[16,128]{1,0:T(8,128)(2,1)S(1)} %get-tuple-element.27, bf16[16,128]{1,0:T(8,128)(2,1)S(1)} %get-tuple-element.26, bf16[16,128]{1,0:T(8,128)(2,1)S(1)} %get-tuple-element.28, ...), dimensions={0} | concatenate | bytes 52224 | tf_op jit(solution)/shard_map/concatenate | solution.py:38
  24.6 1.6 %fusion.23 = f32[128,128]{1,0:T(8,128)} fusion(s32[1024]{0:T(1024)S(1)} %add_bitcast_fusion, s32[1024]{0:T(1024)S(1)} %add_bitcast_fusion.1, pred[1024]{0:T(1024)(128)(4,1)S(1)} %get-tuple-element.34, pred[1024]{0:T(1024)(128)(4,1)S(1)} %get-tuple-element.5), kind=kOutput, calls=%fused_computation.22 | convolution fusion | flops 34078720 | bytes 75776 | tf_op jit(solution)/shard_map/dot_general | solution.py:96
  26.2 9.9 %all-to-all-done = f32[32,48,128]{2,1,0:T(8,128)S(1)} async-done(((f32[32,48,128]{2,1,0:T(8,128)}), f32[32,48,128]{2,1,0:T(8,128)S(1)}, u32[]{:S(2)}, u32[]{:S(2)}) %all-to-all-start) | async-done | bytes 786464 | tf_op jit(solution)/shard_map/all_to_all | solution.py:18
  36.1 0.7 multiply_reduce_fusion.1
  37.0 10.7 %convolution_bitcast_fusion.1 = f32[8,16,128]{2,1,0:T(8,128)} fusion(f32[16,4096,1]{1,0,2:T(8,128)S(1)} %reshape.294, f32[8,128,4096]{2,1,0:T(8,128)} %bitcast.82), kind=kOutput, calls=%fused_computation.11 | convolution fusion | flops 402653184 | bytes 17104896 | tf_op jit(solution)/shard_map/dot_general | solution.py:67
  47.7 3.8 %all-to-all-start.1 = ((f32[8,16,128]{2,1,0:T(8,128)}), f32[8,16,128]{2,1,0:T(8,128)S(1)}, u32[]{:S(2)}, u32[]{:S(2)}) async-start(f32[8,16,128]{2,1,0:T(8,128)} %convolution_bitcast_fusion.1), calls=%async_computation.1 | async-start | bytes 131072 | tf_op jit(solution)/shard_map/all_to_all | solution.py:72
  51.5 0.8 fusion.35
  52.3 4.2 %all-to-all-done.1 = f32[8,16,128]{2,1,0:T(8,128)S(1)} async-done(((f32[8,16,128]{2,1,0:T(8,128)}), f32[8,16,128]{2,1,0:T(8,128)S(1)}, u32[]{:S(2)}, u32[]{:S(2)}) %all-to-all-start.1) | async-done | bytes 65568 | tf_op jit(solution)/shard_map/all_to_all | solution.py:72
  56.6 0.7 broadcast_in_dim.14
  57.3 3.3 %all-to-all-start.2 = ((f32[32,16,128]{2,1,0:T(8,128)}), f32[32,16,128]{2,1,0:T(8,128)}, u32[]{:S(2)}, u32[]{:S(2)}) async-start(f32[32,16,128]{2,1,0:T(8,128)} %broadcast_in_dim.14), calls=%async_computation.2 | async-start | bytes 524288 | tf_op jit(solution)/shard_map/all_to_all | solution.py:18
  60.7 0.6 copy-done.2
  61.3 0.1 concatenate.27
  61.4 1.2 fusion.8
  62.6 8.1 %all-to-all-done.2 = f32[32,16,128]{2,1,0:T(8,128)} async-done(((f32[32,16,128]{2,1,0:T(8,128)}), f32[32,16,128]{2,1,0:T(8,128)}, u32[]{:S(2)}, u32[]{:S(2)}) %all-to-all-start.2) | async-done | bytes 262176 | tf_op jit(solution)/shard_map/all_to_all | solution.py:18
  70.8 1.1 copy.15
  71.9 0.2 copy.42
  72.1 1.7 %convolution_subtract_fusion = f32[16,128]{1,0:T(8,128)S(1)} fusion(f32[128,4096]{1,0:T(8,128)S(1)} %fusion.8, f32[32,128]{1,0:T(8,128)} %copy-done.6, f32[2,8,32,128]{3,2,1,0:T(8,128)S(1)} %bitcast.85), kind=kOutput, calls=%fused_computation.18 | convolution fusion | flops 50333696 | bytes 2375680 | tf_op jit(solution)/shard_map/dot_general | solution.py:45
  73.8 1.0 fusion.21
  74.8 0.7 broadcast_in_dim.15
  75.5 2.7 %all-to-all-start.3 = ((f32[32,16,128]{2,1,0:T(8,128)}), f32[32,16,128]{2,1,0:T(8,128)S(1)}, u32[]{:S(2)}, u32[]{:S(2)}) async-start(f32[32,16,128]{2,1,0:T(8,128)} %broadcast_in_dim.15), calls=%async_computation.3 | async-start | bytes 524288 | tf_op jit(solution)/shard_map/all_to_all | solution.py:18
  78.2 0.8 fusion.51
  78.9 9.4 %all-to-all-done.3 = f32[32,16,128]{2,1,0:T(8,128)S(1)} async-done(((f32[32,16,128]{2,1,0:T(8,128)}), f32[32,16,128]{2,1,0:T(8,128)S(1)}, u32[]{:S(2)}, u32[]{:S(2)}) %all-to-all-start.3) | async-done | bytes 262176 | tf_op jit(solution)/shard_map/all_to_all | solution.py:18
  88.6 10.8 %convolution_bitcast_fusion = f32[8,16,128]{2,1,0:T(8,128)} fusion(f32[16,4096,1]{1,0,2:T(8,128)S(1)} %reshape.295, f32[8,128,4096]{2,1,0:T(8,128)} %bitcast.83), kind=kOutput, calls=%fused_computation.10 | convolution fusion | flops 402653184 | bytes 17104896 | tf_op jit(solution)/shard_map/dot_general | solution.py:67
  99.4 3.5 %all-to-all-start.4 = ((f32[8,16,128]{2,1,0:T(8,128)}), f32[8,16,128]{2,1,0:T(8,128)S(1)}, u32[]{:S(2)}, u32[]{:S(2)}) async-start(f32[8,16,128]{2,1,0:T(8,128)} %convolution_bitcast_fusion), calls=%async_computation.4 | async-start | bytes 131072 | tf_op jit(solution)/shard_map/all_to_all | solution.py:72
  102.9 8.1 %fusion.64 = f32[1024,4096]{1,0:T(8,128)} fusion(bf16[102,1024]{1,0:T(8,128)(2,1)S(1)} %concatenate.26, bf16[102,4096]{1,0:T(8,128)(2,1)S(1)} %concatenate.27), kind=kOutput, calls=%fused_computation.111 | convolution fusion | flops 855638016 | bytes 17821696 | tf_op jit(solution)/shard_map/dot_general | solution.py:40
  111.0 0.1 concatenate.30
  111.2 0.7 broadcast_in_dim.17
  111.9 4.2 %all-to-all-start.5 = ((f32[32,16,128]{2,1,0:T(8,128)}), f32[32,16,128]{2,1,0:T(8,128)S(1)}, u32[]{:S(2)}, u32[]{:S(2)}) async-start(f32[32,16,128]{2,1,0:T(8,128)} %broadcast_in_dim.17), calls=%async_computation.5 | async-start | bytes 524288 | tf_op jit(solution)/shard_map/all_to_all | solution.py:18
  116.2 8.1 %fusion.65 = f32[1024,4096]{1,0:T(8,128)} fusion(bf16[102,1024]{1,0:T(8,128)(2,1)S(1)} %concatenate.26, bf16[102,4096]{1,0:T(8,128)(2,1)S(1)} %concatenate.30), kind=kOutput, calls=%fused_computation.112 | convolution fusion | flops 855638016 | bytes 17821696 | tf_op jit(solution)/shard_map/dot_general | solution.py:40
  124.3 1.8 %fusion.25 = f32[16,1024]{1,0:T(8,128)S(1)} fusion(s32[1024]{0:T(1024)S(1)} %copy-done.10, pred[1024]{0:T(1024)(128)(4,1)S(1)} %copy-done.14, f32[16,4096]{1,0:T(8,128)} %bitcast.93, s32[]{:T(128)S(6)} %select_n.25), kind=kOutput, calls=%fused_computation.23 | convolution fusion | flops 25427968 | bytes 78852 | tf_op jit(solution)/shard_map/dot_general | solution.py:100
  126.2 0.2 all-to-all-done.5
  126.4 0.2 copy.18
  126.5 0.2 copy.41
  126.7 10.7 %fusion = f32[16,1024]{1,0:T(8,128)S(1)} fusion(f32[1024,4096]{1,0:T(8,128)} %fusion.65, f32[2,8,32,128]{3,2,1,0:T(8,128)S(1)} %bitcast.89), kind=kOutput, calls=%fused_computation | convolution fusion | flops 406847488 | bytes 17104896 | tf_op jit(solution)/shard_map/dot_general | solution.py:45
  137.4 1.2 add_add_fusion
  138.7 11.2 %fusion.18 = f32[16,1024]{1,0:T(8,128)} fusion(f32[16,1024]{1,0:T(8,128)S(1)} %fusion, f32[16,1024]{1,0:T(8,128)S(1)} %copy-done.5, f32[1024,4096]{1,0:T(8,128)} %fusion.64, f32[16,1024]{1,0:T(8,128)S(1)} %get-tuple-element.44, f32[16,1024]{1,0:T(8,128)S(1)} %fusion.25, f32[2,8,32,128]{3,2,1,0:T(8,128)S(1)} %bitcast.86), kind=kOutput, calls=%fused_computation.15 | convolution fusion | flops 406945792 | bytes 17367040 | tf_op jit(solution)/shard_map/dot_general | solution.py:45
  (53 shorter events, 1.0 us)
Async XLA Ops:
  4.8 31.3 %copy-start.11 = (pred[1024]{0:T(1024)(128)(4,1)}, pred[1024]{0:T(1024)(128)(4,1)S(1)}, u32[]{:S(2)}) copy-start(pred[1024]{0:T(1024)(128)(4,1)S(1)} %get-tuple-element.34) | copy-start | bytes 3076
  4.8 31.3 %copy-start.13 = (pred[1024]{0:T(1024)(128)(4,1)}, pred[1024]{0:T(1024)(128)(4,1)S(1)}, u32[]{:S(2)}) copy-start(pred[1024]{0:T(1024)(128)(4,1)S(1)} %get-tuple-element.5) | copy-start | bytes 3076
  5.4 30.7 %copy-start.7 = (s32[1024]{0:T(1024)}, s32[1024]{0:T(1024)S(1)}, u32[]{:S(2)}) copy-start(s32[1024]{0:T(1024)S(1)} %add_bitcast_fusion) | copy-start | bytes 12292
  6.8 0.6 copy-start.6
  7.7 28.4 %copy-start.9 = (s32[1024]{0:T(1024)}, s32[1024]{0:T(1024)S(1)}, u32[]{:S(2)}) copy-start(s32[1024]{0:T(1024)S(1)} %add_bitcast_fusion.1) | copy-start | bytes 12292
  9.1 26.9 %all-to-all-start = ((f32[32,48,128]{2,1,0:T(8,128)}), f32[32,48,128]{2,1,0:T(8,128)S(1)}, u32[]{:S(2)}, u32[]{:S(2)}) async-start(f32[32,48,128]{2,1,0:T(8,128)} %broadcast_in_dim.12), calls=%async_computation | async-start | bytes 1572864 | tf_op jit(solution)/shard_map/all_to_all | solution.py:18
  47.7 8.9 %all-to-all-start.1 = ((f32[8,16,128]{2,1,0:T(8,128)}), f32[8,16,128]{2,1,0:T(8,128)S(1)}, u32[]{:S(2)}, u32[]{:S(2)}) async-start(f32[8,16,128]{2,1,0:T(8,128)} %convolution_bitcast_fusion.1), calls=%async_computation.1 | async-start | bytes 131072 | tf_op jit(solution)/shard_map/all_to_all | solution.py:72
  57.3 13.5 %all-to-all-start.2 = ((f32[32,16,128]{2,1,0:T(8,128)}), f32[32,16,128]{2,1,0:T(8,128)}, u32[]{:S(2)}, u32[]{:S(2)}) async-start(f32[32,16,128]{2,1,0:T(8,128)} %broadcast_in_dim.14), calls=%async_computation.2 | async-start | bytes 524288 | tf_op jit(solution)/shard_map/all_to_all | solution.py:18
  60.7 0.6 copy-start.2
  72.0 1.7 %copy-start.4 = (f32[2,8,32,128]{3,1,2,0:T(8,128)}, f32[2,8,32,128]{3,1,2,0:T(8,128)S(1)}, u32[]{:S(2)}) copy-start(f32[2,8,32,128]{3,1,2,0:T(8,128)S(1)} %copy.42) | copy-start | bytes 786436
  75.5 12.9 %all-to-all-start.3 = ((f32[32,16,128]{2,1,0:T(8,128)}), f32[32,16,128]{2,1,0:T(8,128)S(1)}, u32[]{:S(2)}, u32[]{:S(2)}) async-start(f32[32,16,128]{2,1,0:T(8,128)} %broadcast_in_dim.15), calls=%async_computation.3 | async-start | bytes 524288 | tf_op jit(solution)/shard_map/all_to_all | solution.py:18
  88.5 22.5 %copy-start = (bf16[16,4096]{1,0:T(8,128)(2,1)S(1)}, bf16[16,4096]{1,0:T(8,128)(2,1)}, u32[]{:S(2)}) copy-start(bf16[16,4096]{1,0:T(8,128)(2,1)} %get-tuple-element.46) | copy-start | bytes 393220
  88.5 22.5 %copy-start.1 = (bf16[16,4096]{1,0:T(8,128)(2,1)S(1)}, bf16[16,4096]{1,0:T(8,128)(2,1)}, u32[]{:S(2)}) copy-start(bf16[16,4096]{1,0:T(8,128)(2,1)} %get-tuple-element.47) | copy-start | bytes 393220
  88.6 22.5 %copy-start.3 = (bf16[3,4096]{1,0:T(4,128)(2,1)S(1)}, bf16[3,4096]{1,0:T(4,128)(2,1)}, u32[]{:S(2)}) copy-start(bf16[3,4096]{1,0:T(4,128)(2,1)} %copy-done.2) | copy-start | bytes 73732
  99.4 11.8 %all-to-all-start.4 = ((f32[8,16,128]{2,1,0:T(8,128)}), f32[8,16,128]{2,1,0:T(8,128)S(1)}, u32[]{:S(2)}, u32[]{:S(2)}) async-start(f32[8,16,128]{2,1,0:T(8,128)} %convolution_bitcast_fusion), calls=%async_computation.4 | async-start | bytes 131072 | tf_op jit(solution)/shard_map/all_to_all | solution.py:72
  102.9 21.4 %copy-start.10 = (s32[1024]{0:T(1024)S(1)}, s32[1024]{0:T(1024)}, u32[]{:S(2)}) copy-start(s32[1024]{0:T(1024)} %copy-done.9) | copy-start | bytes 12292
  102.9 21.4 %copy-start.14 = (pred[1024]{0:T(1024)(128)(4,1)S(1)}, pred[1024]{0:T(1024)(128)(4,1)}, u32[]{:S(2)}) copy-start(pred[1024]{0:T(1024)(128)(4,1)} %copy-done.13) | copy-start | bytes 3076
  111.9 14.4 %all-to-all-start.5 = ((f32[32,16,128]{2,1,0:T(8,128)}), f32[32,16,128]{2,1,0:T(8,128)S(1)}, u32[]{:S(2)}, u32[]{:S(2)}) async-start(f32[32,16,128]{2,1,0:T(8,128)} %broadcast_in_dim.17), calls=%async_computation.5 | async-start | bytes 524288 | tf_op jit(solution)/shard_map/all_to_all | solution.py:18
  116.2 21.2 %copy-start.8 = (s32[1024]{0:T(1024)S(1)}, s32[1024]{0:T(1024)}, u32[]{:S(2)}) copy-start(s32[1024]{0:T(1024)} %copy-done.7) | copy-start | bytes 12292
  116.2 21.2 %copy-start.12 = (pred[1024]{0:T(1024)(128)(4,1)S(1)}, pred[1024]{0:T(1024)(128)(4,1)}, u32[]{:S(2)}) copy-start(pred[1024]{0:T(1024)(128)(4,1)} %copy-done.11) | copy-start | bytes 3076
  116.2 21.2 %copy-start.15 = (f32[16,1024]{1,0:T(8,128)S(1)}, f32[16,1024]{1,0:T(8,128)}, u32[]{:S(2)}) copy-start(f32[16,1024]{1,0:T(8,128)} %param.8) | copy-start | bytes 196612
  116.2 22.5 %copy-start.5 = (f32[16,1024]{1,0:T(8,128)S(1)}, f32[16,1024]{1,0:T(8,128)}, u32[]{:S(2)}) copy-start(f32[16,1024]{1,0:T(8,128)} %param.7) | copy-start | bytes 196612

commit v3 on v2

--- a/solution.py
+++ b/solution.py
@@ -38,11 +38,28 @@
     left = jnp.concatenate([u1, u1, u2, u1, u3, u2, a1, a2, a3, one_u, one_u, one_u], axis=0)
     right = jnp.concatenate([v1, v2, v1, v3, v1, v2, one_v, one_v, one_v, b1, b2, b3], axis=0)
     dist = lax.dot_general(left, right, (((0,), (0,)), ((), ())), preferred_element_type=jnp.float32)
-    return jnp.exp(-kernel_scale * dist)
+    kernel = jnp.exp(-kernel_scale * dist)
+    k1 = lax.reduce_precision(kernel, exponent_bits=8, mantissa_bits=7)
+    return k1.astype(jnp.bfloat16), (kernel - k1).astype(jnp.bfloat16)
 
 
 def apply_kernel(delta, kernel):
-    return lax.dot_general(delta, kernel, (((1,), (1,)), ((), ())), precision=HIGH)
+    k1, k2 = kernel
+    d1f = lax.reduce_precision(delta, exponent_bits=8, mantissa_bits=7)
+    d1 = d1f.astype(jnp.bfloat16)
+    d2 = (delta - d1f).astype(jnp.bfloat16)
+    rows = delta.shape[0]
+    dims = (((1,), (1,)), ((), ()))
+    both = lax.dot_general(jnp.concatenate([d1, d2], axis=0), k1, dims, preferred_element_type=jnp.float32)
+    low = lax.dot_general(d1, k2, dims, preferred_element_type=jnp.float32)
+    return (both[:rows] + both[rows:]) + low
+
+
+def exact_dot(x, onehot, dims):
+    rows = x.shape[0]
+    parts = jnp.concatenate(split3(x), axis=0)
+    out = lax.dot_general(parts, onehot, dims, preferred_element_type=jnp.float32)
+    return (out[:rows] + out[rows:2 * rows]) + out[2 * rows:]
 
 
 def body(points, residual, coef, block_of, order, inverse):
@@ -60,7 +77,7 @@
         position = jnp.cumsum(inside.astype(jnp.int32)) - 1
         return (
             (position[:, None] == jnp.arange(per, dtype=jnp.int32)[None, :]) & inside[:, None]
-        ).astype(jnp.float32)
+        ).astype(jnp.bfloat16)
 
     def solve(block_res, block_id):
         matrix_rows = lax.dynamic_index_in_dim(inverse, block_id % slots, 0, keepdims=False)
@@ -81,10 +98,13 @@
     block0, block1 = order[0], order[1]
     sel0 = selector(block0)
     sel1 = selector(block1)
-    chosen0 = jnp.dot(jnp.concatenate([residual, points], axis=0), sel0, precision=HIGHEST)
-    chosen1 = jnp.dot(jnp.concatenate([residual, points], axis=0), sel1, precision=HIGHEST)
-    res1_start = chosen1[:rhs]
-    pts1_local = chosen1[rhs:]
+    plain = (((1,), (0,)), ((), ()))
+    chosen = exact_dot(
+        jnp.concatenate([residual, points], axis=0), jnp.concatenate([sel0, sel1], axis=1), plain
+    )
+    chosen0 = chosen[:, :per]
+    res1_start = chosen[:rhs, per:]
+    pts1_local = chosen[rhs:, per:]
     gathered = to_block(gather_all(jnp.concatenate([chosen0, pts1_local], axis=0), n_dev), rhs + 2 * feat)
     block_res0 = gathered[:rhs]
     block_pts0 = gathered[rhs:rhs + feat]
@@ -93,11 +113,12 @@
     delta0 = solve(block_res0, block0)
     owned0 = lax.dynamic_slice_in_dim(delta0, mine * per, per, axis=1)
     early = apply_kernel(delta0, kern(pts1_local, block_pts0))
-    overlap = jnp.dot(sel0.T, sel1, precision=HIGHEST)
-    res1_local = res1_start - early - ridge_weight * jnp.dot(owned0, overlap, precision=HIGHEST)
+    overlap = lax.dot_general(sel0, sel1, (((0,), (0,)), ((), ())), preferred_element_type=jnp.float32)
+    overlap = overlap.astype(jnp.bfloat16)
+    res1_local = res1_start - early - ridge_weight * exact_dot(owned0, overlap, plain)
     block_res1 = to_block(gather_all(res1_local, n_dev), rhs)
 
-    spread0 = lax.dot_general(owned0, sel0, (((1,), (1,)), ((), ())), precision=HIGHEST)
+    spread0 = exact_dot(owned0, sel0, (((1,), (1,)), ((), ())))
     update0 = apply_kernel(delta0, kern(points, block_pts0))
     residual = residual - update0 - ridge_weight * spread0
     coef = coef + spread0
@@ -105,7 +126,7 @@
 
     delta1 = solve(block_res1, block1)
     owned1 = lax.dynamic_slice_in_dim(delta1, mine * per, per, axis=1)
-    spread1 = lax.dot_general(owned1, sel1, (((1,), (1,)), ((), ())), precision=HIGHEST)
+    spread1 = exact_dot(owned1, sel1, (((1,), (1,)), ((), ())))
     update1 = apply_kernel(delta1, kernel1)
     residual = residual - update1 - ridge_weight * spread1
     coef = coef + spread1

time: 151 us -> 149 us (0.987)
  waiting for transfers between devices: 31.8 us -> 24.7 us
  local copies, waits for them, and re-layouts: 13 us -> 16.5 us
    all_to_all x4, waiting for transfers between devices: 27.6 us -> 19.8 us  [gather_all(): return lax.all_to_all(sent, ALL, 0, 0, tiled=True)]
    concatenate x2, local copies, waits for them, and re-layouts: 0.29 us -> 4.81 us  [kern(): jnp.concatenate([v1, v2, v1, v3, v1, v2, one_v, one_v, one_v, b1, b2, b3]...]
    reduce_sum x1 -> x2, other arithmetic: 0.02 us -> 1.58 us  [kern(): nu = jnp.sum(u * u, axis=0, keepdims=True)]
    dot_general x9 -> x10, matrix products: 30.3 us -> 30.3 us  [the longest x3 14.9 us: apply_kernel(): lax.dot_general(jnp.concatenate([d1, d2], axis=0), k1, dims, preferred_el...]
  transfers between devices with their start and end apart: 6 -> 6, of which waited for: 5 -> 5; matrix products, arithmetic and copies ran while one was open for 18% -> 23% of each run, Pallas kernels for 0% -> 0%
where the time goes in v3:
time: 149 us; the launch traced here: 148 us
  matrix products  69.3 us (47%)
  starting transfers between devices  25.1 us (17%)
  waiting for transfers between devices  24.7 us (17%)
  local copies, waits for them, and re-layouts  16.5 us (11%)
  other arithmetic  7.24 us (5%)
  between operations  4.89 us (3%)
    dot_general x2, matrix products, solve(): lax.dot_general(block_res, matrix_rows, (((1,), (1,)), ((), ())), precisi...  21.5 us
    all_to_all x4, waiting for transfers between devices, gather_all(): return lax.all_to_all(sent, ALL, 0, 0, tiled=True)  19.8 us
    all_to_all x4, starting transfers between devices, gather_all(): return lax.all_to_all(sent, ALL, 0, 0, tiled=True)  17.9 us
    dot_general x3, matrix products, kern(): lax.dot_general(left, right, (((0,), (0,)), ((), ())), preferred_element_...  17.5 us
    dot_general x3, matrix products, apply_kernel(): lax.dot_general(jnp.concatenate([d1, d2], axis=0), k1, dims, preferred_el...  14.9 us
    dot_general x3, matrix products, apply_kernel(): low = lax.dot_general(d1, k2, dims, preferred_element_type=jnp.float32)  12.5 us
    all_to_all x2, starting transfers between devices, solve(): scattered = lax.all_to_all(pieces, 'grp', 0, 0, tiled=True)  7.19 us
    all_to_all x2, waiting for transfers between devices, solve(): scattered = lax.all_to_all(pieces, 'grp', 0, 0, tiled=True)  4.85 us
  transfers between devices with their start and end apart: 6, of which 5 were waited for; matrix products, arithmetic and copies ran while one was open for 23% of the time, Pallas kernels for 0%

profile of v3, /device:TPU:0, one launch (start us, length us, event | category | flops | bytes accessed | tf_op | source)
XLA Modules:
  0.0 147.7 jit_solution(15157856665165488139)
XLA Ops:
  0.6 1.4 fusion.86
  2.0 2.0 %convert_bitcast_fusion.1 = (s32[8,128]{1,0:T(8,128)S(1)}, pred[1024]{0:T(1024)(128)(4,1)S(1)}, s32[8,128]{1,0:T(8,128)S(1)}, pred[1024]{0:T(1024)(128)(4,1)S(1)}) fusion(s32[1024]{0:T(1024)} %param.9, s32[]{:T(128)} %bitcast, s32[]{:T(128)} %bitcast.3), kind=kLoop, calls=%fused_computation.141 | loop fusion | flops 4096 | bytes 14344 | tf_op jit(solution)/shard_map/convert
  4.0 0.3 reduce-window.16
  4.6 0.3 reduce-window.24
  5.1 0.9 constant_dynamic-update-slice_fusion.1
  6.0 0.9 multiply_reduce_fusion.2
  6.9 0.9 fusion.37
  7.8 0.3 fusion.33
  8.1 0.6 slice_add_fusion.6
  8.8 0.7 multiply_reduce_fusion.3
  9.5 0.7 slice.133
  10.2 0.9 broadcast_in_dim.12
  11.1 7.3 %all-to-all-start = ((f32[32,48,128]{2,1,0:T(8,128)}), f32[32,48,128]{2,1,0:T(8,128)S(1)}, u32[]{:S(2)}, u32[]{:S(2)}) async-start(f32[32,48,128]{2,1,0:T(8,128)} %broadcast_in_dim.12), calls=%async_computation | async-start | bytes 1572864 | tf_op jit(solution)/shard_map/all_to_all | solution.py:18
  22.3 4.2 %concatenate.56 = bf16[102,128]{1,0:T(8,128)(2,1)} concatenate(bf16[16,128]{1,0:T(8,128)(2,1)S(1)} %get-tuple-element.36, bf16[16,128]{1,0:T(8,128)(2,1)S(1)} %get-tuple-element.36, bf16[16,128]{1,0:T(8,128)(2,1)S(1)} %get-tuple-element.37, bf16[16,128]{1,0:T(8,128)(2,1)S(1)} %get-tuple-element.36, bf16[16,128]{1,0:T(8,128)(2,1)S(1)} %get-tuple-element.38, ...), dimensions={0} | concatenate | bytes 52224 | tf_op jit(solution)/shard_map/concatenate | solution.py:38
  26.6 11.5 %all-to-all-done = f32[32,48,128]{2,1,0:T(8,128)S(1)} async-done(((f32[32,48,128]{2,1,0:T(8,128)}), f32[32,48,128]{2,1,0:T(8,128)S(1)}, u32[]{:S(2)}, u32[]{:S(2)}) %all-to-all-start) | async-done | bytes 786464 | tf_op jit(solution)/shard_map/all_to_all | solution.py:18
  38.4 10.7 %convolution_bitcast_fusion.1 = f32[8,16,128]{2,1,0:T(8,128)} fusion(f32[16,4096,1]{1,0,2:T(8,128)S(1)} %reshape.294, f32[8,128,4096]{2,1,0:T(8,128)} %bitcast.88), kind=kOutput, calls=%fused_computation.18 | convolution fusion | flops 402653184 | bytes 17104896 | tf_op jit(solution)/shard_map/dot_general | solution.py:84
  49.1 3.8 %all-to-all-start.1 = ((f32[8,16,128]{2,1,0:T(8,128)}), f32[8,16,128]{2,1,0:T(8,128)S(1)}, u32[]{:S(2)}, u32[]{:S(2)}) async-start(f32[8,16,128]{2,1,0:T(8,128)} %convolution_bitcast_fusion.1), calls=%async_computation.1 | async-start | bytes 131072 | tf_op jit(solution)/shard_map/all_to_all | solution.py:89
  53.1 4.9 %all-to-all-done.1 = f32[8,16,128]{2,1,0:T(8,128)S(1)} async-done(((f32[8,16,128]{2,1,0:T(8,128)}), f32[8,16,128]{2,1,0:T(8,128)S(1)}, u32[]{:S(2)}, u32[]{:S(2)}) %all-to-all-start.1) | async-done | bytes 65568 | tf_op jit(solution)/shard_map/all_to_all | solution.py:89
  58.0 0.7 broadcast_in_dim.14
  58.7 2.9 %all-to-all-start.2 = ((f32[32,16,128]{2,1,0:T(8,128)}), f32[32,16,128]{2,1,0:T(8,128)S(1)}, u32[]{:S(2)}, u32[]{:S(2)}) async-start(f32[32,16,128]{2,1,0:T(8,128)} %broadcast_in_dim.14), calls=%async_computation.2 | async-start | bytes 524288 | tf_op jit(solution)/shard_map/all_to_all | solution.py:18
  61.8 4.7 %concatenate.58 = bf16[102,4096]{1,0:T(8,128)(2,1)} concatenate(bf16[16,4096]{1,0:T(8,128)(2,1)S(1)} %get-tuple-element.18, bf16[16,4096]{1,0:T(8,128)(2,1)S(1)} %get-tuple-element.17, bf16[16,4096]{1,0:T(8,128)(2,1)S(1)} %get-tuple-element.18, bf16[16,4096]{1,0:T(8,128)(2,1)S(1)} %get-tuple-element.16, bf16[16,4096]{1,0:T(8,128)(2,1)S(1)} %get-tuple-element.18, ...), dimensions={0} | concatenate | bytes 1671168 | tf_op jit(solution)/shard_map/concatenate | solution.py:39
  66.5 1.2 fusion.8
  67.7 4.1 %all-to-all-done.2 = f32[32,16,128]{2,1,0:T(8,128)S(1)} async-done(((f32[32,16,128]{2,1,0:T(8,128)}), f32[32,16,128]{2,1,0:T(8,128)S(1)}, u32[]{:S(2)}, u32[]{:S(2)}) %all-to-all-start.2) | async-done | bytes 262176 | tf_op jit(solution)/shard_map/all_to_all | solution.py:18
  71.8 0.2 copy.15
  72.0 0.2 fusion.39
  72.1 0.2 copy.47
  72.3 1.7 %fusion.28 = f32[48,128]{1,0:T(8,128)S(1)} fusion(bf16[16,128]{1,0:T(8,128)(2,1)S(1)} %get-tuple-element.22, bf16[16,128]{1,0:T(8,128)(2,1)S(1)} %get-tuple-element.23, bf16[16,128]{1,0:T(8,128)(2,1)S(1)} %get-tuple-element.21, s32[1024]{0:T(1024)} %copy-done.3, pred[1024]{0:T(1024)(128)(4,1)} %copy-done.7, s32[1024]{0:T(1024)} %copy-done.5, ...), kind=kOutput, calls=%fused_computation.26 | convolution fusion | flops 35704832 | bytes 47104 | tf_op jit(solution)/shard_map/dot_general | solution.py:61
  74.0 0.5 fusion.32
  74.5 1.1 fusion.30
  75.6 0.7 broadcast_in_dim.15
  76.3 2.9 %all-to-all-start.3 = ((f32[32,16,128]{2,1,0:T(8,128)}), f32[32,16,128]{2,1,0:T(8,128)S(1)}, u32[]{:S(2)}, u32[]{:S(2)}) async-start(f32[32,16,128]{2,1,0:T(8,128)} %broadcast_in_dim.15), calls=%async_computation.3 | async-start | bytes 524288 | tf_op jit(solution)/shard_map/all_to_all | solution.py:18
  79.3 8.1 %fusion.87 = f32[1024,4096]{1,0:T(8,128)} fusion(bf16[102,1024]{1,0:T(8,128)(2,1)S(1)} %concatenate.52, bf16[102,4096]{1,0:T(8,128)(2,1)S(1)} %concatenate.53), kind=kOutput, calls=%fused_computation.164 | convolution fusion | flops 855638016 | bytes 17821696 | tf_op jit(solution)/shard_map/dot_general | solution.py:40
  87.4 1.9 %all-to-all-done.3 = f32[32,16,128]{2,1,0:T(8,128)S(1)} async-done(((f32[32,16,128]{2,1,0:T(8,128)}), f32[32,16,128]{2,1,0:T(8,128)S(1)}, u32[]{:S(2)}, u32[]{:S(2)}) %all-to-all-start.3) | async-done | bytes 262176 | tf_op jit(solution)/shard_map/all_to_all | solution.py:18
  89.4 10.7 %convolution_bitcast_fusion = f32[8,16,128]{2,1,0:T(8,128)} fusion(f32[16,4096,1]{1,0,2:T(8,128)S(1)} %reshape.295, f32[8,128,4096]{2,1,0:T(8,128)} %bitcast.89), kind=kOutput, calls=%fused_computation.17 | convolution fusion | flops 402653184 | bytes 17104896 | tf_op jit(solution)/shard_map/dot_general | solution.py:84
  100.2 3.4 %all-to-all-start.4 = ((f32[8,16,128]{2,1,0:T(8,128)}), f32[8,16,128]{2,1,0:T(8,128)S(1)}, u32[]{:S(2)}, u32[]{:S(2)}) async-start(f32[8,16,128]{2,1,0:T(8,128)} %convolution_bitcast_fusion), calls=%async_computation.4 | async-start | bytes 131072 | tf_op jit(solution)/shard_map/all_to_all | solution.py:89
  103.6 8.1 %fusion.88 = f32[1024,4096]{1,0:T(8,128)} fusion(bf16[102,1024]{1,0:T(8,128)(2,1)S(1)} %concatenate.52, bf16[102,4096]{1,0:T(8,128)(2,1)S(1)} %copy-done), kind=kOutput, calls=%fused_computation.165 | convolution fusion | flops 855638016 | bytes 17821696 | tf_op jit(solution)/shard_map/dot_general | solution.py:40
  111.7 0.7 broadcast_in_dim.17
  112.4 4.8 %all-to-all-start.5 = ((f32[32,16,128]{2,1,0:T(8,128)}), f32[32,16,128]{2,1,0:T(8,128)S(1)}, u32[]{:S(2)}, u32[]{:S(2)}) async-start(f32[32,16,128]{2,1,0:T(8,128)} %broadcast_in_dim.17), calls=%async_computation.5 | async-start | bytes 524288 | tf_op jit(solution)/shard_map/all_to_all | solution.py:18
  117.2 7.1 %fusion.2 = f32[32,1024]{1,0:T(8,128)S(1)} fusion(f32[1024,4096]{1,0:T(8,128)} %fusion.87, bf16[16,4096]{1,0:T(8,128)(2,1)S(1)} %get-tuple-element.19, bf16[16,4096]{1,0:T(8,128)(2,1)S(1)} %get-tuple-element.20), kind=kOutput, calls=%fused_computation.8 | convolution fusion | flops 281542656 | bytes 17170432 | tf_op jit(solution)/shard_map/dot_general | solution.py:53
  124.4 0.5 fusion.65
  124.9 2.3 %all-to-all-done.5 = f32[32,16,128]{2,1,0:T(8,128)S(1)} async-done(((f32[32,16,128]{2,1,0:T(8,128)}), f32[32,16,128]{2,1,0:T(8,128)S(1)}, u32[]{:S(2)}, u32[]{:S(2)}) %all-to-all-start.5) | async-done | bytes 262176 | tf_op jit(solution)/shard_map/all_to_all | solution.py:18
  127.4 0.2 fusion.41
  127.5 0.2 copy.46
  127.7 7.3 %fusion.3 = f32[32,1024]{1,0:T(8,128)S(1)} fusion(f32[1024,4096]{1,0:T(8,128)} %fusion.88, bf16[16,4096]{1,0:T(8,128)(2,1)S(1)} %get-tuple-element.14, bf16[16,4096]{1,0:T(8,128)(2,1)S(1)} %get-tuple-element.15), kind=kOutput, calls=%fused_computation.9 | convolution fusion | flops 281542656 | bytes 17170432 | tf_op jit(solution)/shard_map/dot_general | solution.py:53
  135.0 7.5 %fusion.25 = f32[16,1024]{1,0:T(8,128)S(1)} fusion(bf16[16,4096]{1,0:T(8,128)(2,1)S(1)} %get-tuple-element.15, f32[1024,4096]{1,0:T(8,128)} %fusion.88, f32[32,1024]{1,0:T(8,128)S(1)} %fusion.3), kind=kOutput, calls=%fused_computation.24 | convolution fusion | flops 151027712 | bytes 17104896 | tf_op jit(solution)/shard_map/dot_general | solution.py:54
  142.6 0.5 fusion.55
  143.1 0.7 add_add_fusion
  143.8 3.9 %fusion.22 = f32[16,1024]{1,0:T(8,128)} fusion(f32[16,1024]{1,0:T(8,128)S(1)} %fusion.25, f32[16,1024]{1,0:T(8,128)S(1)} %copy-done.1, bf16[16,4096]{1,0:T(8,128)(2,1)S(1)} %get-tuple-element.20, f32[1024,4096]{1,0:T(8,128)S(1)} %bitcast.87, f32[32,1024]{1,0:T(8,128)S(1)} %fusion.2, f32[48,1024]{1,0:T(8,128)S(1)} %fusion.65, f32[48,1024]{1,0:T(8,128)S(1)} %fusion.55), kind=kOutput, calls=%fused_computation.23 | convolution fusion | flops 151191552 | bytes 17629184 | tf_op jit(solution)/shard_map/dot_general | solution.py:54
  (63 shorter events, 1.7 us)
Async XLA Ops:
  4.0 4.1 %copy-start.7 = (pred[1024]{0:T(1024)(128)(4,1)}, pred[1024]{0:T(1024)(128)(4,1)S(1)}, u32[]{:S(2)}) copy-start(pred[1024]{0:T(1024)(128)(4,1)S(1)} %get-tuple-element.50) | copy-start | bytes 3076
  4.0 4.2 %copy-start.9 = (pred[1024]{0:T(1024)(128)(4,1)}, pred[1024]{0:T(1024)(128)(4,1)S(1)}, u32[]{:S(2)}) copy-start(pred[1024]{0:T(1024)(128)(4,1)S(1)} %get-tuple-element.5) | copy-start | bytes 3076
  4.6 6.6 %copy-start.5 = (s32[1024]{0:T(1024)}, s32[1024]{0:T(1024)S(1)}, u32[]{:S(2)}) copy-start(s32[1024]{0:T(1024)S(1)} %add_bitcast_fusion.1) | copy-start | bytes 12292
  5.1 2.7 %copy-start.3 = (s32[1024]{0:T(1024)}, s32[1024]{0:T(1024)S(1)}, u32[]{:S(2)}) copy-start(s32[1024]{0:T(1024)S(1)} %add_bitcast_fusion) | copy-start | bytes 12292
  11.1 26.9 %all-to-all-start = ((f32[32,48,128]{2,1,0:T(8,128)}), f32[32,48,128]{2,1,0:T(8,128)S(1)}, u32[]{:S(2)}, u32[]{:S(2)}) async-start(f32[32,48,128]{2,1,0:T(8,128)} %broadcast_in_dim.12), calls=%async_computation | async-start | bytes 1572864 | tf_op jit(solution)/shard_map/all_to_all | solution.py:18
  49.1 8.9 %all-to-all-start.1 = ((f32[8,16,128]{2,1,0:T(8,128)}), f32[8,16,128]{2,1,0:T(8,128)S(1)}, u32[]{:S(2)}, u32[]{:S(2)}) async-start(f32[8,16,128]{2,1,0:T(8,128)} %convolution_bitcast_fusion.1), calls=%async_computation.1 | async-start | bytes 131072 | tf_op jit(solution)/shard_map/all_to_all | solution.py:89
  58.7 13.1 %all-to-all-start.2 = ((f32[32,16,128]{2,1,0:T(8,128)}), f32[32,16,128]{2,1,0:T(8,128)S(1)}, u32[]{:S(2)}, u32[]{:S(2)}) async-start(f32[32,16,128]{2,1,0:T(8,128)} %broadcast_in_dim.14), calls=%async_computation.2 | async-start | bytes 524288 | tf_op jit(solution)/shard_map/all_to_all | solution.py:18
  76.3 12.9 %all-to-all-start.3 = ((f32[32,16,128]{2,1,0:T(8,128)}), f32[32,16,128]{2,1,0:T(8,128)S(1)}, u32[]{:S(2)}, u32[]{:S(2)}) async-start(f32[32,16,128]{2,1,0:T(8,128)} %broadcast_in_dim.15), calls=%async_computation.3 | async-start | bytes 524288 | tf_op jit(solution)/shard_map/all_to_all | solution.py:18
  79.2 24.3 %copy-start = (bf16[102,4096]{1,0:T(8,128)(2,1)S(1)}, bf16[102,4096]{1,0:T(8,128)(2,1)}, u32[]{:S(2)}) copy-start(bf16[102,4096]{1,0:T(8,128)(2,1)} %concatenate.58) | copy-start | bytes 2506756
  100.2 11.5 %all-to-all-start.4 = ((f32[8,16,128]{2,1,0:T(8,128)}), f32[8,16,128]{2,1,0:T(8,128)S(1)}, u32[]{:S(2)}, u32[]{:S(2)}) async-start(f32[8,16,128]{2,1,0:T(8,128)} %convolution_bitcast_fusion), calls=%async_computation.4 | async-start | bytes 131072 | tf_op jit(solution)/shard_map/all_to_all | solution.py:89
  103.5 20.8 %copy-start.6 = (s32[1024]{0:T(1024)S(1)}, s32[1024]{0:T(1024)}, u32[]{:S(2)}) copy-start(s32[1024]{0:T(1024)} %copy-done.5) | copy-start | bytes 12292
  103.5 20.8 %copy-start.10 = (pred[1024]{0:T(1024)(128)(4,1)S(1)}, pred[1024]{0:T(1024)(128)(4,1)}, u32[]{:S(2)}) copy-start(pred[1024]{0:T(1024)(128)(4,1)} %copy-done.9) | copy-start | bytes 3076
  112.4 14.8 %all-to-all-start.5 = ((f32[32,16,128]{2,1,0:T(8,128)}), f32[32,16,128]{2,1,0:T(8,128)S(1)}, u32[]{:S(2)}, u32[]{:S(2)}) async-start(f32[32,16,128]{2,1,0:T(8,128)} %broadcast_in_dim.17), calls=%async_computation.5 | async-start | bytes 524288 | tf_op jit(solution)/shard_map/all_to_all | solution.py:18
  127.7 14.9 %copy-start.4 = (s32[1024]{0:T(1024)S(1)}, s32[1024]{0:T(1024)}, u32[]{:S(2)}) copy-start(s32[1024]{0:T(1024)} %copy-done.3) | copy-start | bytes 12292
  127.7 14.9 %copy-start.8 = (pred[1024]{0:T(1024)(128)(4,1)S(1)}, pred[1024]{0:T(1024)(128)(4,1)}, u32[]{:S(2)}) copy-start(pred[1024]{0:T(1024)(128)(4,1)} %copy-done.7) | copy-start | bytes 3076
  127.7 15.4 %copy-start.2 = (f32[16,1024]{1,0:T(8,128)S(1)}, f32[16,1024]{1,0:T(8,128)}, u32[]{:S(2)}) copy-start(f32[16,1024]{1,0:T(8,128)} %param.8) | copy-start | bytes 196612
  127.7 16.1 %slice-start = ((s8[16777216]{0:T(1024)(128)(4,1)}), s8[4194304]{0:T(1024)(128)(4,1)S(1)}, s32[]{:S(2)}) async-start(s8[16777216]{0:T(1024)(128)(4,1)} %bitcast.86), calls=%async_computation.6 | async-start | bytes 8388608
  127.7 16.1 %slice-start.1 = ((s8[16777216]{0:T(1024)(128)(4,1)}), s8[4194304]{0:T(1024)(128)(4,1)S(1)}, s32[]{:S(2)}) async-start(s8[16777216]{0:T(1024)(128)(4,1)} %bitcast.86), calls=%async_computation.7 | async-start | bytes 8388608
  127.7 16.1 %copy-start.1 = (f32[16,1024]{1,0:T(8,128)S(1)}, f32[16,1024]{1,0:T(8,128)}, u32[]{:S(2)}) copy-start(f32[16,1024]{1,0:T(8,128)} %param.7) | copy-start | bytes 196612
  135.0 8.8 %slice-start.2 = ((s8[16777216]{0:T(1024)(128)(4,1)}), s8[4194304]{0:T(1024)(128)(4,1)S(1)}, s32[]{:S(2)}) async-start(s8[16777216]{0:T(1024)(128)(4,1)} %bitcast.86), calls=%async_computation.8 | async-start | bytes 8388608
  135.0 8.8 %slice-start.3 = ((s8[16777216]{0:T(1024)(128)(4,1)}), s8[4194304]{0:T(1024)(128)(4,1)S(1)}, s32[]{:S(2)}) async-start(s8[16777216]{0:T(1024)(128)(4,1)} %bitcast.86), calls=%async_computation.9 | async-start | bytes 8388608

commit v4 on v3

--- a/solution.py
+++ b/solution.py
@@ -2,6 +2,8 @@
 import jax.numpy as jnp
 from jax import lax
 from jax.sharding import PartitionSpec as P
+from jax.experimental import pallas as pl
+from jax.experimental.pallas import tpu as pltpu
 
 B = 4096
 STEPS = 2
@@ -62,6 +64,46 @@
     return (out[:rows] + out[rows:2 * rows]) + out[2 * rows:]
 
 
+def solve_kernel(slot_ref, inv_ref, rcat_ref, r1_ref, o_ref):
+    a = inv_ref[...]
+    hi = a.astype(jnp.bfloat16)
+    lo = (a - hi.astype(jnp.float32)).astype(jnp.bfloat16)
+    dims = (((1,), (1,)), ((), ()))
+    both = lax.dot_general(rcat_ref[...], hi, dims, preferred_element_type=jnp.float32)
+    low = lax.dot_general(r1_ref[...], lo, dims, preferred_element_type=jnp.float32)
+    rows = o_ref.shape[0]
+    o_ref[...] = (both[:rows] + both[rows:]) + low
+
+
+def solve_rows(inverse, slot, block_res, tile=256):
+    _, n, width = inverse.shape
+    rows = block_res.shape[0]
+    r1f = lax.reduce_precision(block_res, exponent_bits=8, mantissa_bits=7)
+    r1 = r1f.astype(jnp.bfloat16)
+    r2 = (block_res - r1f).astype(jnp.bfloat16)
+    rcat = jnp.concatenate([r1, r2], axis=0)
+    tile = min(tile, n)
+    grid_spec = pltpu.PrefetchScalarGridSpec(
+        num_scalar_prefetch=1,
+        grid=(n // tile,),
+        in_specs=[
+            pl.BlockSpec((None, tile, width), lambda i, s: (s[0], i, 0)),
+            pl.BlockSpec((2 * rows, width), lambda i, s: (0, 0)),
+            pl.BlockSpec((rows, width), lambda i, s: (0, 0)),
+        ],
+        out_specs=pl.BlockSpec((rows, tile), lambda i, s: (0, i)),
+    )
+    return pl.pallas_call(
+        solve_kernel,
+        grid_spec=grid_spec,
+        out_shape=jax.ShapeDtypeStruct((rows, n), jnp.float32),
+        compiler_params=pltpu.CompilerParams(vmem_limit_bytes=48 * 1024 * 1024),
+        cost_estimate=pl.CostEstimate(
+            flops=6 * rows * n * width, transcendentals=0, bytes_accessed=4 * n * width
+        ),
+    )(jnp.reshape(slot, (1,)).astype(jnp.int32), inverse, rcat, r1)
+
+
 def body(points, residual, coef, block_of, order, inverse):
     n_grp = lax.axis_size("grp")
     n_mem = lax.axis_size("mem")
@@ -80,10 +122,7 @@
         ).astype(jnp.bfloat16)
 
     def solve(block_res, block_id):
-        matrix_rows = lax.dynamic_index_in_dim(inverse, block_id % slots, 0, keepdims=False)
-        solved = lax.dot_general(
-            block_res, matrix_rows, (((1,), (1,)), ((), ())), precision=HIGH
-        )
+        solved = solve_rows(inverse, block_id % slots, block_res)
         owner = block_id // slots
         pieces = jnp.transpose(solved.reshape(rhs, n_grp, per), (1, 0, 2))
         scattered = lax.all_to_all(pieces, "grp", 0, 0, tiled=True)

time: 149 us -> 145 us (0.973)
  matrix products: 69.3 us -> 47.8 us
  Pallas kernels: 0 us -> 16.6 us
    dot_general x2 -> x0, matrix products: 21.5 us -> none  [solve(): lax.dot_general(block_res, matrix_rows, (((1,), (1,)), ((), ())), precisi...]
    pallas_call x0 -> x2, Pallas kernels: none -> 16.6 us  [solve_rows(): pl.pallas_call(solve_kernel, grid_spec=grid_spec, out_shape=jax.ShapeDtyp...]
  transfers between devices with their start and end apart: 6 -> 6, of which waited for: 5 -> 5; matrix products, arithmetic and copies ran while one was open for 23% -> 24% of each run, Pallas kernels for 0% -> 0%
where the time goes in v4:
time: 145 us; the launch traced here: 144 us
  matrix products  47.8 us (33%)
  waiting for transfers between devices  24.9 us (17%)
  starting transfers between devices  24.7 us (17%)
  local copies, waits for them, and re-layouts  17.6 us (12%)
  Pallas kernels  16.6 us (11%)
  other arithmetic  7.39 us (5%)
  between operations  5.05 us (3%)
    all_to_all x4, waiting for transfers between devices, gather_all(): return lax.all_to_all(sent, ALL, 0, 0, tiled=True)  20 us
    dot_general x3, matrix products, kern(): lax.dot_general(left, right, (((0,), (0,)), ((), ())), preferred_element_...  17.5 us
    all_to_all x4, starting transfers between devices, gather_all(): return lax.all_to_all(sent, ALL, 0, 0, tiled=True)  17.4 us
    pallas_call x2, Pallas kernels, solve_rows(): pl.pallas_call(solve_kernel, grid_spec=grid_spec, out_shape=jax.ShapeDtyp...  16.6 us
    dot_general x3, matrix products, apply_kernel(): lax.dot_general(jnp.concatenate([d1, d2], axis=0), k1, dims, preferred_el...  14.9 us
    dot_general x3, matrix products, apply_kernel(): low = lax.dot_general(d1, k2, dims, preferred_element_type=jnp.float32)  12.5 us
    all_to_all x2, starting transfers between devices, solve(): scattered = lax.all_to_all(pieces, 'grp', 0, 0, tiled=True)  7.37 us
    all_to_all x2, waiting for transfers between devices, solve(): scattered = lax.all_to_all(pieces, 'grp', 0, 0, tiled=True)  4.85 us
  transfers between devices with their start and end apart: 6, of which 5 were waited for; matrix products, arithmetic and copies ran while one was open for 24% of the time, Pallas kernels for 0%

profile of v4, /device:TPU:0, one launch (start us, length us, event | category | flops | bytes accessed | tf_op | source)
XLA Modules:
  0.0 144.0 jit_solution(5005259718853751691)
XLA Ops:
  0.6 1.4 fusion.88
  2.0 2.0 %convert_bitcast_fusion.1 = (s32[8,128]{1,0:T(8,128)S(1)}, pred[1024]{0:T(1024)(128)(4,1)S(1)}, s32[8,128]{1,0:T(8,128)S(1)}, pred[1024]{0:T(1024)(128)(4,1)S(1)}) fusion(s32[1024]{0:T(1024)} %param.9, s32[]{:T(128)} %bitcast, s32[]{:T(128)} %bitcast.3), kind=kLoop, calls=%fused_computation.150 | loop fusion | flops 4096 | bytes 14344 | tf_op jit(solution)/shard_map/convert
  4.0 0.3 reduce-window.16
  4.6 0.3 reduce-window.24
  5.2 0.9 constant_dynamic-update-slice_fusion.1
  6.0 0.9 multiply_reduce_fusion.2
  6.9 0.9 fusion.37
  7.9 0.3 fusion.33
  8.2 0.6 slice_add_fusion.6
  8.8 0.7 multiply_reduce_fusion.3
  9.5 0.7 slice.133
  10.3 0.9 broadcast_in_dim.12
  11.2 7.3 %all-to-all-start = ((f32[32,48,128]{2,1,0:T(8,128)}), f32[32,48,128]{2,1,0:T(8,128)S(1)}, u32[]{:S(2)}, u32[]{:S(2)}) async-start(f32[32,48,128]{2,1,0:T(8,128)} %broadcast_in_dim.12), calls=%async_computation | async-start | bytes 1572864 | tf_op jit(solution)/shard_map/all_to_all | solution.py:20
  22.5 4.2 %concatenate.63 = bf16[102,128]{1,0:T(8,128)(2,1)} concatenate(bf16[16,128]{1,0:T(8,128)(2,1)S(1)} %get-tuple-element.40, bf16[16,128]{1,0:T(8,128)(2,1)S(1)} %get-tuple-element.40, bf16[16,128]{1,0:T(8,128)(2,1)S(1)} %get-tuple-element.41, bf16[16,128]{1,0:T(8,128)(2,1)S(1)} %get-tuple-element.40, bf16[16,128]{1,0:T(8,128)(2,1)S(1)} %get-tuple-element.42, ...), dimensions={0} | concatenate | bytes 52224 | tf_op jit(solution)/shard_map/concatenate | solution.py:40
  26.8 11.3 %all-to-all-done = f32[32,48,128]{2,1,0:T(8,128)S(1)} async-done(((f32[32,48,128]{2,1,0:T(8,128)}), f32[32,48,128]{2,1,0:T(8,128)S(1)}, u32[]{:S(2)}, u32[]{:S(2)}) %all-to-all-start) | async-done | bytes 786464 | tf_op jit(solution)/shard_map/all_to_all | solution.py:20
  38.3 8.3 %shard_map.77 = f32[16,1024]{1,0:T(8,128)S(1)} custom-call(s32[1]{0:T(128)} %constant.67.clone.1.slot_ref, f32[1,1024,4096]{2,1,0:T(8,128)} %inv_ref.3, bf16[32,4096]{1,0:T(8,128)(2,1)S(1)} %pad_maximum_fusion.rcat_ref, bf16[16,4096]{1,0:T(8,128)(2,1)S(1)} %get-tuple-element.29.r1_ref), custom_call_target="tpu_custom_call" | custom-call | flops 402653184 | bytes 16777216 | tf_op jit(solution)/shard_map/pallas_call | solution.py:96
  46.6 0.6 bitcast_bitcast_fusion.1
  47.3 3.8 %all-to-all-start.1 = ((f32[8,16,128]{2,1,0:T(8,128)}), f32[8,16,128]{2,1,0:T(8,128)S(1)}, u32[]{:S(2)}, u32[]{:S(2)}) async-start(f32[8,16,128]{2,1,0:T(8,128)} %bitcast_bitcast_fusion.1), calls=%async_computation.1 | async-start | bytes 131072 | tf_op jit(solution)/shard_map/all_to_all | solution.py:128
  51.3 4.9 %all-to-all-done.1 = f32[8,16,128]{2,1,0:T(8,128)S(1)} async-done(((f32[8,16,128]{2,1,0:T(8,128)}), f32[8,16,128]{2,1,0:T(8,128)S(1)}, u32[]{:S(2)}, u32[]{:S(2)}) %all-to-all-start.1) | async-done | bytes 65568 | tf_op jit(solution)/shard_map/all_to_all | solution.py:128
  56.1 0.7 broadcast_in_dim.14
  56.9 2.9 %all-to-all-start.2 = ((f32[32,16,128]{2,1,0:T(8,128)}), f32[32,16,128]{2,1,0:T(8,128)S(1)}, u32[]{:S(2)}, u32[]{:S(2)}) async-start(f32[32,16,128]{2,1,0:T(8,128)} %broadcast_in_dim.14), calls=%async_computation.2 | async-start | bytes 524288 | tf_op jit(solution)/shard_map/all_to_all | solution.py:20
  60.0 4.7 %concatenate.66 = bf16[102,4096]{1,0:T(8,128)(2,1)} concatenate(bf16[16,4096]{1,0:T(8,128)(2,1)S(1)} %get-tuple-element.18, bf16[16,4096]{1,0:T(8,128)(2,1)S(1)} %get-tuple-element.17, bf16[16,4096]{1,0:T(8,128)(2,1)S(1)} %get-tuple-element.18, bf16[16,4096]{1,0:T(8,128)(2,1)S(1)} %get-tuple-element.16, bf16[16,4096]{1,0:T(8,128)(2,1)S(1)} %get-tuple-element.18, ...), dimensions={0} | concatenate | bytes 1671168 | tf_op jit(solution)/shard_map/concatenate | solution.py:41
  64.7 1.2 fusion.8
  65.9 4.0 %all-to-all-done.2 = f32[32,16,128]{2,1,0:T(8,128)S(1)} async-done(((f32[32,16,128]{2,1,0:T(8,128)}), f32[32,16,128]{2,1,0:T(8,128)S(1)}, u32[]{:S(2)}, u32[]{:S(2)}) %all-to-all-start.2) | async-done | bytes 262176 | tf_op jit(solution)/shard_map/all_to_all | solution.py:20
  70.1 0.2 fusion.40
  70.3 0.2 copy.61
  70.5 1.7 %fusion.28 = f32[48,128]{1,0:T(8,128)S(1)} fusion(bf16[16,128]{1,0:T(8,128)(2,1)S(1)} %get-tuple-element.24, bf16[16,128]{1,0:T(8,128)(2,1)S(1)} %get-tuple-element.25, bf16[16,128]{1,0:T(8,128)(2,1)S(1)} %get-tuple-element.23, s32[1024]{0:T(1024)} %copy-done.3, pred[1024]{0:T(1024)(128)(4,1)} %copy-done.7, s32[1024]{0:T(1024)} %copy-done.5, ...), kind=kOutput, calls=%fused_computation.24 | convolution fusion | flops 35704832 | bytes 47104 | tf_op jit(solution)/shard_map/dot_general | solution.py:63
  72.2 0.5 fusion.32
  72.7 1.1 fusion.30
  73.8 0.7 broadcast_in_dim.15
  74.5 2.7 %all-to-all-start.3 = ((f32[32,16,128]{2,1,0:T(8,128)}), f32[32,16,128]{2,1,0:T(8,128)S(1)}, u32[]{:S(2)}, u32[]{:S(2)}) async-start(f32[32,16,128]{2,1,0:T(8,128)} %broadcast_in_dim.15), calls=%async_computation.3 | async-start | bytes 524288 | tf_op jit(solution)/shard_map/all_to_all | solution.py:20
  77.2 8.1 %fusion.89 = f32[1024,4096]{1,0:T(8,128)} fusion(bf16[102,1024]{1,0:T(8,128)(2,1)S(1)} %concatenate.59, bf16[102,4096]{1,0:T(8,128)(2,1)S(1)} %concatenate.60), kind=kOutput, calls=%fused_computation.173 | convolution fusion | flops 855638016 | bytes 17821696 | tf_op jit(solution)/shard_map/dot_general | solution.py:42
  85.4 2.1 %all-to-all-done.3 = f32[32,16,128]{2,1,0:T(8,128)S(1)} async-done(((f32[32,16,128]{2,1,0:T(8,128)}), f32[32,16,128]{2,1,0:T(8,128)S(1)}, u32[]{:S(2)}, u32[]{:S(2)}) %all-to-all-start.3) | async-done | bytes 262176 | tf_op jit(solution)/shard_map/all_to_all | solution.py:20
  87.5 8.3 %shard_map.78 = f32[16,1024]{1,0:T(8,128)S(1)} custom-call(s32[1]{0:T(128)} %constant.67.clone.1.slot_ref, f32[1,1024,4096]{2,1,0:T(8,128)} %inv_ref.3, bf16[32,4096]{1,0:T(8,128)(2,1)S(1)} %pad_maximum_fusion.2.rcat_ref, bf16[16,4096]{1,0:T(8,128)(2,1)S(1)} %get-tuple-element.19.r1_ref), custom_call_target="tpu_custom_call" | custom-call | flops 402653184 | bytes 16777216 | tf_op jit(solution)/shard_map/pallas_call | solution.py:96
  95.8 0.6 bitcast_bitcast_fusion
  96.5 3.5 %all-to-all-start.4 = ((f32[8,16,128]{2,1,0:T(8,128)}), f32[8,16,128]{2,1,0:T(8,128)S(1)}, u32[]{:S(2)}, u32[]{:S(2)}) async-start(f32[8,16,128]{2,1,0:T(8,128)} %bitcast_bitcast_fusion), calls=%async_computation.4 | async-start | bytes 131072 | tf_op jit(solution)/shard_map/all_to_all | solution.py:128
  100.0 8.1 %fusion.90 = f32[1024,4096]{1,0:T(8,128)} fusion(bf16[102,1024]{1,0:T(8,128)(2,1)S(1)} %concatenate.59, bf16[102,4096]{1,0:T(8,128)(2,1)S(1)} %copy-done), kind=kOutput, calls=%fused_computation.174 | convolution fusion | flops 855638016 | bytes 17821696 | tf_op jit(solution)/shard_map/dot_general | solution.py:42
  108.1 0.7 broadcast_in_dim.17
  108.9 4.4 %all-to-all-start.5 = ((f32[32,16,128]{2,1,0:T(8,128)}), f32[32,16,128]{2,1,0:T(8,128)S(1)}, u32[]{:S(2)}, u32[]{:S(2)}) async-start(f32[32,16,128]{2,1,0:T(8,128)} %broadcast_in_dim.17), calls=%async_computation.5 | async-start | bytes 524288 | tf_op jit(solution)/shard_map/all_to_all | solution.py:20
  113.3 7.1 %fusion.2 = f32[32,1024]{1,0:T(8,128)S(1)} fusion(f32[1024,4096]{1,0:T(8,128)} %fusion.89, bf16[16,4096]{1,0:T(8,128)(2,1)S(1)} %get-tuple-element.21, bf16[16,4096]{1,0:T(8,128)(2,1)S(1)} %get-tuple-element.22), kind=kOutput, calls=%fused_computation.8 | convolution fusion | flops 281542656 | bytes 17170432 | tf_op jit(solution)/shard_map/dot_general | solution.py:55
  120.5 0.5 fusion.67
  120.9 2.6 %all-to-all-done.5 = f32[32,16,128]{2,1,0:T(8,128)S(1)} async-done(((f32[32,16,128]{2,1,0:T(8,128)}), f32[32,16,128]{2,1,0:T(8,128)S(1)}, u32[]{:S(2)}, u32[]{:S(2)}) %all-to-all-start.5) | async-done | bytes 262176 | tf_op jit(solution)/shard_map/all_to_all | solution.py:20
  123.8 0.2 copy.60
  124.1 7.3 %fusion.3 = f32[32,1024]{1,0:T(8,128)S(1)} fusion(f32[1024,4096]{1,0:T(8,128)} %fusion.90, bf16[16,4096]{1,0:T(8,128)(2,1)S(1)} %get-tuple-element.14, bf16[16,4096]{1,0:T(8,128)(2,1)S(1)} %get-tuple-element.15), kind=kOutput, calls=%fused_computation.9 | convolution fusion | flops 281542656 | bytes 17170432 | tf_op jit(solution)/shard_map/dot_general | solution.py:55
  131.4 7.5 %fusion.25 = f32[16,1024]{1,0:T(8,128)S(1)} fusion(bf16[16,4096]{1,0:T(8,128)(2,1)S(1)} %get-tuple-element.15, f32[1024,4096]{1,0:T(8,128)} %fusion.90, f32[32,1024]{1,0:T(8,128)S(1)} %fusion.3), kind=kOutput, calls=%fused_computation.22 | convolution fusion | flops 151027712 | bytes 17104896 | tf_op jit(solution)/shard_map/dot_general | solution.py:56
  138.9 0.5 fusion.57
  139.4 0.7 add_add_fusion
  140.1 3.9 %fusion.22 = f32[16,1024]{1,0:T(8,128)} fusion(f32[16,1024]{1,0:T(8,128)S(1)} %fusion.25, f32[16,1024]{1,0:T(8,128)S(1)} %copy-done.1, bf16[16,4096]{1,0:T(8,128)(2,1)S(1)} %get-tuple-element.22, f32[1024,4096]{1,0:T(8,128)S(1)} %bitcast.103, f32[32,1024]{1,0:T(8,128)S(1)} %fusion.2, f32[48,1024]{1,0:T(8,128)S(1)} %fusion.67, f32[48,1024]{1,0:T(8,128)S(1)} %fusion.57), kind=kOutput, calls=%fused_computation.21 | convolution fusion | flops 151191552 | bytes 17629184 | tf_op jit(solution)/shard_map/dot_general | solution.py:56
  (65 shorter events, 1.9 us)
Async XLA Ops:
  4.0 4.1 %copy-start.7 = (pred[1024]{0:T(1024)(128)(4,1)}, pred[1024]{0:T(1024)(128)(4,1)S(1)}, u32[]{:S(2)}) copy-start(pred[1024]{0:T(1024)(128)(4,1)S(1)} %get-tuple-element.54) | copy-start | bytes 3076
  4.0 4.2 %copy-start.9 = (pred[1024]{0:T(1024)(128)(4,1)}, pred[1024]{0:T(1024)(128)(4,1)S(1)}, u32[]{:S(2)}) copy-start(pred[1024]{0:T(1024)(128)(4,1)S(1)} %get-tuple-element.5) | copy-start | bytes 3076
  4.6 6.6 %copy-start.5 = (s32[1024]{0:T(1024)}, s32[1024]{0:T(1024)S(1)}, u32[]{:S(2)}) copy-start(s32[1024]{0:T(1024)S(1)} %add_bitcast_fusion.1) | copy-start | bytes 12292
  5.2 2.7 %copy-start.3 = (s32[1024]{0:T(1024)}, s32[1024]{0:T(1024)S(1)}, u32[]{:S(2)}) copy-start(s32[1024]{0:T(1024)S(1)} %add_bitcast_fusion) | copy-start | bytes 12292
  11.2 26.9 %all-to-all-start = ((f32[32,48,128]{2,1,0:T(8,128)}), f32[32,48,128]{2,1,0:T(8,128)S(1)}, u32[]{:S(2)}, u32[]{:S(2)}) async-start(f32[32,48,128]{2,1,0:T(8,128)} %broadcast_in_dim.12), calls=%async_computation | async-start | bytes 1572864 | tf_op jit(solution)/shard_map/all_to_all | solution.py:20
  47.3 8.9 %all-to-all-start.1 = ((f32[8,16,128]{2,1,0:T(8,128)}), f32[8,16,128]{2,1,0:T(8,128)S(1)}, u32[]{:S(2)}, u32[]{:S(2)}) async-start(f32[8,16,128]{2,1,0:T(8,128)} %bitcast_bitcast_fusion.1), calls=%async_computation.1 | async-start | bytes 131072 | tf_op jit(solution)/shard_map/all_to_all | solution.py:128
  56.9 13.1 %all-to-all-start.2 = ((f32[32,16,128]{2,1,0:T(8,128)}), f32[32,16,128]{2,1,0:T(8,128)S(1)}, u32[]{:S(2)}, u32[]{:S(2)}) async-start(f32[32,16,128]{2,1,0:T(8,128)} %broadcast_in_dim.14), calls=%async_computation.2 | async-start | bytes 524288 | tf_op jit(solution)/shard_map/all_to_all | solution.py:20
  74.5 12.9 %all-to-all-start.3 = ((f32[32,16,128]{2,1,0:T(8,128)}), f32[32,16,128]{2,1,0:T(8,128)S(1)}, u32[]{:S(2)}, u32[]{:S(2)}) async-start(f32[32,16,128]{2,1,0:T(8,128)} %broadcast_in_dim.15), calls=%async_computation.3 | async-start | bytes 524288 | tf_op jit(solution)/shard_map/all_to_all | solution.py:20
  77.2 22.8 %copy-start = (bf16[102,4096]{1,0:T(8,128)(2,1)S(1)}, bf16[102,4096]{1,0:T(8,128)(2,1)}, u32[]{:S(2)}) copy-start(bf16[102,4096]{1,0:T(8,128)(2,1)} %concatenate.66) | copy-start | bytes 2506756
  96.5 11.7 %all-to-all-start.4 = ((f32[8,16,128]{2,1,0:T(8,128)}), f32[8,16,128]{2,1,0:T(8,128)S(1)}, u32[]{:S(2)}, u32[]{:S(2)}) async-start(f32[8,16,128]{2,1,0:T(8,128)} %bitcast_bitcast_fusion), calls=%async_computation.4 | async-start | bytes 131072 | tf_op jit(solution)/shard_map/all_to_all | solution.py:128
  100.0 20.4 %copy-start.6 = (s32[1024]{0:T(1024)S(1)}, s32[1024]{0:T(1024)}, u32[]{:S(2)}) copy-start(s32[1024]{0:T(1024)} %copy-done.5) | copy-start | bytes 12292
  100.0 20.4 %copy-start.10 = (pred[1024]{0:T(1024)(128)(4,1)S(1)}, pred[1024]{0:T(1024)(128)(4,1)}, u32[]{:S(2)}) copy-start(pred[1024]{0:T(1024)(128)(4,1)} %copy-done.9) | copy-start | bytes 3076
  108.9 14.6 %all-to-all-start.5 = ((f32[32,16,128]{2,1,0:T(8,128)}), f32[32,16,128]{2,1,0:T(8,128)S(1)}, u32[]{:S(2)}, u32[]{:S(2)}) async-start(f32[32,16,128]{2,1,0:T(8,128)} %broadcast_in_dim.17), calls=%async_computation.5 | async-start | bytes 524288 | tf_op jit(solution)/shard_map/all_to_all | solution.py:20
  124.0 14.9 %copy-start.4 = (s32[1024]{0:T(1024)S(1)}, s32[1024]{0:T(1024)}, u32[]{:S(2)}) copy-start(s32[1024]{0:T(1024)} %copy-done.3) | copy-start | bytes 12292
  124.0 14.9 %copy-start.8 = (pred[1024]{0:T(1024)(128)(4,1)S(1)}, pred[1024]{0:T(1024)(128)(4,1)}, u32[]{:S(2)}) copy-start(pred[1024]{0:T(1024)(128)(4,1)} %copy-done.7) | copy-start | bytes 3076
  124.0 15.4 %copy-start.2 = (f32[16,1024]{1,0:T(8,128)S(1)}, f32[16,1024]{1,0:T(8,128)}, u32[]{:S(2)}) copy-start(f32[16,1024]{1,0:T(8,128)} %param.8) | copy-start | bytes 196612
  124.0 16.1 %slice-start = ((s8[16777216]{0:T(1024)(128)(4,1)}), s8[4194304]{0:T(1024)(128)(4,1)S(1)}, s32[]{:S(2)}) async-start(s8[16777216]{0:T(1024)(128)(4,1)} %bitcast.102), calls=%async_computation.6 | async-start | bytes 8388608
  124.0 16.1 %slice-start.1 = ((s8[16777216]{0:T(1024)(128)(4,1)}), s8[4194304]{0:T(1024)(128)(4,1)S(1)}, s32[]{:S(2)}) async-start(s8[16777216]{0:T(1024)(128)(4,1)} %bitcast.102), calls=%async_computation.7 | async-start | bytes 8388608
  124.0 16.1 %copy-start.1 = (f32[16,1024]{1,0:T(8,128)S(1)}, f32[16,1024]{1,0:T(8,128)}, u32[]{:S(2)}) copy-start(f32[16,1024]{1,0:T(8,128)} %param.7) | copy-start | bytes 196612
  131.3 8.8 %slice-start.2 = ((s8[16777216]{0:T(1024)(128)(4,1)}), s8[4194304]{0:T(1024)(128)(4,1)S(1)}, s32[]{:S(2)}) async-start(s8[16777216]{0:T(1024)(128)(4,1)} %bitcast.102), calls=%async_computation.8 | async-start | bytes 8388608
  131.3 8.8 %slice-start.3 = ((s8[16777216]{0:T(1024)(128)(4,1)}), s8[4194304]{0:T(1024)(128)(4,1)S(1)}, s32[]{:S(2)}) async-start(s8[16777216]{0:T(1024)(128)(4,1)} %bitcast.102), calls=%async_computation.9 | async-start | bytes 8388608

commit v5 on v4

--- a/solution.py
+++ b/solution.py
@@ -28,7 +28,31 @@
     return x1.astype(jnp.bfloat16), x2.astype(jnp.bfloat16), r2.astype(jnp.bfloat16)
 
 
-def kern(u, v):
+def update_kernel(left_ref, right_ref, d12_ref, d1_ref, o_ref, acc1, acc2):
+    j = pl.program_id(1)
+
+    @pl.when(j == 0)
+    def _():
+        acc1[...] = jnp.zeros_like(acc1)
+        acc2[...] = jnp.zeros_like(acc2)
+
+    dist = jnp.dot(left_ref[...], right_ref[...], preferred_element_type=jnp.float32)
+    kernel = jnp.exp(-kernel_scale * dist)
+    k1 = kernel.astype(jnp.bfloat16)
+    k2 = (kernel - k1.astype(jnp.float32)).astype(jnp.bfloat16)
+    acc1[...] += jnp.dot(k1, d12_ref[...], preferred_element_type=jnp.float32)
+    acc2[...] += jnp.dot(k2, d1_ref[...], preferred_element_type=jnp.float32)
+
+    @pl.when(j == pl.num_programs(1) - 1)
+    def _():
+        rows = o_ref.shape[1]
+        o_ref[...] = (acc1[:, :rows] + acc1[:, rows:]) + acc2[...]
+
+
+def kernel_update(u, v, delta, tile_n=256, tile_m=512):
+    n = u.shape[1]
+    m = v.shape[1]
+    rows = delta.shape[0]
     nu = jnp.sum(u * u, axis=0, keepdims=True)
     nv = jnp.sum(v * v, axis=0, keepdims=True)
     u1, u2, u3 = split3(u)
@@ -39,22 +63,37 @@
     one_v = jnp.ones_like(b1)
     left = jnp.concatenate([u1, u1, u2, u1, u3, u2, a1, a2, a3, one_u, one_u, one_u], axis=0)
     right = jnp.concatenate([v1, v2, v1, v3, v1, v2, one_v, one_v, one_v, b1, b2, b3], axis=0)
-    dist = lax.dot_general(left, right, (((0,), (0,)), ((), ())), preferred_element_type=jnp.float32)
-    kernel = jnp.exp(-kernel_scale * dist)
-    k1 = lax.reduce_precision(kernel, exponent_bits=8, mantissa_bits=7)
-    return k1.astype(jnp.bfloat16), (kernel - k1).astype(jnp.bfloat16)
-
-
-def apply_kernel(delta, kernel):
-    k1, k2 = kernel
+    depth = 128
+    left = jnp.pad(left, ((0, depth - left.shape[0]), (0, 0))).T
+    right = jnp.pad(right, ((0, depth - right.shape[0]), (0, 0)))
     d1f = lax.reduce_precision(delta, exponent_bits=8, mantissa_bits=7)
     d1 = d1f.astype(jnp.bfloat16)
     d2 = (delta - d1f).astype(jnp.bfloat16)
-    rows = delta.shape[0]
-    dims = (((1,), (1,)), ((), ()))
-    both = lax.dot_general(jnp.concatenate([d1, d2], axis=0), k1, dims, preferred_element_type=jnp.float32)
-    low = lax.dot_general(d1, k2, dims, preferred_element_type=jnp.float32)
-    return (both[:rows] + both[rows:]) + low
+    d12 = jnp.concatenate([d1, d2], axis=0).T
+    d1t = d1.T
+    tile_n = min(tile_n, n)
+    tile_m = min(tile_m, m)
+    out = pl.pallas_call(
+        update_kernel,
+        grid=(n // tile_n, m // tile_m),
+        in_specs=[
+            pl.BlockSpec((tile_n, depth), lambda i, j: (i, 0)),
+            pl.BlockSpec((depth, tile_m), lambda i, j: (0, j)),
+            pl.BlockSpec((tile_m, 2 * rows), lambda i, j: (j, 0)),
+            pl.BlockSpec((tile_m, rows), lambda i, j: (j, 0)),
+        ],
+        out_specs=pl.BlockSpec((tile_n, rows), lambda i, j: (i, 0)),
+        out_shape=jax.ShapeDtypeStruct((n, rows), jnp.float32),
+        scratch_shapes=[
+            pltpu.VMEM((tile_n, 2 * rows), jnp.float32),
+            pltpu.VMEM((tile_n, rows), jnp.float32),
+        ],
+        cost_estimate=pl.CostEstimate(
+            flops=2 * n * m * (depth + 3 * rows), transcendentals=n * m,
+            bytes_accessed=2 * (n + m) * depth + 6 * m * rows + 4 * n * rows,
+        ),
+    )(left, right, d12, d1t)
+    return out.T
 
 
 def exact_dot(x, onehot, dims):
@@ -151,22 +190,21 @@
 
     delta0 = solve(block_res0, block0)
     owned0 = lax.dynamic_slice_in_dim(delta0, mine * per, per, axis=1)
-    early = apply_kernel(delta0, kern(pts1_local, block_pts0))
+    early = kernel_update(pts1_local, block_pts0, delta0)
     overlap = lax.dot_general(sel0, sel1, (((0,), (0,)), ((), ())), preferred_element_type=jnp.float32)
     overlap = overlap.astype(jnp.bfloat16)
     res1_local = res1_start - early - ridge_weight * exact_dot(owned0, overlap, plain)
     block_res1 = to_block(gather_all(res1_local, n_dev), rhs)
 
     spread0 = exact_dot(owned0, sel0, (((1,), (1,)), ((), ())))
-    update0 = apply_kernel(delta0, kern(points, block_pts0))
+    update0 = kernel_update(points, block_pts0, delta0)
     residual = residual - update0 - ridge_weight * spread0
     coef = coef + spread0
-    kernel1 = kern(points, block_pts1)
 
     delta1 = solve(block_res1, block1)
     owned1 = lax.dynamic_slice_in_dim(delta1, mine * per, per, axis=1)
     spread1 = exact_dot(owned1, sel1, (((1,), (1,)), ((), ())))
-    update1 = apply_kernel(delta1, kernel1)
+    update1 = kernel_update(points, block_pts1, delta1)
     residual = residual - update1 - ridge_weight * spread1
     coef = coef + spread1
     return (residual, coef)

time: 145 us -> 191 us (1.32)
  Pallas kernels: 16.6 us -> 74.9 us
  matrix products: 47.8 us -> 3.14 us
  other arithmetic: 7.39 us -> 20.2 us
  local copies, waits for them, and re-layouts: 17.6 us -> 28.3 us
  waiting for transfers between devices: 24.9 us -> 32.6 us
    pallas_call x0 -> x3, Pallas kernels: none -> 58.3 us  [kernel_update(): pl.pallas_call(update_kernel, grid=(n // tile_n, m // tile_m), in_specs=[...]
    dot_general x9 -> x0, matrix products: 44.8 us -> none  [the longest x3 17.5 us: kern(): lax.dot_general(left, right, (((0,), (0,)), ((), ())), preferred_element_...]
    transpose x0 -> x2, other arithmetic: none -> 5.94 us  [kernel_update(): d12 = jnp.concatenate([d1, d2], axis=0).T]
    all_to_all x2, waiting for transfers between devices: 4.85 us -> 9.92 us  [solve(): scattered = lax.all_to_all(pieces, 'grp', 0, 0, tiled=True)]
    unnamed x33 -> x60, local copies, waits for them, and re-layouts: 1.24 us -> 5.51 us
    concatenate x5, local copies, waits for them, and re-layouts: 9.09 us -> 4.9 us  [the longest x3 4.6 us: kernel_update(): jnp.concatenate([u1, u1, u2, u1, u3, u2, a1, a2, a3, one_u, one_u, one_u]...]
    all_to_all x4, waiting for transfers between devices: 20 us -> 22.7 us  [gather_all(): return lax.all_to_all(sent, ALL, 0, 0, tiled=True)]
    convert_element_type x2, other arithmetic: 0.31 us -> 2.95 us  [kernel_update(): d1 = d1f.astype(jnp.bfloat16)]
  transfers between devices with their start and end apart: 6 -> 6, of which waited for: 5 -> 4; matrix products, arithmetic and copies ran while one was open for 24% -> 8% of each run, Pallas kernels for 0% -> 14%
where the time goes in v5:
time: 191 us; the launch traced here: 189 us
  Pallas kernels  74.9 us (39%)
  waiting for transfers between devices  32.6 us (17%)
  local copies, waits for them, and re-layouts  28.3 us (15%)
  starting transfers between devices  24.6 us (13%)
  other arithmetic  20.2 us (11%)
  between operations  4.85 us (3%)
  matrix products  3.14 us (2%)
    pallas_call x3, Pallas kernels, kernel_update(): pl.pallas_call(update_kernel, grid=(n // tile_n, m // tile_m), in_specs=[...  58.3 us
    all_to_all x4, waiting for transfers between devices, gather_all(): return lax.all_to_all(sent, ALL, 0, 0, tiled=True)  22.7 us
    all_to_all x4, starting transfers between devices, gather_all(): return lax.all_to_all(sent, ALL, 0, 0, tiled=True)  16.9 us
    pallas_call x2, Pallas kernels, solve_rows(): pl.pallas_call(solve_kernel, grid_spec=grid_spec, out_shape=jax.ShapeDtyp...  16.6 us
    all_to_all x2, waiting for transfers between devices, solve(): scattered = lax.all_to_all(pieces, 'grp', 0, 0, tiled=True)  9.92 us
    all_to_all x2, starting transfers between devices, solve(): scattered = lax.all_to_all(pieces, 'grp', 0, 0, tiled=True)  7.77 us
    transpose x2, other arithmetic, kernel_update(): d12 = jnp.concatenate([d1, d2], axis=0).T  5.94 us
    unnamed x60, local copies, waits for them, and re-layouts  5.51 us
  transfers between devices with their start and end apart: 6, of which 4 were waited for; matrix products, arithmetic and copies ran while one was open for 8% of the time, Pallas kernels for 14%

profile of v5, /device:TPU:0, one launch (start us, length us, event | category | flops | bytes accessed | tf_op | source)
XLA Modules:
  0.0 188.6 jit_solution(7645714489265633397)
XLA Ops:
  0.6 1.3 fusion.49
  1.9 1.9 %convert_bitcast_fusion.1 = (s32[8,128]{1,0:T(8,128)S(1)}, pred[1024]{0:T(1024)(128)(4,1)S(1)}, s32[8,128]{1,0:T(8,128)S(1)}, pred[1024]{0:T(1024)(128)(4,1)S(1)}) fusion(s32[1024]{0:T(1024)} %param.9, s32[]{:T(128)} %bitcast.2, s32[]{:T(128)} %bitcast.5), kind=kLoop, calls=%fused_computation.121 | loop fusion | flops 4096 | bytes 14344 | tf_op jit(solution)/shard_map/convert
  5.0 0.9 constant_dynamic-update-slice_fusion.1
  5.9 1.5 constant_dynamic-update-slice_fusion
  7.4 0.9 fusion.11
  9.3 1.0 broadcast_in_dim.12
  10.3 7.3 %all-to-all-start = ((f32[32,48,128]{2,1,0:T(8,128)}), f32[32,48,128]{2,1,0:T(8,128)S(1)}, u32[]{:S(2)}, u32[]{:S(2)}) async-start(f32[32,48,128]{2,1,0:T(8,128)} %broadcast_in_dim.12), calls=%async_computation | async-start | bytes 1572864 | tf_op jit(solution)/shard_map/all_to_all | solution.py:20
  18.9 1.0 copy.142
  20.5 1.0 copy.143
  23.4 13.8 %all-to-all-done = f32[32,48,128]{2,1,0:T(8,128)S(1)} async-done(((f32[32,48,128]{2,1,0:T(8,128)}), f32[32,48,128]{2,1,0:T(8,128)S(1)}, u32[]{:S(2)}, u32[]{:S(2)}) %all-to-all-start) | async-done | bytes 786464 | tf_op jit(solution)/shard_map/all_to_all | solution.py:20
  37.4 8.3 %shard_map.77 = f32[16,1024]{1,0:T(8,128)S(1)} custom-call(s32[1]{0:T(128)} %constant.72.clone.1.slot_ref, f32[1,1024,4096]{2,1,0:T(8,128)} %inv_ref.3, bf16[32,4096]{1,0:T(8,128)(2,1)S(1)} %pad_maximum_fusion.rcat_ref, bf16[16,4096]{1,0:T(8,128)(2,1)S(1)} %get-tuple-element.40.r1_ref), custom_call_target="tpu_custom_call" | custom-call | flops 402653184 | bytes 16777216 | tf_op jit(solution)/shard_map/pallas_call | solution.py:135
  45.7 0.6 bitcast_bitcast_fusion.1
  46.4 3.8 %all-to-all-start.1 = ((f32[8,16,128]{2,1,0:T(8,128)}), f32[8,16,128]{2,1,0:T(8,128)S(1)}, u32[]{:S(2)}, u32[]{:S(2)}) async-start(f32[8,16,128]{2,1,0:T(8,128)} %bitcast_bitcast_fusion.1), calls=%async_computation.1 | async-start | bytes 131072 | tf_op jit(solution)/shard_map/all_to_all | solution.py:167
  50.3 5.0 %all-to-all-done.1 = f32[8,16,128]{2,1,0:T(8,128)S(1)} async-done(((f32[8,16,128]{2,1,0:T(8,128)}), f32[8,16,128]{2,1,0:T(8,128)S(1)}, u32[]{:S(2)}, u32[]{:S(2)}) %all-to-all-start.1) | async-done | bytes 65568 | tf_op jit(solution)/shard_map/all_to_all | solution.py:167
  55.2 0.7 broadcast_in_dim.14
  55.9 2.9 %all-to-all-start.2 = ((f32[32,16,128]{2,1,0:T(8,128)}), f32[32,16,128]{2,1,0:T(8,128)S(1)}, u32[]{:S(2)}, u32[]{:S(2)}) async-start(f32[32,16,128]{2,1,0:T(8,128)} %broadcast_in_dim.14), calls=%async_computation.2 | async-start | bytes 524288 | tf_op jit(solution)/shard_map/all_to_all | solution.py:20
  59.1 1.1 pad.18.right_ref
  60.2 8.9 %all-to-all-done.2 = f32[32,16,128]{2,1,0:T(8,128)S(1)} async-done(((f32[32,16,128]{2,1,0:T(8,128)}), f32[32,16,128]{2,1,0:T(8,128)S(1)}, u32[]{:S(2)}, u32[]{:S(2)}) %all-to-all-start.2) | async-done | bytes 262176 | tf_op jit(solution)/shard_map/all_to_all | solution.py:20
  69.1 0.7 copy-done.4
  69.8 1.6 copy.156
  71.3 1.3 reduce-precision_convert_fusion.1
  72.6 0.7 reduce-precision_convert_fusion.18
  73.9 0.8 copy.159
  74.7 0.8 copy.160
  75.6 0.8 copy.158
  76.4 2.8 %maximum_bitcast_fusion.d12_ref = bf16[4096,32]{1,0:T(8,128)(2,1)} fusion(bf16[16,4096]{0,1:T(8,128)(2,1)} %get-tuple-element.23, bf16[16,4096]{0,1:T(8,128)(2,1)S(1)} %get-tuple-element.22), kind=kLoop, calls=%fused_computation.8 | loop fusion | flops 524288 | bytes 524288 | tf_op jit(solution)/shard_map/transpose | solution.py:72
  79.3 1.8 fusion.2
  81.1 6.8 %shard_map.79 = f32[128,16]{1,0:T(8,128)} custom-call(bf16[128,128]{1,0:T(8,128)(2,1)} %pad_bitcast_fusion.1.left_ref, bf16[128,4096]{1,0:T(8,128)(2,1)} %pad.18.right_ref, bf16[4096,32]{1,0:T(8,128)(2,1)} %maximum_bitcast_fusion.d12_ref, bf16[4096,16]{1,0:T(8,128)(2,1)} %bitcast.100), custom_call_target="tpu_custom_call" | custom-call | flops 184549376 | bytes 1482752 | tf_op jit(solution)/shard_map/pallas_call | solution.py:76
  87.9 1.0 fusion.26
  89.0 0.7 broadcast_in_dim.15
  89.7 2.7 %all-to-all-start.3 = ((f32[32,16,128]{2,1,0:T(8,128)}), f32[32,16,128]{2,1,0:T(8,128)S(1)}, u32[]{:S(2)}, u32[]{:S(2)}) async-start(f32[32,16,128]{2,1,0:T(8,128)} %broadcast_in_dim.15), calls=%async_computation.3 | async-start | bytes 524288 | tf_op jit(solution)/shard_map/all_to_all | solution.py:20
  94.8 1.9 copy.181
  97.2 0.8 fusion.7
  98.1 4.4 %concatenate.52 = bf16[102,1024]{0,1:T(8,128)(2,1)S(1)} concatenate(bf16[16,1024]{0,1:T(8,128)(2,1)S(1)} %copy.144, bf16[16,1024]{0,1:T(8,128)(2,1)S(1)} %copy.144, bf16[16,1024]{0,1:T(8,128)(2,1)S(1)} %get-tuple-element.31, bf16[16,1024]{0,1:T(8,128)(2,1)S(1)} %copy.144, bf16[16,1024]{0,1:T(8,128)(2,1)} %get-tuple-element.30, bf16[16,1024]{0,1:T(8,128)(2,1)S(1)} %get-tuple-element.31, ...), dimensions={0} | concatenate | bytes 417792 | tf_op jit(solution)/shard_map/concatenate | solution.py:64
  102.5 0.8 pad_bitcast_fusion.left_ref
  103.4 8.3 %shard_map.80 = f32[16,1024]{1,0:T(8,128)S(1)} custom-call(s32[1]{0:T(128)} %constant.72.clone.1.slot_ref, f32[1,1024,4096]{2,1,0:T(8,128)} %inv_ref.3, bf16[32,4096]{1,0:T(8,128)(2,1)S(1)} %pad_maximum_fusion.1.rcat_ref, bf16[16,4096]{1,0:T(8,128)(2,1)S(1)} %get-tuple-element.35.r1_ref), custom_call_target="tpu_custom_call" | custom-call | flops 402653184 | bytes 16777216 | tf_op jit(solution)/shard_map/pallas_call | solution.py:135
  112.3 3.9 %all-to-all-start.4 = ((f32[8,16,128]{2,1,0:T(8,128)}), f32[8,16,128]{2,1,0:T(8,128)S(1)}, u32[]{:S(2)}, u32[]{:S(2)}) async-start(f32[8,16,128]{2,1,0:T(8,128)} %bitcast_bitcast_fusion), calls=%async_computation.4 | async-start | bytes 131072 | tf_op jit(solution)/shard_map/all_to_all | solution.py:167
  116.3 5.0 %all-to-all-done.4 = f32[8,16,128]{2,1,0:T(8,128)S(1)} async-done(((f32[8,16,128]{2,1,0:T(8,128)}), f32[8,16,128]{2,1,0:T(8,128)S(1)}, u32[]{:S(2)}, u32[]{:S(2)}) %all-to-all-start.4) | async-done | bytes 65568 | tf_op jit(solution)/shard_map/all_to_all | solution.py:167
  121.3 0.7 broadcast_in_dim.17
  122.0 3.9 %all-to-all-start.5 = ((f32[32,16,128]{2,1,0:T(8,128)}), f32[32,16,128]{2,1,0:T(8,128)S(1)}, u32[]{:S(2)}, u32[]{:S(2)}) async-start(f32[32,16,128]{2,1,0:T(8,128)} %broadcast_in_dim.17), calls=%async_computation.5 | async-start | bytes 524288 | tf_op jit(solution)/shard_map/all_to_all | solution.py:20
  126.2 1.1 pad.19.right_ref
  127.3 25.7 %shard_map.78 = f32[1024,16]{1,0:T(8,128)} custom-call(bf16[1024,128]{1,0:T(8,128)(2,1)} %pad_bitcast_fusion.left_ref, bf16[128,4096]{1,0:T(8,128)(2,1)} %pad.18.right_ref, bf16[4096,32]{1,0:T(8,128)(2,1)} %maximum_bitcast_fusion.d12_ref, bf16[4096,16]{1,0:T(8,128)(2,1)} %bitcast.101), custom_call_target="tpu_custom_call" | custom-call | flops 1476395008 | bytes 1769472 | tf_op jit(solution)/shard_map/pallas_call | solution.py:76
  154.1 1.7 reduce-precision_convert_fusion
  156.0 3.1 %maximum_bitcast_fusion.1.d12_ref = bf16[4096,32]{1,0:T(8,128)(2,1)} fusion(bf16[16,4096]{0,1:T(8,128)(2,1)} %get-tuple-element.21, bf16[16,4096]{0,1:T(8,128)(2,1)} %get-tuple-element.20), kind=kLoop, calls=%fused_computation.9 | loop fusion | flops 524288 | bytes 524288 | tf_op jit(solution)/shard_map/transpose | solution.py:72
  159.1 25.8 %shard_map.81 = f32[1024,16]{1,0:T(8,128)} custom-call(bf16[1024,128]{1,0:T(8,128)(2,1)} %pad_bitcast_fusion.left_ref, bf16[128,4096]{1,0:T(8,128)(2,1)} %pad.19.right_ref, bf16[4096,32]{1,0:T(8,128)(2,1)} %maximum_bitcast_fusion.1.d12_ref, bf16[4096,16]{1,0:T(8,128)(2,1)} %bitcast.106), custom_call_target="tpu_custom_call" | custom-call | flops 1476395008 | bytes 1769472 | tf_op jit(solution)/shard_map/pallas_call | solution.py:76
  185.4 1.7 add_add_fusion
  187.0 0.8 copy.182
  187.8 0.8 copy.183
  (114 shorter events, 8.9 us)
Async XLA Ops:
  3.9 4.9 %copy-start.23 = (pred[1024]{0:T(1024)(128)(4,1)}, pred[1024]{0:T(1024)(128)(4,1)S(1)}, u32[]{:S(2)}) copy-start(pred[1024]{0:T(1024)(128)(4,1)S(1)} %get-tuple-element.66) | copy-start | bytes 3076
  3.9 5.0 %copy-start.25 = (pred[1024]{0:T(1024)(128)(4,1)}, pred[1024]{0:T(1024)(128)(4,1)S(1)}, u32[]{:S(2)}) copy-start(pred[1024]{0:T(1024)(128)(4,1)S(1)} %get-tuple-element.15) | copy-start | bytes 3076
  4.4 4.4 %copy-start.12 = (s32[1024]{0:T(1024)}, s32[1024]{0:T(1024)S(1)}, u32[]{:S(2)}) copy-start(s32[1024]{0:T(1024)S(1)} %add_bitcast_fusion) | copy-start | bytes 12292
  5.0 3.3 %copy-start.14 = (s32[1024]{0:T(1024)}, s32[1024]{0:T(1024)S(1)}, u32[]{:S(2)}) copy-start(s32[1024]{0:T(1024)S(1)} %add_bitcast_fusion.1) | copy-start | bytes 12292
  10.3 26.9 %all-to-all-start = ((f32[32,48,128]{2,1,0:T(8,128)}), f32[32,48,128]{2,1,0:T(8,128)S(1)}, u32[]{:S(2)}, u32[]{:S(2)}) async-start(f32[32,48,128]{2,1,0:T(8,128)} %broadcast_in_dim.12), calls=%async_computation | async-start | bytes 1572864 | tf_op jit(solution)/shard_map/all_to_all | solution.py:20
  46.4 8.9 %all-to-all-start.1 = ((f32[8,16,128]{2,1,0:T(8,128)}), f32[8,16,128]{2,1,0:T(8,128)S(1)}, u32[]{:S(2)}, u32[]{:S(2)}) async-start(f32[8,16,128]{2,1,0:T(8,128)} %bitcast_bitcast_fusion.1), calls=%async_computation.1 | async-start | bytes 131072 | tf_op jit(solution)/shard_map/all_to_all | solution.py:167
  55.9 13.1 %all-to-all-start.2 = ((f32[32,16,128]{2,1,0:T(8,128)}), f32[32,16,128]{2,1,0:T(8,128)S(1)}, u32[]{:S(2)}, u32[]{:S(2)}) async-start(f32[32,16,128]{2,1,0:T(8,128)} %broadcast_in_dim.14), calls=%async_computation.2 | async-start | bytes 524288 | tf_op jit(solution)/shard_map/all_to_all | solution.py:20
  58.9 10.1 %copy-start.6 = (bf16[3,4096]{1,0:T(4,128)(2,1)}, bf16[3,4096]{1,0:T(4,128)(2,1)S(1)}, u32[]{:S(2)}) copy-start(bf16[3,4096]{1,0:T(4,128)(2,1)S(1)} %broadcast.60) | copy-start | bytes 73732
  69.1 0.7 copy-start.4
  72.6 8.4 %copy-start = (bf16[16,4096]{0,1:T(8,128)(2,1)}, bf16[16,4096]{0,1:T(8,128)(2,1)S(1)}, u32[]{:S(2)}) copy-start(bf16[16,4096]{0,1:T(8,128)(2,1)S(1)} %get-tuple-element.22) | copy-start | bytes 393220
  74.7 6.3 %copy-start.17 = (bf16[16,128]{1,0:T(8,128)(2,1)}, bf16[16,128]{1,0:T(8,128)(2,1)S(1)}, u32[]{:S(2)}) copy-start(bf16[16,128]{1,0:T(8,128)(2,1)S(1)} %copy.159) | copy-start | bytes 12292
  75.6 5.5 %copy-start.19 = (bf16[16,128]{1,0:T(8,128)(2,1)}, bf16[16,128]{1,0:T(8,128)(2,1)S(1)}, u32[]{:S(2)}) copy-start(bf16[16,128]{1,0:T(8,128)(2,1)S(1)} %copy.160) | copy-start | bytes 12292
  76.4 4.6 %copy-start.21 = (bf16[16,128]{1,0:T(8,128)(2,1)}, bf16[16,128]{1,0:T(8,128)(2,1)S(1)}, u32[]{:S(2)}) copy-start(bf16[16,128]{1,0:T(8,128)(2,1)S(1)} %copy.158) | copy-start | bytes 12292
  81.1 11.4 %copy-start.1 = (f32[1,1024]{0,1:T(8,128)S(1)}, f32[1,1024]{0,1:T(8,128)}, u32[]{:S(2)}) copy-start(f32[1,1024]{0,1:T(8,128)} %copy.142) | copy-start | bytes 12292
  81.1 11.4 %copy-start.2 = (f32[1,1024]{0,1:T(8,128)S(1)}, f32[1,1024]{0,1:T(8,128)}, u32[]{:S(2)}) copy-start(f32[1,1024]{0,1:T(8,128)} %copy.143) | copy-start | bytes 12292
  87.9 4.7 %copy-start.8 = (f32[16,1024]{1,0:T(8,128)S(1)}, f32[16,1024]{1,0:T(8,128)}, u32[]{:S(2)}) copy-start(f32[16,1024]{1,0:T(8,128)} %param.6) | copy-start | bytes 196612
  87.9 6.0 %copy-start.10 = (f32[16,1024]{1,0:T(8,128)S(1)}, f32[16,1024]{1,0:T(8,128)}, u32[]{:S(2)}) copy-start(f32[16,1024]{1,0:T(8,128)} %param.7) | copy-start | bytes 196612
  88.9 5.3 %copy-start.16 = (bf16[1,1024]{1,0:T(2,128)(2,1)S(1)}, bf16[1,1024]{1,0:T(2,128)(2,1)}, u32[]{:S(2)}) copy-start(bf16[1,1024]{1,0:T(2,128)(2,1)} %get-tuple-element.68) | copy-start | bytes 6148
  88.9 5.5 %copy-start.9 = (f32[16,1024]{1,0:T(8,128)S(1)}, f32[16,1024]{1,0:T(8,128)}, u32[]{:S(2)}) copy-start(f32[16,1024]{1,0:T(8,128)} %get-tuple-element.57) | copy-start | bytes 196612
  89.7 4.9 %copy-start.11 = (bf16[16,1024]{1,0:T(8,128)(2,1)S(1)}, bf16[16,1024]{1,0:T(8,128)(2,1)}, u32[]{:S(2)}) copy-start(bf16[16,1024]{1,0:T(8,128)(2,1)} %get-tuple-element.56) | copy-start | bytes 98308
  89.7 13.6 %all-to-all-start.3 = ((f32[32,16,128]{2,1,0:T(8,128)}), f32[32,16,128]{2,1,0:T(8,128)S(1)}, u32[]{:S(2)}, u32[]{:S(2)}) async-start(f32[32,16,128]{2,1,0:T(8,128)} %broadcast_in_dim.15), calls=%async_computation.3 | async-start | bytes 524288 | tf_op jit(solution)/shard_map/all_to_all | solution.py:20
  103.4 22.6 %copy-start.7 = (bf16[3,4096]{1,0:T(4,128)(2,1)S(1)}, bf16[3,4096]{1,0:T(4,128)(2,1)}, u32[]{:S(2)}) copy-start(bf16[3,4096]{1,0:T(4,128)(2,1)} %copy-done.6) | copy-start | bytes 73732
  112.3 9.0 %all-to-all-start.4 = ((f32[8,16,128]{2,1,0:T(8,128)}), f32[8,16,128]{2,1,0:T(8,128)S(1)}, u32[]{:S(2)}, u32[]{:S(2)}) async-start(f32[8,16,128]{2,1,0:T(8,128)} %bitcast_bitcast_fusion), calls=%async_computation.4 | async-start | bytes 131072 | tf_op jit(solution)/shard_map/all_to_all | solution.py:167
  122.0 31.4 %all-to-all-start.5 = ((f32[32,16,128]{2,1,0:T(8,128)}), f32[32,16,128]{2,1,0:T(8,128)S(1)}, u32[]{:S(2)}, u32[]{:S(2)}) async-start(f32[32,16,128]{2,1,0:T(8,128)} %broadcast_in_dim.17), calls=%async_computation.5 | async-start | bytes 524288 | tf_op jit(solution)/shard_map/all_to_all | solution.py:20
  127.3 25.7 %copy-start.15 = (s32[1024]{0:T(1024)S(1)}, s32[1024]{0:T(1024)}, u32[]{:S(2)}) copy-start(s32[1024]{0:T(1024)} %copy-done.14) | copy-start | bytes 12292
  127.3 25.7 %copy-start.18 = (bf16[16,128]{1,0:T(8,128)(2,1)S(1)}, bf16[16,128]{1,0:T(8,128)(2,1)}, u32[]{:S(2)}) copy-start(bf16[16,128]{1,0:T(8,128)(2,1)} %copy-done.17) | copy-start | bytes 12292
  127.3 25.7 %copy-start.20 = (bf16[16,128]{1,0:T(8,128)(2,1)S(1)}, bf16[16,128]{1,0:T(8,128)(2,1)}, u32[]{:S(2)}) copy-start(bf16[16,128]{1,0:T(8,128)(2,1)} %copy-done.19) | copy-start | bytes 12292
  127.3 25.7 %copy-start.22 = (bf16[16,128]{1,0:T(8,128)(2,1)S(1)}, bf16[16,128]{1,0:T(8,128)(2,1)}, u32[]{:S(2)}) copy-start(bf16[16,128]{1,0:T(8,128)(2,1)} %copy-done.21) | copy-start | bytes 12292
  127.3 25.7 %copy-start.26 = (pred[1024]{0:T(1024)(128)(4,1)S(1)}, pred[1024]{0:T(1024)(128)(4,1)}, u32[]{:S(2)}) copy-start(pred[1024]{0:T(1024)(128)(4,1)} %copy-done.25) | copy-start | bytes 3076
  159.1 25.8 %copy-start.13 = (s32[1024]{0:T(1024)S(1)}, s32[1024]{0:T(1024)}, u32[]{:S(2)}) copy-start(s32[1024]{0:T(1024)} %copy-done.12) | copy-start | bytes 12292
  159.1 25.8 %copy-start.24 = (pred[1024]{0:T(1024)(128)(4,1)S(1)}, pred[1024]{0:T(1024)(128)(4,1)}, u32[]{:S(2)}) copy-start(pred[1024]{0:T(1024)(128)(4,1)} %copy-done.23) | copy-start | bytes 3076
  159.1 26.2 %copy-start.3 = (f32[16,1024]{0,1:T(8,128)S(1)}, f32[16,1024]{0,1:T(8,128)}, u32[]{:S(2)}) copy-start(f32[16,1024]{0,1:T(8,128)} %copy.181) | copy-start | bytes 196612
  159.1 26.2 %copy-start.5 = (f32[1024,16]{1,0:T(8,128)S(1)}, f32[1024,16]{1,0:T(8,128)}, u32[]{:S(2)}) copy-start(f32[1024,16]{1,0:T(8,128)} %shard_map.78) | copy-start | bytes 196612

commit v6 on v4

--- a/solution.py
+++ b/solution.py
@@ -42,7 +42,7 @@
     dist = lax.dot_general(left, right, (((0,), (0,)), ((), ())), preferred_element_type=jnp.float32)
     kernel = jnp.exp(-kernel_scale * dist)
     k1 = lax.reduce_precision(kernel, exponent_bits=8, mantissa_bits=7)
-    return k1.astype(jnp.bfloat16), (kernel - k1).astype(jnp.bfloat16)
+    return lax.optimization_barrier((k1.astype(jnp.bfloat16), (kernel - k1).astype(jnp.bfloat16)))
 
 
 def apply_kernel(delta, kernel):

time: 145 us -> 144 us (level)
  local copies, waits for them, and re-layouts: 17.6 us -> 12.6 us
  waiting for transfers between devices: 24.9 us -> 29 us
  starting transfers between devices: 24.7 us -> 28.2 us
  matrix products: 47.8 us -> 46.1 us
    all_to_all x4, waiting for transfers between devices: 20 us -> 24.5 us  [gather_all(): return lax.all_to_all(sent, ALL, 0, 0, tiled=True)]
    concatenate x3, local copies, waits for them, and re-layouts: 4.24 us -> 0.16 us  [kern(): jnp.concatenate([u1, u1, u2, u1, u3, u2, a1, a2, a3, one_u, one_u, one_u]...]
    all_to_all x4, starting transfers between devices: 17.4 us -> 21 us  [gather_all(): return lax.all_to_all(sent, ALL, 0, 0, tiled=True)]
    dot_general x3, matrix products: 14.9 us -> 12.4 us  [apply_kernel(): lax.dot_general(jnp.concatenate([d1, d2], axis=0), k1, dims, preferred_el...]
    dot_general x3, matrix products: 17.5 us -> 19.1 us  [kern(): lax.dot_general(left, right, (((0,), (0,)), ((), ())), preferred_element_...]
  transfers between devices with their start and end apart: 6 -> 6, of which waited for: 5 -> 4; matrix products, arithmetic and copies ran while one was open for 24% -> 25% of each run, Pallas kernels for 0% -> 0%
where the time goes in v6:
time: 144 us; the launch traced here: 143 us
  matrix products  46.1 us (32%)
  waiting for transfers between devices  29 us (20%)
  starting transfers between devices  28.2 us (20%)
  Pallas kernels  16.6 us (12%)
  local copies, waits for them, and re-layouts  12.6 us (9%)
  other arithmetic  5.98 us (4%)
  between operations  4.64 us (3%)
    all_to_all x4, waiting for transfers between devices, gather_all(): return lax.all_to_all(sent, ALL, 0, 0, tiled=True)  24.5 us
    all_to_all x4, starting transfers between devices, gather_all(): return lax.all_to_all(sent, ALL, 0, 0, tiled=True)  21 us
    dot_general x3, matrix products, kern(): lax.dot_general(left, right, (((0,), (0,)), ((), ())), preferred_element_...  19.1 us
    pallas_call x2, Pallas kernels, solve_rows(): pl.pallas_call(solve_kernel, grid_spec=grid_spec, out_shape=jax.ShapeDtyp...  16.6 us
    dot_general x3, matrix products, apply_kernel(): lax.dot_general(jnp.concatenate([d1, d2], axis=0), k1, dims, preferred_el...  12.4 us
    dot_general x3, matrix products, apply_kernel(): low = lax.dot_general(d1, k2, dims, preferred_element_type=jnp.float32)  12.4 us
    all_to_all x2, starting transfers between devices, solve(): scattered = lax.all_to_all(pieces, 'grp', 0, 0, tiled=True)  7.19 us
    concatenate x2, local copies, waits for them, and re-layouts, kern(): jnp.concatenate([v1, v2, v1, v3, v1, v2, one_v, one_v, one_v, b1, b2, b3]...  4.81 us
  transfers between devices with their start and end apart: 6, of which 4 were waited for; matrix products, arithmetic and copies ran while one was open for 25% of the time, Pallas kernels for 0%

profile of v6, /device:TPU:0, one launch (start us, length us, event | category | flops | bytes accessed | tf_op | source)
XLA Modules:
  0.0 143.1 jit_solution(7870958752441713681)
XLA Ops:
  0.6 1.3 fusion.65
  1.9 1.9 %convert_bitcast_fusion.1 = (s32[8,128]{1,0:T(8,128)S(1)}, pred[1024]{0:T(1024)(128)(4,1)S(1)}, s32[8,128]{1,0:T(8,128)S(1)}, pred[1024]{0:T(1024)(128)(4,1)S(1)}) fusion(s32[1024]{0:T(1024)} %param.9, s32[]{:T(128)} %bitcast, s32[]{:T(128)} %bitcast.3), kind=kLoop, calls=%fused_computation.148 | loop fusion | flops 4096 | bytes 14344 | tf_op jit(solution)/shard_map/convert
  3.8 0.3 reduce-window.16
  4.4 0.3 reduce-window.24
  5.0 0.8 constant_dynamic-update-slice_fusion.1
  5.8 0.9 multiply_reduce_fusion.2
  6.7 0.9 fusion.15
  7.7 0.3 fusion.11
  8.0 0.9 broadcast_in_dim.12
  9.0 7.3 %all-to-all-start = ((f32[32,48,128]{2,1,0:T(8,128)}), f32[32,48,128]{2,1,0:T(8,128)S(1)}, u32[]{:S(2)}, u32[]{:S(2)}) async-start(f32[32,48,128]{2,1,0:T(8,128)} %broadcast_in_dim.12), calls=%async_computation | async-start | bytes 1572864 | tf_op jit(solution)/shard_map/all_to_all | solution.py:20
  20.2 15.7 %all-to-all-done = f32[32,48,128]{2,1,0:T(8,128)S(1)} async-done(((f32[32,48,128]{2,1,0:T(8,128)}), f32[32,48,128]{2,1,0:T(8,128)S(1)}, u32[]{:S(2)}, u32[]{:S(2)}) %all-to-all-start) | async-done | bytes 786464 | tf_op jit(solution)/shard_map/all_to_all | solution.py:20
  35.9 0.1 multiply_reduce_fusion
  36.1 8.3 %shard_map.77 = f32[16,1024]{1,0:T(8,128)S(1)} custom-call(s32[1]{0:T(128)} %constant.67.clone.1.slot_ref, f32[1,1024,4096]{2,1,0:T(8,128)} %inv_ref.3, bf16[32,4096]{1,0:T(8,128)(2,1)S(1)} %pad_maximum_fusion.rcat_ref, bf16[16,4096]{1,0:T(8,128)(2,1)S(1)} %get-tuple-element.47.r1_ref), custom_call_target="tpu_custom_call" | custom-call | flops 402653184 | bytes 16777216 | tf_op jit(solution)/shard_map/pallas_call | solution.py:96
  44.4 0.6 bitcast_bitcast_fusion.1
  45.1 3.8 %all-to-all-start.1 = ((f32[8,16,128]{2,1,0:T(8,128)}), f32[8,16,128]{2,1,0:T(8,128)S(1)}, u32[]{:S(2)}, u32[]{:S(2)}) async-start(f32[8,16,128]{2,1,0:T(8,128)} %bitcast_bitcast_fusion.1), calls=%async_computation.1 | async-start | bytes 131072 | tf_op jit(solution)/shard_map/all_to_all | solution.py:128
  49.1 0.1 concatenate.60
  49.3 7.7 %fusion = (bf16[1024,4096]{1,0:T(8,128)(2,1)}, bf16[1024,4096]{1,0:T(8,128)(2,1)}) fusion(bf16[102,1024]{1,0:T(8,128)(2,1)S(1)} %concatenate.59, bf16[102,4096]{1,0:T(8,128)(2,1)S(1)} %concatenate.60), kind=kOutput, calls=%fused_computation.4 | convolution fusion | flops 876609536 | bytes 17821696 | tf_op jit(solution)/shard_map/dot_general | solution.py:42
  57.0 0.7 fusion.3
  57.7 4.7 %concatenate.66 = bf16[102,4096]{1,0:T(8,128)(2,1)} concatenate(bf16[16,4096]{1,0:T(8,128)(2,1)S(1)} %get-tuple-element.36, bf16[16,4096]{1,0:T(8,128)(2,1)S(1)} %get-tuple-element.35, bf16[16,4096]{1,0:T(8,128)(2,1)S(1)} %get-tuple-element.36, bf16[16,4096]{1,0:T(8,128)(2,1)S(1)} %get-tuple-element.34, bf16[16,4096]{1,0:T(8,128)(2,1)S(1)} %get-tuple-element.36, ...), dimensions={0} | concatenate | bytes 1671168 | tf_op jit(solution)/shard_map/concatenate | solution.py:41
  62.4 0.7 broadcast_in_dim.14
  63.1 5.3 %all-to-all-start.2 = ((f32[32,16,128]{2,1,0:T(8,128)}), f32[32,16,128]{2,1,0:T(8,128)S(1)}, u32[]{:S(2)}, u32[]{:S(2)}) async-start(f32[32,16,128]{2,1,0:T(8,128)} %broadcast_in_dim.14), calls=%async_computation.2 | async-start | bytes 524288 | tf_op jit(solution)/shard_map/all_to_all | solution.py:20
  68.4 10.7 %fusion.1 = (bf16[1024,4096]{1,0:T(8,128)(2,1)}, bf16[1024,4096]{1,0:T(8,128)(2,1)}) fusion(bf16[102,1024]{1,0:T(8,128)(2,1)} %copy-done.1, bf16[102,4096]{1,0:T(8,128)(2,1)} %concatenate.66), kind=kOutput, calls=%fused_computation.5 | convolution fusion | flops 876609536 | bytes 17821696 | tf_op jit(solution)/shard_map/dot_general | solution.py:42
  79.1 0.2 copy.18
  79.3 0.2 fusion.18
  79.4 0.2 copy.61
  79.6 1.0 fusion.8
  80.7 0.5 fusion.32
  81.1 0.4 fusion.10
  81.5 0.7 broadcast_in_dim.15
  82.3 5.8 %all-to-all-start.3 = ((f32[32,16,128]{2,1,0:T(8,128)}), f32[32,16,128]{2,1,0:T(8,128)S(1)}, u32[]{:S(2)}, u32[]{:S(2)}) async-start(f32[32,16,128]{2,1,0:T(8,128)} %broadcast_in_dim.15), calls=%async_computation.3 | async-start | bytes 524288 | tf_op jit(solution)/shard_map/all_to_all | solution.py:20
  88.1 6.0 %fusion.33 = f32[32,1024]{1,0:T(8,128)S(1)} fusion(bf16[1024,4096]{1,0:T(8,128)(2,1)} %get-tuple-element.8, bf16[16,4096]{1,0:T(8,128)(2,1)S(1)} %get-tuple-element.42, bf16[16,4096]{1,0:T(8,128)(2,1)S(1)} %get-tuple-element.43), kind=kOutput, calls=%fused_computation.78 | convolution fusion | flops 268959744 | bytes 8781824 | tf_op jit(solution)/shard_map/dot_general | solution.py:55
  94.1 4.2 %all-to-all-done.3 = f32[32,16,128]{2,1,0:T(8,128)S(1)} async-done(((f32[32,16,128]{2,1,0:T(8,128)}), f32[32,16,128]{2,1,0:T(8,128)S(1)}, u32[]{:S(2)}, u32[]{:S(2)}) %all-to-all-start.3) | async-done | bytes 262176 | tf_op jit(solution)/shard_map/all_to_all | solution.py:20
  98.4 8.3 %shard_map.78 = f32[16,1024]{1,0:T(8,128)S(1)} custom-call(s32[1]{0:T(128)} %constant.67.clone.1.slot_ref, f32[1,1024,4096]{2,1,0:T(8,128)} %inv_ref.3, bf16[32,4096]{1,0:T(8,128)(2,1)S(1)} %pad_maximum_fusion.2.rcat_ref, bf16[16,4096]{1,0:T(8,128)(2,1)S(1)} %get-tuple-element.37.r1_ref), custom_call_target="tpu_custom_call" | custom-call | flops 402653184 | bytes 16777216 | tf_op jit(solution)/shard_map/pallas_call | solution.py:96
  106.7 0.6 bitcast_bitcast_fusion
  107.4 3.4 %all-to-all-start.4 = ((f32[8,16,128]{2,1,0:T(8,128)}), f32[8,16,128]{2,1,0:T(8,128)S(1)}, u32[]{:S(2)}, u32[]{:S(2)}) async-start(f32[8,16,128]{2,1,0:T(8,128)} %bitcast_bitcast_fusion), calls=%async_computation.4 | async-start | bytes 131072 | tf_op jit(solution)/shard_map/all_to_all | solution.py:128
  110.7 0.5 fusion.48
  111.2 4.5 %all-to-all-done.4 = f32[8,16,128]{2,1,0:T(8,128)S(1)} async-done(((f32[8,16,128]{2,1,0:T(8,128)}), f32[8,16,128]{2,1,0:T(8,128)S(1)}, u32[]{:S(2)}, u32[]{:S(2)}) %all-to-all-start.4) | async-done | bytes 65568 | tf_op jit(solution)/shard_map/all_to_all | solution.py:128
  115.7 0.7 broadcast_in_dim.17
  116.4 2.6 %all-to-all-start.5 = ((f32[32,16,128]{2,1,0:T(8,128)}), f32[32,16,128]{2,1,0:T(8,128)S(1)}, u32[]{:S(2)}, u32[]{:S(2)}) async-start(f32[32,16,128]{2,1,0:T(8,128)} %broadcast_in_dim.17), calls=%async_computation.5 | async-start | bytes 524288 | tf_op jit(solution)/shard_map/all_to_all | solution.py:20
  119.0 5.7 %fusion.7 = f32[16,1024]{1,0:T(8,128)S(1)} fusion(f32[16,1024]{1,0:T(8,128)S(1)} %copy-done, bf16[16,4096]{1,0:T(8,128)(2,1)S(1)} %get-tuple-element.43, bf16[1024,4096]{1,0:T(8,128)(2,1)} %get-tuple-element.9, f32[32,1024]{1,0:T(8,128)S(1)} %fusion.33, f32[48,1024]{1,0:T(8,128)S(1)} %fusion.48), kind=kOutput, calls=%fused_computation.18 | convolution fusion | flops 134332416 | bytes 8978432 | tf_op jit(solution)/shard_map/dot_general | solution.py:56
  124.7 4.5 %all-to-all-done.5 = f32[32,16,128]{2,1,0:T(8,128)S(1)} async-done(((f32[32,16,128]{2,1,0:T(8,128)}), f32[32,16,128]{2,1,0:T(8,128)S(1)}, u32[]{:S(2)}, u32[]{:S(2)}) %all-to-all-start.5) | async-done | bytes 262176 | tf_op jit(solution)/shard_map/all_to_all | solution.py:20
  129.2 0.2 copy.22
  129.4 0.2 fusion.21
  129.5 0.2 copy.60
  129.7 0.5 fusion.38
  130.2 0.7 add_add_fusion
  130.9 6.0 %fusion.23 = f32[32,1024]{1,0:T(8,128)S(1)} fusion(bf16[1024,4096]{1,0:T(8,128)(2,1)} %get-tuple-element.12, bf16[16,4096]{1,0:T(8,128)(2,1)S(1)} %get-tuple-element.32, bf16[16,4096]{1,0:T(8,128)(2,1)S(1)} %get-tuple-element.33), kind=kOutput, calls=%fused_computation.60 | convolution fusion | flops 268959744 | bytes 8781824 | tf_op jit(solution)/shard_map/dot_general | solution.py:55
  136.8 6.3 %fusion.5 = f32[16,1024]{1,0:T(8,128)} fusion(f32[16,1024]{1,0:T(8,128)S(1)} %fusion.7, bf16[16,4096]{1,0:T(8,128)(2,1)S(1)} %get-tuple-element.33, bf16[1024,4096]{1,0:T(8,128)(2,1)} %get-tuple-element.13, f32[32,1024]{1,0:T(8,128)S(1)} %fusion.23, f32[48,1024]{1,0:T(8,128)S(1)} %fusion.38), kind=kOutput, calls=%fused_computation.15 | convolution fusion | flops 134332416 | bytes 8978432 | tf_op jit(solution)/shard_map/dot_general | solution.py:56
  (52 shorter events, 1.2 us)
Async XLA Ops:
  3.8 16.2 %copy-start.5 = (pred[1024]{0:T(1024)(128)(4,1)}, pred[1024]{0:T(1024)(128)(4,1)S(1)}, u32[]{:S(2)}) copy-start(pred[1024]{0:T(1024)(128)(4,1)S(1)} %get-tuple-element.72) | copy-start | bytes 3076
  3.8 16.2 %copy-start.7 = (pred[1024]{0:T(1024)(128)(4,1)}, pred[1024]{0:T(1024)(128)(4,1)S(1)}, u32[]{:S(2)}) copy-start(pred[1024]{0:T(1024)(128)(4,1)S(1)} %get-tuple-element.17) | copy-start | bytes 3076
  4.4 4.6 %copy-start.3 = (s32[1024]{0:T(1024)}, s32[1024]{0:T(1024)S(1)}, u32[]{:S(2)}) copy-start(s32[1024]{0:T(1024)S(1)} %add_bitcast_fusion.1) | copy-start | bytes 12292
  9.0 26.9 %all-to-all-start = ((f32[32,48,128]{2,1,0:T(8,128)}), f32[32,48,128]{2,1,0:T(8,128)S(1)}, u32[]{:S(2)}, u32[]{:S(2)}) async-start(f32[32,48,128]{2,1,0:T(8,128)} %broadcast_in_dim.12), calls=%async_computation | async-start | bytes 1572864 | tf_op jit(solution)/shard_map/all_to_all | solution.py:20
  20.0 29.3 %copy-start.1 = (bf16[102,1024]{1,0:T(8,128)(2,1)}, bf16[102,1024]{1,0:T(8,128)(2,1)S(1)}, u32[]{:S(2)}) copy-start(bf16[102,1024]{1,0:T(8,128)(2,1)S(1)} %concatenate.59) | copy-start | bytes 626692
  45.1 17.3 %all-to-all-start.1 = ((f32[8,16,128]{2,1,0:T(8,128)}), f32[8,16,128]{2,1,0:T(8,128)S(1)}, u32[]{:S(2)}, u32[]{:S(2)}) async-start(f32[8,16,128]{2,1,0:T(8,128)} %bitcast_bitcast_fusion.1), calls=%async_computation.1 | async-start | bytes 131072 | tf_op jit(solution)/shard_map/all_to_all | solution.py:128
  63.1 16.0 %all-to-all-start.2 = ((f32[32,16,128]{2,1,0:T(8,128)}), f32[32,16,128]{2,1,0:T(8,128)S(1)}, u32[]{:S(2)}, u32[]{:S(2)}) async-start(f32[32,16,128]{2,1,0:T(8,128)} %broadcast_in_dim.14), calls=%async_computation.2 | async-start | bytes 524288 | tf_op jit(solution)/shard_map/all_to_all | solution.py:20
  68.3 11.3 %copy-start.4 = (s32[1024]{0:T(1024)S(1)}, s32[1024]{0:T(1024)}, u32[]{:S(2)}) copy-start(s32[1024]{0:T(1024)} %copy-done.3) | copy-start | bytes 12292
  68.4 11.3 %copy-start.6 = (pred[1024]{0:T(1024)(128)(4,1)S(1)}, pred[1024]{0:T(1024)(128)(4,1)}, u32[]{:S(2)}) copy-start(pred[1024]{0:T(1024)(128)(4,1)} %copy-done.5) | copy-start | bytes 3076
  68.4 11.3 %copy-start.8 = (pred[1024]{0:T(1024)(128)(4,1)S(1)}, pred[1024]{0:T(1024)(128)(4,1)}, u32[]{:S(2)}) copy-start(pred[1024]{0:T(1024)(128)(4,1)} %copy-done.7) | copy-start | bytes 3076
  82.3 16.0 %all-to-all-start.3 = ((f32[32,16,128]{2,1,0:T(8,128)}), f32[32,16,128]{2,1,0:T(8,128)S(1)}, u32[]{:S(2)}, u32[]{:S(2)}) async-start(f32[32,16,128]{2,1,0:T(8,128)} %broadcast_in_dim.15), calls=%async_computation.3 | async-start | bytes 524288 | tf_op jit(solution)/shard_map/all_to_all | solution.py:20
  98.4 20.6 %copy-start = (f32[16,1024]{1,0:T(8,128)S(1)}, f32[16,1024]{1,0:T(8,128)}, u32[]{:S(2)}) copy-start(f32[16,1024]{1,0:T(8,128)} %param.7) | copy-start | bytes 196612
  106.7 23.5 %copy-start.2 = (f32[16,1024]{1,0:T(8,128)S(1)}, f32[16,1024]{1,0:T(8,128)}, u32[]{:S(2)}) copy-start(f32[16,1024]{1,0:T(8,128)} %param.8) | copy-start | bytes 196612
  107.4 8.3 %all-to-all-start.4 = ((f32[8,16,128]{2,1,0:T(8,128)}), f32[8,16,128]{2,1,0:T(8,128)S(1)}, u32[]{:S(2)}, u32[]{:S(2)}) async-start(f32[8,16,128]{2,1,0:T(8,128)} %bitcast_bitcast_fusion), calls=%async_computation.4 | async-start | bytes 131072 | tf_op jit(solution)/shard_map/all_to_all | solution.py:128
  116.4 12.8 %all-to-all-start.5 = ((f32[32,16,128]{2,1,0:T(8,128)}), f32[32,16,128]{2,1,0:T(8,128)S(1)}, u32[]{:S(2)}, u32[]{:S(2)}) async-start(f32[32,16,128]{2,1,0:T(8,128)} %broadcast_in_dim.17), calls=%async_computation.5 | async-start | bytes 524288 | tf_op jit(solution)/shard_map/all_to_all | solution.py:20

commit v7 on v6

--- a/solution.py
+++ b/solution.py
@@ -155,13 +155,16 @@
     overlap = lax.dot_general(sel0, sel1, (((0,), (0,)), ((), ())), preferred_element_type=jnp.float32)
     overlap = overlap.astype(jnp.bfloat16)
     res1_local = res1_start - early - ridge_weight * exact_dot(owned0, overlap, plain)
+    res1_local, pts_late, pts0_late, pts1_late = lax.optimization_barrier(
+        (res1_local, points, block_pts0, block_pts1)
+    )
     block_res1 = to_block(gather_all(res1_local, n_dev), rhs)
 
     spread0 = exact_dot(owned0, sel0, (((1,), (1,)), ((), ())))
-    update0 = apply_kernel(delta0, kern(points, block_pts0))
+    update0 = apply_kernel(delta0, kern(pts_late, pts0_late))
     residual = residual - update0 - ridge_weight * spread0
     coef = coef + spread0
-    kernel1 = kern(points, block_pts1)
+    kernel1 = kern(pts_late, pts1_late)
 
     delta1 = solve(block_res1, block1)
     owned1 = lax.dynamic_slice_in_dim(delta1, mine * per, per, axis=1)

time: 144 us -> 145 us (level)
  waiting for transfers between devices: 29 us -> 33.1 us
  starting transfers between devices: 28.2 us -> 24.7 us
  matrix products: 46.1 us -> 43.8 us
    all_to_all x2, waiting for transfers between devices: 4.47 us -> 9.49 us  [solve(): scattered = lax.all_to_all(pieces, 'grp', 0, 0, tiled=True)]
    concatenate x2 -> x3, local copies, waits for them, and re-layouts: 4.81 us -> 0.44 us  [kern(): jnp.concatenate([v1, v2, v1, v3, v1, v2, one_v, one_v, one_v, b1, b2, b3]...]
    concatenate x3, local copies, waits for them, and re-layouts: 0.16 us -> 4.25 us  [kern(): jnp.concatenate([u1, u1, u2, u1, u3, u2, a1, a2, a3, one_u, one_u, one_u]...]
    all_to_all x4, starting transfers between devices: 21 us -> 17.1 us  [gather_all(): return lax.all_to_all(sent, ALL, 0, 0, tiled=True)]
    dot_general x3, matrix products: 19.1 us -> 16.8 us  [kern(): lax.dot_general(left, right, (((0,), (0,)), ((), ())), preferred_element_...]
  transfers between devices with their start and end apart: 6 -> 6, of which waited for: 4 -> 5; matrix products, arithmetic and copies ran while one was open for 25% -> 18% of each run, Pallas kernels for 0% -> 0%
where the time goes in v7:
time: 145 us; the launch traced here: 144 us
  matrix products  43.8 us (30%)
  waiting for transfers between devices  33.1 us (23%)
  starting transfers between devices  24.7 us (17%)
  Pallas kernels  16.6 us (11%)
  local copies, waits for them, and re-layouts  13.9 us (10%)
  other arithmetic  7.18 us (5%)
  between operations  4.85 us (3%)
    all_to_all x4, waiting for transfers between devices, gather_all(): return lax.all_to_all(sent, ALL, 0, 0, tiled=True)  23.6 us
    all_to_all x4, starting transfers between devices, gather_all(): return lax.all_to_all(sent, ALL, 0, 0, tiled=True)  17.1 us
    dot_general x3, matrix products, kern(): lax.dot_general(left, right, (((0,), (0,)), ((), ())), preferred_element_...  16.8 us
    pallas_call x2, Pallas kernels, solve_rows(): pl.pallas_call(solve_kernel, grid_spec=grid_spec, out_shape=jax.ShapeDtyp...  16.6 us
    dot_general x3, matrix products, apply_kernel(): low = lax.dot_general(d1, k2, dims, preferred_element_type=jnp.float32)  12.4 us
    dot_general x3, matrix products, apply_kernel(): lax.dot_general(jnp.concatenate([d1, d2], axis=0), k1, dims, preferred_el...  12.4 us
    all_to_all x2, waiting for transfers between devices, solve(): scattered = lax.all_to_all(pieces, 'grp', 0, 0, tiled=True)  9.49 us
    all_to_all x2, starting transfers between devices, solve(): scattered = lax.all_to_all(pieces, 'grp', 0, 0, tiled=True)  7.61 us
  transfers between devices with their start and end apart: 6, of which 5 were waited for; matrix products, arithmetic and copies ran while one was open for 18% of the time, Pallas kernels for 0%

profile of v7, /device:TPU:0, one launch (start us, length us, event | category | flops | bytes accessed | tf_op | source)
XLA Modules:
  0.0 144.1 jit_solution(5341423891308644666)
XLA Ops:
  0.6 1.3 fusion.67
  1.9 2.0 %convert_bitcast_fusion.1 = (s32[8,128]{1,0:T(8,128)S(1)}, pred[1024]{0:T(1024)(128)(4,1)S(1)}, s32[8,128]{1,0:T(8,128)S(1)}, pred[1024]{0:T(1024)(128)(4,1)S(1)}) fusion(s32[1024]{0:T(1024)} %param.9, s32[]{:T(128)} %bitcast, s32[]{:T(128)} %bitcast.3), kind=kLoop, calls=%fused_computation.161 | loop fusion | flops 4096 | bytes 14344 | tf_op jit(solution)/shard_map/convert
  3.9 0.3 reduce-window.16
  4.5 0.3 reduce-window.24
  5.1 0.8 constant_dynamic-update-slice_fusion.1
  5.9 0.8 constant_dynamic-update-slice_fusion
  6.8 0.9 fusion.15
  7.7 0.3 fusion.11
  8.1 0.9 broadcast_in_dim.12
  9.0 7.3 %all-to-all-start = ((f32[32,48,128]{2,1,0:T(8,128)}), f32[32,48,128]{2,1,0:T(8,128)S(1)}, u32[]{:S(2)}, u32[]{:S(2)}) async-start(f32[32,48,128]{2,1,0:T(8,128)} %broadcast_in_dim.12), calls=%async_computation | async-start | bytes 1572864 | tf_op jit(solution)/shard_map/all_to_all | solution.py:20
  20.2 4.2 %concatenate.62 = bf16[102,128]{1,0:T(8,128)(2,1)} concatenate(bf16[16,128]{1,0:T(8,128)(2,1)S(1)} %get-tuple-element.69, bf16[16,128]{1,0:T(8,128)(2,1)S(1)} %get-tuple-element.69, bf16[16,128]{1,0:T(8,128)(2,1)S(1)} %get-tuple-element.70, bf16[16,128]{1,0:T(8,128)(2,1)S(1)} %get-tuple-element.69, bf16[16,128]{1,0:T(8,128)(2,1)S(1)} %get-tuple-element.71, ...), dimensions={0} | concatenate | bytes 52224 | tf_op jit(solution)/shard_map/concatenate | solution.py:40
  24.4 11.5 %all-to-all-done = f32[32,48,128]{2,1,0:T(8,128)S(1)} async-done(((f32[32,48,128]{2,1,0:T(8,128)}), f32[32,48,128]{2,1,0:T(8,128)S(1)}, u32[]{:S(2)}, u32[]{:S(2)}) %all-to-all-start) | async-done | bytes 786464 | tf_op jit(solution)/shard_map/all_to_all | solution.py:20
  36.1 8.3 %shard_map.77 = f32[16,1024]{1,0:T(8,128)S(1)} custom-call(s32[1]{0:T(128)} %constant.67.clone.1.slot_ref, f32[1,1024,4096]{2,1,0:T(8,128)} %inv_ref.3, bf16[32,4096]{1,0:T(8,128)(2,1)S(1)} %pad_maximum_fusion.rcat_ref, bf16[16,4096]{1,0:T(8,128)(2,1)S(1)} %get-tuple-element.59.r1_ref), custom_call_target="tpu_custom_call" | custom-call | flops 402653184 | bytes 16777216 | tf_op jit(solution)/shard_map/pallas_call | solution.py:96
  44.4 0.6 bitcast_bitcast_fusion.1
  45.1 3.8 %all-to-all-start.1 = ((f32[8,16,128]{2,1,0:T(8,128)}), f32[8,16,128]{2,1,0:T(8,128)S(1)}, u32[]{:S(2)}, u32[]{:S(2)}) async-start(f32[8,16,128]{2,1,0:T(8,128)} %bitcast_bitcast_fusion.1), calls=%async_computation.1 | async-start | bytes 131072 | tf_op jit(solution)/shard_map/all_to_all | solution.py:128
  49.0 5.0 %all-to-all-done.1 = f32[8,16,128]{2,1,0:T(8,128)S(1)} async-done(((f32[8,16,128]{2,1,0:T(8,128)}), f32[8,16,128]{2,1,0:T(8,128)S(1)}, u32[]{:S(2)}, u32[]{:S(2)}) %all-to-all-start.1) | async-done | bytes 65568 | tf_op jit(solution)/shard_map/all_to_all | solution.py:128
  53.9 0.7 broadcast_in_dim.14
  54.6 2.9 %all-to-all-start.2 = ((f32[32,16,128]{2,1,0:T(8,128)}), f32[32,16,128]{2,1,0:T(8,128)S(1)}, u32[]{:S(2)}, u32[]{:S(2)}) async-start(f32[32,16,128]{2,1,0:T(8,128)} %broadcast_in_dim.14), calls=%async_computation.2 | async-start | bytes 524288 | tf_op jit(solution)/shard_map/all_to_all | solution.py:20
  57.6 0.7 copy.59
  58.5 1.4 fusion.3
  60.0 7.8 %all-to-all-done.2 = f32[32,16,128]{2,1,0:T(8,128)S(1)} async-done(((f32[32,16,128]{2,1,0:T(8,128)}), f32[32,16,128]{2,1,0:T(8,128)S(1)}, u32[]{:S(2)}, u32[]{:S(2)}) %all-to-all-start.2) | async-done | bytes 262176 | tf_op jit(solution)/shard_map/all_to_all | solution.py:20
  67.9 0.2 fusion.18
  68.1 0.2 copy.57
  68.3 1.0 fusion.8
  69.3 0.5 fusion.34
  69.8 0.4 fusion.10
  70.2 0.9 multiply_reduce_fusion.3
  71.1 1.1 multiply_reduce_fusion.1
  72.4 7.7 %fusion = (bf16[1024,4096]{1,0:T(8,128)(2,1)}, bf16[1024,4096]{1,0:T(8,128)(2,1)}) fusion(bf16[102,1024]{1,0:T(8,128)(2,1)S(1)} %concatenate.65, bf16[102,4096]{1,0:T(8,128)(2,1)S(1)} %concatenate.66), kind=kOutput, calls=%fused_computation.4 | convolution fusion | flops 876609536 | bytes 17821696 | tf_op jit(solution)/shard_map/dot_general | solution.py:42
  80.1 0.7 broadcast_in_dim.15
  80.8 2.9 %all-to-all-start.3 = ((f32[32,16,128]{2,1,0:T(8,128)}), f32[32,16,128]{2,1,0:T(8,128)S(1)}, u32[]{:S(2)}, u32[]{:S(2)}) async-start(f32[32,16,128]{2,1,0:T(8,128)} %broadcast_in_dim.15), calls=%async_computation.3 | async-start | bytes 524288 | tf_op jit(solution)/shard_map/all_to_all | solution.py:20
  84.0 7.7 %fusion.1 = (bf16[1024,4096]{1,0:T(8,128)(2,1)}, bf16[1024,4096]{1,0:T(8,128)(2,1)}) fusion(bf16[102,1024]{1,0:T(8,128)(2,1)S(1)} %concatenate.65, bf16[102,4096]{1,0:T(8,128)(2,1)S(1)} %concatenate.69), kind=kOutput, calls=%fused_computation.5 | convolution fusion | flops 876609536 | bytes 17821696 | tf_op jit(solution)/shard_map/dot_general | solution.py:42
  91.7 6.0 %fusion.33 = f32[32,1024]{1,0:T(8,128)S(1)} fusion(bf16[1024,4096]{1,0:T(8,128)(2,1)} %get-tuple-element.16, bf16[16,4096]{1,0:T(8,128)(2,1)S(1)} %get-tuple-element.51, bf16[16,4096]{1,0:T(8,128)(2,1)S(1)} %get-tuple-element.52), kind=kOutput, calls=%fused_computation.85 | convolution fusion | flops 268959744 | bytes 8781824 | tf_op jit(solution)/shard_map/dot_general | solution.py:55
  97.7 8.3 %shard_map.78 = f32[16,1024]{1,0:T(8,128)S(1)} custom-call(s32[1]{0:T(128)} %constant.67.clone.1.slot_ref, f32[1,1024,4096]{2,1,0:T(8,128)} %inv_ref.3, bf16[32,4096]{1,0:T(8,128)(2,1)S(1)} %pad_maximum_fusion.2.rcat_ref, bf16[16,4096]{1,0:T(8,128)(2,1)S(1)} %get-tuple-element.45.r1_ref), custom_call_target="tpu_custom_call" | custom-call | flops 402653184 | bytes 16777216 | tf_op jit(solution)/shard_map/pallas_call | solution.py:96
  106.1 0.6 bitcast_bitcast_fusion
  106.7 3.8 %all-to-all-start.4 = ((f32[8,16,128]{2,1,0:T(8,128)}), f32[8,16,128]{2,1,0:T(8,128)S(1)}, u32[]{:S(2)}, u32[]{:S(2)}) async-start(f32[8,16,128]{2,1,0:T(8,128)} %bitcast_bitcast_fusion), calls=%async_computation.4 | async-start | bytes 131072 | tf_op jit(solution)/shard_map/all_to_all | solution.py:128
  110.5 0.5 fusion.50
  111.0 4.5 %all-to-all-done.4 = f32[8,16,128]{2,1,0:T(8,128)S(1)} async-done(((f32[8,16,128]{2,1,0:T(8,128)}), f32[8,16,128]{2,1,0:T(8,128)S(1)}, u32[]{:S(2)}, u32[]{:S(2)}) %all-to-all-start.4) | async-done | bytes 65568 | tf_op jit(solution)/shard_map/all_to_all | solution.py:128
  115.5 0.7 broadcast_in_dim.17
  116.3 3.9 %all-to-all-start.5 = ((f32[32,16,128]{2,1,0:T(8,128)}), f32[32,16,128]{2,1,0:T(8,128)S(1)}, u32[]{:S(2)}, u32[]{:S(2)}) async-start(f32[32,16,128]{2,1,0:T(8,128)} %broadcast_in_dim.17), calls=%async_computation.5 | async-start | bytes 524288 | tf_op jit(solution)/shard_map/all_to_all | solution.py:20
  120.2 5.7 %fusion.7 = f32[16,1024]{1,0:T(8,128)S(1)} fusion(f32[16,1024]{1,0:T(8,128)S(1)} %copy-done, bf16[16,4096]{1,0:T(8,128)(2,1)S(1)} %get-tuple-element.52, bf16[1024,4096]{1,0:T(8,128)(2,1)} %get-tuple-element.17, f32[32,1024]{1,0:T(8,128)S(1)} %fusion.33, f32[48,1024]{1,0:T(8,128)S(1)} %fusion.50), kind=kOutput, calls=%fused_computation.18 | convolution fusion | flops 134332416 | bytes 8978432 | tf_op jit(solution)/shard_map/dot_general | solution.py:56
  125.9 4.3 %all-to-all-done.5 = f32[32,16,128]{2,1,0:T(8,128)S(1)} async-done(((f32[32,16,128]{2,1,0:T(8,128)}), f32[32,16,128]{2,1,0:T(8,128)S(1)}, u32[]{:S(2)}, u32[]{:S(2)}) %all-to-all-start.5) | async-done | bytes 262176 | tf_op jit(solution)/shard_map/all_to_all | solution.py:20
  130.3 0.2 fusion.22
  130.5 0.2 copy.56
  130.7 0.5 fusion.40
  131.2 0.7 add_add_fusion
  131.8 6.0 %fusion.24 = f32[32,1024]{1,0:T(8,128)S(1)} fusion(bf16[1024,4096]{1,0:T(8,128)(2,1)} %get-tuple-element.20, bf16[16,4096]{1,0:T(8,128)(2,1)S(1)} %get-tuple-element.39, bf16[16,4096]{1,0:T(8,128)(2,1)S(1)} %get-tuple-element.40), kind=kOutput, calls=%fused_computation.68 | convolution fusion | flops 268959744 | bytes 8781824 | tf_op jit(solution)/shard_map/dot_general | solution.py:55
  137.8 6.3 %fusion.5 = f32[16,1024]{1,0:T(8,128)} fusion(f32[16,1024]{1,0:T(8,128)S(1)} %fusion.7, bf16[16,4096]{1,0:T(8,128)(2,1)S(1)} %get-tuple-element.40, bf16[1024,4096]{1,0:T(8,128)(2,1)} %get-tuple-element.21, f32[32,1024]{1,0:T(8,128)S(1)} %fusion.24, f32[48,1024]{1,0:T(8,128)S(1)} %fusion.40), kind=kOutput, calls=%fused_computation.15 | convolution fusion | flops 134332416 | bytes 8978432 | tf_op jit(solution)/shard_map/dot_general | solution.py:56
  (44 shorter events, 2.1 us)
Async XLA Ops:
  9.0 26.9 %all-to-all-start = ((f32[32,48,128]{2,1,0:T(8,128)}), f32[32,48,128]{2,1,0:T(8,128)S(1)}, u32[]{:S(2)}, u32[]{:S(2)}) async-start(f32[32,48,128]{2,1,0:T(8,128)} %broadcast_in_dim.12), calls=%async_computation | async-start | bytes 1572864 | tf_op jit(solution)/shard_map/all_to_all | solution.py:20
  45.1 8.9 %all-to-all-start.1 = ((f32[8,16,128]{2,1,0:T(8,128)}), f32[8,16,128]{2,1,0:T(8,128)S(1)}, u32[]{:S(2)}, u32[]{:S(2)}) async-start(f32[8,16,128]{2,1,0:T(8,128)} %bitcast_bitcast_fusion.1), calls=%async_computation.1 | async-start | bytes 131072 | tf_op jit(solution)/shard_map/all_to_all | solution.py:128
  54.6 13.1 %all-to-all-start.2 = ((f32[32,16,128]{2,1,0:T(8,128)}), f32[32,16,128]{2,1,0:T(8,128)S(1)}, u32[]{:S(2)}, u32[]{:S(2)}) async-start(f32[32,16,128]{2,1,0:T(8,128)} %broadcast_in_dim.14), calls=%async_computation.2 | async-start | bytes 524288 | tf_op jit(solution)/shard_map/all_to_all | solution.py:20
  80.8 16.8 %all-to-all-start.3 = ((f32[32,16,128]{2,1,0:T(8,128)}), f32[32,16,128]{2,1,0:T(8,128)S(1)}, u32[]{:S(2)}, u32[]{:S(2)}) async-start(f32[32,16,128]{2,1,0:T(8,128)} %broadcast_in_dim.15), calls=%async_computation.3 | async-start | bytes 524288 | tf_op jit(solution)/shard_map/all_to_all | solution.py:20
  97.7 22.5 %copy-start = (f32[16,1024]{1,0:T(8,128)S(1)}, f32[16,1024]{1,0:T(8,128)}, u32[]{:S(2)}) copy-start(f32[16,1024]{1,0:T(8,128)} %param.7) | copy-start | bytes 196612
  106.1 25.1 %copy-start.1 = (f32[16,1024]{1,0:T(8,128)S(1)}, f32[16,1024]{1,0:T(8,128)}, u32[]{:S(2)}) copy-start(f32[16,1024]{1,0:T(8,128)} %param.8) | copy-start | bytes 196612
  106.7 8.8 %all-to-all-start.4 = ((f32[8,16,128]{2,1,0:T(8,128)}), f32[8,16,128]{2,1,0:T(8,128)S(1)}, u32[]{:S(2)}, u32[]{:S(2)}) async-start(f32[8,16,128]{2,1,0:T(8,128)} %bitcast_bitcast_fusion), calls=%async_computation.4 | async-start | bytes 131072 | tf_op jit(solution)/shard_map/all_to_all | solution.py:128
  116.3 13.9 %all-to-all-start.5 = ((f32[32,16,128]{2,1,0:T(8,128)}), f32[32,16,128]{2,1,0:T(8,128)S(1)}, u32[]{:S(2)}, u32[]{:S(2)}) async-start(f32[32,16,128]{2,1,0:T(8,128)} %broadcast_in_dim.17), calls=%async_computation.5 | async-start | bytes 524288 | tf_op jit(solution)/shard_map/all_to_all | solution.py:20

commit v8 on v6

--- a/solution.py
+++ b/solution.py
@@ -122,7 +122,9 @@
         ).astype(jnp.bfloat16)
 
     def solve(block_res, block_id):
-        solved = solve_rows(inverse, block_id % slots, block_res)
+        return distribute(solve_rows(inverse, block_id % slots, block_res), block_id)
+
+    def distribute(solved, block_id):
         owner = block_id // slots
         pieces = jnp.transpose(solved.reshape(rhs, n_grp, per), (1, 0, 2))
         scattered = lax.all_to_all(pieces, "grp", 0, 0, tiled=True)
@@ -155,15 +157,18 @@
     overlap = lax.dot_general(sel0, sel1, (((0,), (0,)), ((), ())), preferred_element_type=jnp.float32)
     overlap = overlap.astype(jnp.bfloat16)
     res1_local = res1_start - early - ridge_weight * exact_dot(owned0, overlap, plain)
+    res1_local, pts_late, pts1_late = lax.optimization_barrier((res1_local, points, block_pts1))
     block_res1 = to_block(gather_all(res1_local, n_dev), rhs)
+    kernel1 = kern(pts_late, pts1_late)
 
+    solved1 = solve_rows(inverse, block1 % slots, block_res1)
+    solved1, pts_later, pts0_later = lax.optimization_barrier((solved1, points, block_pts0))
+    delta1 = distribute(solved1, block1)
     spread0 = exact_dot(owned0, sel0, (((1,), (1,)), ((), ())))
-    update0 = apply_kernel(delta0, kern(points, block_pts0))
+    update0 = apply_kernel(delta0, kern(pts_later, pts0_later))
     residual = residual - update0 - ridge_weight * spread0
     coef = coef + spread0
-    kernel1 = kern(points, block_pts1)
 
-    delta1 = solve(block_res1, block1)
     owned1 = lax.dynamic_slice_in_dim(delta1, mine * per, per, axis=1)
     spread1 = exact_dot(owned1, sel1, (((1,), (1,)), ((), ())))
     update1 = apply_kernel(delta1, kernel1)

time: 144 us -> 144 us (level)
  local copies, waits for them, and re-layouts: 12.6 us -> 16 us
  starting transfers between devices: 28.2 us -> 26.4 us
  matrix products: 46.1 us -> 44.5 us
    concatenate x3 -> x4, local copies, waits for them, and re-layouts: 0.16 us -> 4.29 us  [kern(): jnp.concatenate([u1, u1, u2, u1, u3, u2, a1, a2, a3, one_u, one_u, one_u]...]
    concatenate x2 -> x3, local copies, waits for them, and re-layouts: 4.81 us -> 1.19 us  [kern(): jnp.concatenate([v1, v2, v1, v3, v1, v2, one_v, one_v, one_v, b1, b2, b3]...]
    dot_general x3, matrix products: 19.1 us -> 16.8 us  [kern(): lax.dot_general(left, right, (((0,), (0,)), ((), ())), preferred_element_...]
    all_to_all x4, starting transfers between devices: 21 us -> 19.2 us  [gather_all(): return lax.all_to_all(sent, ALL, 0, 0, tiled=True)]
  transfers between devices with their start and end apart: 6 -> 6, of which waited for: 4 -> 5; matrix products, arithmetic and copies ran while one was open for 25% -> 19% of each run, Pallas kernels for 0% -> 0%
where the time goes in v8:
time: 144 us; the launch traced here: 142 us
  matrix products  44.5 us (31%)
  waiting for transfers between devices  28.7 us (20%)
  starting transfers between devices  26.4 us (18%)
  Pallas kernels  16.6 us (12%)
  local copies, waits for them, and re-layouts  16 us (11%)
  other arithmetic  5.4 us (4%)
  between operations  4.84 us (3%)
    all_to_all x4, waiting for transfers between devices, gather_all(): return lax.all_to_all(sent, ALL, 0, 0, tiled=True)  23.8 us
    all_to_all x4, starting transfers between devices, gather_all(): return lax.all_to_all(sent, ALL, 0, 0, tiled=True)  19.2 us
    dot_general x3, matrix products, kern(): lax.dot_general(left, right, (((0,), (0,)), ((), ())), preferred_element_...  16.8 us
    pallas_call x2, Pallas kernels, solve_rows(): pl.pallas_call(solve_kernel, grid_spec=grid_spec, out_shape=jax.ShapeDtyp...  16.6 us
    dot_general x3, matrix products, apply_kernel(): low = lax.dot_general(d1, k2, dims, preferred_element_type=jnp.float32)  13.1 us
    dot_general x3, matrix products, apply_kernel(): lax.dot_general(jnp.concatenate([d1, d2], axis=0), k1, dims, preferred_el...  12.4 us
    all_to_all x2, starting transfers between devices, distribute(): scattered = lax.all_to_all(pieces, 'grp', 0, 0, tiled=True)  7.19 us
    all_to_all x2, waiting for transfers between devices, distribute(): scattered = lax.all_to_all(pieces, 'grp', 0, 0, tiled=True)  4.97 us
  transfers between devices with their start and end apart: 6, of which 5 were waited for; matrix products, arithmetic and copies ran while one was open for 19% of the time, Pallas kernels for 0%

profile of v8, /device:TPU:0, one launch (start us, length us, event | category | flops | bytes accessed | tf_op | source)
XLA Modules:
  0.0 142.5 jit_solution(18102428146083577877)
XLA Ops:
  0.6 1.4 fusion.69
  2.0 2.0 %convert_bitcast_fusion.1 = (s32[8,128]{1,0:T(8,128)S(1)}, pred[1024]{0:T(1024)(128)(4,1)S(1)}, s32[8,128]{1,0:T(8,128)S(1)}, pred[1024]{0:T(1024)(128)(4,1)S(1)}) fusion(s32[1024]{0:T(1024)} %param.9, s32[]{:T(128)} %bitcast, s32[]{:T(128)} %bitcast.3), kind=kLoop, calls=%fused_computation.172 | loop fusion | flops 4096 | bytes 14344 | tf_op jit(solution)/shard_map/convert
  4.0 0.3 reduce-window.16
  4.5 0.3 reduce-window.24
  5.1 0.8 constant_dynamic-update-slice_fusion.1
  6.0 0.8 constant_dynamic-update-slice_fusion
  6.8 0.9 fusion.15
  7.8 0.3 fusion.11
  8.1 0.6 copy-done.5
  8.7 0.9 broadcast_in_dim.12
  9.6 7.3 %all-to-all-start = ((f32[32,48,128]{2,1,0:T(8,128)}), f32[32,48,128]{2,1,0:T(8,128)S(1)}, u32[]{:S(2)}, u32[]{:S(2)}) async-start(f32[32,48,128]{2,1,0:T(8,128)} %broadcast_in_dim.12), calls=%async_computation | async-start | bytes 1572864 | tf_op jit(solution)/shard_map/all_to_all | solution.py:20
  20.8 4.2 %concatenate.64 = bf16[102,128]{1,0:T(8,128)(2,1)} concatenate(bf16[16,128]{1,0:T(8,128)(2,1)S(1)} %get-tuple-element.77, bf16[16,128]{1,0:T(8,128)(2,1)S(1)} %get-tuple-element.77, bf16[16,128]{1,0:T(8,128)(2,1)S(1)} %get-tuple-element.78, bf16[16,128]{1,0:T(8,128)(2,1)S(1)} %get-tuple-element.77, bf16[16,128]{1,0:T(8,128)(2,1)S(1)} %get-tuple-element.79, ...), dimensions={0} | concatenate | bytes 52224 | tf_op jit(solution)/shard_map/concatenate | solution.py:40
  24.9 11.6 %all-to-all-done = f32[32,48,128]{2,1,0:T(8,128)S(1)} async-done(((f32[32,48,128]{2,1,0:T(8,128)}), f32[32,48,128]{2,1,0:T(8,128)S(1)}, u32[]{:S(2)}, u32[]{:S(2)}) %all-to-all-start) | async-done | bytes 786464 | tf_op jit(solution)/shard_map/all_to_all | solution.py:20
  36.7 8.3 %shard_map.77 = f32[16,1024]{1,0:T(8,128)S(1)} custom-call(s32[1]{0:T(128)} %constant.67.clone.1.slot_ref, f32[1,1024,4096]{2,1,0:T(8,128)} %inv_ref.3, bf16[32,4096]{1,0:T(8,128)(2,1)S(1)} %pad_maximum_fusion.rcat_ref, bf16[16,4096]{1,0:T(8,128)(2,1)S(1)} %get-tuple-element.63.r1_ref), custom_call_target="tpu_custom_call" | custom-call | flops 402653184 | bytes 16777216 | tf_op jit(solution)/shard_map/pallas_call | solution.py:96
  45.0 0.6 bitcast_bitcast_fusion.1
  45.7 3.8 %all-to-all-start.1 = ((f32[8,16,128]{2,1,0:T(8,128)}), f32[8,16,128]{2,1,0:T(8,128)S(1)}, u32[]{:S(2)}, u32[]{:S(2)}) async-start(f32[8,16,128]{2,1,0:T(8,128)} %bitcast_bitcast_fusion.1), calls=%async_computation.1 | async-start | bytes 131072 | tf_op jit(solution)/shard_map/all_to_all | solution.py:130
  49.6 5.0 %all-to-all-done.1 = f32[8,16,128]{2,1,0:T(8,128)S(1)} async-done(((f32[8,16,128]{2,1,0:T(8,128)}), f32[8,16,128]{2,1,0:T(8,128)S(1)}, u32[]{:S(2)}, u32[]{:S(2)}) %all-to-all-start.1) | async-done | bytes 65568 | tf_op jit(solution)/shard_map/all_to_all | solution.py:130
  54.5 0.7 broadcast_in_dim.14
  55.2 2.9 %all-to-all-start.2 = ((f32[32,16,128]{2,1,0:T(8,128)}), f32[32,16,128]{2,1,0:T(8,128)S(1)}, u32[]{:S(2)}, u32[]{:S(2)}) async-start(f32[32,16,128]{2,1,0:T(8,128)} %broadcast_in_dim.14), calls=%async_computation.2 | async-start | bytes 524288 | tf_op jit(solution)/shard_map/all_to_all | solution.py:20
  58.2 0.7 copy.59
  59.0 0.6 copy-done.2
  59.7 1.4 fusion.3
  61.2 7.2 %all-to-all-done.2 = f32[32,16,128]{2,1,0:T(8,128)S(1)} async-done(((f32[32,16,128]{2,1,0:T(8,128)}), f32[32,16,128]{2,1,0:T(8,128)S(1)}, u32[]{:S(2)}, u32[]{:S(2)}) %all-to-all-start.2) | async-done | bytes 262176 | tf_op jit(solution)/shard_map/all_to_all | solution.py:20
  68.5 0.2 fusion.18
  68.7 0.2 copy.57
  68.9 1.0 fusion.8
  69.9 0.5 fusion.34
  70.4 1.1 fusion.10
  71.5 0.8 broadcast_in_dim.15
  72.2 2.9 %all-to-all-start.3 = ((f32[32,16,128]{2,1,0:T(8,128)}), f32[32,16,128]{2,1,0:T(8,128)S(1)}, u32[]{:S(2)}, u32[]{:S(2)}) async-start(f32[32,16,128]{2,1,0:T(8,128)} %broadcast_in_dim.15), calls=%async_computation.3 | async-start | bytes 524288 | tf_op jit(solution)/shard_map/all_to_all | solution.py:20
  75.3 0.9 concatenate.72
  76.3 7.7 %fusion.1 = (bf16[1024,4096]{1,0:T(8,128)(2,1)}, bf16[1024,4096]{1,0:T(8,128)(2,1)}) fusion(bf16[102,1024]{1,0:T(8,128)(2,1)S(1)} %concatenate.71, bf16[102,4096]{1,0:T(8,128)(2,1)S(1)} %concatenate.72), kind=kOutput, calls=%fused_computation.5 | convolution fusion | flops 876609536 | bytes 17821696 | tf_op jit(solution)/shard_map/dot_general | solution.py:42
  84.0 0.5 fusion.51
  84.5 0.7 all-to-all-done.3
  85.2 8.3 %shard_map.78 = f32[16,1024]{1,0:T(8,128)S(1)} custom-call(s32[1]{0:T(128)} %constant.67.clone.1.slot_ref, f32[1,1024,4096]{2,1,0:T(8,128)} %inv_ref.3, bf16[32,4096]{1,0:T(8,128)(2,1)S(1)} %pad_maximum_fusion.2.rcat_ref, bf16[16,4096]{1,0:T(8,128)(2,1)S(1)} %get-tuple-element.53.r1_ref), custom_call_target="tpu_custom_call" | custom-call | flops 402653184 | bytes 16777216 | tf_op jit(solution)/shard_map/pallas_call | solution.py:96
  94.0 7.7 %fusion = (bf16[1024,4096]{1,0:T(8,128)(2,1)}, bf16[1024,4096]{1,0:T(8,128)(2,1)}) fusion(bf16[102,1024]{1,0:T(8,128)(2,1)S(1)} %concatenate.68, bf16[102,4096]{1,0:T(8,128)(2,1)S(1)} %concatenate.69), kind=kOutput, calls=%fused_computation.4 | convolution fusion | flops 876609536 | bytes 17821696 | tf_op jit(solution)/shard_map/dot_general | solution.py:42
  101.7 0.6 bitcast_bitcast_fusion
  102.3 3.4 %all-to-all-start.4 = ((f32[8,16,128]{2,1,0:T(8,128)}), f32[8,16,128]{2,1,0:T(8,128)S(1)}, u32[]{:S(2)}, u32[]{:S(2)}) async-start(f32[8,16,128]{2,1,0:T(8,128)} %bitcast_bitcast_fusion), calls=%async_computation.4 | async-start | bytes 131072 | tf_op jit(solution)/shard_map/all_to_all | solution.py:130
  105.7 6.0 %fusion.33 = f32[32,1024]{1,0:T(8,128)S(1)} fusion(bf16[1024,4096]{1,0:T(8,128)(2,1)} %get-tuple-element.19, bf16[16,4096]{1,0:T(8,128)(2,1)S(1)} %get-tuple-element.55, bf16[16,4096]{1,0:T(8,128)(2,1)S(1)} %get-tuple-element.56), kind=kOutput, calls=%fused_computation.85 | convolution fusion | flops 268959744 | bytes 8781824 | tf_op jit(solution)/shard_map/dot_general | solution.py:55
  111.7 0.7 broadcast_in_dim.17
  112.5 6.1 %all-to-all-start.5 = ((f32[32,16,128]{2,1,0:T(8,128)}), f32[32,16,128]{2,1,0:T(8,128)S(1)}, u32[]{:S(2)}, u32[]{:S(2)}) async-start(f32[32,16,128]{2,1,0:T(8,128)} %broadcast_in_dim.17), calls=%async_computation.5 | async-start | bytes 524288 | tf_op jit(solution)/shard_map/all_to_all | solution.py:20
  118.6 5.7 %fusion.7 = f32[16,1024]{1,0:T(8,128)S(1)} fusion(f32[16,1024]{1,0:T(8,128)S(1)} %copy-done.4, bf16[16,4096]{1,0:T(8,128)(2,1)S(1)} %get-tuple-element.56, bf16[1024,4096]{1,0:T(8,128)(2,1)} %get-tuple-element.20, f32[32,1024]{1,0:T(8,128)S(1)} %fusion.33, f32[48,1024]{1,0:T(8,128)S(1)} %fusion.51), kind=kOutput, calls=%fused_computation.18 | convolution fusion | flops 134332416 | bytes 8978432 | tf_op jit(solution)/shard_map/dot_general | solution.py:56
  124.2 4.3 %all-to-all-done.5 = f32[32,16,128]{2,1,0:T(8,128)S(1)} async-done(((f32[32,16,128]{2,1,0:T(8,128)}), f32[32,16,128]{2,1,0:T(8,128)S(1)}, u32[]{:S(2)}, u32[]{:S(2)}) %all-to-all-start.5) | async-done | bytes 262176 | tf_op jit(solution)/shard_map/all_to_all | solution.py:20
  128.9 0.2 copy.56
  129.1 0.5 fusion.41
  129.6 0.7 add_add_fusion
  130.2 6.0 %fusion.24 = f32[32,1024]{1,0:T(8,128)S(1)} fusion(bf16[1024,4096]{1,0:T(8,128)(2,1)} %get-tuple-element.24, bf16[16,4096]{1,0:T(8,128)(2,1)S(1)} %get-tuple-element.43, bf16[16,4096]{1,0:T(8,128)(2,1)S(1)} %get-tuple-element.44), kind=kOutput, calls=%fused_computation.68 | convolution fusion | flops 268959744 | bytes 8781824 | tf_op jit(solution)/shard_map/dot_general | solution.py:55
  136.2 6.3 %fusion.5 = f32[16,1024]{1,0:T(8,128)} fusion(f32[16,1024]{1,0:T(8,128)S(1)} %fusion.7, bf16[16,4096]{1,0:T(8,128)(2,1)S(1)} %get-tuple-element.44, bf16[1024,4096]{1,0:T(8,128)(2,1)} %get-tuple-element.25, f32[32,1024]{1,0:T(8,128)S(1)} %fusion.24, f32[48,1024]{1,0:T(8,128)S(1)} %fusion.41), kind=kOutput, calls=%fused_computation.15 | convolution fusion | flops 134332416 | bytes 8978432 | tf_op jit(solution)/shard_map/dot_general | solution.py:56
  (57 shorter events, 2.3 us)
Async XLA Ops:
  8.1 0.6 copy-start.5
  9.6 26.9 %all-to-all-start = ((f32[32,48,128]{2,1,0:T(8,128)}), f32[32,48,128]{2,1,0:T(8,128)S(1)}, u32[]{:S(2)}, u32[]{:S(2)}) async-start(f32[32,48,128]{2,1,0:T(8,128)} %broadcast_in_dim.12), calls=%async_computation | async-start | bytes 1572864 | tf_op jit(solution)/shard_map/all_to_all | solution.py:20
  45.0 30.1 %copy-start.1 = (f32[16,1024]{1,0:T(8,128)S(1)}, f32[16,1024]{1,0:T(8,128)}, u32[]{:S(2)}) copy-start(f32[16,1024]{1,0:T(8,128)} %param.6) | copy-start | bytes 196612
  45.7 8.9 %all-to-all-start.1 = ((f32[8,16,128]{2,1,0:T(8,128)}), f32[8,16,128]{2,1,0:T(8,128)S(1)}, u32[]{:S(2)}, u32[]{:S(2)}) async-start(f32[8,16,128]{2,1,0:T(8,128)} %bitcast_bitcast_fusion.1), calls=%async_computation.1 | async-start | bytes 131072 | tf_op jit(solution)/shard_map/all_to_all | solution.py:130
  55.2 13.1 %all-to-all-start.2 = ((f32[32,16,128]{2,1,0:T(8,128)}), f32[32,16,128]{2,1,0:T(8,128)S(1)}, u32[]{:S(2)}, u32[]{:S(2)}) async-start(f32[32,16,128]{2,1,0:T(8,128)} %broadcast_in_dim.14), calls=%async_computation.2 | async-start | bytes 524288 | tf_op jit(solution)/shard_map/all_to_all | solution.py:20
  59.0 0.6 copy-start.2
  72.2 12.9 %all-to-all-start.3 = ((f32[32,16,128]{2,1,0:T(8,128)}), f32[32,16,128]{2,1,0:T(8,128)S(1)}, u32[]{:S(2)}, u32[]{:S(2)}) async-start(f32[32,16,128]{2,1,0:T(8,128)} %broadcast_in_dim.15), calls=%async_computation.3 | async-start | bytes 524288 | tf_op jit(solution)/shard_map/all_to_all | solution.py:20
  85.2 8.4 %copy-start = (f32[32,2,8,128]{3,2,0,1:T(8,128)S(1)}, f32[32,2,8,128]{3,2,0,1:T(8,128)}, u32[]{:S(2)}) copy-start(f32[32,2,8,128]{3,2,0,1:T(8,128)} %copy.59) | copy-start | bytes 786436
  85.2 8.6 %copy-start.3 = (bf16[3,4096]{1,0:T(4,128)(2,1)S(1)}, bf16[3,4096]{1,0:T(4,128)(2,1)}, u32[]{:S(2)}) copy-start(bf16[3,4096]{1,0:T(4,128)(2,1)} %copy-done.2) | copy-start | bytes 73732
  101.7 16.9 %copy-start.4 = (f32[16,1024]{1,0:T(8,128)S(1)}, f32[16,1024]{1,0:T(8,128)}, u32[]{:S(2)}) copy-start(f32[16,1024]{1,0:T(8,128)} %param.7) | copy-start | bytes 196612
  102.3 9.4 %all-to-all-start.4 = ((f32[8,16,128]{2,1,0:T(8,128)}), f32[8,16,128]{2,1,0:T(8,128)S(1)}, u32[]{:S(2)}, u32[]{:S(2)}) async-start(f32[8,16,128]{2,1,0:T(8,128)} %bitcast_bitcast_fusion), calls=%async_computation.4 | async-start | bytes 131072 | tf_op jit(solution)/shard_map/all_to_all | solution.py:130
  105.7 23.8 %copy-start.6 = (f32[16,1024]{1,0:T(8,128)S(1)}, f32[16,1024]{1,0:T(8,128)}, u32[]{:S(2)}) copy-start(f32[16,1024]{1,0:T(8,128)} %param.8) | copy-start | bytes 196612
  112.5 16.1 %all-to-all-start.5 = ((f32[32,16,128]{2,1,0:T(8,128)}), f32[32,16,128]{2,1,0:T(8,128)S(1)}, u32[]{:S(2)}, u32[]{:S(2)}) async-start(f32[32,16,128]{2,1,0:T(8,128)} %broadcast_in_dim.17), calls=%async_computation.5 | async-start | bytes 524288 | tf_op jit(solution)/shard_map/all_to_all | solution.py:20

commit v9 on v8

--- a/solution.py
+++ b/solution.py
@@ -45,16 +45,39 @@
     return lax.optimization_barrier((k1.astype(jnp.bfloat16), (kernel - k1).astype(jnp.bfloat16)))
 
 
-def apply_kernel(delta, kernel):
+def product_kernel(k1_ref, k2_ref, d12_ref, d1_ref, o_ref):
+    both = jnp.dot(k1_ref[...], d12_ref[...], preferred_element_type=jnp.float32)
+    low = jnp.dot(k2_ref[...], d1_ref[...], preferred_element_type=jnp.float32)
+    rows = o_ref.shape[1]
+    o_ref[...] = (both[:, :rows] + both[:, rows:]) + low
+
+
+def apply_kernel(delta, kernel, tile=256):
     k1, k2 = kernel
+    n, m = k1.shape
+    rows = delta.shape[0]
     d1f = lax.reduce_precision(delta, exponent_bits=8, mantissa_bits=7)
     d1 = d1f.astype(jnp.bfloat16)
     d2 = (delta - d1f).astype(jnp.bfloat16)
-    rows = delta.shape[0]
-    dims = (((1,), (1,)), ((), ()))
-    both = lax.dot_general(jnp.concatenate([d1, d2], axis=0), k1, dims, preferred_element_type=jnp.float32)
-    low = lax.dot_general(d1, k2, dims, preferred_element_type=jnp.float32)
-    return (both[:rows] + both[rows:]) + low
+    d12 = jnp.concatenate([d1, d2], axis=0).T
+    tile = min(tile, n)
+    out = pl.pallas_call(
+        product_kernel,
+        grid=(n // tile,),
+        in_specs=[
+            pl.BlockSpec((tile, m), lambda i: (i, 0)),
+            pl.BlockSpec((tile, m), lambda i: (i, 0)),
+            pl.BlockSpec((m, 2 * rows), lambda i: (0, 0)),
+            pl.BlockSpec((m, rows), lambda i: (0, 0)),
+        ],
+        out_specs=pl.BlockSpec((tile, rows), lambda i: (i, 0)),
+        out_shape=jax.ShapeDtypeStruct((n, rows), jnp.float32),
+        compiler_params=pltpu.CompilerParams(vmem_limit_bytes=48 * 1024 * 1024),
+        cost_estimate=pl.CostEstimate(
+            flops=6 * rows * n * m, transcendentals=0, bytes_accessed=4 * n * m + 6 * m * rows
+        ),
+    )(k1, k2, d12, d1.T)
+    return out.T
 
 
 def exact_dot(x, onehot, dims):

time: 144 us -> 165 us (1.15)
  matrix products: 44.5 us -> 23.4 us
  Pallas kernels: 16.6 us -> 34.3 us
  other arithmetic: 5.4 us -> 20.1 us
  local copies, waits for them, and re-layouts: 16 us -> 28.9 us
  waiting for transfers between devices: 28.7 us -> 25.9 us
    dot_general x6 -> x0, matrix products: 25.4 us -> none  [the longest x3 13.1 us: apply_kernel(): low = lax.dot_general(d1, k2, dims, preferred_element_type=jnp.float32)]
    pallas_call x0 -> x3, Pallas kernels: none -> 17.6 us  [apply_kernel(): pl.pallas_call(product_kernel, grid=(n // tile,), in_specs=[pl.BlockSpec(...]
    concatenate x3, local copies, waits for them, and re-layouts: 1.19 us -> 9.47 us  [kern(): jnp.concatenate([v1, v2, v1, v3, v1, v2, one_v, one_v, one_v, b1, b2, b3]...]
    convert_element_type x2, other arithmetic: 0.31 us -> 5.81 us  [apply_kernel(): d1 = d1f.astype(jnp.bfloat16)]
    concatenate x4, local copies, waits for them, and re-layouts: 4.29 us -> 0.27 us  [kern(): jnp.concatenate([u1, u1, u2, u1, u3, u2, a1, a2, a3, one_u, one_u, one_u]...]
    transpose x0 -> x2, other arithmetic: none -> 3.63 us  [apply_kernel(): d12 = jnp.concatenate([d1, d2], axis=0).T]
    transpose x2, local copies, waits for them, and re-layouts: 0.31 us -> 3.9 us  [distribute(): jnp.transpose(pieces_all.reshape(n_grp, n_mem, rhs, per), (2, 1, 0, 3))]
    unnamed x17 -> x33, local copies, waits for them, and re-layouts: 2.39 us -> 5.9 us
  transfers between devices with their start and end apart: 6 -> 6, of which waited for: 5 -> 4; matrix products, arithmetic and copies ran while one was open for 19% -> 21% of each run, Pallas kernels for 0% -> 5%
where the time goes in v9:
time: 165 us; the launch traced here: 164 us
  Pallas kernels  34.3 us (21%)
  local copies, waits for them, and re-layouts  28.9 us (18%)
  starting transfers between devices  26.5 us (16%)
  waiting for transfers between devices  25.9 us (16%)
  matrix products  23.4 us (14%)
  other arithmetic  20.1 us (12%)
  between operations  4.95 us (3%)
    all_to_all x4, waiting for transfers between devices, gather_all(): return lax.all_to_all(sent, ALL, 0, 0, tiled=True)  20.7 us
    dot_general x3, matrix products, kern(): lax.dot_general(left, right, (((0,), (0,)), ((), ())), preferred_element_...  19.6 us
    all_to_all x4, starting transfers between devices, gather_all(): return lax.all_to_all(sent, ALL, 0, 0, tiled=True)  18.9 us
    pallas_call x3, Pallas kernels, apply_kernel(): pl.pallas_call(product_kernel, grid=(n // tile,), in_specs=[pl.BlockSpec(...  17.6 us
    pallas_call x2, Pallas kernels, solve_rows(): pl.pallas_call(solve_kernel, grid_spec=grid_spec, out_shape=jax.ShapeDtyp...  16.6 us
    concatenate x3, local copies, waits for them, and re-layouts, kern(): jnp.concatenate([v1, v2, v1, v3, v1, v2, one_v, one_v, one_v, b1, b2, b3]...  9.47 us
    all_to_all x2, starting transfers between devices, distribute(): scattered = lax.all_to_all(pieces, 'grp', 0, 0, tiled=True)  7.6 us
    unnamed x33, local copies, waits for them, and re-layouts  5.9 us
  transfers between devices with their start and end apart: 6, of which 4 were waited for; matrix products, arithmetic and copies ran while one was open for 21% of the time, Pallas kernels for 5%

profile of v9, /device:TPU:0, one launch (start us, length us, event | category | flops | bytes accessed | tf_op | source)
XLA Modules:
  0.0 164.1 jit_solution(340430654173610898)
XLA Ops:
  0.6 1.3 fusion.56
  1.9 2.0 %convert_bitcast_fusion.1 = (s32[8,128]{1,0:T(8,128)S(1)}, pred[1024]{0:T(1024)(128)(4,1)S(1)}, s32[8,128]{1,0:T(8,128)S(1)}, pred[1024]{0:T(1024)(128)(4,1)S(1)}) fusion(s32[1024]{0:T(1024)} %param.9, s32[]{:T(128)} %bitcast, s32[]{:T(128)} %bitcast.3), kind=kLoop, calls=%fused_computation.160 | loop fusion | flops 4096 | bytes 14344 | tf_op jit(solution)/shard_map/convert
  5.1 0.8 constant_dynamic-update-slice_fusion.1
  5.9 0.8 constant_dynamic-update-slice_fusion
  6.8 0.9 fusion.13
  8.7 1.0 broadcast_in_dim.12
  9.7 7.3 %all-to-all-start = ((f32[32,48,128]{2,1,0:T(8,128)}), f32[32,48,128]{2,1,0:T(8,128)S(1)}, u32[]{:S(2)}, u32[]{:S(2)}) async-start(f32[32,48,128]{2,1,0:T(8,128)} %broadcast_in_dim.12), calls=%async_computation | async-start | bytes 1572864 | tf_op jit(solution)/shard_map/all_to_all | solution.py:20
  19.6 1.0 copy.186
  21.0 1.0 copy.198
  23.5 13.1 %all-to-all-done = f32[32,48,128]{2,1,0:T(8,128)S(1)} async-done(((f32[32,48,128]{2,1,0:T(8,128)}), f32[32,48,128]{2,1,0:T(8,128)S(1)}, u32[]{:S(2)}, u32[]{:S(2)}) %all-to-all-start) | async-done | bytes 786464 | tf_op jit(solution)/shard_map/all_to_all | solution.py:20
  36.8 8.3 %shard_map.77 = f32[16,1024]{1,0:T(8,128)S(1)} custom-call(s32[1]{0:T(128)} %constant.67.clone.1.slot_ref, f32[1,1024,4096]{2,1,0:T(8,128)} %inv_ref.3, bf16[32,4096]{1,0:T(8,128)(2,1)S(1)} %pad_maximum_fusion.rcat_ref, bf16[16,4096]{1,0:T(8,128)(2,1)S(1)} %get-tuple-element.75.r1_ref), custom_call_target="tpu_custom_call" | custom-call | flops 402653184 | bytes 16777216 | tf_op jit(solution)/shard_map/pallas_call | solution.py:119
  45.7 3.8 %all-to-all-start.1 = ((f32[8,16,128]{2,1,0:T(8,128)}), f32[8,16,128]{2,1,0:T(8,128)S(1)}, u32[]{:S(2)}, u32[]{:S(2)}) async-start(f32[8,16,128]{2,1,0:T(8,128)} %bitcast_bitcast_fusion.1), calls=%async_computation.1 | async-start | bytes 131072 | tf_op jit(solution)/shard_map/all_to_all | solution.py:153
  49.6 5.0 %all-to-all-done.1 = f32[8,16,128]{2,1,0:T(8,128)S(1)} async-done(((f32[8,16,128]{2,1,0:T(8,128)}), f32[8,16,128]{2,1,0:T(8,128)S(1)}, u32[]{:S(2)}, u32[]{:S(2)}) %all-to-all-start.1) | async-done | bytes 65568 | tf_op jit(solution)/shard_map/all_to_all | solution.py:153
  54.6 0.7 broadcast_in_dim.14
  55.3 2.9 %all-to-all-start.2 = ((f32[32,16,128]{2,1,0:T(8,128)}), f32[32,16,128]{2,1,0:T(8,128)S(1)}, u32[]{:S(2)}, u32[]{:S(2)}) async-start(f32[32,16,128]{2,1,0:T(8,128)} %broadcast_in_dim.14), calls=%async_computation.2 | async-start | bytes 524288 | tf_op jit(solution)/shard_map/all_to_all | solution.py:20
  58.5 1.6 %fusion.3 = (bf16[128,4096]{1,0:T(8,128)(2,1)S(1)}, bf16[128,4096]{1,0:T(8,128)(2,1)}) fusion(bf16[102,128]{0,1:T(8,128)(2,1)S(1)} %concatenate.61, bf16[102,4096]{1,0:T(8,128)(2,1)S(1)} %concatenate.63), kind=kOutput, calls=%fused_computation.16 | convolution fusion | flops 109576192 | bytes 2958848 | tf_op jit(solution)/shard_map/dot_general | solution.py:42
  60.2 0.7 copy.225
  60.9 7.6 %all-to-all-done.2 = f32[32,16,128]{2,1,0:T(8,128)S(1)} async-done(((f32[32,16,128]{2,1,0:T(8,128)}), f32[32,16,128]{2,1,0:T(8,128)S(1)}, u32[]{:S(2)}, u32[]{:S(2)}) %all-to-all-start.2) | async-done | bytes 262176 | tf_op jit(solution)/shard_map/all_to_all | solution.py:20
  68.4 1.9 %copy.176 = f32[16,4,8,128]{0,3,2,1:T(8,128)} copy(f32[16,4,8,128]{3,0,1,2:T(8,128)S(1)} %bitcast.110) | data formatting | bytes 524288 | tf_op jit(solution)/shard_map/transpose | solution.py:156
  70.4 2.9 %reduce-precision_convert_fusion.3 = (bf16[16,4096]{0,1:T(8,128)(2,1)S(1)}, bf16[16,4096]{0,1:T(8,128)(2,1)}) fusion(f32[16,4,8,128]{0,3,2,1:T(8,128)} %copy.176), kind=kLoop, calls=%fused_computation.13 | loop fusion | flops 262144 | bytes 524288 | tf_op jit(solution)/shard_map/convert_element_type | solution.py:60
  73.3 0.9 reduce-precision_convert_fusion.22
  74.2 0.9 reduce-precision_subtract_fusion.21
  75.2 0.7 copy.177
  75.9 1.8 %maximum_bitcast_fusion.d12_ref = bf16[4096,32]{1,0:T(8,128)(2,1)S(1)} fusion(bf16[16,4096]{0,1:T(8,128)(2,1)} %get-tuple-element.51, bf16[16,4096]{0,1:T(8,128)(2,1)S(1)} %get-tuple-element.50), kind=kLoop, calls=%fused_computation.21 | loop fusion | flops 524288 | bytes 524288 | tf_op jit(solution)/shard_map/transpose | solution.py:62
  77.7 2.4 %fusion.6 = f32[48,128]{0,1:T(8,128)} fusion(bf16[16,128]{1,0:T(8,128)(2,1)} %copy.177, bf16[16,128]{1,0:T(8,128)(2,1)S(1)} %copy.179, bf16[16,128]{1,0:T(8,128)(2,1)S(1)} %copy.178, s32[1024]{0:T(1024)S(1)} %add_bitcast_fusion, pred[1024]{0:T(1024)(128)(4,1)} %copy-done.10, s32[1024]{0:T(1024)S(1)} %add_bitcast_fusion.1, pred[1024]{0:T(1024)(128)(4,1)} %copy-done.12), kind=kOutput, calls=%fused_computation.20 | convolution fusion | flops 35704832 | bytes 47104 | tf_op jit(solution)/shard_map/dot_general | solution.py:86
  80.1 1.2 copy-done
  81.3 0.7 shard_map.78
  82.3 0.8 broadcast_in_dim.15
  83.1 2.9 %all-to-all-start.3 = ((f32[32,16,128]{2,1,0:T(8,128)}), f32[32,16,128]{2,1,0:T(8,128)S(1)}, u32[]{:S(2)}, u32[]{:S(2)}) async-start(f32[32,16,128]{2,1,0:T(8,128)} %broadcast_in_dim.15), calls=%async_computation.3 | async-start | bytes 524288 | tf_op jit(solution)/shard_map/all_to_all | solution.py:20
  86.0 1.1 multiply_reduce_fusion
  87.1 0.9 multiply_reduce_fusion.3
  88.0 4.7 %concatenate.71 = bf16[102,4096]{1,0:T(8,128)(2,1)} concatenate(bf16[16,4096]{1,0:T(8,128)(2,1)S(1)} %get-tuple-element.71, bf16[16,4096]{1,0:T(8,128)(2,1)S(1)} %get-tuple-element.70, bf16[16,4096]{1,0:T(8,128)(2,1)S(1)} %get-tuple-element.71, bf16[16,4096]{1,0:T(8,128)(2,1)S(1)} %get-tuple-element.69, bf16[16,4096]{1,0:T(8,128)(2,1)S(1)} %get-tuple-element.71, ...), dimensions={0} | concatenate | bytes 1671168 | tf_op jit(solution)/shard_map/concatenate | solution.py:41
  92.7 9.0 %fusion.1 = (bf16[1024,4096]{1,0:T(8,128)(2,1)}, bf16[1024,4096]{1,0:T(8,128)(2,1)}) fusion(bf16[102,1024]{1,0:T(8,128)(2,1)S(1)} %concatenate.70, bf16[102,4096]{1,0:T(8,128)(2,1)} %concatenate.71), kind=kOutput, calls=%fused_computation.5 | convolution fusion | flops 876609536 | bytes 17821696 | tf_op jit(solution)/shard_map/dot_general | solution.py:42
  102.2 8.3 %shard_map.79 = f32[16,1024]{1,0:T(8,128)S(1)} custom-call(s32[1]{0:T(128)} %constant.67.clone.1.slot_ref, f32[1,1024,4096]{2,1,0:T(8,128)} %inv_ref.3, bf16[32,4096]{1,0:T(8,128)(2,1)S(1)} %pad_maximum_fusion.1.rcat_ref, bf16[16,4096]{1,0:T(8,128)(2,1)S(1)} %get-tuple-element.66.r1_ref), custom_call_target="tpu_custom_call" | custom-call | flops 402653184 | bytes 16777216 | tf_op jit(solution)/shard_map/pallas_call | solution.py:119
  111.4 3.8 %all-to-all-start.4 = ((f32[8,16,128]{2,1,0:T(8,128)}), f32[8,16,128]{2,1,0:T(8,128)S(1)}, u32[]{:S(2)}, u32[]{:S(2)}) async-start(f32[8,16,128]{2,1,0:T(8,128)} %bitcast_bitcast_fusion), calls=%async_computation.4 | async-start | bytes 131072 | tf_op jit(solution)/shard_map/all_to_all | solution.py:153
  115.2 4.7 %concatenate.69 = bf16[102,4096]{1,0:T(8,128)(2,1)} concatenate(bf16[16,4096]{1,0:T(8,128)(2,1)S(1)} %get-tuple-element.65, bf16[16,4096]{1,0:T(8,128)(2,1)S(1)} %get-tuple-element.64, bf16[16,4096]{1,0:T(8,128)(2,1)S(1)} %get-tuple-element.65, bf16[16,4096]{1,0:T(8,128)(2,1)S(1)} %get-tuple-element.63, bf16[16,4096]{1,0:T(8,128)(2,1)S(1)} %get-tuple-element.65, ...), dimensions={0} | concatenate | bytes 1671168 | tf_op jit(solution)/shard_map/concatenate | solution.py:41
  120.2 0.7 broadcast_in_dim.17
  120.9 5.8 %all-to-all-start.5 = ((f32[32,16,128]{2,1,0:T(8,128)}), f32[32,16,128]{2,1,0:T(8,128)S(1)}, u32[]{:S(2)}, u32[]{:S(2)}) async-start(f32[32,16,128]{2,1,0:T(8,128)} %broadcast_in_dim.17), calls=%async_computation.5 | async-start | bytes 524288 | tf_op jit(solution)/shard_map/all_to_all | solution.py:20
  126.8 9.0 %fusion = (bf16[1024,4096]{1,0:T(8,128)(2,1)}, bf16[1024,4096]{1,0:T(8,128)(2,1)}) fusion(bf16[102,1024]{1,0:T(8,128)(2,1)S(1)} %concatenate.68, bf16[102,4096]{1,0:T(8,128)(2,1)} %concatenate.69), kind=kOutput, calls=%fused_computation.4 | convolution fusion | flops 876609536 | bytes 17821696 | tf_op jit(solution)/shard_map/dot_general | solution.py:42
  135.8 8.4 %shard_map.80 = f32[1024,16]{1,0:T(8,128)S(1)} custom-call(bf16[1024,4096]{1,0:T(8,128)(2,1)} %get-tuple-element.19.k1_ref, bf16[1024,4096]{1,0:T(8,128)(2,1)} %get-tuple-element.20.k2_ref, bf16[4096,32]{1,0:T(8,128)(2,1)S(1)} %maximum_bitcast_fusion.d12_ref, bf16[4096,16]{1,0:T(8,128)(2,1)S(1)} %bitcast.103), custom_call_target="tpu_custom_call" | custom-call | flops 402653184 | bytes 17170432 | tf_op jit(solution)/shard_map/pallas_call | solution.py:64
  144.2 1.9 %copy.191 = f32[16,4,8,128]{0,3,2,1:T(8,128)} copy(f32[16,4,8,128]{3,0,1,2:T(8,128)S(1)} %bitcast.111) | data formatting | bytes 524288 | tf_op jit(solution)/shard_map/transpose | solution.py:156
  146.1 2.9 %reduce-precision_convert_fusion.2 = (bf16[16,4096]{0,1:T(8,128)(2,1)S(1)}, bf16[16,4096]{0,1:T(8,128)(2,1)}) fusion(f32[16,4,8,128]{0,3,2,1:T(8,128)} %copy.191), kind=kLoop, calls=%fused_computation.11 | loop fusion | flops 262144 | bytes 524288 | tf_op jit(solution)/shard_map/convert_element_type | solution.py:60
  149.0 0.9 reduce-precision_convert_fusion.16
  149.9 0.9 reduce-precision_subtract_fusion.15
  151.0 1.8 %maximum_bitcast_fusion.1.d12_ref = bf16[4096,32]{1,0:T(8,128)(2,1)S(1)} fusion(bf16[16,4096]{0,1:T(8,128)(2,1)} %get-tuple-element.49, bf16[16,4096]{0,1:T(8,128)(2,1)S(1)} %get-tuple-element.48), kind=kLoop, calls=%fused_computation.22 | loop fusion | flops 524288 | bytes 524288 | tf_op jit(solution)/shard_map/transpose | solution.py:62
  153.3 8.5 %shard_map.81 = f32[1024,16]{1,0:T(8,128)S(1)} custom-call(bf16[1024,4096]{1,0:T(8,128)(2,1)} %get-tuple-element.23.k1_ref, bf16[1024,4096]{1,0:T(8,128)(2,1)} %get-tuple-element.24.k2_ref, bf16[4096,32]{1,0:T(8,128)(2,1)S(1)} %maximum_bitcast_fusion.1.d12_ref, bf16[4096,16]{1,0:T(8,128)(2,1)S(1)} %bitcast.104), custom_call_target="tpu_custom_call" | custom-call | flops 402653184 | bytes 17170432 | tf_op jit(solution)/shard_map/pallas_call | solution.py:64
  162.5 0.8 copy.199
  163.3 0.8 copy.200
  (88 shorter events, 7.2 us)
Async XLA Ops:
  3.9 4.3 %copy-start.10 = (pred[1024]{0:T(1024)(128)(4,1)}, pred[1024]{0:T(1024)(128)(4,1)S(1)}, u32[]{:S(2)}) copy-start(pred[1024]{0:T(1024)(128)(4,1)S(1)} %get-tuple-element.111) | copy-start | bytes 3076
  3.9 4.3 %copy-start.12 = (pred[1024]{0:T(1024)(128)(4,1)}, pred[1024]{0:T(1024)(128)(4,1)S(1)}, u32[]{:S(2)}) copy-start(pred[1024]{0:T(1024)(128)(4,1)S(1)} %get-tuple-element.39) | copy-start | bytes 3076
  8.2 11.4 %copy-start.7 = (f32[16,1024]{1,0:T(8,128)S(1)}, f32[16,1024]{1,0:T(8,128)}, u32[]{:S(2)}) copy-start(f32[16,1024]{1,0:T(8,128)} %param.7) | copy-start | bytes 196612
  8.2 12.7 %copy-start.8 = (f32[16,1024]{1,0:T(8,128)S(1)}, f32[16,1024]{1,0:T(8,128)}, u32[]{:S(2)}) copy-start(f32[16,1024]{1,0:T(8,128)} %param.8) | copy-start | bytes 196612
  9.7 26.9 %all-to-all-start = ((f32[32,48,128]{2,1,0:T(8,128)}), f32[32,48,128]{2,1,0:T(8,128)S(1)}, u32[]{:S(2)}, u32[]{:S(2)}) async-start(f32[32,48,128]{2,1,0:T(8,128)} %broadcast_in_dim.12), calls=%async_computation | async-start | bytes 1572864 | tf_op jit(solution)/shard_map/all_to_all | solution.py:20
  45.7 8.9 %all-to-all-start.1 = ((f32[8,16,128]{2,1,0:T(8,128)}), f32[8,16,128]{2,1,0:T(8,128)S(1)}, u32[]{:S(2)}, u32[]{:S(2)}) async-start(f32[8,16,128]{2,1,0:T(8,128)} %bitcast_bitcast_fusion.1), calls=%async_computation.1 | async-start | bytes 131072 | tf_op jit(solution)/shard_map/all_to_all | solution.py:153
  55.3 13.1 %all-to-all-start.2 = ((f32[32,16,128]{2,1,0:T(8,128)}), f32[32,16,128]{2,1,0:T(8,128)S(1)}, u32[]{:S(2)}, u32[]{:S(2)}) async-start(f32[32,16,128]{2,1,0:T(8,128)} %broadcast_in_dim.14), calls=%async_computation.2 | async-start | bytes 524288 | tf_op jit(solution)/shard_map/all_to_all | solution.py:20
  58.3 1.8 %copy-start.5 = (bf16[3,4096]{1,0:T(4,128)(2,1)}, bf16[3,4096]{1,0:T(4,128)(2,1)S(1)}, u32[]{:S(2)}) copy-start(bf16[3,4096]{1,0:T(4,128)(2,1)S(1)} %broadcast.48) | copy-start | bytes 73732
  80.1 1.2 copy-start
  81.3 0.8 copy-start.3
  82.1 5.8 %copy-start.6 = (bf16[3,4096]{1,0:T(4,128)(2,1)S(1)}, bf16[3,4096]{1,0:T(4,128)(2,1)}, u32[]{:S(2)}) copy-start(bf16[3,4096]{1,0:T(4,128)(2,1)} %copy-done.5) | copy-start | bytes 73732
  83.1 19.1 %all-to-all-start.3 = ((f32[32,16,128]{2,1,0:T(8,128)}), f32[32,16,128]{2,1,0:T(8,128)S(1)}, u32[]{:S(2)}, u32[]{:S(2)}) async-start(f32[32,16,128]{2,1,0:T(8,128)} %broadcast_in_dim.15), calls=%async_computation.3 | async-start | bytes 524288 | tf_op jit(solution)/shard_map/all_to_all | solution.py:20
  92.7 9.0 %copy-start.9 = (bf16[16,128]{1,0:T(8,128)(2,1)S(1)}, bf16[16,128]{1,0:T(8,128)(2,1)}, u32[]{:S(2)}) copy-start(bf16[16,128]{1,0:T(8,128)(2,1)} %copy.177) | copy-start | bytes 12292
  92.7 9.0 %copy-start.13 = (pred[1024]{0:T(1024)(128)(4,1)S(1)}, pred[1024]{0:T(1024)(128)(4,1)}, u32[]{:S(2)}) copy-start(pred[1024]{0:T(1024)(128)(4,1)} %copy-done.12) | copy-start | bytes 3076
  102.2 8.5 %copy-start.4 = (f32[16,1024]{1,0:T(8,128)S(1)}, f32[16,1024]{1,0:T(8,128)}, u32[]{:S(2)}) copy-start(f32[16,1024]{1,0:T(8,128)} %param.6) | copy-start | bytes 196612
  111.4 8.8 %all-to-all-start.4 = ((f32[8,16,128]{2,1,0:T(8,128)}), f32[8,16,128]{2,1,0:T(8,128)S(1)}, u32[]{:S(2)}, u32[]{:S(2)}) async-start(f32[8,16,128]{2,1,0:T(8,128)} %bitcast_bitcast_fusion), calls=%async_computation.4 | async-start | bytes 131072 | tf_op jit(solution)/shard_map/all_to_all | solution.py:153
  120.9 23.2 %all-to-all-start.5 = ((f32[32,16,128]{2,1,0:T(8,128)}), f32[32,16,128]{2,1,0:T(8,128)S(1)}, u32[]{:S(2)}, u32[]{:S(2)}) async-start(f32[32,16,128]{2,1,0:T(8,128)} %broadcast_in_dim.17), calls=%async_computation.5 | async-start | bytes 524288 | tf_op jit(solution)/shard_map/all_to_all | solution.py:20
  149.0 3.8 %copy-start.11 = (pred[1024]{0:T(1024)(128)(4,1)S(1)}, pred[1024]{0:T(1024)(128)(4,1)}, u32[]{:S(2)}) copy-start(pred[1024]{0:T(1024)(128)(4,1)} %copy-done.10) | copy-start | bytes 3076
  153.3 8.5 %copy-start.1 = (f32[16,1024]{0,1:T(8,128)S(1)}, f32[16,1024]{0,1:T(8,128)}, u32[]{:S(2)}) copy-start(f32[16,1024]{0,1:T(8,128)} %copy.186) | copy-start | bytes 196612
  153.3 8.5 %copy-start.2 = (f32[16,1024]{0,1:T(8,128)S(1)}, f32[16,1024]{0,1:T(8,128)}, u32[]{:S(2)}) copy-start(f32[16,1024]{0,1:T(8,128)} %copy.198) | copy-start | bytes 196612

commit v10 on v8

--- a/solution.py
+++ b/solution.py
@@ -29,18 +29,14 @@
 
 
 def kern(u, v):
-    nu = jnp.sum(u * u, axis=0, keepdims=True)
-    nv = jnp.sum(v * v, axis=0, keepdims=True)
+    nu = jnp.sum(u * u, axis=0)
+    nv = jnp.sum(v * v, axis=0)
     u1, u2, u3 = split3(u)
     v1, v2, v3 = split3(-2.0 * v)
-    a1, a2, a3 = split3(nu)
-    b1, b2, b3 = split3(nv)
-    one_u = jnp.ones_like(a1)
-    one_v = jnp.ones_like(b1)
-    left = jnp.concatenate([u1, u1, u2, u1, u3, u2, a1, a2, a3, one_u, one_u, one_u], axis=0)
-    right = jnp.concatenate([v1, v2, v1, v3, v1, v2, one_v, one_v, one_v, b1, b2, b3], axis=0)
-    dist = lax.dot_general(left, right, (((0,), (0,)), ((), ())), preferred_element_type=jnp.float32)
-    kernel = jnp.exp(-kernel_scale * dist)
+    left = jnp.concatenate([u1, u1, u2, u1, u3, u2], axis=0)
+    right = jnp.concatenate([v1, v2, v1, v3, v1, v2], axis=0)
+    cross2 = lax.dot_general(left, right, (((0,), (0,)), ((), ())), preferred_element_type=jnp.float32)
+    kernel = jnp.exp(-kernel_scale * ((nu[:, None] + nv[None, :]) + cross2))
     k1 = lax.reduce_precision(kernel, exponent_bits=8, mantissa_bits=7)
     return lax.optimization_barrier((k1.astype(jnp.bfloat16), (kernel - k1).astype(jnp.bfloat16)))
 

time: 144 us -> 144 us (level)
  local copies, waits for them, and re-layouts: 16 us -> 8.47 us
  waiting for transfers between devices: 28.7 us -> 33.2 us
  matrix products: 44.5 us -> 47.5 us
    concatenate x7 -> x0, local copies, waits for them, and re-layouts: 5.48 us -> none  [the longest x4 4.29 us: kern(): jnp.concatenate([u1, u1, u2, u1, u3, u2, a1, a2, a3, one_u, one_u, one_u]...]
    all_to_all x4, waiting for transfers between devices: 23.8 us -> 28.4 us  [gather_all(): return lax.all_to_all(sent, ALL, 0, 0, tiled=True)]
    dot_general x3, matrix products: 16.8 us -> 19.3 us  [kern(): lax.dot_general(left, right, (((0,), (0,)), ((), ())), preferred_element_...]
  transfers between devices with their start and end apart: 6 -> 6, of which waited for: 5 -> 5; matrix products, arithmetic and copies ran while one was open for 19% -> 16% of each run, Pallas kernels for 0% -> 0%
where the time goes in v10:
time: 144 us; the launch traced here: 143 us
  matrix products  47.5 us (33%)
  waiting for transfers between devices  33.2 us (23%)
  starting transfers between devices  26.2 us (18%)
  Pallas kernels  16.6 us (12%)
  local copies, waits for them, and re-layouts  8.47 us (6%)
  other arithmetic  5.8 us (4%)
  between operations  5.06 us (4%)
    all_to_all x4, waiting for transfers between devices, gather_all(): return lax.all_to_all(sent, ALL, 0, 0, tiled=True)  28.4 us
    dot_general x3, matrix products, kern(): lax.dot_general(left, right, (((0,), (0,)), ((), ())), preferred_element_...  19.3 us
    all_to_all x4, starting transfers between devices, gather_all(): return lax.all_to_all(sent, ALL, 0, 0, tiled=True)  19 us
    pallas_call x2, Pallas kernels, solve_rows(): pl.pallas_call(solve_kernel, grid_spec=grid_spec, out_shape=jax.ShapeDtyp...  16.6 us
    dot_general x3, matrix products, apply_kernel(): lax.dot_general(jnp.concatenate([d1, d2], axis=0), k1, dims, preferred_el...  13.6 us
    dot_general x3, matrix products, apply_kernel(): low = lax.dot_general(d1, k2, dims, preferred_element_type=jnp.float32)  12.4 us
    all_to_all x2, starting transfers between devices, distribute(): scattered = lax.all_to_all(pieces, 'grp', 0, 0, tiled=True)  7.18 us
    all_to_all x2, waiting for transfers between devices, distribute(): scattered = lax.all_to_all(pieces, 'grp', 0, 0, tiled=True)  4.85 us
  transfers between devices with their start and end apart: 6, of which 5 were waited for; matrix products, arithmetic and copies ran while one was open for 16% of the time, Pallas kernels for 0%

profile of v10, /device:TPU:0, one launch (start us, length us, event | category | flops | bytes accessed | tf_op | source)
XLA Modules:
  0.0 142.9 jit_solution(14159322725765576440)
XLA Ops:
  0.6 1.3 fusion.67
  1.9 2.0 %convert_bitcast_fusion.1 = (s32[8,128]{1,0:T(8,128)S(1)}, pred[1024]{0:T(1024)(128)(4,1)S(1)}, s32[8,128]{1,0:T(8,128)S(1)}, pred[1024]{0:T(1024)(128)(4,1)S(1)}) fusion(s32[1024]{0:T(1024)} %param.9, s32[]{:T(128)} %bitcast, s32[]{:T(128)} %bitcast.3), kind=kLoop, calls=%fused_computation.184 | loop fusion | flops 4096 | bytes 14344 | tf_op jit(solution)/shard_map/convert
  3.9 0.3 reduce-window.16
  4.3 0.1 slice_reduce_fusion.1
  4.5 0.3 reduce-window.24
  4.9 0.1 slice_reduce_fusion
  5.1 0.8 constant_dynamic-update-slice_fusion.1
  5.9 0.8 constant_dynamic-update-slice_fusion
  6.8 0.9 fusion.16
  7.7 0.3 fusion.12
  8.1 0.9 broadcast_in_dim.12
  9.0 7.3 %all-to-all-start = ((f32[32,48,128]{2,1,0:T(8,128)}), f32[32,48,128]{2,1,0:T(8,128)S(1)}, u32[]{:S(2)}, u32[]{:S(2)}) async-start(f32[32,48,128]{2,1,0:T(8,128)} %broadcast_in_dim.12), calls=%async_computation | async-start | bytes 1572864 | tf_op jit(solution)/shard_map/all_to_all | solution.py:20
  20.3 15.6 %all-to-all-done = f32[32,48,128]{2,1,0:T(8,128)S(1)} async-done(((f32[32,48,128]{2,1,0:T(8,128)}), f32[32,48,128]{2,1,0:T(8,128)S(1)}, u32[]{:S(2)}, u32[]{:S(2)}) %all-to-all-start) | async-done | bytes 786464 | tf_op jit(solution)/shard_map/all_to_all | solution.py:20
  36.1 8.3 %shard_map.77 = f32[16,1024]{1,0:T(8,128)S(1)} custom-call(s32[1]{0:T(128)} %constant.64.clone.1.slot_ref, f32[1,1024,4096]{2,1,0:T(8,128)} %inv_ref.3, bf16[32,4096]{1,0:T(8,128)(2,1)S(1)} %pad_maximum_fusion.rcat_ref, bf16[16,4096]{1,0:T(8,128)(2,1)S(1)} %get-tuple-element.52.r1_ref), custom_call_target="tpu_custom_call" | custom-call | flops 402653184 | bytes 16777216 | tf_op jit(solution)/shard_map/pallas_call | solution.py:92
  44.4 0.6 bitcast_bitcast_fusion.1
  45.1 3.8 %all-to-all-start.1 = ((f32[8,16,128]{2,1,0:T(8,128)}), f32[8,16,128]{2,1,0:T(8,128)S(1)}, u32[]{:S(2)}, u32[]{:S(2)}) async-start(f32[8,16,128]{2,1,0:T(8,128)} %bitcast_bitcast_fusion.1), calls=%async_computation.1 | async-start | bytes 131072 | tf_op jit(solution)/shard_map/all_to_all | solution.py:126
  49.1 4.8 %all-to-all-done.1 = f32[8,16,128]{2,1,0:T(8,128)S(1)} async-done(((f32[8,16,128]{2,1,0:T(8,128)}), f32[8,16,128]{2,1,0:T(8,128)S(1)}, u32[]{:S(2)}, u32[]{:S(2)}) %all-to-all-start.1) | async-done | bytes 65568 | tf_op jit(solution)/shard_map/all_to_all | solution.py:126
  53.9 0.7 broadcast_in_dim.14
  54.7 2.9 %all-to-all-start.2 = ((f32[32,16,128]{2,1,0:T(8,128)}), f32[32,16,128]{2,1,0:T(8,128)S(1)}, u32[]{:S(2)}, u32[]{:S(2)}) async-start(f32[32,16,128]{2,1,0:T(8,128)} %broadcast_in_dim.14), calls=%async_computation.2 | async-start | bytes 524288 | tf_op jit(solution)/shard_map/all_to_all | solution.py:20
  57.6 2.5 %fusion.4 = (bf16[128,4096]{1,0:T(8,128)(2,1)S(1)}, bf16[128,4096]{1,0:T(8,128)(2,1)}) fusion(bf16[96,128]{1,0:T(8,128)(2,1)} %copy-done.3, bf16[96,4096]{1,0:T(8,128)(2,1)S(1)} %constant_dynamic-update-slice_fusion.8, f32[4096]{0:T(1024)S(1)} %bitcast.128, f32[128]{0:T(128)S(1)} %get-tuple-element.57), kind=kOutput, calls=%fused_computation.13 | convolution fusion | flops 104333312 | bytes 2925056 | tf_op jit(solution)/shard_map/dot_general | solution.py:38
  60.2 7.6 %all-to-all-done.2 = f32[32,16,128]{2,1,0:T(8,128)S(1)} async-done(((f32[32,16,128]{2,1,0:T(8,128)}), f32[32,16,128]{2,1,0:T(8,128)S(1)}, u32[]{:S(2)}, u32[]{:S(2)}) %all-to-all-start.2) | async-done | bytes 262176 | tf_op jit(solution)/shard_map/all_to_all | solution.py:20
  67.8 0.2 copy.18
  67.9 0.2 fusion.19
  68.1 0.2 copy.65
  68.3 1.0 fusion.9
  69.3 1.7 %fusion.35 = f32[32,128]{1,0:T(8,128)S(1)} fusion(bf16[128,4096]{1,0:T(8,128)(2,1)} %get-tuple-element.14, bf16[16,4096]{1,0:T(8,128)(2,1)S(1)} %get-tuple-element.47, bf16[16,4096]{1,0:T(8,128)(2,1)S(1)} %get-tuple-element.48), kind=kOutput, calls=%fused_computation.87 | convolution fusion | flops 34078720 | bytes 1327104 | tf_op jit(solution)/shard_map/dot_general | solution.py:51
  71.0 0.4 fusion.11
  71.5 0.7 broadcast_in_dim.15
  72.2 2.9 %all-to-all-start.3 = ((f32[32,16,128]{2,1,0:T(8,128)}), f32[32,16,128]{2,1,0:T(8,128)S(1)}, u32[]{:S(2)}, u32[]{:S(2)}) async-start(f32[32,16,128]{2,1,0:T(8,128)} %broadcast_in_dim.15), calls=%async_computation.3 | async-start | bytes 524288 | tf_op jit(solution)/shard_map/all_to_all | solution.py:20
  75.4 8.4 %fusion.1 = (bf16[1024,4096]{1,0:T(8,128)(2,1)}, bf16[1024,4096]{1,0:T(8,128)(2,1)}) fusion(f32[4096]{0:T(1024)S(1)} %multiply_reduce_fusion, f32[1024]{0:T(1024)S(1)} %multiply_reduce_fusion.3, bf16[96,1024]{1,0:T(8,128)(2,1)S(1)} %constant_dynamic-update-slice_fusion.24, bf16[96,4096]{1,0:T(8,128)(2,1)S(1)} %constant_dynamic-update-slice_fusion.30), kind=kOutput, calls=%fused_computation.5 | convolution fusion | flops 834666496 | bytes 17780736 | tf_op jit(solution)/shard_map/dot_general | solution.py:38
  83.8 0.5 fusion.52
  84.3 0.9 all-to-all-done.3
  85.2 8.3 %shard_map.78 = f32[16,1024]{1,0:T(8,128)S(1)} custom-call(s32[1]{0:T(128)} %constant.64.clone.1.slot_ref, f32[1,1024,4096]{2,1,0:T(8,128)} %inv_ref.3, bf16[32,4096]{1,0:T(8,128)(2,1)S(1)} %pad_maximum_fusion.2.rcat_ref, bf16[16,4096]{1,0:T(8,128)(2,1)S(1)} %get-tuple-element.45.r1_ref), custom_call_target="tpu_custom_call" | custom-call | flops 402653184 | bytes 16777216 | tf_op jit(solution)/shard_map/pallas_call | solution.py:92
  94.0 8.4 %fusion = (bf16[1024,4096]{1,0:T(8,128)(2,1)}, bf16[1024,4096]{1,0:T(8,128)(2,1)}) fusion(f32[4096]{0:T(1024)S(1)} %multiply_reduce_fusion.1, f32[1024]{0:T(1024)S(1)} %multiply_reduce_fusion.4, bf16[96,1024]{1,0:T(8,128)(2,1)S(1)} %constant_dynamic-update-slice_fusion.13, bf16[96,4096]{1,0:T(8,128)(2,1)S(1)} %constant_dynamic-update-slice_fusion.19), kind=kOutput, calls=%fused_computation.4 | convolution fusion | flops 834666496 | bytes 17780736 | tf_op jit(solution)/shard_map/dot_general | solution.py:38
  102.3 0.6 bitcast_bitcast_fusion
  103.0 3.4 %all-to-all-start.4 = ((f32[8,16,128]{2,1,0:T(8,128)}), f32[8,16,128]{2,1,0:T(8,128)S(1)}, u32[]{:S(2)}, u32[]{:S(2)}) async-start(f32[8,16,128]{2,1,0:T(8,128)} %bitcast_bitcast_fusion), calls=%async_computation.4 | async-start | bytes 131072 | tf_op jit(solution)/shard_map/all_to_all | solution.py:126
  106.4 6.0 %fusion.34 = f32[32,1024]{1,0:T(8,128)S(1)} fusion(bf16[1024,4096]{1,0:T(8,128)(2,1)} %get-tuple-element.19, bf16[16,4096]{1,0:T(8,128)(2,1)S(1)} %get-tuple-element.47, bf16[16,4096]{1,0:T(8,128)(2,1)S(1)} %get-tuple-element.48), kind=kOutput, calls=%fused_computation.86 | convolution fusion | flops 268959744 | bytes 8781824 | tf_op jit(solution)/shard_map/dot_general | solution.py:51
  112.4 0.7 broadcast_in_dim.17
  113.1 5.9 %all-to-all-start.5 = ((f32[32,16,128]{2,1,0:T(8,128)}), f32[32,16,128]{2,1,0:T(8,128)S(1)}, u32[]{:S(2)}, u32[]{:S(2)}) async-start(f32[32,16,128]{2,1,0:T(8,128)} %broadcast_in_dim.17), calls=%async_computation.5 | async-start | bytes 524288 | tf_op jit(solution)/shard_map/all_to_all | solution.py:20
  119.0 5.7 %fusion.8 = f32[16,1024]{1,0:T(8,128)S(1)} fusion(f32[16,1024]{1,0:T(8,128)S(1)} %copy-done.1, bf16[16,4096]{1,0:T(8,128)(2,1)S(1)} %get-tuple-element.48, bf16[1024,4096]{1,0:T(8,128)(2,1)} %get-tuple-element.20, f32[32,1024]{1,0:T(8,128)S(1)} %fusion.34, f32[48,1024]{1,0:T(8,128)S(1)} %fusion.52), kind=kOutput, calls=%fused_computation.19 | convolution fusion | flops 134332416 | bytes 8978432 | tf_op jit(solution)/shard_map/dot_general | solution.py:52
  124.6 4.3 %all-to-all-done.5 = f32[32,16,128]{2,1,0:T(8,128)S(1)} async-done(((f32[32,16,128]{2,1,0:T(8,128)}), f32[32,16,128]{2,1,0:T(8,128)S(1)}, u32[]{:S(2)}, u32[]{:S(2)}) %all-to-all-start.5) | async-done | bytes 262176 | tf_op jit(solution)/shard_map/all_to_all | solution.py:20
  128.9 0.2 copy.23
  129.1 0.2 fusion.23
  129.3 0.2 copy.64
  129.5 0.5 fusion.42
  130.0 0.7 add_add_fusion
  130.6 6.0 %fusion.25 = f32[32,1024]{1,0:T(8,128)S(1)} fusion(bf16[1024,4096]{1,0:T(8,128)(2,1)} %get-tuple-element.24, bf16[16,4096]{1,0:T(8,128)(2,1)S(1)} %get-tuple-element.43, bf16[16,4096]{1,0:T(8,128)(2,1)S(1)} %get-tuple-element.44), kind=kOutput, calls=%fused_computation.69 | convolution fusion | flops 268959744 | bytes 8781824 | tf_op jit(solution)/shard_map/dot_general | solution.py:51
  136.6 6.3 %fusion.6 = f32[16,1024]{1,0:T(8,128)} fusion(f32[16,1024]{1,0:T(8,128)S(1)} %fusion.8, bf16[16,4096]{1,0:T(8,128)(2,1)S(1)} %get-tuple-element.44, bf16[1024,4096]{1,0:T(8,128)(2,1)} %get-tuple-element.25, f32[32,1024]{1,0:T(8,128)S(1)} %fusion.25, f32[48,1024]{1,0:T(8,128)S(1)} %fusion.42), kind=kOutput, calls=%fused_computation.16 | convolution fusion | flops 134332416 | bytes 8978432 | tf_op jit(solution)/shard_map/dot_general | solution.py:52
  (71 shorter events, 1.6 us)
Async XLA Ops:
  9.0 26.9 %all-to-all-start = ((f32[32,48,128]{2,1,0:T(8,128)}), f32[32,48,128]{2,1,0:T(8,128)S(1)}, u32[]{:S(2)}, u32[]{:S(2)}) async-start(f32[32,48,128]{2,1,0:T(8,128)} %broadcast_in_dim.12), calls=%async_computation | async-start | bytes 1572864 | tf_op jit(solution)/shard_map/all_to_all | solution.py:20
  20.3 24.1 %copy-start.3 = (bf16[96,128]{1,0:T(8,128)(2,1)}, bf16[96,128]{1,0:T(8,128)(2,1)S(1)}, u32[]{:S(2)}) copy-start(bf16[96,128]{1,0:T(8,128)(2,1)S(1)} %constant_dynamic-update-slice_fusion.2) | copy-start | bytes 73732
  44.4 27.0 %copy-start = (f32[16,1024]{1,0:T(8,128)S(1)}, f32[16,1024]{1,0:T(8,128)}, u32[]{:S(2)}) copy-start(f32[16,1024]{1,0:T(8,128)} %param.6) | copy-start | bytes 196612
  45.1 8.9 %all-to-all-start.1 = ((f32[8,16,128]{2,1,0:T(8,128)}), f32[8,16,128]{2,1,0:T(8,128)S(1)}, u32[]{:S(2)}, u32[]{:S(2)}) async-start(f32[8,16,128]{2,1,0:T(8,128)} %bitcast_bitcast_fusion.1), calls=%async_computation.1 | async-start | bytes 131072 | tf_op jit(solution)/shard_map/all_to_all | solution.py:126
  54.7 13.1 %all-to-all-start.2 = ((f32[32,16,128]{2,1,0:T(8,128)}), f32[32,16,128]{2,1,0:T(8,128)S(1)}, u32[]{:S(2)}, u32[]{:S(2)}) async-start(f32[32,16,128]{2,1,0:T(8,128)} %broadcast_in_dim.14), calls=%async_computation.2 | async-start | bytes 524288 | tf_op jit(solution)/shard_map/all_to_all | solution.py:20
  72.2 12.9 %all-to-all-start.3 = ((f32[32,16,128]{2,1,0:T(8,128)}), f32[32,16,128]{2,1,0:T(8,128)S(1)}, u32[]{:S(2)}, u32[]{:S(2)}) async-start(f32[32,16,128]{2,1,0:T(8,128)} %broadcast_in_dim.15), calls=%async_computation.3 | async-start | bytes 524288 | tf_op jit(solution)/shard_map/all_to_all | solution.py:20
  102.3 16.6 %copy-start.1 = (f32[16,1024]{1,0:T(8,128)S(1)}, f32[16,1024]{1,0:T(8,128)}, u32[]{:S(2)}) copy-start(f32[16,1024]{1,0:T(8,128)} %param.7) | copy-start | bytes 196612
  103.0 9.4 %all-to-all-start.4 = ((f32[8,16,128]{2,1,0:T(8,128)}), f32[8,16,128]{2,1,0:T(8,128)S(1)}, u32[]{:S(2)}, u32[]{:S(2)}) async-start(f32[8,16,128]{2,1,0:T(8,128)} %bitcast_bitcast_fusion), calls=%async_computation.4 | async-start | bytes 131072 | tf_op jit(solution)/shard_map/all_to_all | solution.py:126
  106.3 23.6 %copy-start.2 = (f32[16,1024]{1,0:T(8,128)S(1)}, f32[16,1024]{1,0:T(8,128)}, u32[]{:S(2)}) copy-start(f32[16,1024]{1,0:T(8,128)} %param.8) | copy-start | bytes 196612
  113.1 15.8 %all-to-all-start.5 = ((f32[32,16,128]{2,1,0:T(8,128)}), f32[32,16,128]{2,1,0:T(8,128)S(1)}, u32[]{:S(2)}, u32[]{:S(2)}) async-start(f32[32,16,128]{2,1,0:T(8,128)} %broadcast_in_dim.17), calls=%async_computation.5 | async-start | bytes 524288 | tf_op jit(solution)/shard_map/all_to_all | solution.py:20

commit v11 on v10

--- a/solution.py
+++ b/solution.py
@@ -149,6 +149,7 @@
 
     delta0 = solve(block_res0, block0)
     owned0 = lax.dynamic_slice_in_dim(delta0, mine * per, per, axis=1)
+    kernel0 = kern(points, block_pts0)
     early = apply_kernel(delta0, kern(pts1_local, block_pts0))
     overlap = lax.dot_general(sel0, sel1, (((0,), (0,)), ((), ())), preferred_element_type=jnp.float32)
     overlap = overlap.astype(jnp.bfloat16)
@@ -158,10 +159,10 @@
     kernel1 = kern(pts_late, pts1_late)
 
     solved1 = solve_rows(inverse, block1 % slots, block_res1)
-    solved1, pts_later, pts0_later = lax.optimization_barrier((solved1, points, block_pts0))
+    solved1, delta0_late = lax.optimization_barrier((solved1, delta0))
     delta1 = distribute(solved1, block1)
     spread0 = exact_dot(owned0, sel0, (((1,), (1,)), ((), ())))
-    update0 = apply_kernel(delta0, kern(pts_later, pts0_later))
+    update0 = apply_kernel(delta0_late, kernel0)
     residual = residual - update0 - ridge_weight * spread0
     coef = coef + spread0
 

time: 144 us -> 137 us (0.951)
  waiting for transfers between devices: 33.2 us -> 20.3 us
  other arithmetic: 5.8 us -> 11.4 us
  starting transfers between devices: 26.2 us -> 28.6 us
  matrix products: 47.5 us -> 45.7 us
    all_to_all x4, waiting for transfers between devices: 28.4 us -> 16.4 us  [gather_all(): return lax.all_to_all(sent, ALL, 0, 0, tiled=True)]
    unnamed x31 -> x26, other arithmetic: 0.66 us -> 4.69 us
    all_to_all x4, starting transfers between devices: 19 us -> 21.4 us  [gather_all(): return lax.all_to_all(sent, ALL, 0, 0, tiled=True)]
  transfers between devices with their start and end apart: 6 -> 6, of which waited for: 5 -> 5; matrix products, arithmetic and copies ran while one was open for 16% -> 27% of each run, Pallas kernels for 0% -> 0%
where the time goes in v11:
time: 137 us; the launch traced here: 135 us
  matrix products  45.7 us (33%)
  starting transfers between devices  28.6 us (21%)
  waiting for transfers between devices  20.3 us (15%)
  Pallas kernels  16.6 us (12%)
  other arithmetic  11.4 us (8%)
  local copies, waits for them, and re-layouts  7.75 us (6%)
  between operations  5 us (4%)
    all_to_all x4, starting transfers between devices, gather_all(): return lax.all_to_all(sent, ALL, 0, 0, tiled=True)  21.4 us
    dot_general x3, matrix products, kern(): lax.dot_general(left, right, (((0,), (0,)), ((), ())), preferred_element_...  18.7 us
    pallas_call x2, Pallas kernels, solve_rows(): pl.pallas_call(solve_kernel, grid_spec=grid_spec, out_shape=jax.ShapeDtyp...  16.6 us
    all_to_all x4, waiting for transfers between devices, gather_all(): return lax.all_to_all(sent, ALL, 0, 0, tiled=True)  16.4 us
    dot_general x3, matrix products, apply_kernel(): lax.dot_general(jnp.concatenate([d1, d2], axis=0), k1, dims, preferred_el...  12.4 us
    dot_general x3, matrix products, apply_kernel(): low = lax.dot_general(d1, k2, dims, preferred_element_type=jnp.float32)  12.4 us
    all_to_all x2, starting transfers between devices, distribute(): scattered = lax.all_to_all(pieces, 'grp', 0, 0, tiled=True)  7.19 us
    unnamed x26, other arithmetic  4.69 us
  transfers between devices with their start and end apart: 6, of which 5 were waited for; matrix products, arithmetic and copies ran while one was open for 27% of the time, Pallas kernels for 0%

profile of v11, /device:TPU:0, one launch (start us, length us, event | category | flops | bytes accessed | tf_op | source)
XLA Modules:
  0.0 135.4 jit_solution(4576414278699211895)
XLA Ops:
  0.6 1.3 fusion.72
  1.9 2.0 %convert_bitcast_fusion.1 = (s32[8,128]{1,0:T(8,128)S(1)}, pred[1024]{0:T(1024)(128)(4,1)S(1)}, s32[8,128]{1,0:T(8,128)S(1)}, pred[1024]{0:T(1024)(128)(4,1)S(1)}) fusion(s32[1024]{0:T(1024)} %param.9, s32[]{:T(128)} %bitcast, s32[]{:T(128)} %bitcast.3), kind=kLoop, calls=%fused_computation.179 | loop fusion | flops 4096 | bytes 14344 | tf_op jit(solution)/shard_map/convert
  3.9 0.3 reduce-window.16
  4.5 0.3 reduce-window.24
  5.1 0.8 constant_dynamic-update-slice_fusion.1
  5.9 0.9 multiply_reduce_fusion.3
  6.8 0.9 fusion.16
  7.8 0.3 fusion.12
  8.1 0.9 broadcast_in_dim.12
  9.0 7.3 %all-to-all-start = ((f32[32,48,128]{2,1,0:T(8,128)}), f32[32,48,128]{2,1,0:T(8,128)S(1)}, u32[]{:S(2)}, u32[]{:S(2)}) async-start(f32[32,48,128]{2,1,0:T(8,128)} %broadcast_in_dim.12), calls=%async_computation | async-start | bytes 1572864 | tf_op jit(solution)/shard_map/all_to_all | solution.py:20
  20.3 0.8 constant_dynamic-update-slice_fusion.18
  21.2 0.8 constant_dynamic-update-slice_fusion.17
  22.0 0.8 constant_dynamic-update-slice_fusion.16
  22.9 0.8 constant_dynamic-update-slice_fusion.15
  23.7 0.9 constant_dynamic-update-slice_fusion.14
  24.6 0.9 constant_dynamic-update-slice_fusion.13
  25.4 10.5 %all-to-all-done = f32[32,48,128]{2,1,0:T(8,128)S(1)} async-done(((f32[32,48,128]{2,1,0:T(8,128)}), f32[32,48,128]{2,1,0:T(8,128)S(1)}, u32[]{:S(2)}, u32[]{:S(2)}) %all-to-all-start) | async-done | bytes 786464 | tf_op jit(solution)/shard_map/all_to_all | solution.py:20
  36.1 8.3 %shard_map.77 = f32[16,1024]{1,0:T(8,128)S(1)} custom-call(s32[1]{0:T(128)} %constant.64.clone.1.slot_ref, f32[1,1024,4096]{2,1,0:T(8,128)} %inv_ref.3, bf16[32,4096]{1,0:T(8,128)(2,1)S(1)} %pad_maximum_fusion.rcat_ref, bf16[16,4096]{1,0:T(8,128)(2,1)S(1)} %get-tuple-element.52.r1_ref), custom_call_target="tpu_custom_call" | custom-call | flops 402653184 | bytes 16777216 | tf_op jit(solution)/shard_map/pallas_call | solution.py:92
  44.5 0.6 bitcast_bitcast_fusion.1
  45.1 3.8 %all-to-all-start.1 = ((f32[8,16,128]{2,1,0:T(8,128)}), f32[8,16,128]{2,1,0:T(8,128)S(1)}, u32[]{:S(2)}, u32[]{:S(2)}) async-start(f32[8,16,128]{2,1,0:T(8,128)} %bitcast_bitcast_fusion.1), calls=%async_computation.1 | async-start | bytes 131072 | tf_op jit(solution)/shard_map/all_to_all | solution.py:126
  49.2 0.8 fusion.4
  50.1 3.9 %all-to-all-done.1 = f32[8,16,128]{2,1,0:T(8,128)S(1)} async-done(((f32[8,16,128]{2,1,0:T(8,128)}), f32[8,16,128]{2,1,0:T(8,128)S(1)}, u32[]{:S(2)}, u32[]{:S(2)}) %all-to-all-start.1) | async-done | bytes 65568 | tf_op jit(solution)/shard_map/all_to_all | solution.py:126
  54.0 0.7 broadcast_in_dim.14
  54.7 2.9 %all-to-all-start.2 = ((f32[32,16,128]{2,1,0:T(8,128)}), f32[32,16,128]{2,1,0:T(8,128)S(1)}, u32[]{:S(2)}, u32[]{:S(2)}) async-start(f32[32,16,128]{2,1,0:T(8,128)} %broadcast_in_dim.14), calls=%async_computation.2 | async-start | bytes 524288 | tf_op jit(solution)/shard_map/all_to_all | solution.py:20
  57.7 9.5 %fusion = (bf16[1024,4096]{1,0:T(8,128)(2,1)}, bf16[1024,4096]{1,0:T(8,128)(2,1)}) fusion(f32[4096]{0:T(1024)S(1)} %bitcast.125, f32[1024]{0:T(1024)S(1)} %get-tuple-element.57, bf16[96,1024]{1,0:T(8,128)(2,1)S(1)} %copy-done.5, bf16[96,4096]{1,0:T(8,128)(2,1)} %copy-done.3), kind=kOutput, calls=%fused_computation.4 | convolution fusion | flops 834666496 | bytes 17780736 | tf_op jit(solution)/shard_map/dot_general | solution.py:38
  67.2 0.7 all-to-all-done.2
  68.1 0.2 copy.68
  68.3 1.0 fusion.9
  69.4 0.5 fusion.25
  69.8 0.4 fusion.11
  70.4 0.7 broadcast_in_dim.15
  71.1 5.4 %all-to-all-start.3 = ((f32[32,16,128]{2,1,0:T(8,128)}), f32[32,16,128]{2,1,0:T(8,128)S(1)}, u32[]{:S(2)}, u32[]{:S(2)}) async-start(f32[32,16,128]{2,1,0:T(8,128)} %broadcast_in_dim.15), calls=%async_computation.3 | async-start | bytes 524288 | tf_op jit(solution)/shard_map/all_to_all | solution.py:20
  76.7 8.4 %fusion.1 = (bf16[1024,4096]{1,0:T(8,128)(2,1)}, bf16[1024,4096]{1,0:T(8,128)(2,1)}) fusion(f32[4096]{0:T(1024)S(1)} %multiply_reduce_fusion, f32[1024]{0:T(1024)S(1)} %multiply_reduce_fusion.2, bf16[96,1024]{1,0:T(8,128)(2,1)S(1)} %constant_dynamic-update-slice_fusion.19, bf16[96,4096]{1,0:T(8,128)(2,1)S(1)} %constant_dynamic-update-slice_fusion.25), kind=kOutput, calls=%fused_computation.5 | convolution fusion | flops 834666496 | bytes 17780736 | tf_op jit(solution)/shard_map/dot_general | solution.py:38
  85.1 0.5 fusion.57
  85.6 0.9 all-to-all-done.3
  86.5 8.3 %shard_map.78 = f32[16,1024]{1,0:T(8,128)S(1)} custom-call(s32[1]{0:T(128)} %constant.64.clone.1.slot_ref, f32[1,1024,4096]{2,1,0:T(8,128)} %inv_ref.3, bf16[32,4096]{1,0:T(8,128)(2,1)S(1)} %pad_maximum_fusion.1.rcat_ref, bf16[16,4096]{1,0:T(8,128)(2,1)S(1)} %get-tuple-element.45.r1_ref), custom_call_target="tpu_custom_call" | custom-call | flops 402653184 | bytes 16777216 | tf_op jit(solution)/shard_map/pallas_call | solution.py:92
  94.9 0.6 bitcast_bitcast_fusion
  95.5 3.4 %all-to-all-start.4 = ((f32[8,16,128]{2,1,0:T(8,128)}), f32[8,16,128]{2,1,0:T(8,128)S(1)}, u32[]{:S(2)}, u32[]{:S(2)}) async-start(f32[8,16,128]{2,1,0:T(8,128)} %bitcast_bitcast_fusion), calls=%async_computation.4 | async-start | bytes 131072 | tf_op jit(solution)/shard_map/all_to_all | solution.py:126
  98.9 6.0 %fusion.29 = f32[32,1024]{1,0:T(8,128)S(1)} fusion(bf16[1024,4096]{1,0:T(8,128)(2,1)} %get-tuple-element.17, bf16[16,4096]{1,0:T(8,128)(2,1)S(1)} %get-tuple-element.43, bf16[16,4096]{1,0:T(8,128)(2,1)S(1)} %get-tuple-element.44), kind=kOutput, calls=%fused_computation.69 | convolution fusion | flops 268959744 | bytes 8781824 | tf_op jit(solution)/shard_map/dot_general | solution.py:51
  104.9 0.7 broadcast_in_dim.17
  105.7 5.9 %all-to-all-start.5 = ((f32[32,16,128]{2,1,0:T(8,128)}), f32[32,16,128]{2,1,0:T(8,128)S(1)}, u32[]{:S(2)}, u32[]{:S(2)}) async-start(f32[32,16,128]{2,1,0:T(8,128)} %broadcast_in_dim.17), calls=%async_computation.5 | async-start | bytes 524288 | tf_op jit(solution)/shard_map/all_to_all | solution.py:20
  111.5 5.7 %fusion.8 = f32[16,1024]{1,0:T(8,128)S(1)} fusion(f32[16,1024]{1,0:T(8,128)S(1)} %copy-done.1, bf16[16,4096]{1,0:T(8,128)(2,1)S(1)} %get-tuple-element.44, bf16[1024,4096]{1,0:T(8,128)(2,1)} %get-tuple-element.18, f32[32,1024]{1,0:T(8,128)S(1)} %fusion.29, f32[48,1024]{1,0:T(8,128)S(1)} %fusion.57), kind=kOutput, calls=%fused_computation.19 | convolution fusion | flops 134332416 | bytes 8978432 | tf_op jit(solution)/shard_map/dot_general | solution.py:52
  117.2 4.3 %all-to-all-done.5 = f32[32,16,128]{2,1,0:T(8,128)S(1)} async-done(((f32[32,16,128]{2,1,0:T(8,128)}), f32[32,16,128]{2,1,0:T(8,128)S(1)}, u32[]{:S(2)}, u32[]{:S(2)}) %all-to-all-start.5) | async-done | bytes 262176 | tf_op jit(solution)/shard_map/all_to_all | solution.py:20
  121.8 0.2 copy.67
  122.0 0.5 fusion.47
  122.5 0.7 add_add_fusion
  123.2 6.0 %fusion.33 = f32[32,1024]{1,0:T(8,128)S(1)} fusion(bf16[1024,4096]{1,0:T(8,128)(2,1)} %get-tuple-element.22, bf16[16,4096]{1,0:T(8,128)(2,1)S(1)} %get-tuple-element.41, bf16[16,4096]{1,0:T(8,128)(2,1)S(1)} %get-tuple-element.42), kind=kOutput, calls=%fused_computation.73 | convolution fusion | flops 268959744 | bytes 8781824 | tf_op jit(solution)/shard_map/dot_general | solution.py:51
  129.1 6.3 %fusion.6 = f32[16,1024]{1,0:T(8,128)} fusion(f32[16,1024]{1,0:T(8,128)S(1)} %fusion.8, bf16[16,4096]{1,0:T(8,128)(2,1)S(1)} %get-tuple-element.42, bf16[1024,4096]{1,0:T(8,128)(2,1)} %get-tuple-element.23, f32[32,1024]{1,0:T(8,128)S(1)} %fusion.33, f32[48,1024]{1,0:T(8,128)S(1)} %fusion.47), kind=kOutput, calls=%fused_computation.16 | convolution fusion | flops 134332416 | bytes 8978432 | tf_op jit(solution)/shard_map/dot_general | solution.py:52
  (67 shorter events, 2.2 us)
Async XLA Ops:
  9.0 26.9 %all-to-all-start = ((f32[32,48,128]{2,1,0:T(8,128)}), f32[32,48,128]{2,1,0:T(8,128)S(1)}, u32[]{:S(2)}, u32[]{:S(2)}) async-start(f32[32,48,128]{2,1,0:T(8,128)} %broadcast_in_dim.12), calls=%async_computation | async-start | bytes 1572864 | tf_op jit(solution)/shard_map/all_to_all | solution.py:20
  25.4 10.6 %copy-start.4 = (bf16[96,1024]{1,0:T(8,128)(2,1)}, bf16[96,1024]{1,0:T(8,128)(2,1)S(1)}, u32[]{:S(2)}) copy-start(bf16[96,1024]{1,0:T(8,128)(2,1)S(1)} %constant_dynamic-update-slice_fusion.13) | copy-start | bytes 589828
  36.1 21.5 %copy-start.5 = (bf16[96,1024]{1,0:T(8,128)(2,1)S(1)}, bf16[96,1024]{1,0:T(8,128)(2,1)}, u32[]{:S(2)}) copy-start(bf16[96,1024]{1,0:T(8,128)(2,1)} %copy-done.4) | copy-start | bytes 589828
  45.1 8.9 %all-to-all-start.1 = ((f32[8,16,128]{2,1,0:T(8,128)}), f32[8,16,128]{2,1,0:T(8,128)S(1)}, u32[]{:S(2)}, u32[]{:S(2)}) async-start(f32[8,16,128]{2,1,0:T(8,128)} %bitcast_bitcast_fusion.1), calls=%async_computation.1 | async-start | bytes 131072 | tf_op jit(solution)/shard_map/all_to_all | solution.py:126
  49.1 0.9 copy-start.3
  54.7 13.1 %all-to-all-start.2 = ((f32[32,16,128]{2,1,0:T(8,128)}), f32[32,16,128]{2,1,0:T(8,128)S(1)}, u32[]{:S(2)}, u32[]{:S(2)}) async-start(f32[32,16,128]{2,1,0:T(8,128)} %broadcast_in_dim.14), calls=%async_computation.2 | async-start | bytes 524288 | tf_op jit(solution)/shard_map/all_to_all | solution.py:20
  57.6 12.6 %copy-start = (f32[16,1024]{1,0:T(8,128)S(1)}, f32[16,1024]{1,0:T(8,128)}, u32[]{:S(2)}) copy-start(f32[16,1024]{1,0:T(8,128)} %param.6) | copy-start | bytes 196612
  71.1 15.4 %all-to-all-start.3 = ((f32[32,16,128]{2,1,0:T(8,128)}), f32[32,16,128]{2,1,0:T(8,128)S(1)}, u32[]{:S(2)}, u32[]{:S(2)}) async-start(f32[32,16,128]{2,1,0:T(8,128)} %broadcast_in_dim.15), calls=%async_computation.3 | async-start | bytes 524288 | tf_op jit(solution)/shard_map/all_to_all | solution.py:20
  94.8 16.7 %copy-start.1 = (f32[16,1024]{1,0:T(8,128)S(1)}, f32[16,1024]{1,0:T(8,128)}, u32[]{:S(2)}) copy-start(f32[16,1024]{1,0:T(8,128)} %param.7) | copy-start | bytes 196612
  95.5 9.4 %all-to-all-start.4 = ((f32[8,16,128]{2,1,0:T(8,128)}), f32[8,16,128]{2,1,0:T(8,128)S(1)}, u32[]{:S(2)}, u32[]{:S(2)}) async-start(f32[8,16,128]{2,1,0:T(8,128)} %bitcast_bitcast_fusion), calls=%async_computation.4 | async-start | bytes 131072 | tf_op jit(solution)/shard_map/all_to_all | solution.py:126
  98.9 23.6 %copy-start.2 = (f32[16,1024]{1,0:T(8,128)S(1)}, f32[16,1024]{1,0:T(8,128)}, u32[]{:S(2)}) copy-start(f32[16,1024]{1,0:T(8,128)} %param.8) | copy-start | bytes 196612
  105.7 15.8 %all-to-all-start.5 = ((f32[32,16,128]{2,1,0:T(8,128)}), f32[32,16,128]{2,1,0:T(8,128)S(1)}, u32[]{:S(2)}, u32[]{:S(2)}) async-start(f32[32,16,128]{2,1,0:T(8,128)} %broadcast_in_dim.17), calls=%async_computation.5 | async-start | bytes 524288 | tf_op jit(solution)/shard_map/all_to_all | solution.py:20

commit v12 on v11

--- a/solution.py
+++ b/solution.py
@@ -142,10 +142,10 @@
     chosen0 = chosen[:, :per]
     res1_start = chosen[:rhs, per:]
     pts1_local = chosen[rhs:, per:]
-    gathered = to_block(gather_all(jnp.concatenate([chosen0, pts1_local], axis=0), n_dev), rhs + 2 * feat)
-    block_res0 = gathered[:rhs]
-    block_pts0 = gathered[rhs:rhs + feat]
-    block_pts1 = gathered[rhs + feat:]
+    block_res0 = to_block(gather_all(chosen0[:rhs], n_dev), rhs)
+    gathered = to_block(gather_all(jnp.concatenate([chosen0[rhs:], pts1_local], axis=0), n_dev), 2 * feat)
+    block_pts0 = gathered[:feat]
+    block_pts1 = gathered[feat:]
 
     delta0 = solve(block_res0, block0)
     owned0 = lax.dynamic_slice_in_dim(delta0, mine * per, per, axis=1)

time: 137 us -> 145 us (1.058)
  waiting for transfers between devices: 20.3 us -> 28.8 us
  starting transfers between devices: 28.6 us -> 31.8 us
  other arithmetic: 11.4 us -> 8.89 us
    all_to_all x4 -> x5, waiting for transfers between devices: 16.4 us -> 23.9 us  [gather_all(): return lax.all_to_all(sent, ALL, 0, 0, tiled=True)]
    all_to_all x4 -> x5, starting transfers between devices: 21.4 us -> 25.1 us  [gather_all(): return lax.all_to_all(sent, ALL, 0, 0, tiled=True)]
    unnamed x26, other arithmetic: 4.69 us -> 2.98 us
    broadcast_in_dim x6 -> x7, local copies, waits for them, and re-layouts: 3.15 us -> 3.75 us  [gather_all(): sent = jnp.broadcast_to(piece[None], (n_dev,) + piece.shape)]
  transfers between devices with their start and end apart: 6 -> 7, of which waited for: 5 -> 6; matrix products, arithmetic and copies ran while one was open for 27% -> 23% of each run, Pallas kernels for 0% -> 0%
where the time goes in v12:
time: 145 us; the launch traced here: 144 us
  matrix products  44.6 us (31%)
  starting transfers between devices  31.8 us (22%)
  waiting for transfers between devices  28.8 us (20%)
  Pallas kernels  16.6 us (11%)
  other arithmetic  8.89 us (6%)
  local copies, waits for them, and re-layouts  8.24 us (6%)
  between operations  5.01 us (3%)
    all_to_all x5, starting transfers between devices, gather_all(): return lax.all_to_all(sent, ALL, 0, 0, tiled=True)  25.1 us
    all_to_all x5, waiting for transfers between devices, gather_all(): return lax.all_to_all(sent, ALL, 0, 0, tiled=True)  23.9 us
    dot_general x3, matrix products, kern(): lax.dot_general(left, right, (((0,), (0,)), ((), ())), preferred_element_...  17.6 us
    pallas_call x2, Pallas kernels, solve_rows(): pl.pallas_call(solve_kernel, grid_spec=grid_spec, out_shape=jax.ShapeDtyp...  16.6 us
    dot_general x3, matrix products, apply_kernel(): lax.dot_general(jnp.concatenate([d1, d2], axis=0), k1, dims, preferred_el...  12.4 us
    dot_general x3, matrix products, apply_kernel(): low = lax.dot_general(d1, k2, dims, preferred_element_type=jnp.float32)  12.4 us
    all_to_all x2, starting transfers between devices, distribute(): scattered = lax.all_to_all(pieces, 'grp', 0, 0, tiled=True)  6.7 us
    all_to_all x2, waiting for transfers between devices, distribute(): scattered = lax.all_to_all(pieces, 'grp', 0, 0, tiled=True)  4.95 us
  transfers between devices with their start and end apart: 7, of which 6 were waited for; matrix products, arithmetic and copies ran while one was open for 23% of the time, Pallas kernels for 0%

profile of v12, /device:TPU:0, one launch (start us, length us, event | category | flops | bytes accessed | tf_op | source)
XLA Modules:
  0.0 144.0 jit_solution(2975255177604952525)
XLA Ops:
  0.6 1.3 fusion.72
  1.9 2.0 %convert_bitcast_fusion.1 = (s32[8,128]{1,0:T(8,128)S(1)}, pred[1024]{0:T(1024)(128)(4,1)S(1)}, s32[8,128]{1,0:T(8,128)S(1)}, pred[1024]{0:T(1024)(128)(4,1)S(1)}) fusion(s32[1024]{0:T(1024)} %param.9, s32[]{:T(128)} %bitcast, s32[]{:T(128)} %bitcast.3), kind=kLoop, calls=%fused_computation.178 | loop fusion | flops 4096 | bytes 14344 | tf_op jit(solution)/shard_map/convert
  3.9 0.3 reduce-window.16
  4.5 0.3 reduce-window.24
  5.1 0.8 constant_dynamic-update-slice_fusion.1
  5.9 0.9 multiply_reduce_fusion.3
  6.8 0.9 fusion.16
  7.8 0.3 fusion.12
  8.1 0.7 broadcast_in_dim.14
  8.8 7.3 %all-to-all-start = ((f32[32,16,128]{2,1,0:T(8,128)}), f32[32,16,128]{2,1,0:T(8,128)S(1)}, u32[]{:S(2)}, u32[]{:S(2)}) async-start(f32[32,16,128]{2,1,0:T(8,128)} %broadcast_in_dim.14), calls=%async_computation | async-start | bytes 524288 | tf_op jit(solution)/shard_map/all_to_all | solution.py:20
  16.1 0.8 constant_dynamic-update-slice_fusion.18
  20.9 0.8 constant_dynamic-update-slice_fusion.17
  21.7 0.8 constant_dynamic-update-slice_fusion.16
  22.6 3.7 %all-to-all-done = f32[32,16,128]{2,1,0:T(8,128)S(1)} async-done(((f32[32,16,128]{2,1,0:T(8,128)}), f32[32,16,128]{2,1,0:T(8,128)S(1)}, u32[]{:S(2)}, u32[]{:S(2)}) %all-to-all-start) | async-done | bytes 262176 | tf_op jit(solution)/shard_map/all_to_all | solution.py:20
  26.4 8.3 %shard_map.77 = f32[16,1024]{1,0:T(8,128)S(1)} custom-call(s32[1]{0:T(128)} %constant.64.clone.1.slot_ref, f32[1,1024,4096]{2,1,0:T(8,128)} %inv_ref.3, bf16[32,4096]{1,0:T(8,128)(2,1)S(1)} %pad_maximum_fusion.rcat_ref, bf16[16,4096]{1,0:T(8,128)(2,1)S(1)} %get-tuple-element.51.r1_ref), custom_call_target="tpu_custom_call" | custom-call | flops 402653184 | bytes 16777216 | tf_op jit(solution)/shard_map/pallas_call | solution.py:92
  34.7 0.6 bitcast_bitcast_fusion.1
  35.3 3.4 %all-to-all-start.1 = ((f32[8,16,128]{2,1,0:T(8,128)}), f32[8,16,128]{2,1,0:T(8,128)S(1)}, u32[]{:S(2)}, u32[]{:S(2)}) async-start(f32[8,16,128]{2,1,0:T(8,128)} %bitcast_bitcast_fusion.1), calls=%async_computation.1 | async-start | bytes 131072 | tf_op jit(solution)/shard_map/all_to_all | solution.py:126
  38.7 4.9 %all-to-all-done.1 = f32[8,16,128]{2,1,0:T(8,128)S(1)} async-done(((f32[8,16,128]{2,1,0:T(8,128)}), f32[8,16,128]{2,1,0:T(8,128)S(1)}, u32[]{:S(2)}, u32[]{:S(2)}) %all-to-all-start.1) | async-done | bytes 65568 | tf_op jit(solution)/shard_map/all_to_all | solution.py:126
  43.6 0.8 broadcast_in_dim.17
  44.5 2.6 %all-to-all-start.3 = ((f32[32,32,128]{2,1,0:T(8,128)}), f32[32,32,128]{2,1,0:T(8,128)S(1)}, u32[]{:S(2)}, u32[]{:S(2)}) async-start(f32[32,32,128]{2,1,0:T(8,128)} %broadcast_in_dim.17), calls=%async_computation.3 | async-start | bytes 1048576 | tf_op jit(solution)/shard_map/all_to_all | solution.py:20
  47.2 14.3 %all-to-all-done.3 = f32[32,32,128]{2,1,0:T(8,128)S(1)} async-done(((f32[32,32,128]{2,1,0:T(8,128)}), f32[32,32,128]{2,1,0:T(8,128)S(1)}, u32[]{:S(2)}, u32[]{:S(2)}) %all-to-all-start.3) | async-done | bytes 524320 | tf_op jit(solution)/shard_map/all_to_all | solution.py:20
  61.5 0.7 broadcast_in_dim.16
  62.2 4.0 %all-to-all-start.2 = ((f32[32,16,128]{2,1,0:T(8,128)}), f32[32,16,128]{2,1,0:T(8,128)S(1)}, u32[]{:S(2)}, u32[]{:S(2)}) async-start(f32[32,16,128]{2,1,0:T(8,128)} %broadcast_in_dim.16), calls=%async_computation.2 | async-start | bytes 524288 | tf_op jit(solution)/shard_map/all_to_all | solution.py:20
  66.5 0.8 fusion.4
  67.3 8.4 %fusion = (bf16[1024,4096]{1,0:T(8,128)(2,1)}, bf16[1024,4096]{1,0:T(8,128)(2,1)}) fusion(f32[4096]{0:T(1024)S(1)} %bitcast.127, f32[1024]{0:T(1024)S(1)} %get-tuple-element.56, bf16[96,1024]{1,0:T(8,128)(2,1)S(1)} %constant_dynamic-update-slice_fusion.13, bf16[96,4096]{1,0:T(8,128)(2,1)S(1)} %constant_dynamic-update-slice_fusion.8), kind=kOutput, calls=%fused_computation.4 | convolution fusion | flops 834666496 | bytes 17780736 | tf_op jit(solution)/shard_map/dot_general | solution.py:38
  75.7 0.7 all-to-all-done.2
  76.8 0.2 copy.62
  76.9 1.0 fusion.9
  78.0 0.5 fusion.25
  78.4 0.4 fusion.11
  79.0 0.7 broadcast_in_dim.18
  79.7 5.3 %all-to-all-start.4 = ((f32[32,16,128]{2,1,0:T(8,128)}), f32[32,16,128]{2,1,0:T(8,128)S(1)}, u32[]{:S(2)}, u32[]{:S(2)}) async-start(f32[32,16,128]{2,1,0:T(8,128)} %broadcast_in_dim.18), calls=%async_computation.4 | async-start | bytes 524288 | tf_op jit(solution)/shard_map/all_to_all | solution.py:20
  85.3 8.4 %fusion.1 = (bf16[1024,4096]{1,0:T(8,128)(2,1)}, bf16[1024,4096]{1,0:T(8,128)(2,1)}) fusion(f32[4096]{0:T(1024)S(1)} %multiply_reduce_fusion, f32[1024]{0:T(1024)S(1)} %multiply_reduce_fusion.2, bf16[96,1024]{1,0:T(8,128)(2,1)S(1)} %constant_dynamic-update-slice_fusion.19, bf16[96,4096]{1,0:T(8,128)(2,1)S(1)} %constant_dynamic-update-slice_fusion.25), kind=kOutput, calls=%fused_computation.5 | convolution fusion | flops 834666496 | bytes 17780736 | tf_op jit(solution)/shard_map/dot_general | solution.py:38
  93.7 0.5 fusion.57
  94.1 0.9 all-to-all-done.4
  95.1 8.3 %shard_map.78 = f32[16,1024]{1,0:T(8,128)S(1)} custom-call(s32[1]{0:T(128)} %constant.64.clone.1.slot_ref, f32[1,1024,4096]{2,1,0:T(8,128)} %inv_ref.3, bf16[32,4096]{1,0:T(8,128)(2,1)S(1)} %pad_maximum_fusion.1.rcat_ref, bf16[16,4096]{1,0:T(8,128)(2,1)S(1)} %get-tuple-element.44.r1_ref), custom_call_target="tpu_custom_call" | custom-call | flops 402653184 | bytes 16777216 | tf_op jit(solution)/shard_map/pallas_call | solution.py:92
  103.4 0.6 bitcast_bitcast_fusion
  104.1 3.4 %all-to-all-start.5 = ((f32[8,16,128]{2,1,0:T(8,128)}), f32[8,16,128]{2,1,0:T(8,128)S(1)}, u32[]{:S(2)}, u32[]{:S(2)}) async-start(f32[8,16,128]{2,1,0:T(8,128)} %bitcast_bitcast_fusion), calls=%async_computation.5 | async-start | bytes 131072 | tf_op jit(solution)/shard_map/all_to_all | solution.py:126
  107.5 6.0 %fusion.29 = f32[32,1024]{1,0:T(8,128)S(1)} fusion(bf16[1024,4096]{1,0:T(8,128)(2,1)} %get-tuple-element.17, bf16[16,4096]{1,0:T(8,128)(2,1)S(1)} %get-tuple-element.42, bf16[16,4096]{1,0:T(8,128)(2,1)S(1)} %get-tuple-element.43), kind=kOutput, calls=%fused_computation.68 | convolution fusion | flops 268959744 | bytes 8781824 | tf_op jit(solution)/shard_map/dot_general | solution.py:51
  113.5 0.7 broadcast_in_dim.20
  114.2 5.9 %all-to-all-start.6 = ((f32[32,16,128]{2,1,0:T(8,128)}), f32[32,16,128]{2,1,0:T(8,128)S(1)}, u32[]{:S(2)}, u32[]{:S(2)}) async-start(f32[32,16,128]{2,1,0:T(8,128)} %broadcast_in_dim.20), calls=%async_computation.6 | async-start | bytes 524288 | tf_op jit(solution)/shard_map/all_to_all | solution.py:20
  120.1 5.7 %fusion.8 = f32[16,1024]{1,0:T(8,128)S(1)} fusion(f32[16,1024]{1,0:T(8,128)S(1)} %copy-done.1, bf16[16,4096]{1,0:T(8,128)(2,1)S(1)} %get-tuple-element.43, bf16[1024,4096]{1,0:T(8,128)(2,1)} %get-tuple-element.18, f32[32,1024]{1,0:T(8,128)S(1)} %fusion.29, f32[48,1024]{1,0:T(8,128)S(1)} %fusion.57), kind=kOutput, calls=%fused_computation.19 | convolution fusion | flops 134332416 | bytes 8978432 | tf_op jit(solution)/shard_map/dot_general | solution.py:52
  125.7 4.3 %all-to-all-done.6 = f32[32,16,128]{2,1,0:T(8,128)S(1)} async-done(((f32[32,16,128]{2,1,0:T(8,128)}), f32[32,16,128]{2,1,0:T(8,128)S(1)}, u32[]{:S(2)}, u32[]{:S(2)}) %all-to-all-start.6) | async-done | bytes 262176 | tf_op jit(solution)/shard_map/all_to_all | solution.py:20
  130.4 0.2 copy.61
  130.6 0.5 fusion.47
  131.1 0.7 add_add_fusion
  131.7 6.0 %fusion.33 = f32[32,1024]{1,0:T(8,128)S(1)} fusion(bf16[1024,4096]{1,0:T(8,128)(2,1)} %get-tuple-element.22, bf16[16,4096]{1,0:T(8,128)(2,1)S(1)} %get-tuple-element.40, bf16[16,4096]{1,0:T(8,128)(2,1)S(1)} %get-tuple-element.41), kind=kOutput, calls=%fused_computation.72 | convolution fusion | flops 268959744 | bytes 8781824 | tf_op jit(solution)/shard_map/dot_general | solution.py:51
  137.7 6.3 %fusion.6 = f32[16,1024]{1,0:T(8,128)} fusion(f32[16,1024]{1,0:T(8,128)S(1)} %fusion.8, bf16[16,4096]{1,0:T(8,128)(2,1)S(1)} %get-tuple-element.41, bf16[1024,4096]{1,0:T(8,128)(2,1)} %get-tuple-element.23, f32[32,1024]{1,0:T(8,128)S(1)} %fusion.33, f32[48,1024]{1,0:T(8,128)S(1)} %fusion.47), kind=kOutput, calls=%fused_computation.16 | convolution fusion | flops 134332416 | bytes 8978432 | tf_op jit(solution)/shard_map/dot_general | solution.py:52
  (63 shorter events, 2.1 us)
Async XLA Ops:
  8.8 17.5 %all-to-all-start = ((f32[32,16,128]{2,1,0:T(8,128)}), f32[32,16,128]{2,1,0:T(8,128)S(1)}, u32[]{:S(2)}, u32[]{:S(2)}) async-start(f32[32,16,128]{2,1,0:T(8,128)} %broadcast_in_dim.14), calls=%async_computation | async-start | bytes 524288 | tf_op jit(solution)/shard_map/all_to_all | solution.py:20
  26.3 20.8 %copy-start = (f32[16,1024]{1,0:T(8,128)S(1)}, f32[16,1024]{1,0:T(8,128)}, u32[]{:S(2)}) copy-start(f32[16,1024]{1,0:T(8,128)} %param.6) | copy-start | bytes 196612
  35.3 8.3 %all-to-all-start.1 = ((f32[8,16,128]{2,1,0:T(8,128)}), f32[8,16,128]{2,1,0:T(8,128)S(1)}, u32[]{:S(2)}, u32[]{:S(2)}) async-start(f32[8,16,128]{2,1,0:T(8,128)} %bitcast_bitcast_fusion.1), calls=%async_computation.1 | async-start | bytes 131072 | tf_op jit(solution)/shard_map/all_to_all | solution.py:126
  44.5 17.0 %all-to-all-start.3 = ((f32[32,32,128]{2,1,0:T(8,128)}), f32[32,32,128]{2,1,0:T(8,128)S(1)}, u32[]{:S(2)}, u32[]{:S(2)}) async-start(f32[32,32,128]{2,1,0:T(8,128)} %broadcast_in_dim.17), calls=%async_computation.3 | async-start | bytes 1048576 | tf_op jit(solution)/shard_map/all_to_all | solution.py:20
  62.2 14.3 %all-to-all-start.2 = ((f32[32,16,128]{2,1,0:T(8,128)}), f32[32,16,128]{2,1,0:T(8,128)S(1)}, u32[]{:S(2)}, u32[]{:S(2)}) async-start(f32[32,16,128]{2,1,0:T(8,128)} %broadcast_in_dim.16), calls=%async_computation.2 | async-start | bytes 524288 | tf_op jit(solution)/shard_map/all_to_all | solution.py:20
  79.7 15.3 %all-to-all-start.4 = ((f32[32,16,128]{2,1,0:T(8,128)}), f32[32,16,128]{2,1,0:T(8,128)S(1)}, u32[]{:S(2)}, u32[]{:S(2)}) async-start(f32[32,16,128]{2,1,0:T(8,128)} %broadcast_in_dim.18), calls=%async_computation.4 | async-start | bytes 524288 | tf_op jit(solution)/shard_map/all_to_all | solution.py:20
  103.4 16.7 %copy-start.1 = (f32[16,1024]{1,0:T(8,128)S(1)}, f32[16,1024]{1,0:T(8,128)}, u32[]{:S(2)}) copy-start(f32[16,1024]{1,0:T(8,128)} %param.7) | copy-start | bytes 196612
  104.1 9.4 %all-to-all-start.5 = ((f32[8,16,128]{2,1,0:T(8,128)}), f32[8,16,128]{2,1,0:T(8,128)S(1)}, u32[]{:S(2)}, u32[]{:S(2)}) async-start(f32[8,16,128]{2,1,0:T(8,128)} %bitcast_bitcast_fusion), calls=%async_computation.5 | async-start | bytes 131072 | tf_op jit(solution)/shard_map/all_to_all | solution.py:126
  107.4 23.6 %copy-start.2 = (f32[16,1024]{1,0:T(8,128)S(1)}, f32[16,1024]{1,0:T(8,128)}, u32[]{:S(2)}) copy-start(f32[16,1024]{1,0:T(8,128)} %param.8) | copy-start | bytes 196612
  114.2 15.8 %all-to-all-start.6 = ((f32[32,16,128]{2,1,0:T(8,128)}), f32[32,16,128]{2,1,0:T(8,128)S(1)}, u32[]{:S(2)}, u32[]{:S(2)}) async-start(f32[32,16,128]{2,1,0:T(8,128)} %broadcast_in_dim.20), calls=%async_computation.6 | async-start | bytes 524288 | tf_op jit(solution)/shard_map/all_to_all | solution.py:20

commit v13 on v11

--- a/solution.py
+++ b/solution.py
@@ -71,7 +71,7 @@
     o_ref[...] = (both[:rows] + both[rows:]) + low
 
 
-def solve_rows(inverse, slot, block_res, tile=256):
+def solve_rows(inverse, slot, block_res, tile=128):
     _, n, width = inverse.shape
     rows = block_res.shape[0]
     r1f = lax.reduce_precision(block_res, exponent_bits=8, mantissa_bits=7)

time: 137 us -> 141 us (1.029)
  Pallas kernels: 16.6 us -> 20.4 us
    pallas_call x2, Pallas kernels: 16.6 us -> 20.4 us  [solve_rows(): pl.pallas_call(solve_kernel, grid_spec=grid_spec, out_shape=jax.ShapeDtyp...]
  transfers between devices with their start and end apart: 6 -> 6, of which waited for: 5 -> 5; matrix products, arithmetic and copies ran while one was open for 27% -> 26% of each run, Pallas kernels for 0% -> 0%
where the time goes in v13:
time: 141 us; the launch traced here: 139 us
  matrix products  45.7 us (32%)
  starting transfers between devices  28.6 us (20%)
  Pallas kernels  20.4 us (14%)
  waiting for transfers between devices  20.3 us (14%)
  other arithmetic  11.4 us (8%)
  local copies, waits for them, and re-layouts  7.75 us (5%)
  between operations  4.99 us (4%)
    all_to_all x4, starting transfers between devices, gather_all(): return lax.all_to_all(sent, ALL, 0, 0, tiled=True)  21.4 us
    pallas_call x2, Pallas kernels, solve_rows(): pl.pallas_call(solve_kernel, grid_spec=grid_spec, out_shape=jax.ShapeDtyp...  20.4 us
    dot_general x3, matrix products, kern(): lax.dot_general(left, right, (((0,), (0,)), ((), ())), preferred_element_...  18.7 us
    all_to_all x4, waiting for transfers between devices, gather_all(): return lax.all_to_all(sent, ALL, 0, 0, tiled=True)  16.4 us
    dot_general x3, matrix products, apply_kernel(): lax.dot_general(jnp.concatenate([d1, d2], axis=0), k1, dims, preferred_el...  12.4 us
    dot_general x3, matrix products, apply_kernel(): low = lax.dot_general(d1, k2, dims, preferred_element_type=jnp.float32)  12.4 us
    all_to_all x2, starting transfers between devices, distribute(): scattered = lax.all_to_all(pieces, 'grp', 0, 0, tiled=True)  7.19 us
    unnamed x26, other arithmetic  4.69 us
  transfers between devices with their start and end apart: 6, of which 5 were waited for; matrix products, arithmetic and copies ran while one was open for 26% of the time, Pallas kernels for 0%

profile of v13, /device:TPU:0, one launch (start us, length us, event | category | flops | bytes accessed | tf_op | source)
XLA Modules:
  0.0 139.2 jit_solution(12024113687214471717)
XLA Ops:
  0.6 1.3 fusion.72
  1.9 2.0 %convert_bitcast_fusion.1 = (s32[8,128]{1,0:T(8,128)S(1)}, pred[1024]{0:T(1024)(128)(4,1)S(1)}, s32[8,128]{1,0:T(8,128)S(1)}, pred[1024]{0:T(1024)(128)(4,1)S(1)}) fusion(s32[1024]{0:T(1024)} %param.9, s32[]{:T(128)} %bitcast, s32[]{:T(128)} %bitcast.3), kind=kLoop, calls=%fused_computation.179 | loop fusion | flops 4096 | bytes 14344 | tf_op jit(solution)/shard_map/convert
  3.9 0.3 reduce-window.16
  4.5 0.3 reduce-window.24
  5.1 0.8 constant_dynamic-update-slice_fusion.1
  5.9 0.9 multiply_reduce_fusion.3
  6.8 0.9 fusion.16
  7.8 0.3 fusion.12
  8.1 0.9 broadcast_in_dim.12
  9.0 7.3 %all-to-all-start = ((f32[32,48,128]{2,1,0:T(8,128)}), f32[32,48,128]{2,1,0:T(8,128)S(1)}, u32[]{:S(2)}, u32[]{:S(2)}) async-start(f32[32,48,128]{2,1,0:T(8,128)} %broadcast_in_dim.12), calls=%async_computation | async-start | bytes 1572864 | tf_op jit(solution)/shard_map/all_to_all | solution.py:20
  20.3 0.8 constant_dynamic-update-slice_fusion.18
  21.2 0.8 constant_dynamic-update-slice_fusion.17
  22.0 0.8 constant_dynamic-update-slice_fusion.16
  22.9 0.8 constant_dynamic-update-slice_fusion.15
  23.7 0.9 constant_dynamic-update-slice_fusion.14
  24.6 0.9 constant_dynamic-update-slice_fusion.13
  25.4 10.5 %all-to-all-done = f32[32,48,128]{2,1,0:T(8,128)S(1)} async-done(((f32[32,48,128]{2,1,0:T(8,128)}), f32[32,48,128]{2,1,0:T(8,128)S(1)}, u32[]{:S(2)}, u32[]{:S(2)}) %all-to-all-start) | async-done | bytes 786464 | tf_op jit(solution)/shard_map/all_to_all | solution.py:20
  36.1 10.2 %shard_map.77 = f32[16,1024]{1,0:T(8,128)S(1)} custom-call(s32[1]{0:T(128)} %constant.64.clone.1.slot_ref, f32[1,1024,4096]{2,1,0:T(8,128)} %inv_ref.3, bf16[32,4096]{1,0:T(8,128)(2,1)S(1)} %pad_maximum_fusion.rcat_ref, bf16[16,4096]{1,0:T(8,128)(2,1)S(1)} %get-tuple-element.52.r1_ref), custom_call_target="tpu_custom_call" | custom-call | flops 402653184 | bytes 16777216 | tf_op jit(solution)/shard_map/pallas_call | solution.py:92
  46.4 0.7 bitcast_bitcast_fusion.1
  47.0 3.8 %all-to-all-start.1 = ((f32[8,16,128]{2,1,0:T(8,128)}), f32[8,16,128]{2,1,0:T(8,128)S(1)}, u32[]{:S(2)}, u32[]{:S(2)}) async-start(f32[8,16,128]{2,1,0:T(8,128)} %bitcast_bitcast_fusion.1), calls=%async_computation.1 | async-start | bytes 131072 | tf_op jit(solution)/shard_map/all_to_all | solution.py:126
  51.0 0.8 fusion.4
  52.0 3.9 %all-to-all-done.1 = f32[8,16,128]{2,1,0:T(8,128)S(1)} async-done(((f32[8,16,128]{2,1,0:T(8,128)}), f32[8,16,128]{2,1,0:T(8,128)S(1)}, u32[]{:S(2)}, u32[]{:S(2)}) %all-to-all-start.1) | async-done | bytes 65568 | tf_op jit(solution)/shard_map/all_to_all | solution.py:126
  55.9 0.7 broadcast_in_dim.14
  56.6 2.9 %all-to-all-start.2 = ((f32[32,16,128]{2,1,0:T(8,128)}), f32[32,16,128]{2,1,0:T(8,128)S(1)}, u32[]{:S(2)}, u32[]{:S(2)}) async-start(f32[32,16,128]{2,1,0:T(8,128)} %broadcast_in_dim.14), calls=%async_computation.2 | async-start | bytes 524288 | tf_op jit(solution)/shard_map/all_to_all | solution.py:20
  59.5 9.5 %fusion = (bf16[1024,4096]{1,0:T(8,128)(2,1)}, bf16[1024,4096]{1,0:T(8,128)(2,1)}) fusion(f32[4096]{0:T(1024)S(1)} %bitcast.125, f32[1024]{0:T(1024)S(1)} %get-tuple-element.57, bf16[96,1024]{1,0:T(8,128)(2,1)S(1)} %copy-done.5, bf16[96,4096]{1,0:T(8,128)(2,1)} %copy-done.3), kind=kOutput, calls=%fused_computation.4 | convolution fusion | flops 834666496 | bytes 17780736 | tf_op jit(solution)/shard_map/dot_general | solution.py:38
  69.1 0.7 all-to-all-done.2
  70.0 0.2 copy.68
  70.2 1.0 fusion.9
  71.3 0.5 fusion.25
  71.7 0.4 fusion.11
  72.2 0.7 broadcast_in_dim.15
  73.0 5.4 %all-to-all-start.3 = ((f32[32,16,128]{2,1,0:T(8,128)}), f32[32,16,128]{2,1,0:T(8,128)S(1)}, u32[]{:S(2)}, u32[]{:S(2)}) async-start(f32[32,16,128]{2,1,0:T(8,128)} %broadcast_in_dim.15), calls=%async_computation.3 | async-start | bytes 524288 | tf_op jit(solution)/shard_map/all_to_all | solution.py:20
  78.6 8.4 %fusion.1 = (bf16[1024,4096]{1,0:T(8,128)(2,1)}, bf16[1024,4096]{1,0:T(8,128)(2,1)}) fusion(f32[4096]{0:T(1024)S(1)} %multiply_reduce_fusion, f32[1024]{0:T(1024)S(1)} %multiply_reduce_fusion.2, bf16[96,1024]{1,0:T(8,128)(2,1)S(1)} %constant_dynamic-update-slice_fusion.19, bf16[96,4096]{1,0:T(8,128)(2,1)S(1)} %constant_dynamic-update-slice_fusion.25), kind=kOutput, calls=%fused_computation.5 | convolution fusion | flops 834666496 | bytes 17780736 | tf_op jit(solution)/shard_map/dot_general | solution.py:38
  87.0 0.5 fusion.57
  87.5 0.9 all-to-all-done.3
  88.4 10.2 %shard_map.78 = f32[16,1024]{1,0:T(8,128)S(1)} custom-call(s32[1]{0:T(128)} %constant.64.clone.1.slot_ref, f32[1,1024,4096]{2,1,0:T(8,128)} %inv_ref.3, bf16[32,4096]{1,0:T(8,128)(2,1)S(1)} %pad_maximum_fusion.1.rcat_ref, bf16[16,4096]{1,0:T(8,128)(2,1)S(1)} %get-tuple-element.45.r1_ref), custom_call_target="tpu_custom_call" | custom-call | flops 402653184 | bytes 16777216 | tf_op jit(solution)/shard_map/pallas_call | solution.py:92
  98.7 0.6 bitcast_bitcast_fusion
  99.3 3.4 %all-to-all-start.4 = ((f32[8,16,128]{2,1,0:T(8,128)}), f32[8,16,128]{2,1,0:T(8,128)S(1)}, u32[]{:S(2)}, u32[]{:S(2)}) async-start(f32[8,16,128]{2,1,0:T(8,128)} %bitcast_bitcast_fusion), calls=%async_computation.4 | async-start | bytes 131072 | tf_op jit(solution)/shard_map/all_to_all | solution.py:126
  102.7 6.0 %fusion.29 = f32[32,1024]{1,0:T(8,128)S(1)} fusion(bf16[1024,4096]{1,0:T(8,128)(2,1)} %get-tuple-element.17, bf16[16,4096]{1,0:T(8,128)(2,1)S(1)} %get-tuple-element.43, bf16[16,4096]{1,0:T(8,128)(2,1)S(1)} %get-tuple-element.44), kind=kOutput, calls=%fused_computation.69 | convolution fusion | flops 268959744 | bytes 8781824 | tf_op jit(solution)/shard_map/dot_general | solution.py:51
  108.7 0.7 broadcast_in_dim.17
  109.4 5.9 %all-to-all-start.5 = ((f32[32,16,128]{2,1,0:T(8,128)}), f32[32,16,128]{2,1,0:T(8,128)S(1)}, u32[]{:S(2)}, u32[]{:S(2)}) async-start(f32[32,16,128]{2,1,0:T(8,128)} %broadcast_in_dim.17), calls=%async_computation.5 | async-start | bytes 524288 | tf_op jit(solution)/shard_map/all_to_all | solution.py:20
  115.3 5.7 %fusion.8 = f32[16,1024]{1,0:T(8,128)S(1)} fusion(f32[16,1024]{1,0:T(8,128)S(1)} %copy-done.1, bf16[16,4096]{1,0:T(8,128)(2,1)S(1)} %get-tuple-element.44, bf16[1024,4096]{1,0:T(8,128)(2,1)} %get-tuple-element.18, f32[32,1024]{1,0:T(8,128)S(1)} %fusion.29, f32[48,1024]{1,0:T(8,128)S(1)} %fusion.57), kind=kOutput, calls=%fused_computation.19 | convolution fusion | flops 134332416 | bytes 8978432 | tf_op jit(solution)/shard_map/dot_general | solution.py:52
  121.0 4.3 %all-to-all-done.5 = f32[32,16,128]{2,1,0:T(8,128)S(1)} async-done(((f32[32,16,128]{2,1,0:T(8,128)}), f32[32,16,128]{2,1,0:T(8,128)S(1)}, u32[]{:S(2)}, u32[]{:S(2)}) %all-to-all-start.5) | async-done | bytes 262176 | tf_op jit(solution)/shard_map/all_to_all | solution.py:20
  125.6 0.2 copy.67
  125.8 0.5 fusion.47
  126.3 0.7 add_add_fusion
  127.0 6.0 %fusion.33 = f32[32,1024]{1,0:T(8,128)S(1)} fusion(bf16[1024,4096]{1,0:T(8,128)(2,1)} %get-tuple-element.22, bf16[16,4096]{1,0:T(8,128)(2,1)S(1)} %get-tuple-element.41, bf16[16,4096]{1,0:T(8,128)(2,1)S(1)} %get-tuple-element.42), kind=kOutput, calls=%fused_computation.73 | convolution fusion | flops 268959744 | bytes 8781824 | tf_op jit(solution)/shard_map/dot_general | solution.py:51
  132.9 6.3 %fusion.6 = f32[16,1024]{1,0:T(8,128)} fusion(f32[16,1024]{1,0:T(8,128)S(1)} %fusion.8, bf16[16,4096]{1,0:T(8,128)(2,1)S(1)} %get-tuple-element.42, bf16[1024,4096]{1,0:T(8,128)(2,1)} %get-tuple-element.23, f32[32,1024]{1,0:T(8,128)S(1)} %fusion.33, f32[48,1024]{1,0:T(8,128)S(1)} %fusion.47), kind=kOutput, calls=%fused_computation.16 | convolution fusion | flops 134332416 | bytes 8978432 | tf_op jit(solution)/shard_map/dot_general | solution.py:52
  (67 shorter events, 2.2 us)
Async XLA Ops:
  9.0 26.9 %all-to-all-start = ((f32[32,48,128]{2,1,0:T(8,128)}), f32[32,48,128]{2,1,0:T(8,128)S(1)}, u32[]{:S(2)}, u32[]{:S(2)}) async-start(f32[32,48,128]{2,1,0:T(8,128)} %broadcast_in_dim.12), calls=%async_computation | async-start | bytes 1572864 | tf_op jit(solution)/shard_map/all_to_all | solution.py:20
  25.4 10.6 %copy-start.4 = (bf16[96,1024]{1,0:T(8,128)(2,1)}, bf16[96,1024]{1,0:T(8,128)(2,1)S(1)}, u32[]{:S(2)}) copy-start(bf16[96,1024]{1,0:T(8,128)(2,1)S(1)} %constant_dynamic-update-slice_fusion.13) | copy-start | bytes 589828
  36.1 23.4 %copy-start.5 = (bf16[96,1024]{1,0:T(8,128)(2,1)S(1)}, bf16[96,1024]{1,0:T(8,128)(2,1)}, u32[]{:S(2)}) copy-start(bf16[96,1024]{1,0:T(8,128)(2,1)} %copy-done.4) | copy-start | bytes 589828
  47.0 8.9 %all-to-all-start.1 = ((f32[8,16,128]{2,1,0:T(8,128)}), f32[8,16,128]{2,1,0:T(8,128)S(1)}, u32[]{:S(2)}, u32[]{:S(2)}) async-start(f32[8,16,128]{2,1,0:T(8,128)} %bitcast_bitcast_fusion.1), calls=%async_computation.1 | async-start | bytes 131072 | tf_op jit(solution)/shard_map/all_to_all | solution.py:126
  51.0 0.9 copy-start.3
  56.6 13.1 %all-to-all-start.2 = ((f32[32,16,128]{2,1,0:T(8,128)}), f32[32,16,128]{2,1,0:T(8,128)S(1)}, u32[]{:S(2)}, u32[]{:S(2)}) async-start(f32[32,16,128]{2,1,0:T(8,128)} %broadcast_in_dim.14), calls=%async_computation.2 | async-start | bytes 524288 | tf_op jit(solution)/shard_map/all_to_all | solution.py:20
  59.5 12.6 %copy-start = (f32[16,1024]{1,0:T(8,128)S(1)}, f32[16,1024]{1,0:T(8,128)}, u32[]{:S(2)}) copy-start(f32[16,1024]{1,0:T(8,128)} %param.6) | copy-start | bytes 196612
  73.0 15.4 %all-to-all-start.3 = ((f32[32,16,128]{2,1,0:T(8,128)}), f32[32,16,128]{2,1,0:T(8,128)S(1)}, u32[]{:S(2)}, u32[]{:S(2)}) async-start(f32[32,16,128]{2,1,0:T(8,128)} %broadcast_in_dim.15), calls=%async_computation.3 | async-start | bytes 524288 | tf_op jit(solution)/shard_map/all_to_all | solution.py:20
  98.6 16.7 %copy-start.1 = (f32[16,1024]{1,0:T(8,128)S(1)}, f32[16,1024]{1,0:T(8,128)}, u32[]{:S(2)}) copy-start(f32[16,1024]{1,0:T(8,128)} %param.7) | copy-start | bytes 196612
  99.3 9.4 %all-to-all-start.4 = ((f32[8,16,128]{2,1,0:T(8,128)}), f32[8,16,128]{2,1,0:T(8,128)S(1)}, u32[]{:S(2)}, u32[]{:S(2)}) async-start(f32[8,16,128]{2,1,0:T(8,128)} %bitcast_bitcast_fusion), calls=%async_computation.4 | async-start | bytes 131072 | tf_op jit(solution)/shard_map/all_to_all | solution.py:126
  102.7 23.6 %copy-start.2 = (f32[16,1024]{1,0:T(8,128)S(1)}, f32[16,1024]{1,0:T(8,128)}, u32[]{:S(2)}) copy-start(f32[16,1024]{1,0:T(8,128)} %param.8) | copy-start | bytes 196612
  109.4 15.8 %all-to-all-start.5 = ((f32[32,16,128]{2,1,0:T(8,128)}), f32[32,16,128]{2,1,0:T(8,128)S(1)}, u32[]{:S(2)}, u32[]{:S(2)}) async-start(f32[32,16,128]{2,1,0:T(8,128)} %broadcast_in_dim.17), calls=%async_computation.5 | async-start | bytes 524288 | tf_op jit(solution)/shard_map/all_to_all | solution.py:20

commit v14 on v13

--- a/solution.py
+++ b/solution.py
@@ -71,7 +71,7 @@
     o_ref[...] = (both[:rows] + both[rows:]) + low
 
 
-def solve_rows(inverse, slot, block_res, tile=128):
+def solve_rows(inverse, slot, block_res, tile=512):
     _, n, width = inverse.shape
     rows = block_res.shape[0]
     r1f = lax.reduce_precision(block_res, exponent_bits=8, mantissa_bits=7)

time: 141 us -> 136 us (0.965)
  Pallas kernels: 20.4 us -> 16.4 us
    pallas_call x2, Pallas kernels: 20.4 us -> 16.4 us  [solve_rows(): pl.pallas_call(solve_kernel, grid_spec=grid_spec, out_shape=jax.ShapeDtyp...]
  transfers between devices with their start and end apart: 6 -> 6, of which waited for: 5 -> 5; matrix products, arithmetic and copies ran while one was open for 26% -> 27% of each run, Pallas kernels for 0% -> 0%
where the time goes in v14:
time: 136 us; the launch traced here: 135 us
  matrix products  45.7 us (34%)
  starting transfers between devices  28.6 us (21%)
  waiting for transfers between devices  20.3 us (15%)
  Pallas kernels  16.4 us (12%)
  other arithmetic  11.4 us (8%)
  local copies, waits for them, and re-layouts  7.75 us (6%)
  between operations  5 us (4%)
    all_to_all x4, starting transfers between devices, gather_all(): return lax.all_to_all(sent, ALL, 0, 0, tiled=True)  21.4 us
    dot_general x3, matrix products, kern(): lax.dot_general(left, right, (((0,), (0,)), ((), ())), preferred_element_...  18.7 us
    pallas_call x2, Pallas kernels, solve_rows(): pl.pallas_call(solve_kernel, grid_spec=grid_spec, out_shape=jax.ShapeDtyp...  16.4 us
    all_to_all x4, waiting for transfers between devices, gather_all(): return lax.all_to_all(sent, ALL, 0, 0, tiled=True)  16.4 us
    dot_general x3, matrix products, apply_kernel(): lax.dot_general(jnp.concatenate([d1, d2], axis=0), k1, dims, preferred_el...  12.4 us
    dot_general x3, matrix products, apply_kernel(): low = lax.dot_general(d1, k2, dims, preferred_element_type=jnp.float32)  12.4 us
    all_to_all x2, starting transfers between devices, distribute(): scattered = lax.all_to_all(pieces, 'grp', 0, 0, tiled=True)  7.19 us
    unnamed x26, other arithmetic  4.69 us
  transfers between devices with their start and end apart: 6, of which 5 were waited for; matrix products, arithmetic and copies ran while one was open for 27% of the time, Pallas kernels for 0%

profile of v14, /device:TPU:0, one launch (start us, length us, event | category | flops | bytes accessed | tf_op | source)
XLA Modules:
  0.0 135.2 jit_solution(9102116099223310343)
XLA Ops:
  0.6 1.3 fusion.72
  1.9 2.0 %convert_bitcast_fusion.1 = (s32[8,128]{1,0:T(8,128)S(1)}, pred[1024]{0:T(1024)(128)(4,1)S(1)}, s32[8,128]{1,0:T(8,128)S(1)}, pred[1024]{0:T(1024)(128)(4,1)S(1)}) fusion(s32[1024]{0:T(1024)} %param.9, s32[]{:T(128)} %bitcast, s32[]{:T(128)} %bitcast.3), kind=kLoop, calls=%fused_computation.179 | loop fusion | flops 4096 | bytes 14344 | tf_op jit(solution)/shard_map/convert
  3.9 0.3 reduce-window.16
  4.5 0.3 reduce-window.24
  5.1 0.8 constant_dynamic-update-slice_fusion.1
  5.9 0.9 multiply_reduce_fusion.3
  6.8 0.9 fusion.16
  7.8 0.3 fusion.12
  8.1 0.9 broadcast_in_dim.12
  9.0 7.3 %all-to-all-start = ((f32[32,48,128]{2,1,0:T(8,128)}), f32[32,48,128]{2,1,0:T(8,128)S(1)}, u32[]{:S(2)}, u32[]{:S(2)}) async-start(f32[32,48,128]{2,1,0:T(8,128)} %broadcast_in_dim.12), calls=%async_computation | async-start | bytes 1572864 | tf_op jit(solution)/shard_map/all_to_all | solution.py:20
  20.3 0.8 constant_dynamic-update-slice_fusion.18
  21.2 0.8 constant_dynamic-update-slice_fusion.17
  22.0 0.8 constant_dynamic-update-slice_fusion.16
  22.9 0.8 constant_dynamic-update-slice_fusion.15
  23.7 0.9 constant_dynamic-update-slice_fusion.14
  24.6 0.9 constant_dynamic-update-slice_fusion.13
  25.4 10.5 %all-to-all-done = f32[32,48,128]{2,1,0:T(8,128)S(1)} async-done(((f32[32,48,128]{2,1,0:T(8,128)}), f32[32,48,128]{2,1,0:T(8,128)S(1)}, u32[]{:S(2)}, u32[]{:S(2)}) %all-to-all-start) | async-done | bytes 786464 | tf_op jit(solution)/shard_map/all_to_all | solution.py:20
  36.1 8.2 %shard_map.77 = f32[16,1024]{1,0:T(8,128)S(1)} custom-call(s32[1]{0:T(128)} %constant.64.clone.1.slot_ref, f32[1,1024,4096]{2,1,0:T(8,128)} %inv_ref.3, bf16[32,4096]{1,0:T(8,128)(2,1)S(1)} %pad_maximum_fusion.rcat_ref, bf16[16,4096]{1,0:T(8,128)(2,1)S(1)} %get-tuple-element.52.r1_ref), custom_call_target="tpu_custom_call" | custom-call | flops 402653184 | bytes 16777216 | tf_op jit(solution)/shard_map/pallas_call | solution.py:92
  44.4 0.6 bitcast_bitcast_fusion.1
  45.0 3.8 %all-to-all-start.1 = ((f32[8,16,128]{2,1,0:T(8,128)}), f32[8,16,128]{2,1,0:T(8,128)S(1)}, u32[]{:S(2)}, u32[]{:S(2)}) async-start(f32[8,16,128]{2,1,0:T(8,128)} %bitcast_bitcast_fusion.1), calls=%async_computation.1 | async-start | bytes 131072 | tf_op jit(solution)/shard_map/all_to_all | solution.py:126
  49.1 0.8 fusion.4
  50.0 3.9 %all-to-all-done.1 = f32[8,16,128]{2,1,0:T(8,128)S(1)} async-done(((f32[8,16,128]{2,1,0:T(8,128)}), f32[8,16,128]{2,1,0:T(8,128)S(1)}, u32[]{:S(2)}, u32[]{:S(2)}) %all-to-all-start.1) | async-done | bytes 65568 | tf_op jit(solution)/shard_map/all_to_all | solution.py:126
  53.9 0.7 broadcast_in_dim.14
  54.6 2.9 %all-to-all-start.2 = ((f32[32,16,128]{2,1,0:T(8,128)}), f32[32,16,128]{2,1,0:T(8,128)S(1)}, u32[]{:S(2)}, u32[]{:S(2)}) async-start(f32[32,16,128]{2,1,0:T(8,128)} %broadcast_in_dim.14), calls=%async_computation.2 | async-start | bytes 524288 | tf_op jit(solution)/shard_map/all_to_all | solution.py:20
  57.5 9.5 %fusion = (bf16[1024,4096]{1,0:T(8,128)(2,1)}, bf16[1024,4096]{1,0:T(8,128)(2,1)}) fusion(f32[4096]{0:T(1024)S(1)} %bitcast.125, f32[1024]{0:T(1024)S(1)} %get-tuple-element.57, bf16[96,1024]{1,0:T(8,128)(2,1)S(1)} %copy-done.5, bf16[96,4096]{1,0:T(8,128)(2,1)} %copy-done.3), kind=kOutput, calls=%fused_computation.4 | convolution fusion | flops 834666496 | bytes 17780736 | tf_op jit(solution)/shard_map/dot_general | solution.py:38
  67.1 0.7 all-to-all-done.2
  68.0 0.2 copy.68
  68.2 1.0 fusion.9
  69.3 0.5 fusion.25
  69.7 0.4 fusion.11
  70.2 0.7 broadcast_in_dim.15
  71.0 5.4 %all-to-all-start.3 = ((f32[32,16,128]{2,1,0:T(8,128)}), f32[32,16,128]{2,1,0:T(8,128)S(1)}, u32[]{:S(2)}, u32[]{:S(2)}) async-start(f32[32,16,128]{2,1,0:T(8,128)} %broadcast_in_dim.15), calls=%async_computation.3 | async-start | bytes 524288 | tf_op jit(solution)/shard_map/all_to_all | solution.py:20
  76.6 8.4 %fusion.1 = (bf16[1024,4096]{1,0:T(8,128)(2,1)}, bf16[1024,4096]{1,0:T(8,128)(2,1)}) fusion(f32[4096]{0:T(1024)S(1)} %multiply_reduce_fusion, f32[1024]{0:T(1024)S(1)} %multiply_reduce_fusion.2, bf16[96,1024]{1,0:T(8,128)(2,1)S(1)} %constant_dynamic-update-slice_fusion.19, bf16[96,4096]{1,0:T(8,128)(2,1)S(1)} %constant_dynamic-update-slice_fusion.25), kind=kOutput, calls=%fused_computation.5 | convolution fusion | flops 834666496 | bytes 17780736 | tf_op jit(solution)/shard_map/dot_general | solution.py:38
  85.0 0.5 fusion.57
  85.5 0.9 all-to-all-done.3
  86.4 8.2 %shard_map.78 = f32[16,1024]{1,0:T(8,128)S(1)} custom-call(s32[1]{0:T(128)} %constant.64.clone.1.slot_ref, f32[1,1024,4096]{2,1,0:T(8,128)} %inv_ref.3, bf16[32,4096]{1,0:T(8,128)(2,1)S(1)} %pad_maximum_fusion.1.rcat_ref, bf16[16,4096]{1,0:T(8,128)(2,1)S(1)} %get-tuple-element.45.r1_ref), custom_call_target="tpu_custom_call" | custom-call | flops 402653184 | bytes 16777216 | tf_op jit(solution)/shard_map/pallas_call | solution.py:92
  94.7 0.6 bitcast_bitcast_fusion
  95.3 3.4 %all-to-all-start.4 = ((f32[8,16,128]{2,1,0:T(8,128)}), f32[8,16,128]{2,1,0:T(8,128)S(1)}, u32[]{:S(2)}, u32[]{:S(2)}) async-start(f32[8,16,128]{2,1,0:T(8,128)} %bitcast_bitcast_fusion), calls=%async_computation.4 | async-start | bytes 131072 | tf_op jit(solution)/shard_map/all_to_all | solution.py:126
  98.7 6.0 %fusion.29 = f32[32,1024]{1,0:T(8,128)S(1)} fusion(bf16[1024,4096]{1,0:T(8,128)(2,1)} %get-tuple-element.17, bf16[16,4096]{1,0:T(8,128)(2,1)S(1)} %get-tuple-element.43, bf16[16,4096]{1,0:T(8,128)(2,1)S(1)} %get-tuple-element.44), kind=kOutput, calls=%fused_computation.69 | convolution fusion | flops 268959744 | bytes 8781824 | tf_op jit(solution)/shard_map/dot_general | solution.py:51
  104.7 0.7 broadcast_in_dim.17
  105.5 5.9 %all-to-all-start.5 = ((f32[32,16,128]{2,1,0:T(8,128)}), f32[32,16,128]{2,1,0:T(8,128)S(1)}, u32[]{:S(2)}, u32[]{:S(2)}) async-start(f32[32,16,128]{2,1,0:T(8,128)} %broadcast_in_dim.17), calls=%async_computation.5 | async-start | bytes 524288 | tf_op jit(solution)/shard_map/all_to_all | solution.py:20
  111.3 5.7 %fusion.8 = f32[16,1024]{1,0:T(8,128)S(1)} fusion(f32[16,1024]{1,0:T(8,128)S(1)} %copy-done.1, bf16[16,4096]{1,0:T(8,128)(2,1)S(1)} %get-tuple-element.44, bf16[1024,4096]{1,0:T(8,128)(2,1)} %get-tuple-element.18, f32[32,1024]{1,0:T(8,128)S(1)} %fusion.29, f32[48,1024]{1,0:T(8,128)S(1)} %fusion.57), kind=kOutput, calls=%fused_computation.19 | convolution fusion | flops 134332416 | bytes 8978432 | tf_op jit(solution)/shard_map/dot_general | solution.py:52
  117.0 4.3 %all-to-all-done.5 = f32[32,16,128]{2,1,0:T(8,128)S(1)} async-done(((f32[32,16,128]{2,1,0:T(8,128)}), f32[32,16,128]{2,1,0:T(8,128)S(1)}, u32[]{:S(2)}, u32[]{:S(2)}) %all-to-all-start.5) | async-done | bytes 262176 | tf_op jit(solution)/shard_map/all_to_all | solution.py:20
  121.6 0.2 copy.67
  121.8 0.5 fusion.47
  122.3 0.7 add_add_fusion
  123.0 6.0 %fusion.33 = f32[32,1024]{1,0:T(8,128)S(1)} fusion(bf16[1024,4096]{1,0:T(8,128)(2,1)} %get-tuple-element.22, bf16[16,4096]{1,0:T(8,128)(2,1)S(1)} %get-tuple-element.41, bf16[16,4096]{1,0:T(8,128)(2,1)S(1)} %get-tuple-element.42), kind=kOutput, calls=%fused_computation.73 | convolution fusion | flops 268959744 | bytes 8781824 | tf_op jit(solution)/shard_map/dot_general | solution.py:51
  128.9 6.3 %fusion.6 = f32[16,1024]{1,0:T(8,128)} fusion(f32[16,1024]{1,0:T(8,128)S(1)} %fusion.8, bf16[16,4096]{1,0:T(8,128)(2,1)S(1)} %get-tuple-element.42, bf16[1024,4096]{1,0:T(8,128)(2,1)} %get-tuple-element.23, f32[32,1024]{1,0:T(8,128)S(1)} %fusion.33, f32[48,1024]{1,0:T(8,128)S(1)} %fusion.47), kind=kOutput, calls=%fused_computation.16 | convolution fusion | flops 134332416 | bytes 8978432 | tf_op jit(solution)/shard_map/dot_general | solution.py:52
  (67 shorter events, 2.2 us)
Async XLA Ops:
  9.0 26.9 %all-to-all-start = ((f32[32,48,128]{2,1,0:T(8,128)}), f32[32,48,128]{2,1,0:T(8,128)S(1)}, u32[]{:S(2)}, u32[]{:S(2)}) async-start(f32[32,48,128]{2,1,0:T(8,128)} %broadcast_in_dim.12), calls=%async_computation | async-start | bytes 1572864 | tf_op jit(solution)/shard_map/all_to_all | solution.py:20
  25.4 10.6 %copy-start.4 = (bf16[96,1024]{1,0:T(8,128)(2,1)}, bf16[96,1024]{1,0:T(8,128)(2,1)S(1)}, u32[]{:S(2)}) copy-start(bf16[96,1024]{1,0:T(8,128)(2,1)S(1)} %constant_dynamic-update-slice_fusion.13) | copy-start | bytes 589828
  36.1 21.4 %copy-start.5 = (bf16[96,1024]{1,0:T(8,128)(2,1)S(1)}, bf16[96,1024]{1,0:T(8,128)(2,1)}, u32[]{:S(2)}) copy-start(bf16[96,1024]{1,0:T(8,128)(2,1)} %copy-done.4) | copy-start | bytes 589828
  45.0 8.9 %all-to-all-start.1 = ((f32[8,16,128]{2,1,0:T(8,128)}), f32[8,16,128]{2,1,0:T(8,128)S(1)}, u32[]{:S(2)}, u32[]{:S(2)}) async-start(f32[8,16,128]{2,1,0:T(8,128)} %bitcast_bitcast_fusion.1), calls=%async_computation.1 | async-start | bytes 131072 | tf_op jit(solution)/shard_map/all_to_all | solution.py:126
  49.0 0.9 copy-start.3
  54.6 13.1 %all-to-all-start.2 = ((f32[32,16,128]{2,1,0:T(8,128)}), f32[32,16,128]{2,1,0:T(8,128)S(1)}, u32[]{:S(2)}, u32[]{:S(2)}) async-start(f32[32,16,128]{2,1,0:T(8,128)} %broadcast_in_dim.14), calls=%async_computation.2 | async-start | bytes 524288 | tf_op jit(solution)/shard_map/all_to_all | solution.py:20
  57.5 12.6 %copy-start = (f32[16,1024]{1,0:T(8,128)S(1)}, f32[16,1024]{1,0:T(8,128)}, u32[]{:S(2)}) copy-start(f32[16,1024]{1,0:T(8,128)} %param.6) | copy-start | bytes 196612
  71.0 15.4 %all-to-all-start.3 = ((f32[32,16,128]{2,1,0:T(8,128)}), f32[32,16,128]{2,1,0:T(8,128)S(1)}, u32[]{:S(2)}, u32[]{:S(2)}) async-start(f32[32,16,128]{2,1,0:T(8,128)} %broadcast_in_dim.15), calls=%async_computation.3 | async-start | bytes 524288 | tf_op jit(solution)/shard_map/all_to_all | solution.py:20
  94.6 16.7 %copy-start.1 = (f32[16,1024]{1,0:T(8,128)S(1)}, f32[16,1024]{1,0:T(8,128)}, u32[]{:S(2)}) copy-start(f32[16,1024]{1,0:T(8,128)} %param.7) | copy-start | bytes 196612
  95.3 9.4 %all-to-all-start.4 = ((f32[8,16,128]{2,1,0:T(8,128)}), f32[8,16,128]{2,1,0:T(8,128)S(1)}, u32[]{:S(2)}, u32[]{:S(2)}) async-start(f32[8,16,128]{2,1,0:T(8,128)} %bitcast_bitcast_fusion), calls=%async_computation.4 | async-start | bytes 131072 | tf_op jit(solution)/shard_map/all_to_all | solution.py:126
  98.7 23.6 %copy-start.2 = (f32[16,1024]{1,0:T(8,128)S(1)}, f32[16,1024]{1,0:T(8,128)}, u32[]{:S(2)}) copy-start(f32[16,1024]{1,0:T(8,128)} %param.8) | copy-start | bytes 196612
  105.5 15.9 %all-to-all-start.5 = ((f32[32,16,128]{2,1,0:T(8,128)}), f32[32,16,128]{2,1,0:T(8,128)S(1)}, u32[]{:S(2)}, u32[]{:S(2)}) async-start(f32[32,16,128]{2,1,0:T(8,128)} %broadcast_in_dim.17), calls=%async_computation.5 | async-start | bytes 524288 | tf_op jit(solution)/shard_map/all_to_all | solution.py:20

commit v15 on v14

--- a/solution.py
+++ b/solution.py
@@ -37,20 +37,11 @@
     right = jnp.concatenate([v1, v2, v1, v3, v1, v2], axis=0)
     cross2 = lax.dot_general(left, right, (((0,), (0,)), ((), ())), preferred_element_type=jnp.float32)
     kernel = jnp.exp(-kernel_scale * ((nu[:, None] + nv[None, :]) + cross2))
-    k1 = lax.reduce_precision(kernel, exponent_bits=8, mantissa_bits=7)
-    return lax.optimization_barrier((k1.astype(jnp.bfloat16), (kernel - k1).astype(jnp.bfloat16)))
+    return lax.optimization_barrier(kernel)
 
 
 def apply_kernel(delta, kernel):
-    k1, k2 = kernel
-    d1f = lax.reduce_precision(delta, exponent_bits=8, mantissa_bits=7)
-    d1 = d1f.astype(jnp.bfloat16)
-    d2 = (delta - d1f).astype(jnp.bfloat16)
-    rows = delta.shape[0]
-    dims = (((1,), (1,)), ((), ()))
-    both = lax.dot_general(jnp.concatenate([d1, d2], axis=0), k1, dims, preferred_element_type=jnp.float32)
-    low = lax.dot_general(d1, k2, dims, preferred_element_type=jnp.float32)
-    return (both[:rows] + both[rows:]) + low
+    return lax.dot_general(delta, kernel, (((1,), (1,)), ((), ())), precision=HIGH)
 
 
 def exact_dot(x, onehot, dims):

time: 136 us -> 132 us (0.971)
  matrix products: 45.7 us -> 41.5 us
  other arithmetic: 11.4 us -> 15.2 us
  starting transfers between devices: 28.6 us -> 24.9 us
    all_to_all x4, waiting for transfers between devices: 16.4 us -> 10.8 us  [gather_all(): return lax.all_to_all(sent, ALL, 0, 0, tiled=True)]
    all_to_all x2, waiting for transfers between devices: 3.92 us -> 8.87 us  [distribute(): scattered = lax.all_to_all(pieces, 'grp', 0, 0, tiled=True)]
    all_to_all x4, starting transfers between devices: 21.4 us -> 17.6 us  [gather_all(): return lax.all_to_all(sent, ALL, 0, 0, tiled=True)]
    unnamed x26, other arithmetic: 4.69 us -> 7.74 us
    dot_general x6 -> x3, matrix products: 24.8 us -> 21.9 us  [apply_kernel(): lax.dot_general(delta, kernel, (((1,), (1,)), ((), ())), precision=HIGH)]
    dot_general x3, matrix products: 18.7 us -> 16.6 us  [kern(): lax.dot_general(left, right, (((0,), (0,)), ((), ())), preferred_element_...]
  transfers between devices with their start and end apart: 6 -> 6, of which waited for: 5 -> 5; matrix products, arithmetic and copies ran while one was open for 27% -> 28% of each run, Pallas kernels for 0% -> 0%
where the time goes in v15:
time: 132 us; the launch traced here: 131 us
  matrix products  41.5 us (31%)
  starting transfers between devices  24.9 us (19%)
  waiting for transfers between devices  19.7 us (15%)
  Pallas kernels  16.4 us (12%)
  other arithmetic  15.2 us (12%)
  local copies, waits for them, and re-layouts  8.35 us (6%)
  between operations  4.98 us (4%)
    dot_general x3, matrix products, apply_kernel(): lax.dot_general(delta, kernel, (((1,), (1,)), ((), ())), precision=HIGH)  21.9 us
    all_to_all x4, starting transfers between devices, gather_all(): return lax.all_to_all(sent, ALL, 0, 0, tiled=True)  17.6 us
    dot_general x3, matrix products, kern(): lax.dot_general(left, right, (((0,), (0,)), ((), ())), preferred_element_...  16.6 us
    pallas_call x2, Pallas kernels, solve_rows(): pl.pallas_call(solve_kernel, grid_spec=grid_spec, out_shape=jax.ShapeDtyp...  16.4 us
    all_to_all x4, waiting for transfers between devices, gather_all(): return lax.all_to_all(sent, ALL, 0, 0, tiled=True)  10.8 us
    all_to_all x2, waiting for transfers between devices, distribute(): scattered = lax.all_to_all(pieces, 'grp', 0, 0, tiled=True)  8.87 us
    unnamed x26, other arithmetic  7.74 us
    all_to_all x2, starting transfers between devices, distribute(): scattered = lax.all_to_all(pieces, 'grp', 0, 0, tiled=True)  7.32 us
  transfers between devices with their start and end apart: 6, of which 5 were waited for; matrix products, arithmetic and copies ran while one was open for 28% of the time, Pallas kernels for 0%

profile of v15, /device:TPU:0, one launch (start us, length us, event | category | flops | bytes accessed | tf_op | source)
XLA Modules:
  0.0 131.1 jit_solution(353772309925778446)
XLA Ops:
  0.6 1.3 %fusion.48 = (s32[1]{0:T(128)}, s32[1]{0:T(128)}) fusion(s32[2]{0:T(128)} %param.10), kind=kLoop, calls=%fused_computation.153 | loop fusion | bytes 16 | tf_op jit(solution)/shard_map/slice | solution.py:126
  2.0 2.0 %convert_bitcast_fusion.1 = (s32[8,128]{1,0:T(8,128)S(1)}, pred[1024]{0:T(1024)(128)(4,1)S(1)}, s32[8,128]{1,0:T(8,128)S(1)}, pred[1024]{0:T(1024)(128)(4,1)S(1)}) fusion(s32[1024]{0:T(1024)} %param.9, s32[]{:T(128)} %bitcast, s32[]{:T(128)} %bitcast.3), kind=kLoop, calls=%fused_computation.143 | loop fusion | flops 4096 | bytes 14344 | tf_op jit(solution)/shard_map/convert
  3.9 0.3 reduce-window.16
  4.5 0.3 reduce-window.24
  5.1 0.8 constant_dynamic-update-slice_fusion.1
  5.9 0.9 multiply_reduce_fusion.3
  6.8 0.9 fusion.10
  7.8 0.3 fusion.6
  8.1 0.5 multiply_reduce_fusion.4
  8.6 0.9 broadcast_in_dim.12
  9.5 7.3 %all-to-all-start = ((f32[32,48,128]{2,1,0:T(8,128)}), f32[32,48,128]{2,1,0:T(8,128)S(1)}, u32[]{:S(2)}, u32[]{:S(2)}) async-start(f32[32,48,128]{2,1,0:T(8,128)} %broadcast_in_dim.12), calls=%async_computation | async-start | bytes 1572864 | tf_op jit(solution)/shard_map/all_to_all | solution.py:20
  20.8 1.5 %constant_dynamic-update-slice_fusion.18 = bf16[96,1024]{1,0:T(8,128)(2,1)} fusion(f32[16,1024]{1,0:T(8,128)} %param.6), kind=kLoop, calls=%fused_computation.85 | loop fusion | flops 32767 | bytes 98304
  22.2 1.5 %constant_dynamic-update-slice_fusion.17 = bf16[96,1024]{1,0:T(8,128)(2,1)} fusion(bf16[96,1024]{1,0:T(8,128)(2,1)} %constant_dynamic-update-slice_fusion.18, f32[16,1024]{1,0:T(8,128)} %param.6), kind=kLoop, calls=%fused_computation.84 | loop fusion | flops 32768 | bytes 98304
  23.7 1.5 %constant_dynamic-update-slice_fusion.16 = bf16[96,1024]{1,0:T(8,128)(2,1)} fusion(bf16[96,1024]{1,0:T(8,128)(2,1)} %constant_dynamic-update-slice_fusion.17, f32[16,1024]{1,0:T(8,128)} %param.6), kind=kLoop, calls=%fused_computation.83 | loop fusion | flops 65536 | bytes 98304
  25.1 1.4 %constant_dynamic-update-slice_fusion.15 = bf16[96,1024]{1,0:T(8,128)(2,1)} fusion(bf16[96,1024]{1,0:T(8,128)(2,1)} %constant_dynamic-update-slice_fusion.16, f32[16,1024]{1,0:T(8,128)} %param.6), kind=kLoop, calls=%fused_computation.82 | loop fusion | flops 32768 | bytes 98304
  26.6 1.5 %constant_dynamic-update-slice_fusion.14 = bf16[96,1024]{1,0:T(8,128)(2,1)} fusion(bf16[96,1024]{1,0:T(8,128)(2,1)} %constant_dynamic-update-slice_fusion.15, f32[16,1024]{1,0:T(8,128)} %param.6), kind=kLoop, calls=%fused_computation.81 | loop fusion | flops 81920 | bytes 98304
  28.0 1.5 %constant_dynamic-update-slice_fusion.13 = bf16[96,1024]{1,0:T(8,128)(2,1)} fusion(bf16[96,1024]{1,0:T(8,128)(2,1)} %constant_dynamic-update-slice_fusion.14, f32[16,1024]{1,0:T(8,128)} %param.6), kind=kLoop, calls=%fused_computation.80 | loop fusion | flops 65536 | bytes 98304 | tf_op jit(solution)/shard_map/concatenate | solution.py:36
  29.5 6.9 %all-to-all-done = f32[32,48,128]{2,1,0:T(8,128)S(1)} async-done(((f32[32,48,128]{2,1,0:T(8,128)}), f32[32,48,128]{2,1,0:T(8,128)S(1)}, u32[]{:S(2)}, u32[]{:S(2)}) %all-to-all-start) | async-done | bytes 786464 | tf_op jit(solution)/shard_map/all_to_all | solution.py:20
  36.8 8.2 %shard_map.77 = f32[16,1024]{1,0:T(8,128)S(1)} custom-call(s32[1]{0:T(128)} %constant.64.clone.1.slot_ref, f32[1,1024,4096]{2,1,0:T(8,128)} %inv_ref.3, bf16[32,4096]{1,0:T(8,128)(2,1)S(1)} %pad_maximum_fusion.rcat_ref, bf16[16,4096]{1,0:T(8,128)(2,1)S(1)} %get-tuple-element.28.r1_ref), custom_call_target="tpu_custom_call" | custom-call | flops 402653184 | bytes 16777216 | tf_op jit(solution)/shard_map/pallas_call | solution.py:83
  45.0 0.6 bitcast_bitcast_fusion.1
  45.7 4.0 %all-to-all-start.1 = ((f32[8,16,128]{2,1,0:T(8,128)}), f32[8,16,128]{2,1,0:T(8,128)}, u32[]{:S(2)}, u32[]{:S(2)}) async-start(f32[8,16,128]{2,1,0:T(8,128)} %bitcast_bitcast_fusion.1), calls=%async_computation.1 | async-start | bytes 131072 | tf_op jit(solution)/shard_map/all_to_all | solution.py:117
  49.6 0.6 fusion.1
  50.2 4.4 %all-to-all-done.1 = f32[8,16,128]{2,1,0:T(8,128)} async-done(((f32[8,16,128]{2,1,0:T(8,128)}), f32[8,16,128]{2,1,0:T(8,128)}, u32[]{:S(2)}, u32[]{:S(2)}) %all-to-all-start.1) | async-done | bytes 65568 | tf_op jit(solution)/shard_map/all_to_all | solution.py:117
  54.7 0.7 dynamic-slice_bitcast_fusion.1
  55.4 0.7 broadcast_in_dim.14
  56.1 3.5 %all-to-all-start.2 = ((f32[32,16,128]{2,1,0:T(8,128)}), f32[32,16,128]{2,1,0:T(8,128)S(1)}, u32[]{:S(2)}, u32[]{:S(2)}) async-start(f32[32,16,128]{2,1,0:T(8,128)} %broadcast_in_dim.14), calls=%async_computation.2 | async-start | bytes 524288 | tf_op jit(solution)/shard_map/all_to_all | solution.py:20
  59.6 8.4 %multiply_exponential_fusion.1 = f32[1024,4096]{1,0:T(8,128)} fusion(bf16[96,1024]{1,0:T(8,128)(2,1)} %constant_dynamic-update-slice_fusion.13, bf16[96,4096]{1,0:T(8,128)(2,1)S(1)} %constant_dynamic-update-slice_fusion.8, f32[4096]{0:T(1024)S(1)} %bitcast.114, f32[1024]{0:T(1024)S(1)} %get-tuple-element.33), kind=kOutput, calls=%fused_computation.1 | convolution fusion | flops 817889280 | bytes 17780736 | tf_op jit(solution)/shard_map/dot_general | solution.py:38
  68.0 1.8 %all-to-all-done.2 = f32[32,16,128]{2,1,0:T(8,128)S(1)} async-done(((f32[32,16,128]{2,1,0:T(8,128)}), f32[32,16,128]{2,1,0:T(8,128)S(1)}, u32[]{:S(2)}, u32[]{:S(2)}) %all-to-all-start.2) | async-done | bytes 262176 | tf_op jit(solution)/shard_map/all_to_all | solution.py:20
  69.9 0.2 copy.62
  70.1 1.7 %fusion.4 = f32[48,128]{1,0:T(8,128)S(1)} fusion(bf16[16,128]{1,0:T(8,128)(2,1)S(1)} %get-tuple-element.27, bf16[16,128]{1,0:T(8,128)(2,1)S(1)} %get-tuple-element.26, bf16[16,128]{1,0:T(8,128)(2,1)S(1)} %get-tuple-element.25, s32[1024]{0:T(1024)S(1)} %add_bitcast_fusion, pred[1024]{0:T(1024)(128)(4,1)} %copy-done.5, s32[1024]{0:T(1024)} %copy-done.3, ...), kind=kOutput, calls=%fused_computation.10 | convolution fusion | flops 35704832 | bytes 47104 | tf_op jit(solution)/shard_map/dot_general | solution.py:50
  71.8 1.0 fusion.5
  73.0 0.7 broadcast_in_dim.15
  73.7 4.3 %all-to-all-start.3 = ((f32[32,16,128]{2,1,0:T(8,128)}), f32[32,16,128]{2,1,0:T(8,128)S(1)}, u32[]{:S(2)}, u32[]{:S(2)}) async-start(f32[32,16,128]{2,1,0:T(8,128)} %broadcast_in_dim.15), calls=%async_computation.3 | async-start | bytes 524288 | tf_op jit(solution)/shard_map/all_to_all | solution.py:20
  78.3 7.6 %multiply_exponential_fusion = f32[1024,4096]{1,0:T(8,128)} fusion(bf16[96,1024]{1,0:T(8,128)(2,1)S(1)} %constant_dynamic-update-slice_fusion.19, bf16[96,4096]{1,0:T(8,128)(2,1)S(1)} %constant_dynamic-update-slice_fusion.25, f32[4096]{0:T(1024)S(1)} %multiply_reduce_fusion, f32[1024]{0:T(1024)S(1)} %multiply_reduce_fusion.2), kind=kOutput, calls=%fused_computation | convolution fusion | flops 817889280 | bytes 17780736 | tf_op jit(solution)/shard_map/dot_general | solution.py:38
  85.9 2.1 %all-to-all-done.3 = f32[32,16,128]{2,1,0:T(8,128)S(1)} async-done(((f32[32,16,128]{2,1,0:T(8,128)}), f32[32,16,128]{2,1,0:T(8,128)S(1)}, u32[]{:S(2)}, u32[]{:S(2)}) %all-to-all-start.3) | async-done | bytes 262176 | tf_op jit(solution)/shard_map/all_to_all | solution.py:20
  88.1 8.2 %shard_map.78 = f32[16,1024]{1,0:T(8,128)S(1)} custom-call(s32[1]{0:T(128)} %constant.64.clone.1.slot_ref, f32[1,1024,4096]{2,1,0:T(8,128)} %inv_ref.3, bf16[32,4096]{1,0:T(8,128)(2,1)S(1)} %pad_maximum_fusion.1.rcat_ref, bf16[16,4096]{1,0:T(8,128)(2,1)S(1)} %get-tuple-element.23.r1_ref), custom_call_target="tpu_custom_call" | custom-call | flops 402653184 | bytes 16777216 | tf_op jit(solution)/shard_map/pallas_call | solution.py:83
  96.3 0.6 bitcast_bitcast_fusion
  96.9 3.4 %all-to-all-start.4 = ((f32[8,16,128]{2,1,0:T(8,128)}), f32[8,16,128]{2,1,0:T(8,128)S(1)}, u32[]{:S(2)}, u32[]{:S(2)}) async-start(f32[8,16,128]{2,1,0:T(8,128)} %bitcast_bitcast_fusion), calls=%async_computation.4 | async-start | bytes 131072 | tf_op jit(solution)/shard_map/all_to_all | solution.py:117
  100.3 0.5 fusion.36
  100.8 4.4 %all-to-all-done.4 = f32[8,16,128]{2,1,0:T(8,128)S(1)} async-done(((f32[8,16,128]{2,1,0:T(8,128)}), f32[8,16,128]{2,1,0:T(8,128)S(1)}, u32[]{:S(2)}, u32[]{:S(2)}) %all-to-all-start.4) | async-done | bytes 65568 | tf_op jit(solution)/shard_map/all_to_all | solution.py:117
  105.2 0.7 broadcast_in_dim.17
  106.0 2.6 %all-to-all-start.5 = ((f32[32,16,128]{2,1,0:T(8,128)}), f32[32,16,128]{2,1,0:T(8,128)S(1)}, u32[]{:S(2)}, u32[]{:S(2)}) async-start(f32[32,16,128]{2,1,0:T(8,128)} %broadcast_in_dim.17), calls=%async_computation.5 | async-start | bytes 524288 | tf_op jit(solution)/shard_map/all_to_all | solution.py:20
  108.6 10.2 %fusion.3 = f32[16,1024]{1,0:T(8,128)S(1)} fusion(f32[16,1024]{1,0:T(8,128)S(1)} %copy-done.1, f32[16,4096]{1,0:T(8,128)S(1)} %bitcast.109, f32[1024,4096]{1,0:T(8,128)} %multiply_exponential_fusion.1, f32[48,1024]{1,0:T(8,128)S(1)} %fusion.36), kind=kOutput, calls=%fused_computation.8 | convolution fusion | flops 402735104 | bytes 17367040 | tf_op jit(solution)/shard_map/dot_general | solution.py:44
  118.8 0.2 copy.23
  118.9 0.2 copy.61
  119.1 0.5 fusion.26
  119.6 0.7 add_add_fusion
  120.3 10.8 %fusion.2 = f32[16,1024]{1,0:T(8,128)} fusion(f32[16,1024]{1,0:T(8,128)S(1)} %fusion.3, f32[1024,4096]{1,0:T(8,128)} %multiply_exponential_fusion, f32[2,8,32,128]{3,2,1,0:T(8,128)S(1)} %bitcast.105, f32[48,1024]{1,0:T(8,128)S(1)} %fusion.26), kind=kOutput, calls=%fused_computation.6 | convolution fusion | flops 402735104 | bytes 17367040 | tf_op jit(solution)/shard_map/dot_general | solution.py:44
  (69 shorter events, 1.6 us)
Async XLA Ops:
  3.9 5.6 %copy-start.5 = (pred[1024]{0:T(1024)(128)(4,1)}, pred[1024]{0:T(1024)(128)(4,1)S(1)}, u32[]{:S(2)}) copy-start(pred[1024]{0:T(1024)(128)(4,1)S(1)} %get-tuple-element.38) | copy-start | bytes 3076
  3.9 5.6 %copy-start.7 = (pred[1024]{0:T(1024)(128)(4,1)}, pred[1024]{0:T(1024)(128)(4,1)S(1)}, u32[]{:S(2)}) copy-start(pred[1024]{0:T(1024)(128)(4,1)S(1)} %get-tuple-element.13) | copy-start | bytes 3076
  4.5 5.0 %copy-start.3 = (s32[1024]{0:T(1024)}, s32[1024]{0:T(1024)S(1)}, u32[]{:S(2)}) copy-start(s32[1024]{0:T(1024)S(1)} %add_bitcast_fusion.1) | copy-start | bytes 12292
  9.5 26.9 %all-to-all-start = ((f32[32,48,128]{2,1,0:T(8,128)}), f32[32,48,128]{2,1,0:T(8,128)S(1)}, u32[]{:S(2)}, u32[]{:S(2)}) async-start(f32[32,48,128]{2,1,0:T(8,128)} %broadcast_in_dim.12), calls=%async_computation | async-start | bytes 1572864 | tf_op jit(solution)/shard_map/all_to_all | solution.py:20
  36.5 13.1 %copy-start.9 = (f32[128]{0:T(128)S(1)}, f32[128]{0:T(128)}, u32[]{:S(2)}) copy-start(f32[128]{0:T(128)} %get-tuple-element.35) | copy-start | bytes 1540
  45.0 27.9 %copy-start = (f32[16,1024]{1,0:T(8,128)S(1)}, f32[16,1024]{1,0:T(8,128)}, u32[]{:S(2)}) copy-start(f32[16,1024]{1,0:T(8,128)} %param.6) | copy-start | bytes 196612
  45.7 9.0 %all-to-all-start.1 = ((f32[8,16,128]{2,1,0:T(8,128)}), f32[8,16,128]{2,1,0:T(8,128)}, u32[]{:S(2)}, u32[]{:S(2)}) async-start(f32[8,16,128]{2,1,0:T(8,128)} %bitcast_bitcast_fusion.1), calls=%async_computation.1 | async-start | bytes 131072 | tf_op jit(solution)/shard_map/all_to_all | solution.py:117
  56.1 13.7 %all-to-all-start.2 = ((f32[32,16,128]{2,1,0:T(8,128)}), f32[32,16,128]{2,1,0:T(8,128)S(1)}, u32[]{:S(2)}, u32[]{:S(2)}) async-start(f32[32,16,128]{2,1,0:T(8,128)} %broadcast_in_dim.14), calls=%async_computation.2 | async-start | bytes 524288 | tf_op jit(solution)/shard_map/all_to_all | solution.py:20
  73.7 14.3 %all-to-all-start.3 = ((f32[32,16,128]{2,1,0:T(8,128)}), f32[32,16,128]{2,1,0:T(8,128)S(1)}, u32[]{:S(2)}, u32[]{:S(2)}) async-start(f32[32,16,128]{2,1,0:T(8,128)} %broadcast_in_dim.15), calls=%async_computation.3 | async-start | bytes 524288 | tf_op jit(solution)/shard_map/all_to_all | solution.py:20
  78.2 22.0 %copy-start.4 = (s32[1024]{0:T(1024)S(1)}, s32[1024]{0:T(1024)}, u32[]{:S(2)}) copy-start(s32[1024]{0:T(1024)} %copy-done.3) | copy-start | bytes 12292
  78.3 22.0 %copy-start.8 = (pred[1024]{0:T(1024)(128)(4,1)S(1)}, pred[1024]{0:T(1024)(128)(4,1)}, u32[]{:S(2)}) copy-start(pred[1024]{0:T(1024)(128)(4,1)} %copy-done.7) | copy-start | bytes 3076
  78.3 30.3 %copy-start.1 = (f32[16,1024]{1,0:T(8,128)S(1)}, f32[16,1024]{1,0:T(8,128)}, u32[]{:S(2)}) copy-start(f32[16,1024]{1,0:T(8,128)} %param.7) | copy-start | bytes 196612
  88.0 31.1 %copy-start.6 = (pred[1024]{0:T(1024)(128)(4,1)S(1)}, pred[1024]{0:T(1024)(128)(4,1)}, u32[]{:S(2)}) copy-start(pred[1024]{0:T(1024)(128)(4,1)} %copy-done.5) | copy-start | bytes 3076
  88.0 31.6 %copy-start.2 = (f32[16,1024]{1,0:T(8,128)S(1)}, f32[16,1024]{1,0:T(8,128)}, u32[]{:S(2)}) copy-start(f32[16,1024]{1,0:T(8,128)} %param.8) | copy-start | bytes 196612
  96.9 8.3 %all-to-all-start.4 = ((f32[8,16,128]{2,1,0:T(8,128)}), f32[8,16,128]{2,1,0:T(8,128)S(1)}, u32[]{:S(2)}, u32[]{:S(2)}) async-start(f32[8,16,128]{2,1,0:T(8,128)} %bitcast_bitcast_fusion), calls=%async_computation.4 | async-start | bytes 131072 | tf_op jit(solution)/shard_map/all_to_all | solution.py:117
  106.0 12.8 %all-to-all-start.5 = ((f32[32,16,128]{2,1,0:T(8,128)}), f32[32,16,128]{2,1,0:T(8,128)S(1)}, u32[]{:S(2)}, u32[]{:S(2)}) async-start(f32[32,16,128]{2,1,0:T(8,128)} %broadcast_in_dim.17), calls=%async_computation.5 | async-start | bytes 524288 | tf_op jit(solution)/shard_map/all_to_all | solution.py:20

commit v16 on v15

--- a/solution.py
+++ b/solution.py
@@ -153,7 +153,10 @@
     solved1, delta0_late = lax.optimization_barrier((solved1, delta0))
     delta1 = distribute(solved1, block1)
     spread0 = exact_dot(owned0, sel0, (((1,), (1,)), ((), ())))
-    update0 = apply_kernel(delta0_late, kernel0)
+    half = kernel0.shape[0] // 2
+    update0 = jnp.concatenate(
+        [apply_kernel(delta0_late, kernel0[:half]), apply_kernel(delta0_late, kernel0[half:])], axis=1
+    )
     residual = residual - update0 - ridge_weight * spread0
     coef = coef + spread0
 

time: 132 us -> 135 us (1.023)
  matrix products: 41.5 us -> 45.5 us
    dot_general x3 -> x4, matrix products: 21.9 us -> 25.3 us  [apply_kernel(): lax.dot_general(delta, kernel, (((1,), (1,)), ((), ())), precision=HIGH)]
  transfers between devices with their start and end apart: 6 -> 6, of which waited for: 5 -> 5; matrix products, arithmetic and copies ran while one was open for 28% -> 30% of each run, Pallas kernels for 0% -> 0%
where the time goes in v16:
time: 135 us; the launch traced here: 134 us
  matrix products  45.5 us (34%)
  starting transfers between devices  24.9 us (18%)
  waiting for transfers between devices  19.1 us (14%)
  Pallas kernels  16.4 us (12%)
  other arithmetic  15.2 us (11%)
  local copies, waits for them, and re-layouts  8.28 us (6%)
  between operations  4.73 us (4%)
    dot_general x4, matrix products, apply_kernel(): lax.dot_general(delta, kernel, (((1,), (1,)), ((), ())), precision=HIGH)  25.3 us
    all_to_all x4, starting transfers between devices, gather_all(): return lax.all_to_all(sent, ALL, 0, 0, tiled=True)  17.6 us
    dot_general x3, matrix products, kern(): lax.dot_general(left, right, (((0,), (0,)), ((), ())), preferred_element_...  17.2 us
    pallas_call x2, Pallas kernels, solve_rows(): pl.pallas_call(solve_kernel, grid_spec=grid_spec, out_shape=jax.ShapeDtyp...  16.4 us
    all_to_all x4, waiting for transfers between devices, gather_all(): return lax.all_to_all(sent, ALL, 0, 0, tiled=True)  11.1 us
    all_to_all x2, waiting for transfers between devices, distribute(): scattered = lax.all_to_all(pieces, 'grp', 0, 0, tiled=True)  8.01 us
    unnamed x26, other arithmetic  7.71 us
    all_to_all x2, starting transfers between devices, distribute(): scattered = lax.all_to_all(pieces, 'grp', 0, 0, tiled=True)  7.33 us
  transfers between devices with their start and end apart: 6, of which 5 were waited for; matrix products, arithmetic and copies ran while one was open for 30% of the time, Pallas kernels for 0%

profile of v16, /device:TPU:0, one launch (start us, length us, event | category | flops | bytes accessed | tf_op | source)
XLA Modules:
  0.0 134.1 jit_solution(82732099168801771)
XLA Ops:
  0.6 1.3 fusion.52
  1.9 1.9 %convert_bitcast_fusion.1 = (s32[8,128]{1,0:T(8,128)S(1)}, pred[1024]{0:T(1024)(128)(4,1)S(1)}, s32[8,128]{1,0:T(8,128)S(1)}, pred[1024]{0:T(1024)(128)(4,1)S(1)}) fusion(s32[1024]{0:T(1024)} %param.9, s32[]{:T(128)} %bitcast, s32[]{:T(128)} %bitcast.3), kind=kLoop, calls=%fused_computation.147 | loop fusion | flops 4096 | bytes 14344 | tf_op jit(solution)/shard_map/convert
  3.8 0.3 reduce-window.24
  4.4 0.3 reduce-window.16
  5.0 0.9 constant_dynamic-update-slice_fusion.1
  5.8 0.9 multiply_reduce_fusion.3
  6.7 0.9 fusion.13
  7.6 0.3 fusion.9
  7.9 0.6 multiply_reduce_fusion.4
  8.5 0.9 broadcast_in_dim.12
  9.5 7.3 %all-to-all-start = ((f32[32,48,128]{2,1,0:T(8,128)}), f32[32,48,128]{2,1,0:T(8,128)S(1)}, u32[]{:S(2)}, u32[]{:S(2)}) async-start(f32[32,48,128]{2,1,0:T(8,128)} %broadcast_in_dim.12), calls=%async_computation | async-start | bytes 1572864 | tf_op jit(solution)/shard_map/all_to_all | solution.py:20
  20.5 1.4 %constant_dynamic-update-slice_fusion.18 = bf16[96,1024]{1,0:T(8,128)(2,1)} fusion(f32[16,1024]{1,0:T(8,128)} %param.6), kind=kLoop, calls=%fused_computation.87 | loop fusion | flops 32767 | bytes 98304
  21.9 1.4 %constant_dynamic-update-slice_fusion.17 = bf16[96,1024]{1,0:T(8,128)(2,1)} fusion(bf16[96,1024]{1,0:T(8,128)(2,1)} %constant_dynamic-update-slice_fusion.18, f32[16,1024]{1,0:T(8,128)} %param.6), kind=kLoop, calls=%fused_computation.86 | loop fusion | flops 32768 | bytes 98304
  23.4 1.5 %constant_dynamic-update-slice_fusion.16 = bf16[96,1024]{1,0:T(8,128)(2,1)} fusion(bf16[96,1024]{1,0:T(8,128)(2,1)} %constant_dynamic-update-slice_fusion.17, f32[16,1024]{1,0:T(8,128)} %param.6), kind=kLoop, calls=%fused_computation.85 | loop fusion | flops 65536 | bytes 98304
  24.8 1.4 %constant_dynamic-update-slice_fusion.15 = bf16[96,1024]{1,0:T(8,128)(2,1)} fusion(bf16[96,1024]{1,0:T(8,128)(2,1)} %constant_dynamic-update-slice_fusion.16, f32[16,1024]{1,0:T(8,128)} %param.6), kind=kLoop, calls=%fused_computation.84 | loop fusion | flops 32768 | bytes 98304
  26.3 1.4 %constant_dynamic-update-slice_fusion.14 = bf16[96,1024]{1,0:T(8,128)(2,1)} fusion(bf16[96,1024]{1,0:T(8,128)(2,1)} %constant_dynamic-update-slice_fusion.15, f32[16,1024]{1,0:T(8,128)} %param.6), kind=kLoop, calls=%fused_computation.83 | loop fusion | flops 81920 | bytes 98304
  27.7 1.5 %constant_dynamic-update-slice_fusion.13 = bf16[96,1024]{1,0:T(8,128)(2,1)} fusion(bf16[96,1024]{1,0:T(8,128)(2,1)} %constant_dynamic-update-slice_fusion.14, f32[16,1024]{1,0:T(8,128)} %param.6), kind=kLoop, calls=%fused_computation.82 | loop fusion | flops 65536 | bytes 98304 | tf_op jit(solution)/shard_map/concatenate | solution.py:36
  29.2 7.2 %all-to-all-done = f32[32,48,128]{2,1,0:T(8,128)S(1)} async-done(((f32[32,48,128]{2,1,0:T(8,128)}), f32[32,48,128]{2,1,0:T(8,128)S(1)}, u32[]{:S(2)}, u32[]{:S(2)}) %all-to-all-start) | async-done | bytes 786464 | tf_op jit(solution)/shard_map/all_to_all | solution.py:20
  36.6 8.2 %shard_map.77 = f32[16,1024]{1,0:T(8,128)S(1)} custom-call(s32[1]{0:T(128)} %constant.64.clone.1.slot_ref, f32[1,1024,4096]{2,1,0:T(8,128)} %inv_ref.3, bf16[32,4096]{1,0:T(8,128)(2,1)S(1)} %pad_maximum_fusion.rcat_ref, bf16[16,4096]{1,0:T(8,128)(2,1)S(1)} %get-tuple-element.28.r1_ref), custom_call_target="tpu_custom_call" | custom-call | flops 402653184 | bytes 16777216 | tf_op jit(solution)/shard_map/pallas_call | solution.py:83
  44.8 0.6 bitcast_bitcast_fusion.1
  45.4 4.0 %all-to-all-start.1 = ((f32[8,16,128]{2,1,0:T(8,128)}), f32[8,16,128]{2,1,0:T(8,128)}, u32[]{:S(2)}, u32[]{:S(2)}) async-start(f32[8,16,128]{2,1,0:T(8,128)} %bitcast_bitcast_fusion.1), calls=%async_computation.1 | async-start | bytes 131072 | tf_op jit(solution)/shard_map/all_to_all | solution.py:117
  49.6 1.2 fusion.5
  50.8 3.6 %all-to-all-done.1 = f32[8,16,128]{2,1,0:T(8,128)} async-done(((f32[8,16,128]{2,1,0:T(8,128)}), f32[8,16,128]{2,1,0:T(8,128)}, u32[]{:S(2)}, u32[]{:S(2)}) %all-to-all-start.1) | async-done | bytes 65568 | tf_op jit(solution)/shard_map/all_to_all | solution.py:117
  54.4 0.7 dynamic-slice_bitcast_fusion.1
  55.1 0.7 broadcast_in_dim.14
  55.8 3.5 %all-to-all-start.2 = ((f32[32,16,128]{2,1,0:T(8,128)}), f32[32,16,128]{2,1,0:T(8,128)S(1)}, u32[]{:S(2)}, u32[]{:S(2)}) async-start(f32[32,16,128]{2,1,0:T(8,128)} %broadcast_in_dim.14), calls=%async_computation.2 | async-start | bytes 524288 | tf_op jit(solution)/shard_map/all_to_all | solution.py:20
  59.3 8.4 %multiply_exponential_fusion.1 = f32[1024,4096]{1,0:T(8,128)} fusion(bf16[96,1024]{1,0:T(8,128)(2,1)} %constant_dynamic-update-slice_fusion.13, bf16[96,4096]{1,0:T(8,128)(2,1)S(1)} %constant_dynamic-update-slice_fusion.8, f32[4096]{0:T(1024)S(1)} %bitcast.115, f32[1024]{0:T(1024)S(1)} %get-tuple-element.33), kind=kOutput, calls=%fused_computation.1 | convolution fusion | flops 817889280 | bytes 17780736 | tf_op jit(solution)/shard_map/dot_general | solution.py:38
  67.7 1.8 %all-to-all-done.2 = f32[32,16,128]{2,1,0:T(8,128)S(1)} async-done(((f32[32,16,128]{2,1,0:T(8,128)}), f32[32,16,128]{2,1,0:T(8,128)S(1)}, u32[]{:S(2)}, u32[]{:S(2)}) %all-to-all-start.2) | async-done | bytes 262176 | tf_op jit(solution)/shard_map/all_to_all | solution.py:20
  69.8 1.7 %fusion.7 = f32[48,128]{1,0:T(8,128)S(1)} fusion(bf16[16,128]{1,0:T(8,128)(2,1)S(1)} %get-tuple-element.27, bf16[16,128]{1,0:T(8,128)(2,1)S(1)} %get-tuple-element.26, bf16[16,128]{1,0:T(8,128)(2,1)S(1)} %get-tuple-element.25, s32[1024]{0:T(1024)S(1)} %add_bitcast_fusion, pred[1024]{0:T(1024)(128)(4,1)} %copy-done.5, s32[1024]{0:T(1024)} %copy-done.3, ...), kind=kOutput, calls=%fused_computation.12 | convolution fusion | flops 35704832 | bytes 47104 | tf_op jit(solution)/shard_map/dot_general | solution.py:50
  71.6 1.0 fusion.8
  72.7 0.7 broadcast_in_dim.15
  73.4 4.2 %all-to-all-start.3 = ((f32[32,16,128]{2,1,0:T(8,128)}), f32[32,16,128]{2,1,0:T(8,128)S(1)}, u32[]{:S(2)}, u32[]{:S(2)}) async-start(f32[32,16,128]{2,1,0:T(8,128)} %broadcast_in_dim.15), calls=%async_computation.3 | async-start | bytes 524288 | tf_op jit(solution)/shard_map/all_to_all | solution.py:20
  78.0 7.6 %multiply_exponential_fusion = f32[1024,4096]{1,0:T(8,128)} fusion(bf16[96,1024]{1,0:T(8,128)(2,1)S(1)} %constant_dynamic-update-slice_fusion.19, bf16[96,4096]{1,0:T(8,128)(2,1)S(1)} %constant_dynamic-update-slice_fusion.25, f32[4096]{0:T(1024)S(1)} %multiply_reduce_fusion, f32[1024]{0:T(1024)S(1)} %multiply_reduce_fusion.2), kind=kOutput, calls=%fused_computation | convolution fusion | flops 817889280 | bytes 17780736 | tf_op jit(solution)/shard_map/dot_general | solution.py:38
  85.6 2.1 %all-to-all-done.3 = f32[32,16,128]{2,1,0:T(8,128)S(1)} async-done(((f32[32,16,128]{2,1,0:T(8,128)}), f32[32,16,128]{2,1,0:T(8,128)S(1)}, u32[]{:S(2)}, u32[]{:S(2)}) %all-to-all-start.3) | async-done | bytes 262176 | tf_op jit(solution)/shard_map/all_to_all | solution.py:20
  87.8 8.2 %shard_map.78 = f32[16,1024]{1,0:T(8,128)S(1)} custom-call(s32[1]{0:T(128)} %constant.64.clone.1.slot_ref, f32[1,1024,4096]{2,1,0:T(8,128)} %inv_ref.3, bf16[32,4096]{1,0:T(8,128)(2,1)S(1)} %pad_maximum_fusion.1.rcat_ref, bf16[16,4096]{1,0:T(8,128)(2,1)S(1)} %get-tuple-element.23.r1_ref), custom_call_target="tpu_custom_call" | custom-call | flops 402653184 | bytes 16777216 | tf_op jit(solution)/shard_map/pallas_call | solution.py:83
  96.0 0.6 bitcast_bitcast_fusion
  96.7 3.4 %all-to-all-start.4 = ((f32[8,16,128]{2,1,0:T(8,128)}), f32[8,16,128]{2,1,0:T(8,128)S(1)}, u32[]{:S(2)}, u32[]{:S(2)}) async-start(f32[8,16,128]{2,1,0:T(8,128)} %bitcast_bitcast_fusion), calls=%async_computation.4 | async-start | bytes 131072 | tf_op jit(solution)/shard_map/all_to_all | solution.py:117
  100.0 0.5 fusion.40
  100.5 4.4 %all-to-all-done.4 = f32[8,16,128]{2,1,0:T(8,128)S(1)} async-done(((f32[8,16,128]{2,1,0:T(8,128)}), f32[8,16,128]{2,1,0:T(8,128)S(1)}, u32[]{:S(2)}, u32[]{:S(2)}) %all-to-all-start.4) | async-done | bytes 65568 | tf_op jit(solution)/shard_map/all_to_all | solution.py:117
  105.0 0.7 broadcast_in_dim.17
  105.7 2.6 %all-to-all-start.5 = ((f32[32,16,128]{2,1,0:T(8,128)}), f32[32,16,128]{2,1,0:T(8,128)S(1)}, u32[]{:S(2)}, u32[]{:S(2)}) async-start(f32[32,16,128]{2,1,0:T(8,128)} %broadcast_in_dim.17), calls=%async_computation.5 | async-start | bytes 524288 | tf_op jit(solution)/shard_map/all_to_all | solution.py:20
  108.3 6.7 %fusion.2 = f32[16,512]{1,0:T(8,128)S(1)} fusion(f32[16,4096]{1,0:T(8,128)S(1)} %bitcast.105, f32[1024,4096]{1,0:T(8,128)} %multiply_exponential_fusion.1), kind=kOutput, calls=%fused_computation.4 | convolution fusion | flops 201326592 | bytes 8683520 | tf_op jit(solution)/shard_map/dot_general | solution.py:44
  115.0 6.7 %fusion = f32[16,512]{1,0:T(8,128)S(1)} fusion(f32[16,4096]{1,0:T(8,128)S(1)} %bitcast.106, f32[1024,4096]{1,0:T(8,128)} %multiply_exponential_fusion.1), kind=kOutput, calls=%fused_computation.2 | convolution fusion | flops 201326592 | bytes 8683520 | tf_op jit(solution)/shard_map/dot_general | solution.py:44
  121.8 0.2 copy.23
  121.9 0.2 copy.61
  122.1 0.5 fusion.30
  122.6 0.7 add_add_fusion
  123.3 10.8 %fusion.6 = f32[16,1024]{1,0:T(8,128)} fusion(f32[1024,4096]{1,0:T(8,128)} %multiply_exponential_fusion, f32[16,1024]{1,0:T(8,128)S(1)} %copy-done.1, f32[16,512]{1,0:T(8,128)S(1)} %fusion, f32[16,512]{1,0:T(8,128)S(1)} %fusion.2, f32[2,8,32,128]{3,2,1,0:T(8,128)S(1)} %bitcast.108, f32[48,1024]{1,0:T(8,128)S(1)} %fusion.40, f32[48,1024]{1,0:T(8,128)S(1)} %fusion.30), kind=kOutput, calls=%fused_computation.10 | convolution fusion | flops 402833408 | bytes 17629184 | tf_op jit(solution)/shard_map/dot_general | solution.py:44
  (68 shorter events, 1.8 us)
Async XLA Ops:
  3.8 13.6 %copy-start.5 = (pred[1024]{0:T(1024)(128)(4,1)}, pred[1024]{0:T(1024)(128)(4,1)S(1)}, u32[]{:S(2)}) copy-start(pred[1024]{0:T(1024)(128)(4,1)S(1)} %get-tuple-element.38) | copy-start | bytes 3076
  3.8 13.6 %copy-start.7 = (pred[1024]{0:T(1024)(128)(4,1)}, pred[1024]{0:T(1024)(128)(4,1)S(1)}, u32[]{:S(2)}) copy-start(pred[1024]{0:T(1024)(128)(4,1)S(1)} %get-tuple-element.13) | copy-start | bytes 3076
  5.0 12.5 %copy-start.3 = (s32[1024]{0:T(1024)}, s32[1024]{0:T(1024)S(1)}, u32[]{:S(2)}) copy-start(s32[1024]{0:T(1024)S(1)} %add_bitcast_fusion.1) | copy-start | bytes 12292
  9.5 26.9 %all-to-all-start = ((f32[32,48,128]{2,1,0:T(8,128)}), f32[32,48,128]{2,1,0:T(8,128)S(1)}, u32[]{:S(2)}, u32[]{:S(2)}) async-start(f32[32,48,128]{2,1,0:T(8,128)} %broadcast_in_dim.12), calls=%async_computation | async-start | bytes 1572864 | tf_op jit(solution)/shard_map/all_to_all | solution.py:20
  44.8 27.9 %copy-start = (f32[16,1024]{1,0:T(8,128)S(1)}, f32[16,1024]{1,0:T(8,128)}, u32[]{:S(2)}) copy-start(f32[16,1024]{1,0:T(8,128)} %param.6) | copy-start | bytes 196612
  45.4 9.0 %all-to-all-start.1 = ((f32[8,16,128]{2,1,0:T(8,128)}), f32[8,16,128]{2,1,0:T(8,128)}, u32[]{:S(2)}, u32[]{:S(2)}) async-start(f32[8,16,128]{2,1,0:T(8,128)} %bitcast_bitcast_fusion.1), calls=%async_computation.1 | async-start | bytes 131072 | tf_op jit(solution)/shard_map/all_to_all | solution.py:117
  55.8 13.7 %all-to-all-start.2 = ((f32[32,16,128]{2,1,0:T(8,128)}), f32[32,16,128]{2,1,0:T(8,128)S(1)}, u32[]{:S(2)}, u32[]{:S(2)}) async-start(f32[32,16,128]{2,1,0:T(8,128)} %broadcast_in_dim.14), calls=%async_computation.2 | async-start | bytes 524288 | tf_op jit(solution)/shard_map/all_to_all | solution.py:20
  73.4 14.3 %all-to-all-start.3 = ((f32[32,16,128]{2,1,0:T(8,128)}), f32[32,16,128]{2,1,0:T(8,128)S(1)}, u32[]{:S(2)}, u32[]{:S(2)}) async-start(f32[32,16,128]{2,1,0:T(8,128)} %broadcast_in_dim.15), calls=%async_computation.3 | async-start | bytes 524288 | tf_op jit(solution)/shard_map/all_to_all | solution.py:20
  78.0 22.1 %copy-start.4 = (s32[1024]{0:T(1024)S(1)}, s32[1024]{0:T(1024)}, u32[]{:S(2)}) copy-start(s32[1024]{0:T(1024)} %copy-done.3) | copy-start | bytes 12292
  78.0 22.1 %copy-start.8 = (pred[1024]{0:T(1024)(128)(4,1)S(1)}, pred[1024]{0:T(1024)(128)(4,1)}, u32[]{:S(2)}) copy-start(pred[1024]{0:T(1024)(128)(4,1)} %copy-done.7) | copy-start | bytes 3076
  87.7 34.4 %copy-start.6 = (pred[1024]{0:T(1024)(128)(4,1)S(1)}, pred[1024]{0:T(1024)(128)(4,1)}, u32[]{:S(2)}) copy-start(pred[1024]{0:T(1024)(128)(4,1)} %copy-done.5) | copy-start | bytes 3076
  87.8 34.9 %copy-start.2 = (f32[16,1024]{1,0:T(8,128)S(1)}, f32[16,1024]{1,0:T(8,128)}, u32[]{:S(2)}) copy-start(f32[16,1024]{1,0:T(8,128)} %param.8) | copy-start | bytes 196612
  87.8 35.5 %copy-start.1 = (f32[16,1024]{1,0:T(8,128)S(1)}, f32[16,1024]{1,0:T(8,128)}, u32[]{:S(2)}) copy-start(f32[16,1024]{1,0:T(8,128)} %param.7) | copy-start | bytes 196612
  96.7 8.3 %all-to-all-start.4 = ((f32[8,16,128]{2,1,0:T(8,128)}), f32[8,16,128]{2,1,0:T(8,128)S(1)}, u32[]{:S(2)}, u32[]{:S(2)}) async-start(f32[8,16,128]{2,1,0:T(8,128)} %bitcast_bitcast_fusion), calls=%async_computation.4 | async-start | bytes 131072 | tf_op jit(solution)/shard_map/all_to_all | solution.py:117
  105.7 16.1 %all-to-all-start.5 = ((f32[32,16,128]{2,1,0:T(8,128)}), f32[32,16,128]{2,1,0:T(8,128)S(1)}, u32[]{:S(2)}, u32[]{:S(2)}) async-start(f32[32,16,128]{2,1,0:T(8,128)} %broadcast_in_dim.17), calls=%async_computation.5 | async-start | bytes 524288 | tf_op jit(solution)/shard_map/all_to_all | solution.py:20

commit v17 on v15

--- a/solution.py
+++ b/solution.py
@@ -56,10 +56,10 @@
     hi = a.astype(jnp.bfloat16)
     lo = (a - hi.astype(jnp.float32)).astype(jnp.bfloat16)
     dims = (((1,), (1,)), ((), ()))
-    both = lax.dot_general(rcat_ref[...], hi, dims, preferred_element_type=jnp.float32)
-    low = lax.dot_general(r1_ref[...], lo, dims, preferred_element_type=jnp.float32)
-    rows = o_ref.shape[0]
-    o_ref[...] = (both[:rows] + both[rows:]) + low
+    both = lax.dot_general(hi, rcat_ref[...], dims, preferred_element_type=jnp.float32)
+    low = lax.dot_general(lo, r1_ref[...], dims, preferred_element_type=jnp.float32)
+    rows = o_ref.shape[1]
+    o_ref[...] = (both[:, :rows] + both[:, rows:]) + low
 
 
 def solve_rows(inverse, slot, block_res, tile=512):
@@ -78,17 +78,17 @@
             pl.BlockSpec((2 * rows, width), lambda i, s: (0, 0)),
             pl.BlockSpec((rows, width), lambda i, s: (0, 0)),
         ],
-        out_specs=pl.BlockSpec((rows, tile), lambda i, s: (0, i)),
+        out_specs=pl.BlockSpec((tile, rows), lambda i, s: (i, 0)),
     )
     return pl.pallas_call(
         solve_kernel,
         grid_spec=grid_spec,
-        out_shape=jax.ShapeDtypeStruct((rows, n), jnp.float32),
+        out_shape=jax.ShapeDtypeStruct((n, rows), jnp.float32),
         compiler_params=pltpu.CompilerParams(vmem_limit_bytes=48 * 1024 * 1024),
         cost_estimate=pl.CostEstimate(
             flops=6 * rows * n * width, transcendentals=0, bytes_accessed=4 * n * width
         ),
-    )(jnp.reshape(slot, (1,)).astype(jnp.int32), inverse, rcat, r1)
+    )(jnp.reshape(slot, (1,)).astype(jnp.int32), inverse, rcat, r1).T
 
 
 def body(points, residual, coef, block_of, order, inverse):

time: 132 us -> 133 us (level)
  waiting for transfers between devices: 19.7 us -> 23.3 us
  other arithmetic: 15.2 us -> 12.3 us
    all_to_all x4, waiting for transfers between devices: 10.8 us -> 14.4 us  [gather_all(): return lax.all_to_all(sent, ALL, 0, 0, tiled=True)]
    unnamed x26, other arithmetic: 7.74 us -> 5.36 us
    reshape x0 -> x2, local copies, waits for them, and re-layouts: none -> 1.6 us  [distribute(): pieces = jnp.transpose(solved.reshape(rhs, n_grp, per), (1, 0, 2))]
  transfers between devices with their start and end apart: 6 -> 6, of which waited for: 5 -> 5; matrix products, arithmetic and copies ran while one was open for 28% -> 25% of each run, Pallas kernels for 0% -> 0%
where the time goes in v17:
time: 133 us; the launch traced here: 132 us
  matrix products  41.5 us (31%)
  starting transfers between devices  25 us (19%)
  waiting for transfers between devices  23.3 us (18%)
  Pallas kernels  16.5 us (12%)
  other arithmetic  12.3 us (9%)
  local copies, waits for them, and re-layouts  8.71 us (7%)
  between operations  4.99 us (4%)
    dot_general x3, matrix products, apply_kernel(): lax.dot_general(delta, kernel, (((1,), (1,)), ((), ())), precision=HIGH)  21.9 us
    all_to_all x4, starting transfers between devices, gather_all(): return lax.all_to_all(sent, ALL, 0, 0, tiled=True)  17.6 us
    dot_general x3, matrix products, kern(): lax.dot_general(left, right, (((0,), (0,)), ((), ())), preferred_element_...  16.6 us
    pallas_call x2, Pallas kernels, solve_rows(): pl.pallas_call(solve_kernel, grid_spec=grid_spec, out_shape=jax.ShapeDtyp...  16.5 us
    all_to_all x4, waiting for transfers between devices, gather_all(): return lax.all_to_all(sent, ALL, 0, 0, tiled=True)  14.4 us
    all_to_all x2, waiting for transfers between devices, distribute(): scattered = lax.all_to_all(pieces, 'grp', 0, 0, tiled=True)  8.85 us
    all_to_all x2, starting transfers between devices, distribute(): scattered = lax.all_to_all(pieces, 'grp', 0, 0, tiled=True)  7.32 us
    unnamed x26, other arithmetic  5.36 us
  transfers between devices with their start and end apart: 6, of which 5 were waited for; matrix products, arithmetic and copies ran while one was open for 25% of the time, Pallas kernels for 0%

profile of v17, /device:TPU:0, one launch (start us, length us, event | category | flops | bytes accessed | tf_op | source)
XLA Modules:
  0.0 132.3 jit_solution(9935835029540063734)
XLA Ops:
  0.6 1.3 %fusion.48 = (s32[1]{0:T(128)}, s32[1]{0:T(128)}) fusion(s32[2]{0:T(128)} %param.10), kind=kLoop, calls=%fused_computation.151 | loop fusion | bytes 16 | tf_op jit(solution)/shard_map/slice | solution.py:126
  2.0 2.0 %convert_bitcast_fusion.1 = (s32[8,128]{1,0:T(8,128)S(1)}, pred[1024]{0:T(1024)(128)(4,1)S(1)}, s32[8,128]{1,0:T(8,128)S(1)}, pred[1024]{0:T(1024)(128)(4,1)S(1)}) fusion(s32[1024]{0:T(1024)} %param.9, s32[]{:T(128)} %bitcast, s32[]{:T(128)} %bitcast.3), kind=kLoop, calls=%fused_computation.141 | loop fusion | flops 4096 | bytes 14344 | tf_op jit(solution)/shard_map/convert
  3.9 0.3 reduce-window.16
  4.5 0.3 reduce-window.24
  5.1 0.8 constant_dynamic-update-slice_fusion.1
  5.9 0.9 multiply_reduce_fusion.3
  6.8 0.9 fusion.10
  7.8 0.3 fusion.6
  8.1 0.6 multiply_reduce_fusion.4
  8.7 0.9 broadcast_in_dim.12
  9.6 7.3 %all-to-all-start = ((f32[32,48,128]{2,1,0:T(8,128)}), f32[32,48,128]{2,1,0:T(8,128)S(1)}, u32[]{:S(2)}, u32[]{:S(2)}) async-start(f32[32,48,128]{2,1,0:T(8,128)} %broadcast_in_dim.12), calls=%async_computation | async-start | bytes 1572864 | tf_op jit(solution)/shard_map/all_to_all | solution.py:20
  20.9 0.8 constant_dynamic-update-slice_fusion.18
  21.7 0.8 constant_dynamic-update-slice_fusion.17
  22.6 0.8 constant_dynamic-update-slice_fusion.16
  23.4 0.8 constant_dynamic-update-slice_fusion.15
  24.3 0.9 constant_dynamic-update-slice_fusion.14
  25.1 0.9 constant_dynamic-update-slice_fusion.13
  26.0 10.6 %all-to-all-done = f32[32,48,128]{2,1,0:T(8,128)S(1)} async-done(((f32[32,48,128]{2,1,0:T(8,128)}), f32[32,48,128]{2,1,0:T(8,128)S(1)}, u32[]{:S(2)}, u32[]{:S(2)}) %all-to-all-start) | async-done | bytes 786464 | tf_op jit(solution)/shard_map/all_to_all | solution.py:20
  36.5 0.8 slice_bitcast_fusion
  37.6 8.2 %shard_map.77 = f32[1024,16]{1,0:T(8,128)S(1)} custom-call(s32[1]{0:T(128)} %constant.64.clone.1.slot_ref, f32[1,1024,4096]{2,1,0:T(8,128)} %inv_ref.3, bf16[32,4096]{1,0:T(8,128)(2,1)S(1)} %pad_maximum_fusion.rcat_ref, bf16[16,4096]{1,0:T(8,128)(2,1)S(1)} %get-tuple-element.28.r1_ref), custom_call_target="tpu_custom_call" | custom-call | flops 402653184 | bytes 16777216 | tf_op jit(solution)/shard_map/pallas_call | solution.py:83
  45.8 0.8 copy.21
  46.6 4.0 %all-to-all-start.1 = ((f32[8,16,128]{2,1,0:T(8,128)}), f32[8,16,128]{2,1,0:T(8,128)}, u32[]{:S(2)}, u32[]{:S(2)}) async-start(f32[8,16,128]{2,1,0:T(8,128)} %bitcast.9), calls=%async_computation.1 | async-start | bytes 131072 | tf_op jit(solution)/shard_map/all_to_all | solution.py:117
  50.6 0.6 fusion.1
  51.2 4.4 %all-to-all-done.1 = f32[8,16,128]{2,1,0:T(8,128)} async-done(((f32[8,16,128]{2,1,0:T(8,128)}), f32[8,16,128]{2,1,0:T(8,128)}, u32[]{:S(2)}, u32[]{:S(2)}) %all-to-all-start.1) | async-done | bytes 65568 | tf_op jit(solution)/shard_map/all_to_all | solution.py:117
  55.6 0.7 dynamic-slice_bitcast_fusion.1
  56.3 0.7 broadcast_in_dim.14
  57.0 3.5 %all-to-all-start.2 = ((f32[32,16,128]{2,1,0:T(8,128)}), f32[32,16,128]{2,1,0:T(8,128)S(1)}, u32[]{:S(2)}, u32[]{:S(2)}) async-start(f32[32,16,128]{2,1,0:T(8,128)} %broadcast_in_dim.14), calls=%async_computation.2 | async-start | bytes 524288 | tf_op jit(solution)/shard_map/all_to_all | solution.py:20
  60.5 8.5 %multiply_exponential_fusion.1 = f32[1024,4096]{1,0:T(8,128)} fusion(bf16[96,1024]{1,0:T(8,128)(2,1)} %copy-done.2, bf16[96,4096]{1,0:T(8,128)(2,1)S(1)} %constant_dynamic-update-slice_fusion.8, f32[4096]{0:T(1024)S(1)} %bitcast.109, f32[1024]{0:T(1024)S(1)} %get-tuple-element.33), kind=kOutput, calls=%fused_computation.1 | convolution fusion | flops 817889280 | bytes 17780736 | tf_op jit(solution)/shard_map/dot_general | solution.py:38
  69.0 1.7 %all-to-all-done.2 = f32[32,16,128]{2,1,0:T(8,128)S(1)} async-done(((f32[32,16,128]{2,1,0:T(8,128)}), f32[32,16,128]{2,1,0:T(8,128)S(1)}, u32[]{:S(2)}, u32[]{:S(2)}) %all-to-all-start.2) | async-done | bytes 262176 | tf_op jit(solution)/shard_map/all_to_all | solution.py:20
  70.9 0.2 copy.62
  71.1 1.7 %fusion.4 = f32[48,128]{1,0:T(8,128)S(1)} fusion(bf16[16,128]{1,0:T(8,128)(2,1)S(1)} %get-tuple-element.27, bf16[16,128]{1,0:T(8,128)(2,1)S(1)} %get-tuple-element.26, bf16[16,128]{1,0:T(8,128)(2,1)S(1)} %get-tuple-element.25, s32[1024]{0:T(1024)S(1)} %add_bitcast_fusion, pred[1024]{0:T(1024)(128)(4,1)} %copy-done.7, s32[1024]{0:T(1024)} %copy-done.5, ...), kind=kOutput, calls=%fused_computation.10 | convolution fusion | flops 35704832 | bytes 47104 | tf_op jit(solution)/shard_map/dot_general | solution.py:50
  72.8 1.0 fusion.5
  73.9 0.7 broadcast_in_dim.15
  74.6 4.3 %all-to-all-start.3 = ((f32[32,16,128]{2,1,0:T(8,128)}), f32[32,16,128]{2,1,0:T(8,128)S(1)}, u32[]{:S(2)}, u32[]{:S(2)}) async-start(f32[32,16,128]{2,1,0:T(8,128)} %broadcast_in_dim.15), calls=%async_computation.3 | async-start | bytes 524288 | tf_op jit(solution)/shard_map/all_to_all | solution.py:20
  79.3 7.6 %multiply_exponential_fusion = f32[1024,4096]{1,0:T(8,128)} fusion(bf16[96,1024]{1,0:T(8,128)(2,1)S(1)} %constant_dynamic-update-slice_fusion.19, bf16[96,4096]{1,0:T(8,128)(2,1)S(1)} %constant_dynamic-update-slice_fusion.25, f32[4096]{0:T(1024)S(1)} %multiply_reduce_fusion, f32[1024]{0:T(1024)S(1)} %multiply_reduce_fusion.2), kind=kOutput, calls=%fused_computation | convolution fusion | flops 817889280 | bytes 17780736 | tf_op jit(solution)/shard_map/dot_general | solution.py:38
  86.9 2.1 %all-to-all-done.3 = f32[32,16,128]{2,1,0:T(8,128)S(1)} async-done(((f32[32,16,128]{2,1,0:T(8,128)}), f32[32,16,128]{2,1,0:T(8,128)S(1)}, u32[]{:S(2)}, u32[]{:S(2)}) %all-to-all-start.3) | async-done | bytes 262176 | tf_op jit(solution)/shard_map/all_to_all | solution.py:20
  89.0 8.3 %shard_map.78 = f32[1024,16]{1,0:T(8,128)S(1)} custom-call(s32[1]{0:T(128)} %constant.64.clone.1.slot_ref, f32[1,1024,4096]{2,1,0:T(8,128)} %inv_ref.3, bf16[32,4096]{1,0:T(8,128)(2,1)S(1)} %pad_maximum_fusion.1.rcat_ref, bf16[16,4096]{1,0:T(8,128)(2,1)S(1)} %get-tuple-element.23.r1_ref), custom_call_target="tpu_custom_call" | custom-call | flops 402653184 | bytes 16777216 | tf_op jit(solution)/shard_map/pallas_call | solution.py:83
  97.3 0.8 copy.26
  98.1 3.4 %all-to-all-start.4 = ((f32[8,16,128]{2,1,0:T(8,128)}), f32[8,16,128]{2,1,0:T(8,128)S(1)}, u32[]{:S(2)}, u32[]{:S(2)}) async-start(f32[8,16,128]{2,1,0:T(8,128)} %bitcast.17), calls=%async_computation.4 | async-start | bytes 131072 | tf_op jit(solution)/shard_map/all_to_all | solution.py:117
  101.5 0.5 fusion.36
  102.0 4.4 %all-to-all-done.4 = f32[8,16,128]{2,1,0:T(8,128)S(1)} async-done(((f32[8,16,128]{2,1,0:T(8,128)}), f32[8,16,128]{2,1,0:T(8,128)S(1)}, u32[]{:S(2)}, u32[]{:S(2)}) %all-to-all-start.4) | async-done | bytes 65568 | tf_op jit(solution)/shard_map/all_to_all | solution.py:117
  106.4 0.7 broadcast_in_dim.17
  107.2 2.6 %all-to-all-start.5 = ((f32[32,16,128]{2,1,0:T(8,128)}), f32[32,16,128]{2,1,0:T(8,128)S(1)}, u32[]{:S(2)}, u32[]{:S(2)}) async-start(f32[32,16,128]{2,1,0:T(8,128)} %broadcast_in_dim.17), calls=%async_computation.5 | async-start | bytes 524288 | tf_op jit(solution)/shard_map/all_to_all | solution.py:20
  109.8 10.2 %fusion.3 = f32[16,1024]{1,0:T(8,128)S(1)} fusion(f32[16,1024]{1,0:T(8,128)S(1)} %copy-done.3, f32[16,4096]{1,0:T(8,128)S(1)} %bitcast.104, f32[1024,4096]{1,0:T(8,128)} %multiply_exponential_fusion.1, f32[48,1024]{1,0:T(8,128)S(1)} %fusion.36), kind=kOutput, calls=%fused_computation.8 | convolution fusion | flops 402735104 | bytes 17367040 | tf_op jit(solution)/shard_map/dot_general | solution.py:44
  120.1 0.2 copy.61
  120.3 0.5 fusion.26
  120.8 0.7 add_add_fusion
  121.5 10.8 %fusion.2 = f32[16,1024]{1,0:T(8,128)} fusion(f32[16,1024]{1,0:T(8,128)S(1)} %fusion.3, f32[1024,4096]{1,0:T(8,128)} %multiply_exponential_fusion, f32[2,8,32,128]{3,2,1,0:T(8,128)S(1)} %bitcast.100, f32[48,1024]{1,0:T(8,128)S(1)} %fusion.26), kind=kOutput, calls=%fused_computation.6 | convolution fusion | flops 402735104 | bytes 17367040 | tf_op jit(solution)/shard_map/dot_general | solution.py:44
  (73 shorter events, 1.7 us)
Async XLA Ops:
  3.9 5.7 %copy-start.7 = (pred[1024]{0:T(1024)(128)(4,1)}, pred[1024]{0:T(1024)(128)(4,1)S(1)}, u32[]{:S(2)}) copy-start(pred[1024]{0:T(1024)(128)(4,1)S(1)} %get-tuple-element.38) | copy-start | bytes 3076
  3.9 5.7 %copy-start.9 = (pred[1024]{0:T(1024)(128)(4,1)}, pred[1024]{0:T(1024)(128)(4,1)S(1)}, u32[]{:S(2)}) copy-start(pred[1024]{0:T(1024)(128)(4,1)S(1)} %get-tuple-element.13) | copy-start | bytes 3076
  4.5 5.1 %copy-start.5 = (s32[1024]{0:T(1024)}, s32[1024]{0:T(1024)S(1)}, u32[]{:S(2)}) copy-start(s32[1024]{0:T(1024)S(1)} %add_bitcast_fusion.1) | copy-start | bytes 12292
  9.6 26.9 %all-to-all-start = ((f32[32,48,128]{2,1,0:T(8,128)}), f32[32,48,128]{2,1,0:T(8,128)S(1)}, u32[]{:S(2)}, u32[]{:S(2)}) async-start(f32[32,48,128]{2,1,0:T(8,128)} %broadcast_in_dim.12), calls=%async_computation | async-start | bytes 1572864 | tf_op jit(solution)/shard_map/all_to_all | solution.py:20
  26.0 11.3 %copy-start.2 = (bf16[96,1024]{1,0:T(8,128)(2,1)}, bf16[96,1024]{1,0:T(8,128)(2,1)S(1)}, u32[]{:S(2)}) copy-start(bf16[96,1024]{1,0:T(8,128)(2,1)S(1)} %constant_dynamic-update-slice_fusion.13) | copy-start | bytes 589828
  37.3 13.3 %copy-start.11 = (f32[128]{0:T(128)S(1)}, f32[128]{0:T(128)}, u32[]{:S(2)}) copy-start(f32[128]{0:T(128)} %get-tuple-element.35) | copy-start | bytes 1540
  37.3 13.9 %copy-start.1 = (f32[32,2,8,128]{3,2,1,0:T(8,128)S(1)}, f32[32,2,8,128]{3,2,1,0:T(8,128)}, u32[]{:S(2)}) copy-start(f32[32,2,8,128]{3,2,1,0:T(8,128)} %get-tuple-element.16) | copy-start | bytes 786436
  45.8 28.1 %copy-start = (f32[16,1024]{1,0:T(8,128)S(1)}, f32[16,1024]{1,0:T(8,128)}, u32[]{:S(2)}) copy-start(f32[16,1024]{1,0:T(8,128)} %param.6) | copy-start | bytes 196612
  46.6 9.0 %all-to-all-start.1 = ((f32[8,16,128]{2,1,0:T(8,128)}), f32[8,16,128]{2,1,0:T(8,128)}, u32[]{:S(2)}, u32[]{:S(2)}) async-start(f32[8,16,128]{2,1,0:T(8,128)} %bitcast.9), calls=%async_computation.1 | async-start | bytes 131072 | tf_op jit(solution)/shard_map/all_to_all | solution.py:117
  57.0 13.7 %all-to-all-start.2 = ((f32[32,16,128]{2,1,0:T(8,128)}), f32[32,16,128]{2,1,0:T(8,128)S(1)}, u32[]{:S(2)}, u32[]{:S(2)}) async-start(f32[32,16,128]{2,1,0:T(8,128)} %broadcast_in_dim.14), calls=%async_computation.2 | async-start | bytes 524288 | tf_op jit(solution)/shard_map/all_to_all | solution.py:20
  74.6 14.3 %all-to-all-start.3 = ((f32[32,16,128]{2,1,0:T(8,128)}), f32[32,16,128]{2,1,0:T(8,128)S(1)}, u32[]{:S(2)}, u32[]{:S(2)}) async-start(f32[32,16,128]{2,1,0:T(8,128)} %broadcast_in_dim.15), calls=%async_computation.3 | async-start | bytes 524288 | tf_op jit(solution)/shard_map/all_to_all | solution.py:20
  79.2 22.3 %copy-start.6 = (s32[1024]{0:T(1024)S(1)}, s32[1024]{0:T(1024)}, u32[]{:S(2)}) copy-start(s32[1024]{0:T(1024)} %copy-done.5) | copy-start | bytes 12292
  79.2 22.3 %copy-start.10 = (pred[1024]{0:T(1024)(128)(4,1)S(1)}, pred[1024]{0:T(1024)(128)(4,1)}, u32[]{:S(2)}) copy-start(pred[1024]{0:T(1024)(128)(4,1)} %copy-done.9) | copy-start | bytes 3076
  79.2 30.5 %copy-start.3 = (f32[16,1024]{1,0:T(8,128)S(1)}, f32[16,1024]{1,0:T(8,128)}, u32[]{:S(2)}) copy-start(f32[16,1024]{1,0:T(8,128)} %param.7) | copy-start | bytes 196612
  89.0 31.3 %copy-start.8 = (pred[1024]{0:T(1024)(128)(4,1)S(1)}, pred[1024]{0:T(1024)(128)(4,1)}, u32[]{:S(2)}) copy-start(pred[1024]{0:T(1024)(128)(4,1)} %copy-done.7) | copy-start | bytes 3076
  89.0 31.8 %copy-start.4 = (f32[16,1024]{1,0:T(8,128)S(1)}, f32[16,1024]{1,0:T(8,128)}, u32[]{:S(2)}) copy-start(f32[16,1024]{1,0:T(8,128)} %param.8) | copy-start | bytes 196612
  98.1 8.3 %all-to-all-start.4 = ((f32[8,16,128]{2,1,0:T(8,128)}), f32[8,16,128]{2,1,0:T(8,128)S(1)}, u32[]{:S(2)}, u32[]{:S(2)}) async-start(f32[8,16,128]{2,1,0:T(8,128)} %bitcast.17), calls=%async_computation.4 | async-start | bytes 131072 | tf_op jit(solution)/shard_map/all_to_all | solution.py:117
  107.2 12.8 %all-to-all-start.5 = ((f32[32,16,128]{2,1,0:T(8,128)}), f32[32,16,128]{2,1,0:T(8,128)S(1)}, u32[]{:S(2)}, u32[]{:S(2)}) async-start(f32[32,16,128]{2,1,0:T(8,128)} %broadcast_in_dim.17), calls=%async_computation.5 | async-start | bytes 524288 | tf_op jit(solution)/shard_map/all_to_all | solution.py:20

commit v18 on v14

--- a/solution.py
+++ b/solution.py
@@ -41,16 +41,40 @@
     return lax.optimization_barrier((k1.astype(jnp.bfloat16), (kernel - k1).astype(jnp.bfloat16)))
 
 
-def apply_kernel(delta, kernel):
+def product_kernel(k1_ref, k2_ref, d12_ref, d1_ref, o_ref):
+    dims = (((1,), (1,)), ((), ()))
+    both = lax.dot_general(k1_ref[...], d12_ref[...], dims, preferred_element_type=jnp.float32)
+    low = lax.dot_general(k2_ref[...], d1_ref[...], dims, preferred_element_type=jnp.float32)
+    rows = o_ref.shape[1]
+    o_ref[...] = (both[:, :rows] + both[:, rows:]) + low
+
+
+def apply_kernel(delta, kernel, tile=256):
     k1, k2 = kernel
+    n, m = k1.shape
+    rows = delta.shape[0]
     d1f = lax.reduce_precision(delta, exponent_bits=8, mantissa_bits=7)
     d1 = d1f.astype(jnp.bfloat16)
     d2 = (delta - d1f).astype(jnp.bfloat16)
-    rows = delta.shape[0]
-    dims = (((1,), (1,)), ((), ()))
-    both = lax.dot_general(jnp.concatenate([d1, d2], axis=0), k1, dims, preferred_element_type=jnp.float32)
-    low = lax.dot_general(d1, k2, dims, preferred_element_type=jnp.float32)
-    return (both[:rows] + both[rows:]) + low
+    d12 = jnp.concatenate([d1, d2], axis=0)
+    tile = min(tile, n)
+    out = pl.pallas_call(
+        product_kernel,
+        grid=(n // tile,),
+        in_specs=[
+            pl.BlockSpec((tile, m), lambda i: (i, 0)),
+            pl.BlockSpec((tile, m), lambda i: (i, 0)),
+            pl.BlockSpec((2 * rows, m), lambda i: (0, 0)),
+            pl.BlockSpec((rows, m), lambda i: (0, 0)),
+        ],
+        out_specs=pl.BlockSpec((tile, rows), lambda i: (i, 0)),
+        out_shape=jax.ShapeDtypeStruct((n, rows), jnp.float32),
+        compiler_params=pltpu.CompilerParams(vmem_limit_bytes=48 * 1024 * 1024),
+        cost_estimate=pl.CostEstimate(
+            flops=6 * rows * n * m, transcendentals=0, bytes_accessed=4 * n * m + 6 * m * rows
+        ),
+    )(k1, k2, d12, d1)
+    return out.T
 
 
 def exact_dot(x, onehot, dims):

time: 136 us -> 136 us (level)
  matrix products: 45.7 us -> 21.9 us
  Pallas kernels: 16.4 us -> 34.4 us
  local copies, waits for them, and re-layouts: 7.75 us -> 12.6 us
  other arithmetic: 11.4 us -> 13.9 us
  starting transfers between devices: 28.6 us -> 26.7 us
    dot_general x6 -> x0, matrix products: 24.8 us -> none  [the longest x3 12.4 us: apply_kernel(): lax.dot_general(jnp.concatenate([d1, d2], axis=0), k1, dims, preferred_el...]
    pallas_call x0 -> x3, Pallas kernels: none -> 17.9 us  [apply_kernel(): pl.pallas_call(product_kernel, grid=(n // tile,), in_specs=[pl.BlockSpec(...]
    all_to_all x2, waiting for transfers between devices: 3.92 us -> 9.46 us  [distribute(): scattered = lax.all_to_all(pieces, 'grp', 0, 0, tiled=True)]
    all_to_all x4, waiting for transfers between devices: 16.4 us -> 11.2 us  [gather_all(): return lax.all_to_all(sent, ALL, 0, 0, tiled=True)]
    unnamed x15 -> x29, local copies, waits for them, and re-layouts: 1.29 us -> 4.88 us
    all_to_all x4, starting transfers between devices: 21.4 us -> 19.5 us  [gather_all(): return lax.all_to_all(sent, ALL, 0, 0, tiled=True)]
    unnamed x26 -> x21, other arithmetic: 4.69 us -> 5.3 us
  transfers between devices with their start and end apart: 6 -> 6, of which waited for: 5 -> 5; matrix products, arithmetic and copies ran while one was open for 27% -> 20% of each run, Pallas kernels for 0% -> 6%
where the time goes in v18:
time: 136 us; the launch traced here: 135 us
  Pallas kernels  34.4 us (25%)
  starting transfers between devices  26.7 us (20%)
  matrix products  21.9 us (16%)
  waiting for transfers between devices  20.6 us (15%)
  other arithmetic  13.9 us (10%)
  local copies, waits for them, and re-layouts  12.6 us (9%)
  between operations  5.1 us (4%)
    all_to_all x4, starting transfers between devices, gather_all(): return lax.all_to_all(sent, ALL, 0, 0, tiled=True)  19.5 us
    dot_general x3, matrix products, kern(): lax.dot_general(left, right, (((0,), (0,)), ((), ())), preferred_element_...  18.7 us
    pallas_call x3, Pallas kernels, apply_kernel(): pl.pallas_call(product_kernel, grid=(n // tile,), in_specs=[pl.BlockSpec(...  17.9 us
    pallas_call x2, Pallas kernels, solve_rows(): pl.pallas_call(solve_kernel, grid_spec=grid_spec, out_shape=jax.ShapeDtyp...  16.4 us
    all_to_all x4, waiting for transfers between devices, gather_all(): return lax.all_to_all(sent, ALL, 0, 0, tiled=True)  11.2 us
    all_to_all x2, waiting for transfers between devices, distribute(): scattered = lax.all_to_all(pieces, 'grp', 0, 0, tiled=True)  9.46 us
    all_to_all x2, starting transfers between devices, distribute(): scattered = lax.all_to_all(pieces, 'grp', 0, 0, tiled=True)  7.19 us
    unnamed x21, other arithmetic  5.3 us
  transfers between devices with their start and end apart: 6, of which 5 were waited for; matrix products, arithmetic and copies ran while one was open for 20% of the time, Pallas kernels for 6%

profile of v18, /device:TPU:0, one launch (start us, length us, event | category | flops | bytes accessed | tf_op | source)
XLA Modules:
  0.0 135.1 jit_solution(2447167144913353835)
XLA Ops:
  0.6 1.3 fusion.54
  1.9 2.0 %convert_bitcast_fusion.1 = (s32[8,128]{1,0:T(8,128)S(1)}, pred[1024]{0:T(1024)(128)(4,1)S(1)}, s32[8,128]{1,0:T(8,128)S(1)}, pred[1024]{0:T(1024)(128)(4,1)S(1)}) fusion(s32[1024]{0:T(1024)} %param.9, s32[]{:T(128)} %bitcast, s32[]{:T(128)} %bitcast.3), kind=kLoop, calls=%fused_computation.158 | loop fusion | flops 4096 | bytes 14344 | tf_op jit(solution)/shard_map/convert
  5.1 0.8 constant_dynamic-update-slice_fusion.1
  5.9 0.9 multiply_reduce_fusion.4
  6.8 0.9 fusion.12
  7.8 0.5 fusion.6
  8.7 1.0 broadcast_in_dim.12
  9.7 7.3 %all-to-all-start = ((f32[32,48,128]{2,1,0:T(8,128)}), f32[32,48,128]{2,1,0:T(8,128)S(1)}, u32[]{:S(2)}, u32[]{:S(2)}) async-start(f32[32,48,128]{2,1,0:T(8,128)} %broadcast_in_dim.12), calls=%async_computation | async-start | bytes 1572864 | tf_op jit(solution)/shard_map/all_to_all | solution.py:20
  19.6 1.0 copy.113
  20.6 1.0 copy.122
  23.1 0.8 constant_dynamic-update-slice_fusion.7
  24.0 0.8 constant_dynamic-update-slice_fusion.6
  24.8 0.8 constant_dynamic-update-slice_fusion.5
  25.7 0.8 constant_dynamic-update-slice_fusion.4
  26.5 0.9 constant_dynamic-update-slice_fusion.3
  27.4 0.9 constant_dynamic-update-slice_fusion.2
  28.2 8.4 %all-to-all-done = f32[32,48,128]{2,1,0:T(8,128)S(1)} async-done(((f32[32,48,128]{2,1,0:T(8,128)}), f32[32,48,128]{2,1,0:T(8,128)S(1)}, u32[]{:S(2)}, u32[]{:S(2)}) %all-to-all-start) | async-done | bytes 786464 | tf_op jit(solution)/shard_map/all_to_all | solution.py:20
  36.6 0.8 slice_bitcast_fusion
  37.6 8.2 %shard_map.77 = f32[16,1024]{1,0:T(8,128)S(1)} custom-call(s32[1]{0:T(128)} %constant.69.clone.1.slot_ref, f32[1,1024,4096]{2,1,0:T(8,128)} %inv_ref.3, bf16[32,4096]{1,0:T(8,128)(2,1)S(1)} %pad_maximum_fusion.rcat_ref, bf16[16,4096]{1,0:T(8,128)(2,1)S(1)} %get-tuple-element.64.r1_ref), custom_call_target="tpu_custom_call" | custom-call | flops 402653184 | bytes 16777216 | tf_op jit(solution)/shard_map/pallas_call | solution.py:116
  45.8 0.6 bitcast_bitcast_fusion.1
  46.4 3.8 %all-to-all-start.1 = ((f32[8,16,128]{2,1,0:T(8,128)}), f32[8,16,128]{2,1,0:T(8,128)S(1)}, u32[]{:S(2)}, u32[]{:S(2)}) async-start(f32[8,16,128]{2,1,0:T(8,128)} %bitcast_bitcast_fusion.1), calls=%async_computation.1 | async-start | bytes 131072 | tf_op jit(solution)/shard_map/all_to_all | solution.py:150
  50.3 5.0 %all-to-all-done.1 = f32[8,16,128]{2,1,0:T(8,128)S(1)} async-done(((f32[8,16,128]{2,1,0:T(8,128)}), f32[8,16,128]{2,1,0:T(8,128)S(1)}, u32[]{:S(2)}, u32[]{:S(2)}) %all-to-all-start.1) | async-done | bytes 65568 | tf_op jit(solution)/shard_map/all_to_all | solution.py:150
  55.3 0.7 broadcast_in_dim.14
  56.0 3.3 %all-to-all-start.2 = ((f32[32,16,128]{2,1,0:T(8,128)}), f32[32,16,128]{2,1,0:T(8,128)}, u32[]{:S(2)}, u32[]{:S(2)}) async-start(f32[32,16,128]{2,1,0:T(8,128)} %broadcast_in_dim.14), calls=%async_computation.2 | async-start | bytes 524288 | tf_op jit(solution)/shard_map/all_to_all | solution.py:20
  59.3 8.4 %fusion = (bf16[1024,4096]{1,0:T(8,128)(2,1)}, bf16[1024,4096]{1,0:T(8,128)(2,1)}) fusion(f32[4096]{0:T(1024)S(1)} %bitcast.126, f32[1024]{0:T(1024)S(1)} %get-tuple-element.74, bf16[96,1024]{1,0:T(8,128)(2,1)S(1)} %constant_dynamic-update-slice_fusion.2, bf16[96,4096]{1,0:T(8,128)(2,1)S(1)} %constant_dynamic-update-slice_fusion.8), kind=kOutput, calls=%fused_computation.4 | convolution fusion | flops 834666496 | bytes 17780736 | tf_op jit(solution)/shard_map/dot_general | solution.py:38
  67.8 1.9 %fusion.4 = (bf16[128,4096]{1,0:T(8,128)(2,1)S(1)}, bf16[128,4096]{1,0:T(8,128)(2,1)S(1)}) fusion(bf16[96,128]{0,1:T(8,128)(2,1)S(1)} %concatenate.60, bf16[96,4096]{1,0:T(8,128)(2,1)} %copy-done.5, f32[4096]{0:T(1024)S(1)} %bitcast.127, f32[128]{0:T(128)S(1)} %get-tuple-element.66), kind=kOutput, calls=%fused_computation.13 | convolution fusion | flops 104333312 | bytes 2925056 | tf_op jit(solution)/shard_map/dot_general | solution.py:38
  69.7 1.1 copy.106
  71.2 0.6 reduce-precision_convert_fusion.23
  71.8 0.7 shard_map.78
  72.6 1.8 %fusion.5 = f32[48,128]{0,1:T(8,128)S(1)} fusion(bf16[16,128]{1,0:T(8,128)(2,1)S(1)} %get-tuple-element.62, bf16[16,128]{1,0:T(8,128)(2,1)} %get-tuple-element.63, bf16[16,128]{1,0:T(8,128)(2,1)S(1)} %get-tuple-element.61, s32[1024]{0:T(1024)S(1)} %add_bitcast_fusion, pred[1024]{0:T(1024)(128)(4,1)} %copy-done.7, s32[1024]{0:T(1024)S(1)} %add_bitcast_fusion.1, ...), kind=kOutput, calls=%fused_computation.15 | convolution fusion | flops 35704832 | bytes 47104 | tf_op jit(solution)/shard_map/dot_general | solution.py:83
  74.4 0.9 fusion.33
  75.5 0.7 broadcast_in_dim.15
  76.2 5.9 %all-to-all-start.3 = ((f32[32,16,128]{2,1,0:T(8,128)}), f32[32,16,128]{2,1,0:T(8,128)S(1)}, u32[]{:S(2)}, u32[]{:S(2)}) async-start(f32[32,16,128]{2,1,0:T(8,128)} %broadcast_in_dim.15), calls=%async_computation.3 | async-start | bytes 524288 | tf_op jit(solution)/shard_map/all_to_all | solution.py:20
  82.5 8.4 %fusion.1 = (bf16[1024,4096]{1,0:T(8,128)(2,1)}, bf16[1024,4096]{1,0:T(8,128)(2,1)}) fusion(f32[4096]{0:T(1024)S(1)} %multiply_reduce_fusion, f32[1024]{0:T(1024)S(1)} %multiply_reduce_fusion.2, bf16[96,1024]{1,0:T(8,128)(2,1)S(1)} %constant_dynamic-update-slice_fusion.13, bf16[96,4096]{1,0:T(8,128)(2,1)S(1)} %constant_dynamic-update-slice_fusion.19), kind=kOutput, calls=%fused_computation.5 | convolution fusion | flops 834666496 | bytes 17780736 | tf_op jit(solution)/shard_map/dot_general | solution.py:38
  90.9 1.3 all-to-all-done.3
  92.3 8.2 %shard_map.79 = f32[16,1024]{1,0:T(8,128)S(1)} custom-call(s32[1]{0:T(128)} %constant.69.clone.1.slot_ref, f32[1,1024,4096]{2,1,0:T(8,128)} %inv_ref.3, bf16[32,4096]{1,0:T(8,128)(2,1)S(1)} %pad_maximum_fusion.2.rcat_ref, bf16[16,4096]{1,0:T(8,128)(2,1)S(1)} %get-tuple-element.57.r1_ref), custom_call_target="tpu_custom_call" | custom-call | flops 402653184 | bytes 16777216 | tf_op jit(solution)/shard_map/pallas_call | solution.py:116
  100.5 0.6 bitcast_bitcast_fusion
  101.1 3.4 %all-to-all-start.4 = ((f32[8,16,128]{2,1,0:T(8,128)}), f32[8,16,128]{2,1,0:T(8,128)S(1)}, u32[]{:S(2)}, u32[]{:S(2)}) async-start(f32[8,16,128]{2,1,0:T(8,128)} %bitcast_bitcast_fusion), calls=%async_computation.4 | async-start | bytes 131072 | tf_op jit(solution)/shard_map/all_to_all | solution.py:150
  104.5 0.5 fusion.42
  105.0 4.5 %all-to-all-done.4 = f32[8,16,128]{2,1,0:T(8,128)S(1)} async-done(((f32[8,16,128]{2,1,0:T(8,128)}), f32[8,16,128]{2,1,0:T(8,128)S(1)}, u32[]{:S(2)}, u32[]{:S(2)}) %all-to-all-start.4) | async-done | bytes 65568 | tf_op jit(solution)/shard_map/all_to_all | solution.py:150
  109.4 0.7 broadcast_in_dim.17
  110.2 2.9 %all-to-all-start.5 = ((f32[32,16,128]{2,1,0:T(8,128)}), f32[32,16,128]{2,1,0:T(8,128)S(1)}, u32[]{:S(2)}, u32[]{:S(2)}) async-start(f32[32,16,128]{2,1,0:T(8,128)} %broadcast_in_dim.17), calls=%async_computation.5 | async-start | bytes 524288 | tf_op jit(solution)/shard_map/all_to_all | solution.py:20
  113.2 8.6 %shard_map.80 = f32[1024,16]{1,0:T(8,128)S(1)} custom-call(bf16[1024,4096]{1,0:T(8,128)(2,1)} %get-tuple-element.13.k1_ref, bf16[1024,4096]{1,0:T(8,128)(2,1)} %get-tuple-element.14.k2_ref, bf16[32,4096]{1,0:T(8,128)(2,1)S(1)} %pad_maximum_fusion.3.d12_ref, bf16[16,4096]{1,0:T(8,128)(2,1)S(1)} %get-tuple-element.53.d1_ref), custom_call_target="tpu_custom_call" | custom-call | flops 402653184 | bytes 17170432 | tf_op jit(solution)/shard_map/pallas_call | solution.py:61
  121.8 1.5 %all-to-all-done.5 = f32[32,16,128]{2,1,0:T(8,128)S(1)} async-done(((f32[32,16,128]{2,1,0:T(8,128)}), f32[32,16,128]{2,1,0:T(8,128)S(1)}, u32[]{:S(2)}, u32[]{:S(2)}) %all-to-all-start.5) | async-done | bytes 262176 | tf_op jit(solution)/shard_map/all_to_all | solution.py:20
  123.8 8.6 %shard_map.81 = f32[1024,16]{1,0:T(8,128)S(1)} custom-call(bf16[1024,4096]{1,0:T(8,128)(2,1)} %get-tuple-element.21.k1_ref, bf16[1024,4096]{1,0:T(8,128)(2,1)} %get-tuple-element.22.k2_ref, bf16[32,4096]{1,0:T(8,128)(2,1)S(1)} %pad_maximum_fusion.4.d12_ref, bf16[16,4096]{1,0:T(8,128)(2,1)S(1)} %get-tuple-element.55.d1_ref), custom_call_target="tpu_custom_call" | custom-call | flops 402653184 | bytes 17170432 | tf_op jit(solution)/shard_map/pallas_call | solution.py:61
  132.9 0.6 add_add_fusion
  133.5 0.8 copy.123
  134.3 0.8 copy.124
  (80 shorter events, 3.8 us)
Async XLA Ops:
  3.9 15.0 %copy-start.7 = (pred[1024]{0:T(1024)(128)(4,1)}, pred[1024]{0:T(1024)(128)(4,1)S(1)}, u32[]{:S(2)}) copy-start(pred[1024]{0:T(1024)(128)(4,1)S(1)} %get-tuple-element.77) | copy-start | bytes 3076
  3.9 15.0 %copy-start.9 = (pred[1024]{0:T(1024)(128)(4,1)}, pred[1024]{0:T(1024)(128)(4,1)S(1)}, u32[]{:S(2)}) copy-start(pred[1024]{0:T(1024)(128)(4,1)S(1)} %get-tuple-element.35) | copy-start | bytes 3076
  8.4 10.6 %copy-start.4 = (f32[32,256]{0,1:T(8,128)}, f32[32,256]{0,1:T(8,128)S(1)}, u32[]{:S(2)}) copy-start(f32[32,256]{0,1:T(8,128)S(1)} %slice_add_fusion.4) | copy-start | bytes 98308
  9.7 26.9 %all-to-all-start = ((f32[32,48,128]{2,1,0:T(8,128)}), f32[32,48,128]{2,1,0:T(8,128)S(1)}, u32[]{:S(2)}, u32[]{:S(2)}) async-start(f32[32,48,128]{2,1,0:T(8,128)} %broadcast_in_dim.12), calls=%async_computation | async-start | bytes 1572864 | tf_op jit(solution)/shard_map/all_to_all | solution.py:20
  46.4 8.9 %all-to-all-start.1 = ((f32[8,16,128]{2,1,0:T(8,128)}), f32[8,16,128]{2,1,0:T(8,128)S(1)}, u32[]{:S(2)}, u32[]{:S(2)}) async-start(f32[8,16,128]{2,1,0:T(8,128)} %bitcast_bitcast_fusion.1), calls=%async_computation.1 | async-start | bytes 131072 | tf_op jit(solution)/shard_map/all_to_all | solution.py:150
  50.3 17.5 %copy-start.5 = (bf16[96,4096]{1,0:T(8,128)(2,1)}, bf16[96,4096]{1,0:T(8,128)(2,1)S(1)}, u32[]{:S(2)}) copy-start(bf16[96,4096]{1,0:T(8,128)(2,1)S(1)} %constant_dynamic-update-slice_fusion.8) | copy-start | bytes 2359300
  56.0 13.7 %all-to-all-start.2 = ((f32[32,16,128]{2,1,0:T(8,128)}), f32[32,16,128]{2,1,0:T(8,128)}, u32[]{:S(2)}, u32[]{:S(2)}) async-start(f32[32,16,128]{2,1,0:T(8,128)} %broadcast_in_dim.14), calls=%async_computation.2 | async-start | bytes 524288 | tf_op jit(solution)/shard_map/all_to_all | solution.py:20
  59.3 10.3 %copy-start.3 = (f32[32,2,8,128]{3,2,1,0:T(8,128)S(1)}, f32[32,2,8,128]{3,2,1,0:T(8,128)}, u32[]{:S(2)}) copy-start(f32[32,2,8,128]{3,2,1,0:T(8,128)} %get-tuple-element.46) | copy-start | bytes 786436
  59.3 16.1 %copy-start = (f32[16,1024]{1,0:T(8,128)S(1)}, f32[16,1024]{1,0:T(8,128)}, u32[]{:S(2)}) copy-start(f32[16,1024]{1,0:T(8,128)} %param.6) | copy-start | bytes 196612
  71.1 1.4 %copy-start.1 = (f32[2,8,32,128]{3,1,2,0:T(8,128)}, f32[2,8,32,128]{3,1,2,0:T(8,128)S(1)}, u32[]{:S(2)}) copy-start(f32[2,8,32,128]{3,1,2,0:T(8,128)S(1)} %copy.173) | copy-start | bytes 786436
  76.2 16.0 %all-to-all-start.3 = ((f32[32,16,128]{2,1,0:T(8,128)}), f32[32,16,128]{2,1,0:T(8,128)S(1)}, u32[]{:S(2)}, u32[]{:S(2)}) async-start(f32[32,16,128]{2,1,0:T(8,128)} %broadcast_in_dim.15), calls=%async_computation.3 | async-start | bytes 524288 | tf_op jit(solution)/shard_map/all_to_all | solution.py:20
  90.9 13.6 %copy-start.6 = (bf16[16,128]{1,0:T(8,128)(2,1)S(1)}, bf16[16,128]{1,0:T(8,128)(2,1)}, u32[]{:S(2)}) copy-start(bf16[16,128]{1,0:T(8,128)(2,1)} %get-tuple-element.63) | copy-start | bytes 12292
  90.9 13.6 %copy-start.10 = (pred[1024]{0:T(1024)(128)(4,1)S(1)}, pred[1024]{0:T(1024)(128)(4,1)}, u32[]{:S(2)}) copy-start(pred[1024]{0:T(1024)(128)(4,1)} %copy-done.9) | copy-start | bytes 3076
  90.9 22.2 %copy-start.2 = (f32[2,8,32,128]{3,1,2,0:T(8,128)S(1)}, f32[2,8,32,128]{3,1,2,0:T(8,128)}, u32[]{:S(2)}) copy-start(f32[2,8,32,128]{3,1,2,0:T(8,128)} %copy-done.1) | copy-start | bytes 786436
  101.1 8.3 %all-to-all-start.4 = ((f32[8,16,128]{2,1,0:T(8,128)}), f32[8,16,128]{2,1,0:T(8,128)S(1)}, u32[]{:S(2)}, u32[]{:S(2)}) async-start(f32[8,16,128]{2,1,0:T(8,128)} %bitcast_bitcast_fusion), calls=%async_computation.4 | async-start | bytes 131072 | tf_op jit(solution)/shard_map/all_to_all | solution.py:150
  110.2 13.1 %all-to-all-start.5 = ((f32[32,16,128]{2,1,0:T(8,128)}), f32[32,16,128]{2,1,0:T(8,128)S(1)}, u32[]{:S(2)}, u32[]{:S(2)}) async-start(f32[32,16,128]{2,1,0:T(8,128)} %broadcast_in_dim.17), calls=%async_computation.5 | async-start | bytes 524288 | tf_op jit(solution)/shard_map/all_to_all | solution.py:20
  113.2 19.3 %copy-start.8 = (pred[1024]{0:T(1024)(128)(4,1)S(1)}, pred[1024]{0:T(1024)(128)(4,1)}, u32[]{:S(2)}) copy-start(pred[1024]{0:T(1024)(128)(4,1)} %copy-done.7) | copy-start | bytes 3076

commit v19 on v15

--- a/solution.py
+++ b/solution.py
@@ -28,7 +28,7 @@
     return x1.astype(jnp.bfloat16), x2.astype(jnp.bfloat16), r2.astype(jnp.bfloat16)
 
 
-def kern(u, v):
+def kern(u, v, keep=True):
     nu = jnp.sum(u * u, axis=0)
     nv = jnp.sum(v * v, axis=0)
     u1, u2, u3 = split3(u)
@@ -37,7 +37,7 @@
     right = jnp.concatenate([v1, v2, v1, v3, v1, v2], axis=0)
     cross2 = lax.dot_general(left, right, (((0,), (0,)), ((), ())), preferred_element_type=jnp.float32)
     kernel = jnp.exp(-kernel_scale * ((nu[:, None] + nv[None, :]) + cross2))
-    return lax.optimization_barrier(kernel)
+    return lax.optimization_barrier(kernel) if keep else kernel
 
 
 def apply_kernel(delta, kernel):
@@ -141,7 +141,7 @@
     delta0 = solve(block_res0, block0)
     owned0 = lax.dynamic_slice_in_dim(delta0, mine * per, per, axis=1)
     kernel0 = kern(points, block_pts0)
-    early = apply_kernel(delta0, kern(pts1_local, block_pts0))
+    early = apply_kernel(delta0, kern(pts1_local, block_pts0, keep=False))
     overlap = lax.dot_general(sel0, sel1, (((0,), (0,)), ((), ())), preferred_element_type=jnp.float32)
     overlap = overlap.astype(jnp.bfloat16)
     res1_local = res1_start - early - ridge_weight * exact_dot(owned0, overlap, plain)

time: 132 us -> 131 us (level)
  waiting for transfers between devices: 19.7 us -> 23.6 us
  other arithmetic: 15.2 us -> 11.6 us
    all_to_all x4, waiting for transfers between devices: 10.8 us -> 14.1 us  [gather_all(): return lax.all_to_all(sent, ALL, 0, 0, tiled=True)]
    unnamed x26, other arithmetic: 7.74 us -> 4.7 us
  transfers between devices with their start and end apart: 6 -> 6, of which waited for: 5 -> 5; matrix products, arithmetic and copies ran while one was open for 28% -> 25% of each run, Pallas kernels for 0% -> 0%
where the time goes in v19:
time: 131 us; the launch traced here: 130 us
  matrix products  41.2 us (31%)
  starting transfers between devices  24.6 us (19%)
  waiting for transfers between devices  23.6 us (18%)
  Pallas kernels  16.4 us (13%)
  other arithmetic  11.6 us (9%)
  local copies, waits for them, and re-layouts  7.66 us (6%)
  between operations  4.92 us (4%)
    dot_general x3, matrix products, apply_kernel(): lax.dot_general(delta, kernel, (((1,), (1,)), ((), ())), precision=HIGH)  21.9 us
    all_to_all x4, starting transfers between devices, gather_all(): return lax.all_to_all(sent, ALL, 0, 0, tiled=True)  17.4 us
    pallas_call x2, Pallas kernels, solve_rows(): pl.pallas_call(solve_kernel, grid_spec=grid_spec, out_shape=jax.ShapeDtyp...  16.4 us
    dot_general x3, matrix products, kern(): lax.dot_general(left, right, (((0,), (0,)), ((), ())), preferred_element_...  16.3 us
    all_to_all x4, waiting for transfers between devices, gather_all(): return lax.all_to_all(sent, ALL, 0, 0, tiled=True)  14.1 us
    all_to_all x2, waiting for transfers between devices, distribute(): scattered = lax.all_to_all(pieces, 'grp', 0, 0, tiled=True)  9.45 us
    all_to_all x2, starting transfers between devices, distribute(): scattered = lax.all_to_all(pieces, 'grp', 0, 0, tiled=True)  7.18 us
    unnamed x26, other arithmetic  4.7 us
  transfers between devices with their start and end apart: 6, of which 5 were waited for; matrix products, arithmetic and copies ran while one was open for 25% of the time, Pallas kernels for 0%

profile of v19, /device:TPU:0, one launch (start us, length us, event | category | flops | bytes accessed | tf_op | source)
XLA Modules:
  0.0 130.0 jit_solution(9837943685443417264)
XLA Ops:
  0.6 1.4 %fusion.48 = (s32[1]{0:T(128)}, s32[1]{0:T(128)}) fusion(s32[2]{0:T(128)} %param.10), kind=kLoop, calls=%fused_computation.153 | loop fusion | bytes 16 | tf_op jit(solution)/shard_map/slice | solution.py:126
  2.0 2.0 %convert_bitcast_fusion.1 = (s32[8,128]{1,0:T(8,128)S(1)}, pred[1024]{0:T(1024)(128)(4,1)S(1)}, s32[8,128]{1,0:T(8,128)S(1)}, pred[1024]{0:T(1024)(128)(4,1)S(1)}) fusion(s32[1024]{0:T(1024)} %param.9, s32[]{:T(128)} %bitcast, s32[]{:T(128)} %bitcast.3), kind=kLoop, calls=%fused_computation.143 | loop fusion | flops 4096 | bytes 14344 | tf_op jit(solution)/shard_map/convert
  4.0 0.3 reduce-window.16
  4.6 0.3 reduce-window.24
  5.1 0.8 constant_dynamic-update-slice_fusion.1
  6.0 0.9 multiply_reduce_fusion.3
  6.9 0.9 fusion.10
  7.8 0.3 fusion.6
  8.1 0.5 multiply_reduce_fusion.4
  8.7 0.9 broadcast_in_dim.12
  9.6 7.3 %all-to-all-start = ((f32[32,48,128]{2,1,0:T(8,128)}), f32[32,48,128]{2,1,0:T(8,128)S(1)}, u32[]{:S(2)}, u32[]{:S(2)}) async-start(f32[32,48,128]{2,1,0:T(8,128)} %broadcast_in_dim.12), calls=%async_computation | async-start | bytes 1572864 | tf_op jit(solution)/shard_map/all_to_all | solution.py:20
  20.8 0.8 constant_dynamic-update-slice_fusion.18
  21.7 0.8 constant_dynamic-update-slice_fusion.17
  22.5 0.8 constant_dynamic-update-slice_fusion.16
  23.4 0.8 constant_dynamic-update-slice_fusion.15
  24.2 0.9 constant_dynamic-update-slice_fusion.14
  25.1 0.9 constant_dynamic-update-slice_fusion.13
  25.9 10.6 %all-to-all-done = f32[32,48,128]{2,1,0:T(8,128)S(1)} async-done(((f32[32,48,128]{2,1,0:T(8,128)}), f32[32,48,128]{2,1,0:T(8,128)S(1)}, u32[]{:S(2)}, u32[]{:S(2)}) %all-to-all-start) | async-done | bytes 786464 | tf_op jit(solution)/shard_map/all_to_all | solution.py:20
  36.8 8.2 %shard_map.77 = f32[16,1024]{1,0:T(8,128)S(1)} custom-call(s32[1]{0:T(128)} %constant.64.clone.1.slot_ref, f32[1,1024,4096]{2,1,0:T(8,128)} %inv_ref.3, bf16[32,4096]{1,0:T(8,128)(2,1)S(1)} %pad_maximum_fusion.rcat_ref, bf16[16,4096]{1,0:T(8,128)(2,1)S(1)} %get-tuple-element.28.r1_ref), custom_call_target="tpu_custom_call" | custom-call | flops 402653184 | bytes 16777216 | tf_op jit(solution)/shard_map/pallas_call | solution.py:83
  45.1 0.6 bitcast_bitcast_fusion.1
  45.7 3.8 %all-to-all-start.1 = ((f32[8,16,128]{2,1,0:T(8,128)}), f32[8,16,128]{2,1,0:T(8,128)S(1)}, u32[]{:S(2)}, u32[]{:S(2)}) async-start(f32[8,16,128]{2,1,0:T(8,128)} %bitcast_bitcast_fusion.1), calls=%async_computation.1 | async-start | bytes 131072 | tf_op jit(solution)/shard_map/all_to_all | solution.py:117
  49.5 5.0 %all-to-all-done.1 = f32[8,16,128]{2,1,0:T(8,128)S(1)} async-done(((f32[8,16,128]{2,1,0:T(8,128)}), f32[8,16,128]{2,1,0:T(8,128)S(1)}, u32[]{:S(2)}, u32[]{:S(2)}) %all-to-all-start.1) | async-done | bytes 65568 | tf_op jit(solution)/shard_map/all_to_all | solution.py:117
  54.5 0.7 broadcast_in_dim.14
  55.3 2.9 %all-to-all-start.2 = ((f32[32,16,128]{2,1,0:T(8,128)}), f32[32,16,128]{2,1,0:T(8,128)S(1)}, u32[]{:S(2)}, u32[]{:S(2)}) async-start(f32[32,16,128]{2,1,0:T(8,128)} %broadcast_in_dim.14), calls=%async_computation.2 | async-start | bytes 524288 | tf_op jit(solution)/shard_map/all_to_all | solution.py:20
  58.2 7.6 %multiply_exponential_fusion.1 = f32[1024,4096]{1,0:T(8,128)} fusion(bf16[96,1024]{1,0:T(8,128)(2,1)S(1)} %constant_dynamic-update-slice_fusion.13, bf16[96,4096]{1,0:T(8,128)(2,1)S(1)} %constant_dynamic-update-slice_fusion.8, f32[4096]{0:T(1024)S(1)} %bitcast.113, f32[1024]{0:T(1024)S(1)} %get-tuple-element.33), kind=kOutput, calls=%fused_computation.1 | convolution fusion | flops 817889280 | bytes 17780736 | tf_op jit(solution)/shard_map/dot_general | solution.py:38
  65.8 1.2 fusion.1
  67.0 1.4 %all-to-all-done.2 = f32[32,16,128]{2,1,0:T(8,128)S(1)} async-done(((f32[32,16,128]{2,1,0:T(8,128)}), f32[32,16,128]{2,1,0:T(8,128)S(1)}, u32[]{:S(2)}, u32[]{:S(2)}) %all-to-all-start.2) | async-done | bytes 262176 | tf_op jit(solution)/shard_map/all_to_all | solution.py:20
  68.4 0.2 copy.18
  68.5 0.2 copy.62
  68.7 1.7 %fusion.4 = f32[48,128]{1,0:T(8,128)S(1)} fusion(bf16[16,128]{1,0:T(8,128)(2,1)S(1)} %get-tuple-element.27, bf16[16,128]{1,0:T(8,128)(2,1)S(1)} %get-tuple-element.26, bf16[16,128]{1,0:T(8,128)(2,1)S(1)} %get-tuple-element.25, s32[1024]{0:T(1024)S(1)} %add_bitcast_fusion, pred[1024]{0:T(1024)(128)(4,1)} %copy-done.3, s32[1024]{0:T(1024)S(1)} %add_bitcast_fusion.1, ...), kind=kOutput, calls=%fused_computation.10 | convolution fusion | flops 35704832 | bytes 47104 | tf_op jit(solution)/shard_map/dot_general | solution.py:50
  70.5 1.0 fusion.5
  71.6 0.7 broadcast_in_dim.15
  72.3 4.6 %all-to-all-start.3 = ((f32[32,16,128]{2,1,0:T(8,128)}), f32[32,16,128]{2,1,0:T(8,128)S(1)}, u32[]{:S(2)}, u32[]{:S(2)}) async-start(f32[32,16,128]{2,1,0:T(8,128)} %broadcast_in_dim.15), calls=%async_computation.3 | async-start | bytes 524288 | tf_op jit(solution)/shard_map/all_to_all | solution.py:20
  77.2 7.6 %multiply_exponential_fusion = f32[1024,4096]{1,0:T(8,128)} fusion(bf16[96,1024]{1,0:T(8,128)(2,1)S(1)} %constant_dynamic-update-slice_fusion.19, bf16[96,4096]{1,0:T(8,128)(2,1)S(1)} %constant_dynamic-update-slice_fusion.25, f32[4096]{0:T(1024)S(1)} %multiply_reduce_fusion, f32[1024]{0:T(1024)S(1)} %multiply_reduce_fusion.2), kind=kOutput, calls=%fused_computation | convolution fusion | flops 817889280 | bytes 17780736 | tf_op jit(solution)/shard_map/dot_general | solution.py:38
  84.8 2.1 %all-to-all-done.3 = f32[32,16,128]{2,1,0:T(8,128)S(1)} async-done(((f32[32,16,128]{2,1,0:T(8,128)}), f32[32,16,128]{2,1,0:T(8,128)S(1)}, u32[]{:S(2)}, u32[]{:S(2)}) %all-to-all-start.3) | async-done | bytes 262176 | tf_op jit(solution)/shard_map/all_to_all | solution.py:20
  87.0 8.2 %shard_map.78 = f32[16,1024]{1,0:T(8,128)S(1)} custom-call(s32[1]{0:T(128)} %constant.64.clone.1.slot_ref, f32[1,1024,4096]{2,1,0:T(8,128)} %inv_ref.3, bf16[32,4096]{1,0:T(8,128)(2,1)S(1)} %pad_maximum_fusion.1.rcat_ref, bf16[16,4096]{1,0:T(8,128)(2,1)S(1)} %get-tuple-element.23.r1_ref), custom_call_target="tpu_custom_call" | custom-call | flops 402653184 | bytes 16777216 | tf_op jit(solution)/shard_map/pallas_call | solution.py:83
  95.3 0.6 bitcast_bitcast_fusion
  95.9 3.4 %all-to-all-start.4 = ((f32[8,16,128]{2,1,0:T(8,128)}), f32[8,16,128]{2,1,0:T(8,128)S(1)}, u32[]{:S(2)}, u32[]{:S(2)}) async-start(f32[8,16,128]{2,1,0:T(8,128)} %bitcast_bitcast_fusion), calls=%async_computation.4 | async-start | bytes 131072 | tf_op jit(solution)/shard_map/all_to_all | solution.py:117
  99.3 0.5 fusion.36
  99.8 4.5 %all-to-all-done.4 = f32[8,16,128]{2,1,0:T(8,128)S(1)} async-done(((f32[8,16,128]{2,1,0:T(8,128)}), f32[8,16,128]{2,1,0:T(8,128)S(1)}, u32[]{:S(2)}, u32[]{:S(2)}) %all-to-all-start.4) | async-done | bytes 65568 | tf_op jit(solution)/shard_map/all_to_all | solution.py:117
  104.2 0.7 broadcast_in_dim.17
  104.9 2.6 %all-to-all-start.5 = ((f32[32,16,128]{2,1,0:T(8,128)}), f32[32,16,128]{2,1,0:T(8,128)S(1)}, u32[]{:S(2)}, u32[]{:S(2)}) async-start(f32[32,16,128]{2,1,0:T(8,128)} %broadcast_in_dim.17), calls=%async_computation.5 | async-start | bytes 524288 | tf_op jit(solution)/shard_map/all_to_all | solution.py:20
  107.5 10.2 %fusion.3 = f32[16,1024]{1,0:T(8,128)S(1)} fusion(f32[16,1024]{1,0:T(8,128)S(1)} %copy-done.1, f32[16,4096]{1,0:T(8,128)S(1)} %bitcast.109, f32[1024,4096]{1,0:T(8,128)} %multiply_exponential_fusion.1, f32[48,1024]{1,0:T(8,128)S(1)} %fusion.36), kind=kOutput, calls=%fused_computation.8 | convolution fusion | flops 402735104 | bytes 17367040 | tf_op jit(solution)/shard_map/dot_general | solution.py:44
  117.7 0.2 copy.23
  117.9 0.2 copy.61
  118.1 0.5 fusion.26
  118.6 0.7 add_add_fusion
  119.2 10.8 %fusion.2 = f32[16,1024]{1,0:T(8,128)} fusion(f32[16,1024]{1,0:T(8,128)S(1)} %fusion.3, f32[1024,4096]{1,0:T(8,128)} %multiply_exponential_fusion, f32[2,8,32,128]{3,2,1,0:T(8,128)S(1)} %bitcast.105, f32[48,1024]{1,0:T(8,128)S(1)} %fusion.26), kind=kOutput, calls=%fused_computation.6 | convolution fusion | flops 402735104 | bytes 17367040 | tf_op jit(solution)/shard_map/dot_general | solution.py:44
  (63 shorter events, 1.5 us)
Async XLA Ops:
  4.0 32.5 %copy-start.3 = (pred[1024]{0:T(1024)(128)(4,1)}, pred[1024]{0:T(1024)(128)(4,1)S(1)}, u32[]{:S(2)}) copy-start(pred[1024]{0:T(1024)(128)(4,1)S(1)} %get-tuple-element.38) | copy-start | bytes 3076
  4.0 32.5 %copy-start.5 = (pred[1024]{0:T(1024)(128)(4,1)}, pred[1024]{0:T(1024)(128)(4,1)S(1)}, u32[]{:S(2)}) copy-start(pred[1024]{0:T(1024)(128)(4,1)S(1)} %get-tuple-element.13) | copy-start | bytes 3076
  9.6 26.9 %all-to-all-start = ((f32[32,48,128]{2,1,0:T(8,128)}), f32[32,48,128]{2,1,0:T(8,128)S(1)}, u32[]{:S(2)}, u32[]{:S(2)}) async-start(f32[32,48,128]{2,1,0:T(8,128)} %broadcast_in_dim.12), calls=%async_computation | async-start | bytes 1572864 | tf_op jit(solution)/shard_map/all_to_all | solution.py:20
  45.0 26.5 %copy-start = (f32[16,1024]{1,0:T(8,128)S(1)}, f32[16,1024]{1,0:T(8,128)}, u32[]{:S(2)}) copy-start(f32[16,1024]{1,0:T(8,128)} %param.6) | copy-start | bytes 196612
  45.7 8.9 %all-to-all-start.1 = ((f32[8,16,128]{2,1,0:T(8,128)}), f32[8,16,128]{2,1,0:T(8,128)S(1)}, u32[]{:S(2)}, u32[]{:S(2)}) async-start(f32[8,16,128]{2,1,0:T(8,128)} %bitcast_bitcast_fusion.1), calls=%async_computation.1 | async-start | bytes 131072 | tf_op jit(solution)/shard_map/all_to_all | solution.py:117
  55.3 13.1 %all-to-all-start.2 = ((f32[32,16,128]{2,1,0:T(8,128)}), f32[32,16,128]{2,1,0:T(8,128)S(1)}, u32[]{:S(2)}, u32[]{:S(2)}) async-start(f32[32,16,128]{2,1,0:T(8,128)} %broadcast_in_dim.14), calls=%async_computation.2 | async-start | bytes 524288 | tf_op jit(solution)/shard_map/all_to_all | solution.py:20
  72.3 14.7 %all-to-all-start.3 = ((f32[32,16,128]{2,1,0:T(8,128)}), f32[32,16,128]{2,1,0:T(8,128)S(1)}, u32[]{:S(2)}, u32[]{:S(2)}) async-start(f32[32,16,128]{2,1,0:T(8,128)} %broadcast_in_dim.15), calls=%async_computation.3 | async-start | bytes 524288 | tf_op jit(solution)/shard_map/all_to_all | solution.py:20
  77.2 22.0 %copy-start.6 = (pred[1024]{0:T(1024)(128)(4,1)S(1)}, pred[1024]{0:T(1024)(128)(4,1)}, u32[]{:S(2)}) copy-start(pred[1024]{0:T(1024)(128)(4,1)} %copy-done.5) | copy-start | bytes 3076
  77.2 30.3 %copy-start.1 = (f32[16,1024]{1,0:T(8,128)S(1)}, f32[16,1024]{1,0:T(8,128)}, u32[]{:S(2)}) copy-start(f32[16,1024]{1,0:T(8,128)} %param.7) | copy-start | bytes 196612
  87.0 31.1 %copy-start.4 = (pred[1024]{0:T(1024)(128)(4,1)S(1)}, pred[1024]{0:T(1024)(128)(4,1)}, u32[]{:S(2)}) copy-start(pred[1024]{0:T(1024)(128)(4,1)} %copy-done.3) | copy-start | bytes 3076
  87.0 31.6 %copy-start.2 = (f32[16,1024]{1,0:T(8,128)S(1)}, f32[16,1024]{1,0:T(8,128)}, u32[]{:S(2)}) copy-start(f32[16,1024]{1,0:T(8,128)} %param.8) | copy-start | bytes 196612
  95.9 8.3 %all-to-all-start.4 = ((f32[8,16,128]{2,1,0:T(8,128)}), f32[8,16,128]{2,1,0:T(8,128)S(1)}, u32[]{:S(2)}, u32[]{:S(2)}) async-start(f32[8,16,128]{2,1,0:T(8,128)} %bitcast_bitcast_fusion), calls=%async_computation.4 | async-start | bytes 131072 | tf_op jit(solution)/shard_map/all_to_all | solution.py:117
  104.9 12.8 %all-to-all-start.5 = ((f32[32,16,128]{2,1,0:T(8,128)}), f32[32,16,128]{2,1,0:T(8,128)S(1)}, u32[]{:S(2)}, u32[]{:S(2)}) async-start(f32[32,16,128]{2,1,0:T(8,128)} %broadcast_in_dim.17), calls=%async_computation.5 | async-start | bytes 524288 | tf_op jit(solution)/shard_map/all_to_all | solution.py:20

commit v20 on v19

--- a/solution.py
+++ b/solution.py
@@ -144,9 +144,11 @@
     early = apply_kernel(delta0, kern(pts1_local, block_pts0, keep=False))
     overlap = lax.dot_general(sel0, sel1, (((0,), (0,)), ((), ())), preferred_element_type=jnp.float32)
     overlap = overlap.astype(jnp.bfloat16)
-    res1_local = res1_start - early - ridge_weight * exact_dot(owned0, overlap, plain)
-    res1_local, pts_late, pts1_late = lax.optimization_barrier((res1_local, points, block_pts1))
-    block_res1 = to_block(gather_all(res1_local, n_dev), rhs)
+    wide = lambda x: jnp.broadcast_to(x[None], (n_dev,) + x.shape)
+    sent1 = wide(res1_start) - wide(early) - ridge_weight * wide(exact_dot(owned0, overlap, plain))
+    res1_local = sent1[0]
+    sent1, pts_late, pts1_late = lax.optimization_barrier((sent1, points, block_pts1))
+    block_res1 = to_block(lax.all_to_all(sent1, ALL, 0, 0, tiled=True), rhs)
     kernel1 = kern(pts_late, pts1_late)
 
     solved1 = solve_rows(inverse, block1 % slots, block_res1)

time: 131 us -> 131 us (level)
    all_to_all x0 -> x1, starting transfers between devices: none -> 4.64 us  [body(): block_res1 = to_block(lax.all_to_all(sent1, ALL, 0, 0, tiled=True), rhs)]
    all_to_all x4 -> x3, starting transfers between devices: 17.4 us -> 12.8 us  [gather_all(): return lax.all_to_all(sent, ALL, 0, 0, tiled=True)]
    all_to_all x0 -> x1, waiting for transfers between devices: none -> 2.12 us  [body(): block_res1 = to_block(lax.all_to_all(sent1, ALL, 0, 0, tiled=True), rhs)]
    all_to_all x4 -> x3, waiting for transfers between devices: 14.1 us -> 12 us  [gather_all(): return lax.all_to_all(sent, ALL, 0, 0, tiled=True)]
    broadcast_in_dim x6 -> x5, local copies, waits for them, and re-layouts: 3.09 us -> 2.37 us  [gather_all(): sent = jnp.broadcast_to(piece[None], (n_dev,) + piece.shape)]
where the time goes in v20:
time: 131 us; the launch traced here: 130 us
  matrix products  41.2 us (31%)
  starting transfers between devices  24.6 us (19%)
  waiting for transfers between devices  23.6 us (18%)
  Pallas kernels  16.4 us (13%)
  other arithmetic  11.6 us (9%)
  local copies, waits for them, and re-layouts  7.68 us (6%)
  between operations  4.92 us (4%)
    dot_general x3, matrix products, apply_kernel(): lax.dot_general(delta, kernel, (((1,), (1,)), ((), ())), precision=HIGH)  21.9 us
    pallas_call x2, Pallas kernels, solve_rows(): pl.pallas_call(solve_kernel, grid_spec=grid_spec, out_shape=jax.ShapeDtyp...  16.4 us
    dot_general x3, matrix products, kern(): lax.dot_general(left, right, (((0,), (0,)), ((), ())), preferred_element_...  16.3 us
    all_to_all x3, starting transfers between devices, gather_all(): return lax.all_to_all(sent, ALL, 0, 0, tiled=True)  12.8 us
    all_to_all x3, waiting for transfers between devices, gather_all(): return lax.all_to_all(sent, ALL, 0, 0, tiled=True)  12 us
    all_to_all x2, waiting for transfers between devices, distribute(): scattered = lax.all_to_all(pieces, 'grp', 0, 0, tiled=True)  9.45 us
    all_to_all x2, starting transfers between devices, distribute(): scattered = lax.all_to_all(pieces, 'grp', 0, 0, tiled=True)  7.18 us
    unnamed x26, other arithmetic  4.68 us
  transfers between devices with their start and end apart: 6, of which 5 were waited for; matrix products, arithmetic and copies ran while one was open for 25% of the time, Pallas kernels for 0%

profile of v20, /device:TPU:0, one launch (start us, length us, event | category | flops | bytes accessed | tf_op | source)
XLA Modules:
  0.0 130.0 jit_solution(15960248240979000705)
XLA Ops:
  0.6 1.4 %fusion.48 = (s32[1]{0:T(128)}, s32[1]{0:T(128)}) fusion(s32[2]{0:T(128)} %param.10), kind=kLoop, calls=%fused_computation.153 | loop fusion | bytes 16 | tf_op jit(solution)/shard_map/slice | solution.py:126
  2.0 2.0 %convert_bitcast_fusion.1 = (s32[8,128]{1,0:T(8,128)S(1)}, pred[1024]{0:T(1024)(128)(4,1)S(1)}, s32[8,128]{1,0:T(8,128)S(1)}, pred[1024]{0:T(1024)(128)(4,1)S(1)}) fusion(s32[1024]{0:T(1024)} %param.9, s32[]{:T(128)} %bitcast, s32[]{:T(128)} %bitcast.3), kind=kLoop, calls=%fused_computation.143 | loop fusion | flops 4096 | bytes 14344 | tf_op jit(solution)/shard_map/convert
  4.0 0.3 reduce-window.16
  4.6 0.3 reduce-window.24
  5.1 0.8 constant_dynamic-update-slice_fusion.1
  6.0 0.9 multiply_reduce_fusion.3
  6.9 0.9 fusion.10
  7.8 0.3 fusion.6
  8.1 0.5 multiply_reduce_fusion.4
  8.7 0.9 broadcast_in_dim.12
  9.6 7.3 %all-to-all-start = ((f32[32,48,128]{2,1,0:T(8,128)}), f32[32,48,128]{2,1,0:T(8,128)S(1)}, u32[]{:S(2)}, u32[]{:S(2)}) async-start(f32[32,48,128]{2,1,0:T(8,128)} %broadcast_in_dim.12), calls=%async_computation | async-start | bytes 1572864 | tf_op jit(solution)/shard_map/all_to_all | solution.py:20
  20.8 0.8 constant_dynamic-update-slice_fusion.18
  21.7 0.8 constant_dynamic-update-slice_fusion.17
  22.5 0.8 constant_dynamic-update-slice_fusion.16
  23.4 0.8 constant_dynamic-update-slice_fusion.15
  24.2 0.9 constant_dynamic-update-slice_fusion.14
  25.1 0.9 constant_dynamic-update-slice_fusion.13
  25.9 10.6 %all-to-all-done = f32[32,48,128]{2,1,0:T(8,128)S(1)} async-done(((f32[32,48,128]{2,1,0:T(8,128)}), f32[32,48,128]{2,1,0:T(8,128)S(1)}, u32[]{:S(2)}, u32[]{:S(2)}) %all-to-all-start) | async-done | bytes 786464 | tf_op jit(solution)/shard_map/all_to_all | solution.py:20
  36.8 8.2 %shard_map.77 = f32[16,1024]{1,0:T(8,128)S(1)} custom-call(s32[1]{0:T(128)} %constant.64.clone.1.slot_ref, f32[1,1024,4096]{2,1,0:T(8,128)} %inv_ref.3, bf16[32,4096]{1,0:T(8,128)(2,1)S(1)} %pad_maximum_fusion.rcat_ref, bf16[16,4096]{1,0:T(8,128)(2,1)S(1)} %get-tuple-element.28.r1_ref), custom_call_target="tpu_custom_call" | custom-call | flops 402653184 | bytes 16777216 | tf_op jit(solution)/shard_map/pallas_call | solution.py:83
  45.1 0.6 bitcast_bitcast_fusion.1
  45.7 3.8 %all-to-all-start.1 = ((f32[8,16,128]{2,1,0:T(8,128)}), f32[8,16,128]{2,1,0:T(8,128)S(1)}, u32[]{:S(2)}, u32[]{:S(2)}) async-start(f32[8,16,128]{2,1,0:T(8,128)} %bitcast_bitcast_fusion.1), calls=%async_computation.1 | async-start | bytes 131072 | tf_op jit(solution)/shard_map/all_to_all | solution.py:117
  49.5 5.0 %all-to-all-done.1 = f32[8,16,128]{2,1,0:T(8,128)S(1)} async-done(((f32[8,16,128]{2,1,0:T(8,128)}), f32[8,16,128]{2,1,0:T(8,128)S(1)}, u32[]{:S(2)}, u32[]{:S(2)}) %all-to-all-start.1) | async-done | bytes 65568 | tf_op jit(solution)/shard_map/all_to_all | solution.py:117
  54.5 0.7 broadcast_in_dim.14
  55.3 2.9 %all-to-all-start.2 = ((f32[32,16,128]{2,1,0:T(8,128)}), f32[32,16,128]{2,1,0:T(8,128)S(1)}, u32[]{:S(2)}, u32[]{:S(2)}) async-start(f32[32,16,128]{2,1,0:T(8,128)} %broadcast_in_dim.14), calls=%async_computation.2 | async-start | bytes 524288 | tf_op jit(solution)/shard_map/all_to_all | solution.py:20
  58.2 7.6 %multiply_exponential_fusion.1 = f32[1024,4096]{1,0:T(8,128)} fusion(bf16[96,1024]{1,0:T(8,128)(2,1)S(1)} %constant_dynamic-update-slice_fusion.13, bf16[96,4096]{1,0:T(8,128)(2,1)S(1)} %constant_dynamic-update-slice_fusion.8, f32[4096]{0:T(1024)S(1)} %bitcast.113, f32[1024]{0:T(1024)S(1)} %get-tuple-element.33), kind=kOutput, calls=%fused_computation.1 | convolution fusion | flops 817889280 | bytes 17780736 | tf_op jit(solution)/shard_map/dot_general | solution.py:38
  65.8 1.2 fusion.1
  67.0 1.4 %all-to-all-done.2 = f32[32,16,128]{2,1,0:T(8,128)S(1)} async-done(((f32[32,16,128]{2,1,0:T(8,128)}), f32[32,16,128]{2,1,0:T(8,128)S(1)}, u32[]{:S(2)}, u32[]{:S(2)}) %all-to-all-start.2) | async-done | bytes 262176 | tf_op jit(solution)/shard_map/all_to_all | solution.py:20
  68.4 0.2 copy.18
  68.5 0.2 copy.62
  68.7 1.7 %fusion.4 = f32[48,128]{1,0:T(8,128)S(1)} fusion(bf16[16,128]{1,0:T(8,128)(2,1)S(1)} %get-tuple-element.27, bf16[16,128]{1,0:T(8,128)(2,1)S(1)} %get-tuple-element.26, bf16[16,128]{1,0:T(8,128)(2,1)S(1)} %get-tuple-element.25, s32[1024]{0:T(1024)S(1)} %add_bitcast_fusion, pred[1024]{0:T(1024)(128)(4,1)} %copy-done.3, s32[1024]{0:T(1024)S(1)} %add_bitcast_fusion.1, ...), kind=kOutput, calls=%fused_computation.10 | convolution fusion | flops 35704832 | bytes 47104 | tf_op jit(solution)/shard_map/dot_general | solution.py:50
  70.5 1.0 fusion.5
  71.4 0.7 broadcast_in_dim.15
  72.3 4.6 %all-to-all-start.3 = ((f32[32,16,128]{2,1,0:T(8,128)}), f32[32,16,128]{2,1,0:T(8,128)S(1)}, u32[]{:S(2)}, u32[]{:S(2)}) async-start(f32[32,16,128]{2,1,0:T(8,128)} %broadcast_in_dim.15), calls=%async_computation.3 | async-start | bytes 524288 | tf_op jit(solution)/shard_map/all_to_all | solution.py:151
  77.2 7.6 %multiply_exponential_fusion = f32[1024,4096]{1,0:T(8,128)} fusion(bf16[96,1024]{1,0:T(8,128)(2,1)S(1)} %constant_dynamic-update-slice_fusion.19, bf16[96,4096]{1,0:T(8,128)(2,1)S(1)} %constant_dynamic-update-slice_fusion.25, f32[4096]{0:T(1024)S(1)} %multiply_reduce_fusion, f32[1024]{0:T(1024)S(1)} %multiply_reduce_fusion.2), kind=kOutput, calls=%fused_computation | convolution fusion | flops 817889280 | bytes 17780736 | tf_op jit(solution)/shard_map/dot_general | solution.py:38
  84.8 2.1 %all-to-all-done.3 = f32[32,16,128]{2,1,0:T(8,128)S(1)} async-done(((f32[32,16,128]{2,1,0:T(8,128)}), f32[32,16,128]{2,1,0:T(8,128)S(1)}, u32[]{:S(2)}, u32[]{:S(2)}) %all-to-all-start.3) | async-done | bytes 262176 | tf_op jit(solution)/shard_map/all_to_all | solution.py:151
  87.0 8.2 %shard_map.78 = f32[16,1024]{1,0:T(8,128)S(1)} custom-call(s32[1]{0:T(128)} %constant.64.clone.1.slot_ref, f32[1,1024,4096]{2,1,0:T(8,128)} %inv_ref.3, bf16[32,4096]{1,0:T(8,128)(2,1)S(1)} %pad_maximum_fusion.1.rcat_ref, bf16[16,4096]{1,0:T(8,128)(2,1)S(1)} %get-tuple-element.23.r1_ref), custom_call_target="tpu_custom_call" | custom-call | flops 402653184 | bytes 16777216 | tf_op jit(solution)/shard_map/pallas_call | solution.py:83
  95.3 0.6 bitcast_bitcast_fusion
  95.9 3.4 %all-to-all-start.4 = ((f32[8,16,128]{2,1,0:T(8,128)}), f32[8,16,128]{2,1,0:T(8,128)S(1)}, u32[]{:S(2)}, u32[]{:S(2)}) async-start(f32[8,16,128]{2,1,0:T(8,128)} %bitcast_bitcast_fusion), calls=%async_computation.4 | async-start | bytes 131072 | tf_op jit(solution)/shard_map/all_to_all | solution.py:117
  99.3 0.5 fusion.36
  99.8 4.5 %all-to-all-done.4 = f32[8,16,128]{2,1,0:T(8,128)S(1)} async-done(((f32[8,16,128]{2,1,0:T(8,128)}), f32[8,16,128]{2,1,0:T(8,128)S(1)}, u32[]{:S(2)}, u32[]{:S(2)}) %all-to-all-start.4) | async-done | bytes 65568 | tf_op jit(solution)/shard_map/all_to_all | solution.py:117
  104.2 0.7 broadcast_in_dim.17
  104.9 2.6 %all-to-all-start.5 = ((f32[32,16,128]{2,1,0:T(8,128)}), f32[32,16,128]{2,1,0:T(8,128)S(1)}, u32[]{:S(2)}, u32[]{:S(2)}) async-start(f32[32,16,128]{2,1,0:T(8,128)} %broadcast_in_dim.17), calls=%async_computation.5 | async-start | bytes 524288 | tf_op jit(solution)/shard_map/all_to_all | solution.py:20
  107.5 10.2 %fusion.3 = f32[16,1024]{1,0:T(8,128)S(1)} fusion(f32[16,1024]{1,0:T(8,128)S(1)} %copy-done.1, f32[16,4096]{1,0:T(8,128)S(1)} %bitcast.109, f32[1024,4096]{1,0:T(8,128)} %multiply_exponential_fusion.1, f32[48,1024]{1,0:T(8,128)S(1)} %fusion.36), kind=kOutput, calls=%fused_computation.8 | convolution fusion | flops 402735104 | bytes 17367040 | tf_op jit(solution)/shard_map/dot_general | solution.py:44
  117.7 0.2 copy.23
  117.9 0.2 copy.61
  118.1 0.5 fusion.26
  118.6 0.7 add_add_fusion
  119.2 10.8 %fusion.2 = f32[16,1024]{1,0:T(8,128)} fusion(f32[16,1024]{1,0:T(8,128)S(1)} %fusion.3, f32[1024,4096]{1,0:T(8,128)} %multiply_exponential_fusion, f32[2,8,32,128]{3,2,1,0:T(8,128)S(1)} %bitcast.105, f32[48,1024]{1,0:T(8,128)S(1)} %fusion.26), kind=kOutput, calls=%fused_computation.6 | convolution fusion | flops 402735104 | bytes 17367040 | tf_op jit(solution)/shard_map/dot_general | solution.py:44
  (63 shorter events, 1.4 us)
Async XLA Ops:
  4.0 32.5 %copy-start.3 = (pred[1024]{0:T(1024)(128)(4,1)}, pred[1024]{0:T(1024)(128)(4,1)S(1)}, u32[]{:S(2)}) copy-start(pred[1024]{0:T(1024)(128)(4,1)S(1)} %get-tuple-element.38) | copy-start | bytes 3076
  4.0 32.5 %copy-start.5 = (pred[1024]{0:T(1024)(128)(4,1)}, pred[1024]{0:T(1024)(128)(4,1)S(1)}, u32[]{:S(2)}) copy-start(pred[1024]{0:T(1024)(128)(4,1)S(1)} %get-tuple-element.13) | copy-start | bytes 3076
  9.6 26.9 %all-to-all-start = ((f32[32,48,128]{2,1,0:T(8,128)}), f32[32,48,128]{2,1,0:T(8,128)S(1)}, u32[]{:S(2)}, u32[]{:S(2)}) async-start(f32[32,48,128]{2,1,0:T(8,128)} %broadcast_in_dim.12), calls=%async_computation | async-start | bytes 1572864 | tf_op jit(solution)/shard_map/all_to_all | solution.py:20
  45.0 27.2 %copy-start = (f32[16,1024]{1,0:T(8,128)S(1)}, f32[16,1024]{1,0:T(8,128)}, u32[]{:S(2)}) copy-start(f32[16,1024]{1,0:T(8,128)} %param.6) | copy-start | bytes 196612
  45.7 8.9 %all-to-all-start.1 = ((f32[8,16,128]{2,1,0:T(8,128)}), f32[8,16,128]{2,1,0:T(8,128)S(1)}, u32[]{:S(2)}, u32[]{:S(2)}) async-start(f32[8,16,128]{2,1,0:T(8,128)} %bitcast_bitcast_fusion.1), calls=%async_computation.1 | async-start | bytes 131072 | tf_op jit(solution)/shard_map/all_to_all | solution.py:117
  55.3 13.1 %all-to-all-start.2 = ((f32[32,16,128]{2,1,0:T(8,128)}), f32[32,16,128]{2,1,0:T(8,128)S(1)}, u32[]{:S(2)}, u32[]{:S(2)}) async-start(f32[32,16,128]{2,1,0:T(8,128)} %broadcast_in_dim.14), calls=%async_computation.2 | async-start | bytes 524288 | tf_op jit(solution)/shard_map/all_to_all | solution.py:20
  72.3 14.7 %all-to-all-start.3 = ((f32[32,16,128]{2,1,0:T(8,128)}), f32[32,16,128]{2,1,0:T(8,128)S(1)}, u32[]{:S(2)}, u32[]{:S(2)}) async-start(f32[32,16,128]{2,1,0:T(8,128)} %broadcast_in_dim.15), calls=%async_computation.3 | async-start | bytes 524288 | tf_op jit(solution)/shard_map/all_to_all | solution.py:151
  77.2 22.0 %copy-start.6 = (pred[1024]{0:T(1024)(128)(4,1)S(1)}, pred[1024]{0:T(1024)(128)(4,1)}, u32[]{:S(2)}) copy-start(pred[1024]{0:T(1024)(128)(4,1)} %copy-done.5) | copy-start | bytes 3076
  77.2 30.3 %copy-start.1 = (f32[16,1024]{1,0:T(8,128)S(1)}, f32[16,1024]{1,0:T(8,128)}, u32[]{:S(2)}) copy-start(f32[16,1024]{1,0:T(8,128)} %param.7) | copy-start | bytes 196612
  87.0 31.1 %copy-start.4 = (pred[1024]{0:T(1024)(128)(4,1)S(1)}, pred[1024]{0:T(1024)(128)(4,1)}, u32[]{:S(2)}) copy-start(pred[1024]{0:T(1024)(128)(4,1)} %copy-done.3) | copy-start | bytes 3076
  87.0 31.6 %copy-start.2 = (f32[16,1024]{1,0:T(8,128)S(1)}, f32[16,1024]{1,0:T(8,128)}, u32[]{:S(2)}) copy-start(f32[16,1024]{1,0:T(8,128)} %param.8) | copy-start | bytes 196612
  95.9 8.3 %all-to-all-start.4 = ((f32[8,16,128]{2,1,0:T(8,128)}), f32[8,16,128]{2,1,0:T(8,128)S(1)}, u32[]{:S(2)}, u32[]{:S(2)}) async-start(f32[8,16,128]{2,1,0:T(8,128)} %bitcast_bitcast_fusion), calls=%async_computation.4 | async-start | bytes 131072 | tf_op jit(solution)/shard_map/all_to_all | solution.py:117
  104.9 12.8 %all-to-all-start.5 = ((f32[32,16,128]{2,1,0:T(8,128)}), f32[32,16,128]{2,1,0:T(8,128)S(1)}, u32[]{:S(2)}, u32[]{:S(2)}) async-start(f32[32,16,128]{2,1,0:T(8,128)} %broadcast_in_dim.17), calls=%async_computation.5 | async-start | bytes 524288 | tf_op jit(solution)/shard_map/all_to_all | solution.py:20

commit v21 on v20

--- a/solution.py
+++ b/solution.py
@@ -133,7 +133,14 @@
     chosen0 = chosen[:, :per]
     res1_start = chosen[:rhs, per:]
     pts1_local = chosen[rhs:, per:]
-    gathered = to_block(gather_all(jnp.concatenate([chosen0, pts1_local], axis=0), n_dev), rhs + 2 * feat)
+    src = jnp.concatenate(split3(jnp.concatenate([residual, points], axis=0)), axis=0)
+    partial = lax.dot_general(src, jnp.concatenate([sel0, sel1], axis=1), plain, preferred_element_type=jnp.float32)
+    rows_src = rhs + feat
+    wide = lambda x: jnp.broadcast_to(x[None], (n_dev,) + x.shape)
+    terms = [partial[k * rows_src:(k + 1) * rows_src] for k in range(3)]
+    terms = [wide(jnp.concatenate([t[:, :per], t[rhs:, per:]], axis=0)) for t in terms]
+    sent0 = (terms[0] + terms[1]) + terms[2]
+    gathered = to_block(lax.all_to_all(sent0, ALL, 0, 0, tiled=True), rhs + 2 * feat)
     block_res0 = gathered[:rhs]
     block_pts0 = gathered[rhs:rhs + feat]
     block_pts1 = gathered[rhs + feat:]

time: 131 us -> 131 us (level)
    all_to_all x3 -> x2, waiting for transfers between devices: 12 us -> 1.41 us  [gather_all(): return lax.all_to_all(sent, ALL, 0, 0, tiled=True)]
    all_to_all x0 -> x1, waiting for transfers between devices: none -> 10 us  [body(): lax.all_to_all(sent0, ALL, 0, 0, tiled=True)]
    all_to_all x3 -> x2, starting transfers between devices: 12.8 us -> 5.5 us  [gather_all(): return lax.all_to_all(sent, ALL, 0, 0, tiled=True)]
    all_to_all x0 -> x1, starting transfers between devices: none -> 7.3 us  [body(): lax.all_to_all(sent0, ALL, 0, 0, tiled=True)]
where the time goes in v21:
time: 131 us; the launch traced here: 130 us
  matrix products  41.2 us (31%)
  starting transfers between devices  24.6 us (19%)
  waiting for transfers between devices  23 us (18%)
  Pallas kernels  16.4 us (13%)
  other arithmetic  11.6 us (9%)
  local copies, waits for them, and re-layouts  7.69 us (6%)
  between operations  4.94 us (4%)
    dot_general x3, matrix products, apply_kernel(): lax.dot_general(delta, kernel, (((1,), (1,)), ((), ())), precision=HIGH)  21.9 us
    pallas_call x2, Pallas kernels, solve_rows(): pl.pallas_call(solve_kernel, grid_spec=grid_spec, out_shape=jax.ShapeDtyp...  16.4 us
    dot_general x3, matrix products, kern(): lax.dot_general(left, right, (((0,), (0,)), ((), ())), preferred_element_...  16.4 us
    all_to_all x1, waiting for transfers between devices, body(): lax.all_to_all(sent0, ALL, 0, 0, tiled=True)  10 us
    all_to_all x2, waiting for transfers between devices, distribute(): scattered = lax.all_to_all(pieces, 'grp', 0, 0, tiled=True)  9.44 us
    all_to_all x1, starting transfers between devices, body(): lax.all_to_all(sent0, ALL, 0, 0, tiled=True)  7.3 us
    all_to_all x2, starting transfers between devices, distribute(): scattered = lax.all_to_all(pieces, 'grp', 0, 0, tiled=True)  7.19 us
    all_to_all x2, starting transfers between devices, gather_all(): return lax.all_to_all(sent, ALL, 0, 0, tiled=True)  5.5 us
  transfers between devices with their start and end apart: 6, of which 5 were waited for; matrix products, arithmetic and copies ran while one was open for 25% of the time, Pallas kernels for 0%

profile of v21, /device:TPU:0, one launch (start us, length us, event | category | flops | bytes accessed | tf_op | source)
XLA Modules:
  0.0 129.5 jit_solution(16742596140195112872)
XLA Ops:
  0.6 1.4 %fusion.51 = (s32[1]{0:T(128)}, s32[1]{0:T(128)}) fusion(s32[2]{0:T(128)} %param.10), kind=kLoop, calls=%fused_computation.156 | loop fusion | bytes 16 | tf_op jit(solution)/shard_map/slice | solution.py:126
  2.0 2.0 %convert_bitcast_fusion.1 = (s32[8,128]{1,0:T(8,128)S(1)}, pred[1024]{0:T(1024)(128)(4,1)S(1)}, s32[8,128]{1,0:T(8,128)S(1)}, pred[1024]{0:T(1024)(128)(4,1)S(1)}) fusion(s32[1024]{0:T(1024)} %param.9, s32[]{:T(128)} %bitcast, s32[]{:T(128)} %bitcast.3), kind=kLoop, calls=%fused_computation.144 | loop fusion | flops 4096 | bytes 14344 | tf_op jit(solution)/shard_map/convert
  4.0 0.3 reduce-window.16
  4.6 0.3 reduce-window.24
  5.1 0.8 constant_dynamic-update-slice_fusion.1
  6.0 0.9 multiply_reduce_fusion.3
  6.9 0.9 fusion.10
  7.8 0.3 fusion.6
  8.1 0.9 broadcast_in_dim.12
  9.1 7.3 %all-to-all-start = ((f32[32,48,128]{2,1,0:T(8,128)}), f32[32,48,128]{2,1,0:T(8,128)S(1)}, u32[]{:S(2)}, u32[]{:S(2)}) async-start(f32[32,48,128]{2,1,0:T(8,128)} %broadcast_in_dim.12), calls=%async_computation | async-start | bytes 1572864 | tf_op jit(solution)/shard_map/all_to_all | solution.py:143
  20.3 0.5 multiply_reduce_fusion.4
  20.9 0.8 constant_dynamic-update-slice_fusion.18
  21.7 0.8 constant_dynamic-update-slice_fusion.17
  22.6 0.8 constant_dynamic-update-slice_fusion.16
  23.4 0.8 constant_dynamic-update-slice_fusion.15
  24.2 0.9 constant_dynamic-update-slice_fusion.14
  25.1 0.9 constant_dynamic-update-slice_fusion.13
  26.0 10.0 %all-to-all-done = f32[32,48,128]{2,1,0:T(8,128)S(1)} async-done(((f32[32,48,128]{2,1,0:T(8,128)}), f32[32,48,128]{2,1,0:T(8,128)S(1)}, u32[]{:S(2)}, u32[]{:S(2)}) %all-to-all-start) | async-done | bytes 786464 | tf_op jit(solution)/shard_map/all_to_all | solution.py:143
  36.3 8.2 %shard_map.77 = f32[16,1024]{1,0:T(8,128)S(1)} custom-call(s32[1]{0:T(128)} %constant.64.clone.1.slot_ref, f32[1,1024,4096]{2,1,0:T(8,128)} %inv_ref.3, bf16[32,4096]{1,0:T(8,128)(2,1)S(1)} %pad_maximum_fusion.rcat_ref, bf16[16,4096]{1,0:T(8,128)(2,1)S(1)} %get-tuple-element.28.r1_ref), custom_call_target="tpu_custom_call" | custom-call | flops 402653184 | bytes 16777216 | tf_op jit(solution)/shard_map/pallas_call | solution.py:83
  44.5 0.6 bitcast_bitcast_fusion.1
  45.2 3.8 %all-to-all-start.1 = ((f32[8,16,128]{2,1,0:T(8,128)}), f32[8,16,128]{2,1,0:T(8,128)S(1)}, u32[]{:S(2)}, u32[]{:S(2)}) async-start(f32[8,16,128]{2,1,0:T(8,128)} %bitcast_bitcast_fusion.1), calls=%async_computation.1 | async-start | bytes 131072 | tf_op jit(solution)/shard_map/all_to_all | solution.py:117
  49.0 5.0 %all-to-all-done.1 = f32[8,16,128]{2,1,0:T(8,128)S(1)} async-done(((f32[8,16,128]{2,1,0:T(8,128)}), f32[8,16,128]{2,1,0:T(8,128)S(1)}, u32[]{:S(2)}, u32[]{:S(2)}) %all-to-all-start.1) | async-done | bytes 65568 | tf_op jit(solution)/shard_map/all_to_all | solution.py:117
  54.0 0.7 broadcast_in_dim.14
  54.7 2.9 %all-to-all-start.2 = ((f32[32,16,128]{2,1,0:T(8,128)}), f32[32,16,128]{2,1,0:T(8,128)S(1)}, u32[]{:S(2)}, u32[]{:S(2)}) async-start(f32[32,16,128]{2,1,0:T(8,128)} %broadcast_in_dim.14), calls=%async_computation.2 | async-start | bytes 524288 | tf_op jit(solution)/shard_map/all_to_all | solution.py:20
  57.7 7.6 %multiply_exponential_fusion.1 = f32[1024,4096]{1,0:T(8,128)} fusion(bf16[96,1024]{1,0:T(8,128)(2,1)S(1)} %constant_dynamic-update-slice_fusion.13, bf16[96,4096]{1,0:T(8,128)(2,1)S(1)} %constant_dynamic-update-slice_fusion.8, f32[4096]{0:T(1024)S(1)} %bitcast.113, f32[1024]{0:T(1024)S(1)} %get-tuple-element.39), kind=kOutput, calls=%fused_computation.1 | convolution fusion | flops 817889280 | bytes 17780736 | tf_op jit(solution)/shard_map/dot_general | solution.py:38
  65.3 1.2 fusion.1
  66.5 1.4 %all-to-all-done.2 = f32[32,16,128]{2,1,0:T(8,128)S(1)} async-done(((f32[32,16,128]{2,1,0:T(8,128)}), f32[32,16,128]{2,1,0:T(8,128)S(1)}, u32[]{:S(2)}, u32[]{:S(2)}) %all-to-all-start.2) | async-done | bytes 262176 | tf_op jit(solution)/shard_map/all_to_all | solution.py:20
  67.9 0.2 copy.18
  68.0 0.2 copy.62
  68.2 1.7 %fusion.4 = f32[48,128]{1,0:T(8,128)S(1)} fusion(bf16[16,128]{1,0:T(8,128)(2,1)S(1)} %get-tuple-element.27, bf16[16,128]{1,0:T(8,128)(2,1)S(1)} %get-tuple-element.26, bf16[16,128]{1,0:T(8,128)(2,1)S(1)} %get-tuple-element.25, s32[1024]{0:T(1024)S(1)} %add_bitcast_fusion, pred[1024]{0:T(1024)(128)(4,1)} %copy-done.3, s32[1024]{0:T(1024)S(1)} %add_bitcast_fusion.1, ...), kind=kOutput, calls=%fused_computation.10 | convolution fusion | flops 35704832 | bytes 47104 | tf_op jit(solution)/shard_map/dot_general | solution.py:50
  69.9 1.0 fusion.5
  70.9 0.7 broadcast_in_dim.15
  71.8 4.6 %all-to-all-start.3 = ((f32[32,16,128]{2,1,0:T(8,128)}), f32[32,16,128]{2,1,0:T(8,128)S(1)}, u32[]{:S(2)}, u32[]{:S(2)}) async-start(f32[32,16,128]{2,1,0:T(8,128)} %broadcast_in_dim.15), calls=%async_computation.3 | async-start | bytes 524288 | tf_op jit(solution)/shard_map/all_to_all | solution.py:158
  76.7 7.6 %multiply_exponential_fusion = f32[1024,4096]{1,0:T(8,128)} fusion(bf16[96,1024]{1,0:T(8,128)(2,1)S(1)} %constant_dynamic-update-slice_fusion.19, bf16[96,4096]{1,0:T(8,128)(2,1)S(1)} %constant_dynamic-update-slice_fusion.25, f32[4096]{0:T(1024)S(1)} %multiply_reduce_fusion, f32[1024]{0:T(1024)S(1)} %multiply_reduce_fusion.2), kind=kOutput, calls=%fused_computation | convolution fusion | flops 817889280 | bytes 17780736 | tf_op jit(solution)/shard_map/dot_general | solution.py:38
  84.3 2.1 %all-to-all-done.3 = f32[32,16,128]{2,1,0:T(8,128)S(1)} async-done(((f32[32,16,128]{2,1,0:T(8,128)}), f32[32,16,128]{2,1,0:T(8,128)S(1)}, u32[]{:S(2)}, u32[]{:S(2)}) %all-to-all-start.3) | async-done | bytes 262176 | tf_op jit(solution)/shard_map/all_to_all | solution.py:158
  86.5 8.2 %shard_map.78 = f32[16,1024]{1,0:T(8,128)S(1)} custom-call(s32[1]{0:T(128)} %constant.64.clone.1.slot_ref, f32[1,1024,4096]{2,1,0:T(8,128)} %inv_ref.3, bf16[32,4096]{1,0:T(8,128)(2,1)S(1)} %pad_maximum_fusion.1.rcat_ref, bf16[16,4096]{1,0:T(8,128)(2,1)S(1)} %get-tuple-element.23.r1_ref), custom_call_target="tpu_custom_call" | custom-call | flops 402653184 | bytes 16777216 | tf_op jit(solution)/shard_map/pallas_call | solution.py:83
  94.8 0.6 bitcast_bitcast_fusion
  95.4 3.4 %all-to-all-start.4 = ((f32[8,16,128]{2,1,0:T(8,128)}), f32[8,16,128]{2,1,0:T(8,128)S(1)}, u32[]{:S(2)}, u32[]{:S(2)}) async-start(f32[8,16,128]{2,1,0:T(8,128)} %bitcast_bitcast_fusion), calls=%async_computation.4 | async-start | bytes 131072 | tf_op jit(solution)/shard_map/all_to_all | solution.py:117
  98.8 0.5 fusion.37
  99.3 4.5 %all-to-all-done.4 = f32[8,16,128]{2,1,0:T(8,128)S(1)} async-done(((f32[8,16,128]{2,1,0:T(8,128)}), f32[8,16,128]{2,1,0:T(8,128)S(1)}, u32[]{:S(2)}, u32[]{:S(2)}) %all-to-all-start.4) | async-done | bytes 65568 | tf_op jit(solution)/shard_map/all_to_all | solution.py:117
  103.7 0.7 broadcast_in_dim.17
  104.4 2.6 %all-to-all-start.5 = ((f32[32,16,128]{2,1,0:T(8,128)}), f32[32,16,128]{2,1,0:T(8,128)S(1)}, u32[]{:S(2)}, u32[]{:S(2)}) async-start(f32[32,16,128]{2,1,0:T(8,128)} %broadcast_in_dim.17), calls=%async_computation.5 | async-start | bytes 524288 | tf_op jit(solution)/shard_map/all_to_all | solution.py:20
  107.0 10.2 %fusion.3 = f32[16,1024]{1,0:T(8,128)S(1)} fusion(f32[16,1024]{1,0:T(8,128)S(1)} %copy-done.1, f32[16,4096]{1,0:T(8,128)S(1)} %bitcast.109, f32[1024,4096]{1,0:T(8,128)} %multiply_exponential_fusion.1, f32[48,1024]{1,0:T(8,128)S(1)} %fusion.37), kind=kOutput, calls=%fused_computation.8 | convolution fusion | flops 402735104 | bytes 17367040 | tf_op jit(solution)/shard_map/dot_general | solution.py:44
  117.2 0.2 copy.23
  117.4 0.2 copy.61
  117.6 0.5 fusion.27
  118.1 0.7 add_add_fusion
  118.7 10.8 %fusion.2 = f32[16,1024]{1,0:T(8,128)} fusion(f32[16,1024]{1,0:T(8,128)S(1)} %fusion.3, f32[1024,4096]{1,0:T(8,128)} %multiply_exponential_fusion, f32[2,8,32,128]{3,2,1,0:T(8,128)S(1)} %bitcast.105, f32[48,1024]{1,0:T(8,128)S(1)} %fusion.27), kind=kOutput, calls=%fused_computation.6 | convolution fusion | flops 402735104 | bytes 17367040 | tf_op jit(solution)/shard_map/dot_general | solution.py:44
  (64 shorter events, 1.5 us)
Async XLA Ops:
  4.0 3.8 %copy-start.3 = (pred[1024]{0:T(1024)(128)(4,1)}, pred[1024]{0:T(1024)(128)(4,1)S(1)}, u32[]{:S(2)}) copy-start(pred[1024]{0:T(1024)(128)(4,1)S(1)} %get-tuple-element.42) | copy-start | bytes 3076
  4.0 3.8 %copy-start.5 = (pred[1024]{0:T(1024)(128)(4,1)}, pred[1024]{0:T(1024)(128)(4,1)S(1)}, u32[]{:S(2)}) copy-start(pred[1024]{0:T(1024)(128)(4,1)S(1)} %get-tuple-element.13) | copy-start | bytes 3076
  9.1 26.9 %all-to-all-start = ((f32[32,48,128]{2,1,0:T(8,128)}), f32[32,48,128]{2,1,0:T(8,128)S(1)}, u32[]{:S(2)}, u32[]{:S(2)}) async-start(f32[32,48,128]{2,1,0:T(8,128)} %broadcast_in_dim.12), calls=%async_computation | async-start | bytes 1572864 | tf_op jit(solution)/shard_map/all_to_all | solution.py:143
  44.5 27.2 %copy-start = (f32[16,1024]{1,0:T(8,128)S(1)}, f32[16,1024]{1,0:T(8,128)}, u32[]{:S(2)}) copy-start(f32[16,1024]{1,0:T(8,128)} %param.6) | copy-start | bytes 196612
  45.2 8.9 %all-to-all-start.1 = ((f32[8,16,128]{2,1,0:T(8,128)}), f32[8,16,128]{2,1,0:T(8,128)S(1)}, u32[]{:S(2)}, u32[]{:S(2)}) async-start(f32[8,16,128]{2,1,0:T(8,128)} %bitcast_bitcast_fusion.1), calls=%async_computation.1 | async-start | bytes 131072 | tf_op jit(solution)/shard_map/all_to_all | solution.py:117
  54.7 13.1 %all-to-all-start.2 = ((f32[32,16,128]{2,1,0:T(8,128)}), f32[32,16,128]{2,1,0:T(8,128)S(1)}, u32[]{:S(2)}, u32[]{:S(2)}) async-start(f32[32,16,128]{2,1,0:T(8,128)} %broadcast_in_dim.14), calls=%async_computation.2 | async-start | bytes 524288 | tf_op jit(solution)/shard_map/all_to_all | solution.py:20
  71.8 14.7 %all-to-all-start.3 = ((f32[32,16,128]{2,1,0:T(8,128)}), f32[32,16,128]{2,1,0:T(8,128)S(1)}, u32[]{:S(2)}, u32[]{:S(2)}) async-start(f32[32,16,128]{2,1,0:T(8,128)} %broadcast_in_dim.15), calls=%async_computation.3 | async-start | bytes 524288 | tf_op jit(solution)/shard_map/all_to_all | solution.py:158
  76.7 22.0 %copy-start.6 = (pred[1024]{0:T(1024)(128)(4,1)S(1)}, pred[1024]{0:T(1024)(128)(4,1)}, u32[]{:S(2)}) copy-start(pred[1024]{0:T(1024)(128)(4,1)} %copy-done.5) | copy-start | bytes 3076
  76.7 30.3 %copy-start.1 = (f32[16,1024]{1,0:T(8,128)S(1)}, f32[16,1024]{1,0:T(8,128)}, u32[]{:S(2)}) copy-start(f32[16,1024]{1,0:T(8,128)} %param.7) | copy-start | bytes 196612
  86.5 31.1 %copy-start.4 = (pred[1024]{0:T(1024)(128)(4,1)S(1)}, pred[1024]{0:T(1024)(128)(4,1)}, u32[]{:S(2)}) copy-start(pred[1024]{0:T(1024)(128)(4,1)} %copy-done.3) | copy-start | bytes 3076
  86.5 31.6 %copy-start.2 = (f32[16,1024]{1,0:T(8,128)S(1)}, f32[16,1024]{1,0:T(8,128)}, u32[]{:S(2)}) copy-start(f32[16,1024]{1,0:T(8,128)} %param.8) | copy-start | bytes 196612
  95.4 8.3 %all-to-all-start.4 = ((f32[8,16,128]{2,1,0:T(8,128)}), f32[8,16,128]{2,1,0:T(8,128)S(1)}, u32[]{:S(2)}, u32[]{:S(2)}) async-start(f32[8,16,128]{2,1,0:T(8,128)} %bitcast_bitcast_fusion), calls=%async_computation.4 | async-start | bytes 131072 | tf_op jit(solution)/shard_map/all_to_all | solution.py:117
  104.4 12.8 %all-to-all-start.5 = ((f32[32,16,128]{2,1,0:T(8,128)}), f32[32,16,128]{2,1,0:T(8,128)S(1)}, u32[]{:S(2)}, u32[]{:S(2)}) async-start(f32[32,16,128]{2,1,0:T(8,128)} %broadcast_in_dim.17), calls=%async_computation.5 | async-start | bytes 524288 | tf_op jit(solution)/shard_map/all_to_all | solution.py:20

commit v22 on v21

--- a/solution.py
+++ b/solution.py
@@ -115,8 +115,8 @@
         owner = block_id // slots
         pieces = jnp.transpose(solved.reshape(rhs, n_grp, per), (1, 0, 2))
         scattered = lax.all_to_all(pieces, "grp", 0, 0, tiled=True)
-        piece = lax.dynamic_index_in_dim(scattered, owner, 0, keepdims=False)
-        pieces_all = gather_all(piece, n_dev)
+        sent = scattered[jnp.full((n_dev,), owner, dtype=jnp.int32)]
+        pieces_all = lax.all_to_all(sent, ALL, 0, 0, tiled=True)
         pieces_all = jnp.transpose(pieces_all.reshape(n_grp, n_mem, rhs, per), (2, 1, 0, 3))
         return pieces_all.reshape(rhs, B)
 

time: 131 us -> 132 us (level)
    gather x0 -> x2, local copies, waits for them, and re-layouts: none -> 2.68 us  [distribute(): sent = scattered[jnp.full((n_dev,), owner, dtype=jnp.int32)]]
    broadcast_in_dim x4 -> x2, local copies, waits for them, and re-layouts: 1.44 us -> 0.01 us  [distribute(): sent = scattered[jnp.full((n_dev,), owner, dtype=jnp.int32)]]
  transfers between devices with their start and end apart: 6 -> 6, of which waited for: 5 -> 5; matrix products, arithmetic and copies ran while one was open for 25% -> 26% of each run, Pallas kernels for 0% -> 0%
where the time goes in v22:
time: 132 us; the launch traced here: 131 us
  matrix products  41.2 us (31%)
  starting transfers between devices  24.6 us (19%)
  waiting for transfers between devices  22.3 us (17%)
  Pallas kernels  16.4 us (12%)
  other arithmetic  12.2 us (9%)
  local copies, waits for them, and re-layouts  8.87 us (7%)
  between operations  5.02 us (4%)
    dot_general x3, matrix products, apply_kernel(): lax.dot_general(delta, kernel, (((1,), (1,)), ((), ())), precision=HIGH)  21.9 us
    pallas_call x2, Pallas kernels, solve_rows(): pl.pallas_call(solve_kernel, grid_spec=grid_spec, out_shape=jax.ShapeDtyp...  16.4 us
    dot_general x3, matrix products, kern(): lax.dot_general(left, right, (((0,), (0,)), ((), ())), preferred_element_...  16.4 us
    all_to_all x2, waiting for transfers between devices, distribute(): scattered = lax.all_to_all(pieces, 'grp', 0, 0, tiled=True)  9.44 us
    all_to_all x1, waiting for transfers between devices, body(): lax.all_to_all(sent0, ALL, 0, 0, tiled=True)  9.36 us
    all_to_all x1, starting transfers between devices, body(): lax.all_to_all(sent0, ALL, 0, 0, tiled=True)  7.3 us
    all_to_all x2, starting transfers between devices, distribute(): scattered = lax.all_to_all(pieces, 'grp', 0, 0, tiled=True)  7.19 us
    all_to_all x2, starting transfers between devices, distribute(): pieces_all = lax.all_to_all(sent, ALL, 0, 0, tiled=True)  5.5 us
  transfers between devices with their start and end apart: 6, of which 5 were waited for; matrix products, arithmetic and copies ran while one was open for 26% of the time, Pallas kernels for 0%

profile of v22, /device:TPU:0, one launch (start us, length us, event | category | flops | bytes accessed | tf_op | source)
XLA Modules:
  0.0 130.7 jit_solution(8061503575196997124)
XLA Ops:
  0.6 1.3 %fusion.51 = (s32[1]{0:T(128)}, s32[1]{0:T(128)}) fusion(s32[2]{0:T(128)} %param.10), kind=kLoop, calls=%fused_computation.158 | loop fusion | bytes 16 | tf_op jit(solution)/shard_map/slice | solution.py:126
  1.9 2.0 %convert_bitcast_fusion.1 = (s32[8,128]{1,0:T(8,128)S(1)}, pred[1024]{0:T(1024)(128)(4,1)S(1)}, s32[8,128]{1,0:T(8,128)S(1)}, pred[1024]{0:T(1024)(128)(4,1)S(1)}) fusion(s32[1024]{0:T(1024)} %param.9, s32[]{:T(128)} %bitcast, s32[]{:T(128)} %bitcast.3), kind=kLoop, calls=%fused_computation.146 | loop fusion | flops 4096 | bytes 14344 | tf_op jit(solution)/shard_map/convert
  3.9 0.3 reduce-window.16
  4.5 0.3 reduce-window.24
  5.1 0.8 constant_dynamic-update-slice_fusion.1
  5.9 0.9 multiply_reduce_fusion.3
  6.8 0.9 fusion.10
  7.8 0.3 fusion.6
  8.1 0.9 broadcast_in_dim.8
  9.0 7.3 %all-to-all-start = ((f32[32,48,128]{2,1,0:T(8,128)}), f32[32,48,128]{2,1,0:T(8,128)S(1)}, u32[]{:S(2)}, u32[]{:S(2)}) async-start(f32[32,48,128]{2,1,0:T(8,128)} %broadcast_in_dim.8), calls=%async_computation | async-start | bytes 1572864 | tf_op jit(solution)/shard_map/all_to_all | solution.py:143
  20.4 0.6 pad_clamp_fusion
  21.0 0.5 multiply_reduce_fusion.4
  21.5 0.8 constant_dynamic-update-slice_fusion.18
  22.3 0.8 constant_dynamic-update-slice_fusion.17
  23.2 0.8 constant_dynamic-update-slice_fusion.16
  24.0 0.8 constant_dynamic-update-slice_fusion.15
  24.9 0.9 constant_dynamic-update-slice_fusion.14
  25.7 0.9 constant_dynamic-update-slice_fusion.13
  26.6 9.4 %all-to-all-done = f32[32,48,128]{2,1,0:T(8,128)S(1)} async-done(((f32[32,48,128]{2,1,0:T(8,128)}), f32[32,48,128]{2,1,0:T(8,128)S(1)}, u32[]{:S(2)}, u32[]{:S(2)}) %all-to-all-start) | async-done | bytes 786464 | tf_op jit(solution)/shard_map/all_to_all | solution.py:143
  36.3 8.2 %shard_map.77 = f32[16,1024]{1,0:T(8,128)S(1)} custom-call(s32[1]{0:T(128)} %constant.60.clone.1.slot_ref, f32[1,1024,4096]{2,1,0:T(8,128)} %inv_ref.3, bf16[32,4096]{1,0:T(8,128)(2,1)S(1)} %pad_maximum_fusion.rcat_ref, bf16[16,4096]{1,0:T(8,128)(2,1)S(1)} %get-tuple-element.28.r1_ref), custom_call_target="tpu_custom_call" | custom-call | flops 402653184 | bytes 16777216 | tf_op jit(solution)/shard_map/pallas_call | solution.py:83
  44.5 0.6 bitcast_bitcast_fusion.1
  45.1 3.8 %all-to-all-start.1 = ((f32[8,16,128]{2,1,0:T(8,128)}), f32[8,16,128]{2,1,0:T(8,128)S(1)}, u32[]{:S(2)}, u32[]{:S(2)}) async-start(f32[8,16,128]{2,1,0:T(8,128)} %bitcast_bitcast_fusion.1), calls=%async_computation.1 | async-start | bytes 131072 | tf_op jit(solution)/shard_map/all_to_all | solution.py:117
  49.0 5.0 %all-to-all-done.1 = f32[8,16,128]{2,1,0:T(8,128)S(1)} async-done(((f32[8,16,128]{2,1,0:T(8,128)}), f32[8,16,128]{2,1,0:T(8,128)S(1)}, u32[]{:S(2)}, u32[]{:S(2)}) %all-to-all-start.1) | async-done | bytes 65568 | tf_op jit(solution)/shard_map/all_to_all | solution.py:117
  54.0 1.3 gather_fusion
  55.3 2.9 %all-to-all-start.2 = ((f32[32,16,128]{2,1,0:T(8,128)}), f32[32,16,128]{2,1,0:T(8,128)S(1)}, u32[]{:S(2)}, u32[]{:S(2)}) async-start(f32[32,16,128]{2,1,0:T(8,128)} %gather_fusion), calls=%async_computation.2 | async-start | bytes 524288 | tf_op jit(solution)/shard_map/all_to_all | solution.py:119
  58.2 7.6 %multiply_exponential_fusion.1 = f32[1024,4096]{1,0:T(8,128)} fusion(bf16[96,1024]{1,0:T(8,128)(2,1)S(1)} %constant_dynamic-update-slice_fusion.13, bf16[96,4096]{1,0:T(8,128)(2,1)S(1)} %constant_dynamic-update-slice_fusion.8, f32[4096]{0:T(1024)S(1)} %bitcast.107, f32[1024]{0:T(1024)S(1)} %get-tuple-element.39), kind=kOutput, calls=%fused_computation.3 | convolution fusion | flops 817889280 | bytes 17780736 | tf_op jit(solution)/shard_map/dot_general | solution.py:38
  65.8 1.2 fusion.1
  67.0 1.4 %all-to-all-done.2 = f32[32,16,128]{2,1,0:T(8,128)S(1)} async-done(((f32[32,16,128]{2,1,0:T(8,128)}), f32[32,16,128]{2,1,0:T(8,128)S(1)}, u32[]{:S(2)}, u32[]{:S(2)}) %all-to-all-start.2) | async-done | bytes 262176 | tf_op jit(solution)/shard_map/all_to_all | solution.py:119
  68.4 0.2 copy.20
  68.5 0.2 copy.64
  68.7 1.7 %fusion.4 = f32[48,128]{1,0:T(8,128)S(1)} fusion(bf16[16,128]{1,0:T(8,128)(2,1)S(1)} %get-tuple-element.27, bf16[16,128]{1,0:T(8,128)(2,1)S(1)} %get-tuple-element.26, bf16[16,128]{1,0:T(8,128)(2,1)S(1)} %get-tuple-element.25, s32[1024]{0:T(1024)S(1)} %add_bitcast_fusion, pred[1024]{0:T(1024)(128)(4,1)} %copy-done.3, s32[1024]{0:T(1024)S(1)} %add_bitcast_fusion.1, ...), kind=kOutput, calls=%fused_computation.12 | convolution fusion | flops 35704832 | bytes 47104 | tf_op jit(solution)/shard_map/dot_general | solution.py:50
  70.4 1.0 fusion.5
  71.4 0.7 broadcast_in_dim.10
  72.3 4.6 %all-to-all-start.3 = ((f32[32,16,128]{2,1,0:T(8,128)}), f32[32,16,128]{2,1,0:T(8,128)S(1)}, u32[]{:S(2)}, u32[]{:S(2)}) async-start(f32[32,16,128]{2,1,0:T(8,128)} %broadcast_in_dim.10), calls=%async_computation.3 | async-start | bytes 524288 | tf_op jit(solution)/shard_map/all_to_all | solution.py:158
  77.2 7.6 %multiply_exponential_fusion = f32[1024,4096]{1,0:T(8,128)} fusion(bf16[96,1024]{1,0:T(8,128)(2,1)S(1)} %constant_dynamic-update-slice_fusion.19, bf16[96,4096]{1,0:T(8,128)(2,1)S(1)} %constant_dynamic-update-slice_fusion.25, f32[4096]{0:T(1024)S(1)} %multiply_reduce_fusion, f32[1024]{0:T(1024)S(1)} %multiply_reduce_fusion.2), kind=kOutput, calls=%fused_computation.2 | convolution fusion | flops 817889280 | bytes 17780736 | tf_op jit(solution)/shard_map/dot_general | solution.py:38
  84.8 2.1 %all-to-all-done.3 = f32[32,16,128]{2,1,0:T(8,128)S(1)} async-done(((f32[32,16,128]{2,1,0:T(8,128)}), f32[32,16,128]{2,1,0:T(8,128)S(1)}, u32[]{:S(2)}, u32[]{:S(2)}) %all-to-all-start.3) | async-done | bytes 262176 | tf_op jit(solution)/shard_map/all_to_all | solution.py:158
  87.0 8.2 %shard_map.78 = f32[16,1024]{1,0:T(8,128)S(1)} custom-call(s32[1]{0:T(128)} %constant.60.clone.1.slot_ref, f32[1,1024,4096]{2,1,0:T(8,128)} %inv_ref.3, bf16[32,4096]{1,0:T(8,128)(2,1)S(1)} %pad_maximum_fusion.1.rcat_ref, bf16[16,4096]{1,0:T(8,128)(2,1)S(1)} %get-tuple-element.23.r1_ref), custom_call_target="tpu_custom_call" | custom-call | flops 402653184 | bytes 16777216 | tf_op jit(solution)/shard_map/pallas_call | solution.py:83
  95.3 0.6 bitcast_bitcast_fusion
  95.9 3.4 %all-to-all-start.4 = ((f32[8,16,128]{2,1,0:T(8,128)}), f32[8,16,128]{2,1,0:T(8,128)S(1)}, u32[]{:S(2)}, u32[]{:S(2)}) async-start(f32[8,16,128]{2,1,0:T(8,128)} %bitcast_bitcast_fusion), calls=%async_computation.4 | async-start | bytes 131072 | tf_op jit(solution)/shard_map/all_to_all | solution.py:117
  99.3 0.5 fusion.37
  99.8 4.5 %all-to-all-done.4 = f32[8,16,128]{2,1,0:T(8,128)S(1)} async-done(((f32[8,16,128]{2,1,0:T(8,128)}), f32[8,16,128]{2,1,0:T(8,128)S(1)}, u32[]{:S(2)}, u32[]{:S(2)}) %all-to-all-start.4) | async-done | bytes 65568 | tf_op jit(solution)/shard_map/all_to_all | solution.py:117
  104.2 1.4 %gather_fusion.1 = f32[32,16,128]{2,1,0:T(8,128)} fusion(f32[8,16,128]{2,1,0:T(8,128)S(1)} %all-to-all-done.4, s32[1024]{0:T(1024)} %pad_clamp_fusion), kind=kCustom, calls=%fused_computation.1 | custom fusion | bytes 524416 | tf_op jit(solution)/shard_map/gather | solution.py:118
  105.6 2.6 %all-to-all-start.5 = ((f32[32,16,128]{2,1,0:T(8,128)}), f32[32,16,128]{2,1,0:T(8,128)S(1)}, u32[]{:S(2)}, u32[]{:S(2)}) async-start(f32[32,16,128]{2,1,0:T(8,128)} %gather_fusion.1), calls=%async_computation.5 | async-start | bytes 524288 | tf_op jit(solution)/shard_map/all_to_all | solution.py:119
  108.2 10.2 %fusion.3 = f32[16,1024]{1,0:T(8,128)S(1)} fusion(f32[16,1024]{1,0:T(8,128)S(1)} %copy-done.1, f32[16,4096]{1,0:T(8,128)S(1)} %bitcast.103, f32[1024,4096]{1,0:T(8,128)} %multiply_exponential_fusion.1, f32[48,1024]{1,0:T(8,128)S(1)} %fusion.37), kind=kOutput, calls=%fused_computation.10 | convolution fusion | flops 402735104 | bytes 17367040 | tf_op jit(solution)/shard_map/dot_general | solution.py:44
  118.6 0.2 copy.63
  118.8 0.5 fusion.27
  119.3 0.7 add_add_fusion
  119.9 10.8 %fusion.2 = f32[16,1024]{1,0:T(8,128)} fusion(f32[16,1024]{1,0:T(8,128)S(1)} %fusion.3, f32[1024,4096]{1,0:T(8,128)} %multiply_exponential_fusion, f32[2,8,32,128]{3,2,1,0:T(8,128)S(1)} %bitcast.99, f32[48,1024]{1,0:T(8,128)S(1)} %fusion.27), kind=kOutput, calls=%fused_computation.8 | convolution fusion | flops 402735104 | bytes 17367040 | tf_op jit(solution)/shard_map/dot_general | solution.py:44
  (66 shorter events, 1.6 us)
Async XLA Ops:
  3.9 3.8 %copy-start.3 = (pred[1024]{0:T(1024)(128)(4,1)}, pred[1024]{0:T(1024)(128)(4,1)S(1)}, u32[]{:S(2)}) copy-start(pred[1024]{0:T(1024)(128)(4,1)S(1)} %get-tuple-element.42) | copy-start | bytes 3076
  3.9 3.8 %copy-start.5 = (pred[1024]{0:T(1024)(128)(4,1)}, pred[1024]{0:T(1024)(128)(4,1)S(1)}, u32[]{:S(2)}) copy-start(pred[1024]{0:T(1024)(128)(4,1)S(1)} %get-tuple-element.13) | copy-start | bytes 3076
  9.0 26.9 %all-to-all-start = ((f32[32,48,128]{2,1,0:T(8,128)}), f32[32,48,128]{2,1,0:T(8,128)S(1)}, u32[]{:S(2)}, u32[]{:S(2)}) async-start(f32[32,48,128]{2,1,0:T(8,128)} %broadcast_in_dim.8), calls=%async_computation | async-start | bytes 1572864 | tf_op jit(solution)/shard_map/all_to_all | solution.py:143
  44.5 27.8 %copy-start = (f32[16,1024]{1,0:T(8,128)S(1)}, f32[16,1024]{1,0:T(8,128)}, u32[]{:S(2)}) copy-start(f32[16,1024]{1,0:T(8,128)} %param.6) | copy-start | bytes 196612
  45.1 8.9 %all-to-all-start.1 = ((f32[8,16,128]{2,1,0:T(8,128)}), f32[8,16,128]{2,1,0:T(8,128)S(1)}, u32[]{:S(2)}, u32[]{:S(2)}) async-start(f32[8,16,128]{2,1,0:T(8,128)} %bitcast_bitcast_fusion.1), calls=%async_computation.1 | async-start | bytes 131072 | tf_op jit(solution)/shard_map/all_to_all | solution.py:117
  55.3 13.1 %all-to-all-start.2 = ((f32[32,16,128]{2,1,0:T(8,128)}), f32[32,16,128]{2,1,0:T(8,128)S(1)}, u32[]{:S(2)}, u32[]{:S(2)}) async-start(f32[32,16,128]{2,1,0:T(8,128)} %gather_fusion), calls=%async_computation.2 | async-start | bytes 524288 | tf_op jit(solution)/shard_map/all_to_all | solution.py:119
  72.3 14.7 %all-to-all-start.3 = ((f32[32,16,128]{2,1,0:T(8,128)}), f32[32,16,128]{2,1,0:T(8,128)S(1)}, u32[]{:S(2)}, u32[]{:S(2)}) async-start(f32[32,16,128]{2,1,0:T(8,128)} %broadcast_in_dim.10), calls=%async_computation.3 | async-start | bytes 524288 | tf_op jit(solution)/shard_map/all_to_all | solution.py:158
  77.2 22.0 %copy-start.6 = (pred[1024]{0:T(1024)(128)(4,1)S(1)}, pred[1024]{0:T(1024)(128)(4,1)}, u32[]{:S(2)}) copy-start(pred[1024]{0:T(1024)(128)(4,1)} %copy-done.5) | copy-start | bytes 3076
  77.2 31.0 %copy-start.1 = (f32[16,1024]{1,0:T(8,128)S(1)}, f32[16,1024]{1,0:T(8,128)}, u32[]{:S(2)}) copy-start(f32[16,1024]{1,0:T(8,128)} %param.7) | copy-start | bytes 196612
  87.0 31.7 %copy-start.4 = (pred[1024]{0:T(1024)(128)(4,1)S(1)}, pred[1024]{0:T(1024)(128)(4,1)}, u32[]{:S(2)}) copy-start(pred[1024]{0:T(1024)(128)(4,1)} %copy-done.3) | copy-start | bytes 3076
  87.0 32.2 %copy-start.2 = (f32[16,1024]{1,0:T(8,128)S(1)}, f32[16,1024]{1,0:T(8,128)}, u32[]{:S(2)}) copy-start(f32[16,1024]{1,0:T(8,128)} %param.8) | copy-start | bytes 196612
  95.9 8.3 %all-to-all-start.4 = ((f32[8,16,128]{2,1,0:T(8,128)}), f32[8,16,128]{2,1,0:T(8,128)S(1)}, u32[]{:S(2)}, u32[]{:S(2)}) async-start(f32[8,16,128]{2,1,0:T(8,128)} %bitcast_bitcast_fusion), calls=%async_computation.4 | async-start | bytes 131072 | tf_op jit(solution)/shard_map/all_to_all | solution.py:117
  105.6 12.8 %all-to-all-start.5 = ((f32[32,16,128]{2,1,0:T(8,128)}), f32[32,16,128]{2,1,0:T(8,128)S(1)}, u32[]{:S(2)}, u32[]{:S(2)}) async-start(f32[32,16,128]{2,1,0:T(8,128)} %gather_fusion.1), calls=%async_computation.5 | async-start | bytes 524288 | tf_op jit(solution)/shard_map/all_to_all | solution.py:119
